TPU v7x, 32 devices: a whole 2x2x4 slice. The times are simulated.
32 devices in a mesh: groups: 2 (over y), ctx: 4 (over z), head: 4 (over x, core).
Axes of the slice: x: 2, y: 2, z: 4, core: 2. Of those that a mesh axis runs over, the one named last changes fastest.
Arguments:
- q_block: bfloat16 [2048, 8192], P(('groups', 'ctx'), 'head'), parts along dimension 0, may hold values from -6 to 6
- kv_block: bfloat16 [2, 2048, 1024], P(None, ('groups', 'ctx'), 'head'), parts along dimension 1, may hold values from -6 to 6
- anchor_kv: bfloat16 [2, 1024, 1024], P(None, ('groups', 'ctx'), 'head'), parts along dimension 1, may hold values from -6 to 6
- cache_kv: bfloat16 [2, 32768, 1024], P(None, ('groups', 'ctx'), 'head'), parts along dimension 1, may hold values from -6 to 6
- cache_len: int32 [8], P(('groups', 'ctx')), parts along dimension 0, may hold values from 1 to 4096, 8192 in all
- query_q: bfloat16 [128, 8192], P(('groups', 'ctx'), 'head'), parts along dimension 0, may hold values from -6 to 6
- query_kv: bfloat16 [2, 128, 1024], P(None, ('groups', 'ctx'), 'head'), parts along dimension 1, may hold values from -6 to 6
- query_pos: int32 [128], P('groups'), parts along dimension 0, may hold values from 0 to 63, each once
Outputs:
- block_out: bfloat16 [2048, 8192], P(('groups', 'ctx'), 'head'), parts along dimension 0
- query_out: bfloat16 [128, 8192], P(('groups', 'ctx'), 'head'), parts along dimension 0
There are 2 independent parts, one for each index of `groups`. A program takes and returns all parts, laid end to end along the dimension named above; each array names one. Nothing has to cross between parts.
All inputs are finite; a program needn't handle non-finite values. No bound on the sum of `cache_len` on one device may be relied on, other than what follows from the above.
Results may differ from a plain program's by a relative error of at most 0.0034.
Values may be sent and summed in bfloat16 or wider, within the bound.
No kernel may reach another device: no remote copies, remote signals or barrier semaphores. Data moves between devices by JAX's collectives and lax.ppermute only.
A program may use at most 128 MiB of HBM per device.

v0:
```python
import jax
import jax.numpy as jnp
from jax import lax
from jax.sharding import PartitionSpec as P

HD = 128


masked_score = -1e30


def combined_all(value, axis, join):
    pieces = jax.tree.map(lambda part: lax.all_gather(part, axis), value)
    head = jax.tree.map(lambda part: part[0], pieces)
    tail = jax.tree.map(lambda part: part[1:], pieces)
    subtotal, _ = lax.scan(lambda subtotal, section: (join(subtotal, section), None), head, tail)
    return subtotal


def widen(per_head):
    return jnp.repeat(per_head, HD, axis=-1)


def partial_attention(queries, key_rows, value_rows, visible):
    row_count = queries.shape[0]
    key_count = key_rows.shape[0]
    kv_heads = key_rows.shape[1] // HD
    query_heads = queries.shape[1] // HD
    group_size = query_heads // kv_heads
    grouped = queries.reshape(row_count, kv_heads, group_size, HD)
    key_heads = key_rows.reshape(key_count, kv_heads, HD)
    scores = jnp.einsum(
        "rkgd,skd->rkgs", grouped, key_heads, preferred_element_type=jnp.float32
    ) * (1.0 / jnp.sqrt(jnp.float32(HD)))
    scores = jnp.where(visible[:, None, None, :], scores, masked_score)
    peak_score = jnp.max(scores, axis=-1)
    weights = jnp.exp(scores - peak_score[..., None])
    totals = jnp.sum(weights, axis=-1)
    value_heads = value_rows.reshape(key_count, kv_heads, HD)
    output = jnp.einsum(
        "rkgs,skd->rkgd",
        weights.astype(jnp.bfloat16),
        value_heads,
        preferred_element_type=jnp.float32,
    )
    return (
        peak_score.reshape(row_count, query_heads),
        totals.reshape(row_count, query_heads),
        output.reshape(row_count, query_heads * HD),
    )


def combine_parts(first, second):
    top_score = jnp.maximum(first[0], second[0])
    left_factor = jnp.exp(first[0] - top_score)
    right_factor = jnp.exp(second[0] - top_score)
    return (
        top_score,
        first[1] * left_factor + second[1] * right_factor,
        first[2] * widen(left_factor) + second[2] * widen(right_factor),
    )


def local(q_block, kv_block, anchor_kv, cache_kv, cache_len, query_q, query_kv, query_pos):
    anchor = lax.all_gather(anchor_kv, "ctx", axis=1, tiled=True)
    anchor_count = anchor.shape[1]
    block_count = q_block.shape[0]
    causal = jnp.arange(block_count)[None, :] <= jnp.arange(block_count)[:, None]
    block_visible = jnp.concatenate([jnp.ones((block_count, anchor_count), bool), causal], axis=1)
    block_parts = partial_attention(
        q_block,
        jnp.concatenate([anchor[0], kv_block[0]], axis=0),
        jnp.concatenate([anchor[1], kv_block[1]], axis=0),
        block_visible,
    )
    block_out = (block_parts[2] / widen(block_parts[1])).astype(jnp.bfloat16)
    all_queries, all_query_kv = (
        lax.all_gather(query_q, "ctx", axis=0, tiled=True),
        lax.all_gather(query_kv, "ctx", axis=1, tiled=True),
    )
    query_total = all_queries.shape[0]
    cache_count = cache_kv.shape[1]
    in_cache = jnp.arange(cache_count, dtype=jnp.int32) < cache_len[0]
    context_visible = jnp.concatenate(
        [
            jnp.broadcast_to(in_cache[None, :], (query_total, cache_count)),
            jnp.ones((query_total, block_count), bool),
        ],
        axis=1,
    )
    context_peak, context_totals, context_output = partial_attention(
        all_queries,
        jnp.concatenate([cache_kv[0], kv_block[0]], axis=0),
        jnp.concatenate([cache_kv[1], kv_block[1]], axis=0),
        context_visible,
    )
    own_count = query_q.shape[0]
    first_row = lax.axis_index("ctx") * own_count
    own_positions = lax.dynamic_slice_in_dim(query_pos, first_row, own_count)
    local_visible = jnp.concatenate(
        [jnp.ones((own_count, anchor_count), bool), query_pos[None, :] <= own_positions[:, None]],
        axis=1,
    )
    local_parts = partial_attention(
        query_q,
        jnp.concatenate([anchor[0], all_query_kv[0]], axis=0),
        jnp.concatenate([anchor[1], all_query_kv[1]], axis=0),
        local_visible,
    )
    merged = combined_all((context_peak, context_totals, context_output), "ctx", combine_parts)
    remote = tuple(
        (lax.dynamic_slice_in_dim(merged_part, first_row, own_count, 0) for merged_part in merged)
    )
    final_parts = combine_parts(remote, local_parts)
    query_out = (final_parts[2] / widen(final_parts[1])).astype(jnp.bfloat16)
    return (block_out, query_out)


def solution(mesh):
    in_specs = (
        P(("groups", "ctx"), "head"),
        P(None, ("groups", "ctx"), "head"),
        P(None, ("groups", "ctx"), "head"),
        P(None, ("groups", "ctx"), "head"),
        P(("groups", "ctx")),
        P(("groups", "ctx"), "head"),
        P(None, ("groups", "ctx"), "head"),
        P("groups"),
    )
    out_specs = (P(("groups", "ctx"), "head"), P(("groups", "ctx"), "head"))
    return jax.shard_map(local, mesh=mesh, in_specs=in_specs, out_specs=out_specs, check_vma=False)
```

profile of v0, /device:TPU:0, one launch (start us, length us, event | category | flops | bytes accessed | tf_op | source)
XLA Modules:
  0.0 164.5 jit_solution(15794202108696513625)
XLA Ops:
  7.2 0.0 all-gather.2.cloned.1.call-start
  7.2 1.0 fusion.62
  8.2 0.1 copy.89
  8.3 0.1 copy.58
  9.1 4.4 %fusion.60 = (bf16[1,4096,256]{2,1,0:T(8,128)(2,1)}, bf16[1,4096,256]{2,1,0:T(8,128)(2,1)}) fusion(bf16[2,4096,256]{2,1,0:T(8,128)(2,1)} %param.13), kind=kLoop, calls=%fused_computation.85 | loop fusion | bytes 8388608 | tf_op jit(solution)/shard_map/slice | solution.py:94
  13.5 2.9 %copy.90 = bf16[1,4096,256]{1,2,0:T(8,128)(2,1)S(1)} copy(bf16[1,4096,256]{2,1,0:T(8,128)(2,1)} %get-tuple-element.66) | data formatting | bytes 4194304
  16.5 2.5 %copy.64 = bf16[4096,2,128]{2,0,1:T(8,128)(2,1)} copy(bf16[4096,2,128]{0,2,1:T(8,128)(2,1)S(1)} %bitcast.172) | data formatting | bytes 4194304 | tf_op jit(solution)/shard_map/concatenate | solution.py:93
  19.0 15.6 %all_gather.19 = bf16[64,2048]{1,0:T(8,128)(2,1)S(1)} all-gather(bf16[16,2048]{1,0:T(8,128)(2,1)S(1)} %copy-done.3), channel_id=1, replica_groups=mesh['groups'=2,'ctx'=4,'head'=4] {'ctx'}, dimensions={0}, use_global_device_ids=true | all-gather | bytes 327680 | tf_op jit(solution)/shard_map/all_gather | solution.py:78
  34.6 0.1 copy.55
  34.8 0.1 copy.69
  34.9 2.9 %copy.91 = bf16[1,4096,256]{1,2,0:T(8,128)(2,1)S(1)} copy(bf16[1,4096,256]{2,1,0:T(8,128)(2,1)} %get-tuple-element.65) | data formatting | bytes 4194304
  37.8 2.5 %copy.68 = bf16[4096,2,128]{2,0,1:T(8,128)(2,1)} copy(bf16[4096,2,128]{0,2,1:T(8,128)(2,1)S(1)} %bitcast.173) | data formatting | bytes 4194304 | tf_op jit(solution)/shard_map/concatenate | solution.py:94
  40.3 9.4 %bitcast_reduce_fusion = (f32[64,2,8]{0,2,1:T(8,128)S(1)}, f32[2,4352,64,8]{1,2,3,0:T(8,128)}) fusion(pred[4352]{0:T(1024)(128)(4,1)S(1)} %concatenate.56, bf16[64,2,8,128]{3,2,1,0:T(8,128)(2,1)S(1)} %bitcast.190, bf16[256,2,128]{2,0,1:T(8,128)(2,1)S(1)} %copy.58, bf16[4096,2,128]{2,0,1:T(8,128)(2,1)} %copy.64), kind=kOutput, calls=%fused_computation.10 | convolution fusion | flops 1158675456 | bytes 20324608 | tf_op jit(solution)/shard_map/rkgd,skd->rkgs/dot_general | solution.py:32
  49.6 7.8 %fusion.23 = f32[64,2,8,128]{3,0,2,1:T(8,128)S(1)} fusion(f32[2,4352,64,8]{1,2,3,0:T(8,128)} %get-tuple-element.78, f32[64,2,8]{0,2,1:T(8,128)S(1)} %get-tuple-element.77, pred[4352]{0:T(1024)(128)(4,1)S(1)} %concatenate.56, bf16[256,2,128]{2,0,1:T(8,128)(2,1)S(1)} %copy.69, bf16[4096,2,128]{2,0,1:T(8,128)(2,1)S(1)} %copy-done.1), kind=kOutput, calls=%fused_computation.36 | convolution fusion | flops 1163132928 | bytes 20586752 | tf_op jit(solution)/shard_map/rkgs,skd->rkgd/dot_general | solution.py:40
  57.5 0.3 copy.70
  57.8 0.9 all_gather_reshape.11
  58.7 0.0 all-gather.2.cloned.1.call-update
  58.8 10.1 %fusion.5 = f32[64,2,8]{0,2,1:T(8,128)S(1)} fusion(f32[2,4352,64,8]{1,2,3,0:T(8,128)} %get-tuple-element.78, f32[64,2,8]{0,2,1:T(8,128)S(1)} %get-tuple-element.77, pred[4352]{0:T(1024)(128)(4,1)S(1)} %concatenate.56), kind=kLoop, calls=%fused_computation.14 | loop fusion | flops 17824768 | bytes 17838336 | tf_op jit(solution)/shard_map/reduce_sum | solution.py:38
  68.9 13.6 %all_gather.21 = f32[4,64,16]{1,2,0:T(8,128)S(1)} all-gather(f32[1,64,16]{1,2,0:T(8,128)S(1)} %bitcast.194), channel_id=1, replica_groups=mesh['groups'=2,'ctx'=4,'head'=4] {'ctx'}, dimensions={0}, use_global_device_ids=true | all-gather | bytes 20480 | tf_op jit(solution)/shard_map/all_gather | solution.py:13
  82.5 13.2 %all_gather.20 = f32[4,64,16]{1,2,0:T(8,128)S(1)} all-gather(f32[1,64,16]{1,2,0:T(8,128)S(1)} %bitcast.193), channel_id=1, replica_groups=mesh['groups'=2,'ctx'=4,'head'=4] {'ctx'}, dimensions={0}, use_global_device_ids=true | all-gather | bytes 20480 | tf_op jit(solution)/shard_map/all_gather | solution.py:13
  95.7 0.1 dynamic_slice.25
  95.8 0.1 broadcast_compare_fusion
  95.9 0.1 copy.54
  96.0 20.8 %all_gather.18 = bf16[2,512,256]{1,2,0:T(8,128)(2,1)S(1)} all-gather(bf16[2,128,256]{1,2,0:T(8,128)(2,1)S(1)} %copy.54), channel_id=1, replica_groups=mesh['groups'=2,'ctx'=4,'head'=4] {'ctx'}, dimensions={1}, use_global_device_ids=true | all-gather | bytes 655360 | tf_op jit(solution)/shard_map/all_gather | solution.py:65
  116.9 0.2 copy.57
  117.1 13.3 %all_gather.23 = bf16[2,64,256]{2,1,0:T(8,128)(2,1)S(1)} all-gather(bf16[2,16,256]{2,1,0:T(8,128)(2,1)S(1)} %copy-done.7), channel_id=1, replica_groups=mesh['groups'=2,'ctx'=4,'head'=4] {'ctx'}, dimensions={1}, use_global_device_ids=true | all-gather | bytes 81920 | tf_op jit(solution)/shard_map/all_gather | solution.py:79
  130.5 0.1 copy.75
  130.6 0.2 copy.94
  130.9 2.2 %fusion.8 = (f32[256,2,8]{0,2,1:T(8,128)S(1)}, f32[2,768,256,8]{2,1,3,0:T(8,128)S(1)}) fusion(pred[256,768]{0,1:T(8,128)(4,1)S(1)} %concatenate.52, bf16[256,2,8,128]{3,2,1,0:T(8,128)(2,1)S(1)} %bitcast.174, bf16[256,2,128]{2,0,1:T(8,128)(2,1)S(1)} %copy.58, bf16[512,2,128]{2,0,1:T(8,128)(2,1)S(1)} %copy.57), kind=kOutput, calls=%fused_computation.19 | convolution fusion | flops 815525888 | bytes 14237696 | tf_op jit(solution)/shard_map/rkgd,skd->rkgs/dot_general | solution.py:32
  133.1 0.3 fusion.64
  133.4 0.3 convolution_bitcast_fusion
  133.8 4.4 %fusion.12 = f32[2,128,256,8]{2,1,3,0:T(8,128)} fusion(f32[2,768,256,8]{2,1,3,0:T(8,128)S(1)} %get-tuple-element.74, f32[256,2,8]{0,2,1:T(8,128)S(1)} %get-tuple-element.73, pred[256,768]{0,1:T(8,128)(4,1)S(1)} %concatenate.52, bf16[256,2,128]{0,2,1:T(8,128)(2,1)S(1)} %bitcast.186, bf16[512,2,128]{0,2,1:T(8,128)(2,1)S(1)} %bitcast.179), kind=kOutput, calls=%fused_computation.22 | convolution fusion | flops 818675712 | bytes 15286272 | tf_op jit(solution)/shard_map/rkgs,skd->rkgd/dot_general | solution.py:40
  138.2 1.9 %copy.62 = f32[256,2048]{1,0:T(8,128)S(1)} copy(f32[256,2048]{0,1:T(8,128)} %bitcast.175) | data formatting | bytes 4194304 | tf_op jit(solution)/shard_map/reshape | solution.py:49
  140.2 7.2 %fusion.6 = f32[256,2,8]{0,2,1:T(8,128)S(1)} fusion(f32[2,768,256,8]{2,1,3,0:T(8,128)} %copy-done, f32[256,2,8]{0,2,1:T(8,128)S(1)} %get-tuple-element.73, pred[256,768]{0,1:T(8,128)(4,1)S(1)} %concatenate.52), kind=kLoop, calls=%fused_computation.17 | loop fusion | flops 12578816 | bytes 12812288 | tf_op jit(solution)/shard_map/reduce_sum | solution.py:38
  147.3 0.1 copy.61
  147.4 0.2 fusion.28
  147.7 0.6 broadcast_in_dim.73
  148.3 1.8 %fusion.20 = bf16[256,2048]{1,0:T(8,128)(2,1)} fusion(f32[256,2048]{1,0:T(8,128)S(1)} %copy.62, f32[32,8,16,128]{3,2,1,0:T(8,128)S(1)} %bitcast.171), kind=kLoop, calls=%fused_computation.32 | loop fusion | flops 1048576 | bytes 5242880 | tf_op jit(solution)/shard_map/convert_element_type | solution.py:76
  150.1 1.5 slice.67
  151.6 1.1 slice_bitcast_fusion
  152.7 3.5 %while.14 = (s32[]{:T(128)}, f32[64,16]{0,1:T(8,128)S(1)}, f32[64,16]{0,1:T(8,128)S(1)}, f32[64,2048]{1,0:T(8,128)S(1)}, f32[3,64,16]{1,2,0:T(8,128)S(1)}, /*ind...) while((s32[]{:T(128)}, f32[64,16]{0,1:T(8,128)S(1)}, f32[64,16]{0,1:T(8,128)S(1)}, ...), condition=%wide.region_5.6_spmd, body=%wide.region_4.5_spmd.sunk | while | flops 399362 | bytes 3727453 | solution.py:16
  152.8 0.1 copy.127
  152.9 0.2 broadcast_in_dim.109
  153.1 0.1 copy.128
  153.1 0.2 broadcast_in_dim.110
  153.3 0.5 fusion.68
  153.9 0.1 copy.127
  154.0 0.2 broadcast_in_dim.109
  154.2 0.1 copy.128
  154.3 0.2 broadcast_in_dim.110
  154.5 0.5 fusion.68
  155.1 0.1 copy.127
  155.2 0.2 broadcast_in_dim.109
  155.4 0.1 copy.128
  155.4 0.2 broadcast_in_dim.110
  155.7 0.5 fusion.68
  156.2 0.1 fusion.46
  156.3 0.1 copy.74
  156.4 0.1 copy.78
  156.4 0.1 copy.79
  156.5 0.1 broadcast_in_dim.78
  156.6 0.1 broadcast_in_dim.79
  156.7 0.1 broadcast_in_dim.80
  156.8 0.8 fusion.41
  (40 shorter events, 0.4 us)
Async XLA Ops:
  7.2 11.8 %copy-start.3 = (bf16[16,2048]{1,0:T(8,128)(2,1)S(1)}, bf16[16,2048]{1,0:T(8,128)(2,1)}, u32[]{:S(2)}) copy-start(bf16[16,2048]{1,0:T(8,128)(2,1)} %param.15) | copy-start | bytes 196612
  7.2 142.9 %all-gather.2.cloned.1.call-start = ((), (), s32[]{:S(2)}) async-start(), calls=%async_computation | async-start | bytes 2621440 | tf_op jit(solution)/shard_map/all_gather | solution.py:13
  40.3 9.4 %copy-start.1 = (bf16[4096,2,128]{2,0,1:T(8,128)(2,1)S(1)}, bf16[4096,2,128]{2,0,1:T(8,128)(2,1)}, u32[]{:S(2)}) copy-start(bf16[4096,2,128]{2,0,1:T(8,128)(2,1)} %copy.68) | copy-start | bytes 6291460
  58.7 37.0 %copy-start.8 = (s32[64]{0:T(128)S(1)}, s32[64]{0:T(128)}, u32[]{:S(2)}) copy-start(s32[64]{0:T(128)} %param.17) | copy-start | bytes 772
  58.7 37.2 %copy-start.6 = (bf16[2,128,256]{2,1,0:T(8,128)(2,1)S(1)}, bf16[2,128,256]{2,1,0:T(8,128)(2,1)}, u32[]{:S(2)}) copy-start(bf16[2,128,256]{2,1,0:T(8,128)(2,1)} %param.12) | copy-start | bytes 393220
  58.7 58.3 %copy-start.7 = (bf16[2,16,256]{2,1,0:T(8,128)(2,1)S(1)}, bf16[2,16,256]{2,1,0:T(8,128)(2,1)}, u32[]{:S(2)}) copy-start(bf16[2,16,256]{2,1,0:T(8,128)(2,1)} %param.16) | copy-start | bytes 49156
  58.7 71.9 %copy-start.2 = (bf16[256,2048]{1,0:T(8,128)(2,1)S(1)}, bf16[256,2048]{1,0:T(8,128)(2,1)}, u32[]{:S(2)}) copy-start(bf16[256,2048]{1,0:T(8,128)(2,1)} %param.10) | copy-start | bytes 3145732
  82.5 65.2 %copy-start.4 = (f32[4,64,16]{1,2,0:T(8,128)}, f32[4,64,16]{1,2,0:T(8,128)S(1)}, u32[]{:S(2)}) copy-start(f32[4,64,16]{1,2,0:T(8,128)S(1)} %all_gather.21) | copy-start | bytes 49156
  95.7 52.0 %copy-start.5 = (f32[4,64,16]{1,2,0:T(8,128)}, f32[4,64,16]{1,2,0:T(8,128)S(1)}, u32[]{:S(2)}) copy-start(f32[4,64,16]{1,2,0:T(8,128)S(1)} %all_gather.20) | copy-start | bytes 49156
  133.1 5.2 %copy-start = (f32[2,768,256,8]{2,1,3,0:T(8,128)}, f32[2,768,256,8]{2,1,3,0:T(8,128)S(1)}, u32[]{:S(2)}) copy-start(f32[2,768,256,8]{2,1,3,0:T(8,128)S(1)} %get-tuple-element.74) | copy-start | bytes 37748740
  147.7 5.0 %slice-start = ((f32[4,64,16]{1,2,0:T(8,128)}), f32[3,64,16]{1,2,0:T(8,128)S(1)}, s32[]{:S(2)}) async-start(f32[4,64,16]{1,2,0:T(8,128)} %copy-done.4), calls=%async_computation.1 | async-start | bytes 49152 | tf_op jit(solution)/shard_map/slice | solution.py:15
  147.7 5.0 %slice-start.1 = ((f32[4,64,16]{1,2,0:T(8,128)}), f32[3,64,16]{1,2,0:T(8,128)S(1)}, s32[]{:S(2)}) async-start(f32[4,64,16]{1,2,0:T(8,128)} %copy-done.5), calls=%async_computation.2 | async-start | bytes 49152 | tf_op jit(solution)/shard_map/slice | solution.py:15
Sparse Core Ops, SparseCore 0:
  58.8 55.0 all-gather.1
where the time goes:
time: 165 us; the launch traced here: 164 us
  blocking collectives  76.6 us (46%)
  local copies, waits for them, and re-layouts  26.2 us (16%)
  matrix products  24.5 us (15%)
  other arithmetic  21.9 us (13%)
  between operations  15 us (9%)
    all_gather x2, blocking collectives, combined_all(): pieces = jax.tree.map(lambda part: lax.all_gather(part, axis), value)  26.9 us
    all_gather x1, blocking collectives, local(): anchor = lax.all_gather(anchor_kv, 'ctx', axis=1, tiled=True)  20.8 us
    reduce_sum x3, other arithmetic, partial_attention(): totals = jnp.sum(weights, axis=-1)  17.5 us
    all_gather x1, blocking collectives, local(): lax.all_gather(query_q, 'ctx', axis=0, tiled=True)  15.6 us
    all_gather x1, blocking collectives, local(): lax.all_gather(query_kv, 'ctx', axis=1, tiled=True)  13.3 us
    dot_general x3, matrix products, partial_attention(): jnp.einsum('rkgs,skd->rkgd', weights.astype(jnp.bfloat16), value_heads, p...  12.6 us
    dot_general x3, matrix products, partial_attention(): jnp.einsum('rkgd,skd->rkgs', grouped, key_heads, preferred_element_type=j...  11.9 us
    unnamed x25, local copies, waits for them, and re-layouts  6.36 us
  transfers between devices with their start and end apart: 1, of which 0 were waited for; matrix products, arithmetic and copies ran while one was open for 18% of the time, Pallas kernels for 0%

commit v1 on v0

v1 whole, which is shorter than its diff:
```python
import jax
import jax.numpy as jnp
from jax import lax
from jax.sharding import PartitionSpec as P

HD = 128


masked_score = -1e30


def widen(per_head):
    return jnp.repeat(per_head, HD, axis=-1)


def partial_attention(queries, parts):
    row_count = queries.shape[0]
    kv_heads = parts[0][0].shape[1] // HD
    query_heads = queries.shape[1] // HD
    group_size = query_heads // kv_heads
    grouped = queries.reshape(row_count, kv_heads, group_size, HD)
    scale = 1.0 / jnp.sqrt(jnp.float32(HD))
    all_scores = []
    for key_rows, _, visible in parts:
        key_heads = key_rows.reshape(key_rows.shape[0], kv_heads, HD)
        scores = jnp.einsum(
            "rkgd,skd->rkgs", grouped, key_heads, preferred_element_type=jnp.float32
        ) * scale
        if visible is not None:
            scores = jnp.where(visible[:, None, None, :], scores, masked_score)
        all_scores.append(scores)
    peak_score = all_scores[0].max(axis=-1)
    for scores in all_scores[1:]:
        peak_score = jnp.maximum(peak_score, scores.max(axis=-1))
    totals = None
    output = None
    for scores, (_, value_rows, _) in zip(all_scores, parts):
        weights = jnp.exp(scores - peak_score[..., None])
        part_total = jnp.sum(weights, axis=-1)
        value_heads = value_rows.reshape(value_rows.shape[0], kv_heads, HD)
        part_output = jnp.einsum(
            "rkgs,skd->rkgd",
            weights.astype(jnp.bfloat16),
            value_heads,
            preferred_element_type=jnp.float32,
        )
        totals = part_total if totals is None else totals + part_total
        output = part_output if output is None else output + part_output
    return (
        peak_score.reshape(row_count, query_heads),
        totals.reshape(row_count, query_heads),
        output.reshape(row_count, query_heads * HD),
    )


def shifted(value, shift, count):
    return lax.ppermute(value, "ctx", [(j, (j + shift) % count) for j in range(count)])


def make_local(ctx_count):
    def local(q_block, kv_block, anchor_kv, cache_kv, cache_len, query_q, query_kv, query_pos):
        me = lax.axis_index("ctx")
        own_count = query_q.shape[0]
        anchor_rows = anchor_kv.shape[1]
        width = kv_block.shape[2]
        pieces = (anchor_kv.reshape(-1), query_q.reshape(-1), query_kv.reshape(-1))
        sizes = [piece.shape[0] for piece in pieces]
        packed = jnp.concatenate(pieces)
        slots = [packed] + [shifted(packed, k, ctx_count) for k in range(1, ctx_count)]

        def unpack(slot):
            a = slot[: sizes[0]].reshape(2, anchor_rows, width)
            q = slot[sizes[0] : sizes[0] + sizes[1]].reshape(own_count, -1)
            kv = slot[sizes[0] + sizes[1] :].reshape(2, own_count, width)
            return a, q, kv

        unpacked = [unpack(slot) for slot in slots]
        anchor = jnp.concatenate([u[0] for u in unpacked], axis=1)
        all_queries = jnp.concatenate([u[1] for u in unpacked], axis=0)
        all_query_kv = jnp.concatenate([u[2] for u in unpacked], axis=1)
        slot_pos = jnp.concatenate(
            [
                lax.dynamic_slice_in_dim(query_pos, ((me - k) % ctx_count) * own_count, own_count)
                for k in range(ctx_count)
            ]
        )
        own_pos = slot_pos[:own_count]

        block_count = q_block.shape[0]
        causal = jnp.arange(block_count)[None, :] <= jnp.arange(block_count)[:, None]
        block_parts = partial_attention(
            q_block,
            [(anchor[0], anchor[1], None), (kv_block[0], kv_block[1], causal)],
        )
        block_out = (block_parts[2] / widen(block_parts[1])).astype(jnp.bfloat16)

        cache_count = cache_kv.shape[1]
        in_cache = (jnp.arange(cache_count, dtype=jnp.int32) < cache_len[0])[None, :]
        context_peak, context_totals, context_output = partial_attention(
            all_queries,
            [(cache_kv[0], cache_kv[1], in_cache), (kv_block[0], kv_block[1], None)],
        )
        local_parts = partial_attention(
            query_q,
            [
                (anchor[0], anchor[1], None),
                (all_query_kv[0], all_query_kv[1], slot_pos[None, :] <= own_pos[:, None]),
            ],
        )
        heads = context_peak.shape[1]
        context_packed = jnp.concatenate([context_output, context_peak, context_totals], axis=1)
        remote = [context_packed[:own_count]]
        for k in range(1, ctx_count):
            section = context_packed[k * own_count : (k + 1) * own_count]
            remote.append(shifted(section, -k, ctx_count))
        peaks = [local_parts[0]] + [r[:, -2 * heads : -heads] for r in remote]
        totals = [local_parts[1]] + [r[:, -heads:] for r in remote]
        outputs = [local_parts[2]] + [r[:, : -2 * heads] for r in remote]
        top_score = peaks[0]
        for peak in peaks[1:]:
            top_score = jnp.maximum(top_score, peak)
        merged_totals = None
        merged_output = None
        for peak, total, output in zip(peaks, totals, outputs):
            factor = jnp.exp(peak - top_score)
            t = total * factor
            o = output * widen(factor)
            merged_totals = t if merged_totals is None else merged_totals + t
            merged_output = o if merged_output is None else merged_output + o
        query_out = (merged_output / widen(merged_totals)).astype(jnp.bfloat16)
        return (block_out, query_out)

    return local


def solution(mesh):
    in_specs = (
        P(("groups", "ctx"), "head"),
        P(None, ("groups", "ctx"), "head"),
        P(None, ("groups", "ctx"), "head"),
        P(None, ("groups", "ctx"), "head"),
        P(("groups", "ctx")),
        P(("groups", "ctx"), "head"),
        P(None, ("groups", "ctx"), "head"),
        P("groups"),
    )
    out_specs = (P(("groups", "ctx"), "head"), P(("groups", "ctx"), "head"))
    return jax.shard_map(
        make_local(mesh.shape["ctx"]),
        mesh=mesh,
        in_specs=in_specs,
        out_specs=out_specs,
        check_vma=False,
    )
```

time: 165 us -> 105 us (0.64)
  blocking collectives: 76.6 us -> 0 us
  between operations: 15 us -> 1.92 us
  local copies, waits for them, and re-layouts: 26.2 us -> 37.9 us
  matrix products: 24.5 us -> 35.1 us
  starting transfers between devices: 0.04 us -> 9.11 us
  other arithmetic: 21.9 us -> 19.5 us
    all_gather x5 -> x0, blocking collectives: 76.6 us -> none  [the longest x2 26.9 us: combined_all(): pieces = jax.tree.map(lambda part: lax.all_gather(part, axis), value)]
    unnamed x25 -> x50, local copies, waits for them, and re-layouts: 6.36 us -> 18.6 us
    ppermute x0 -> x6, starting transfers between devices: none -> 9.11 us  [shifted(): lax.ppermute(value, 'ctx', [(j, (j + shift) % count) for j in range(count)])]
    dot_general x3 -> x6, matrix products: 11.9 us -> 18.5 us  [partial_attention(): jnp.einsum('rkgd,skd->rkgs', grouped, key_heads, preferred_element_type=j...]
    slice x6 -> x30, local copies, waits for them, and re-layouts: 5.95 us -> 11.9 us  [the longest x1 3.83 us: local(): cache_kv[0]]
    concatenate x10 -> x4, local copies, waits for them, and re-layouts: 5.48 us -> 1.35 us  [the longest x1 0.66 us: local(): anchor = jnp.concatenate([u[0] for u in unpacked], axis=1)]
    dot_general x3 -> x6, matrix products: 12.6 us -> 16.6 us  [partial_attention(): jnp.einsum('rkgs,skd->rkgd', weights.astype(jnp.bfloat16), value_heads, p...]
    reduce_sum x3 -> x6, other arithmetic: 17.5 us -> 14.6 us  [partial_attention(): part_total = jnp.sum(weights, axis=-1)]
  transfers between devices with their start and end apart: 1 -> 6, of which waited for: 0 -> 0; matrix products, arithmetic and copies ran while one was open for 18% -> 35% of each run, Pallas kernels for 0% -> 0%
where the time goes in v1:
time: 105 us; the launch traced here: 104 us
  local copies, waits for them, and re-layouts  37.9 us (36%)
  matrix products  35.1 us (33%)
  other arithmetic  19.5 us (19%)
  starting transfers between devices  9.11 us (9%)
  between operations  1.92 us (2%)
    unnamed x50, local copies, waits for them, and re-layouts  18.6 us
    dot_general x6, matrix products, partial_attention(): jnp.einsum('rkgd,skd->rkgs', grouped, key_heads, preferred_element_type=j...  18.5 us
    dot_general x6, matrix products, partial_attention(): jnp.einsum('rkgs,skd->rkgd', weights.astype(jnp.bfloat16), value_heads, p...  16.6 us
    reduce_sum x6, other arithmetic, partial_attention(): part_total = jnp.sum(weights, axis=-1)  14.6 us
    ppermute x6, starting transfers between devices, shifted(): lax.ppermute(value, 'ctx', [(j, (j + shift) % count) for j in range(count)])  9.11 us
    slice x1, local copies, waits for them, and re-layouts, local(): cache_kv[0]  3.83 us
  transfers between devices with their start and end apart: 6, of which 0 were waited for; matrix products, arithmetic and copies ran while one was open for 35% of the time, Pallas kernels for 0%

profile of v1, /device:TPU:0, one launch (start us, length us, event | category | flops | bytes accessed | tf_op | source)
XLA Modules:
  0.0 103.5 jit_solution(10412410085042964785)
XLA Ops:
  0.6 1.0 copy.179
  1.6 0.7 constant_dynamic-update-slice_fusion
  2.3 0.8 copy.180
  3.2 0.7 copy.181
  3.9 0.6 constant_dynamic-update-slice_fusion.10
  4.5 0.6 constant_dynamic-update-slice_fusion.9
  5.1 3.0 %collective-permute-start = (bf16[106496]{0:T(1024)(128)(2,1)}, bf16[106496]{0:T(1024)(128)(2,1)S(1)}, u32[]{:S(2)}, u32[]{:S(2)}) collective-permute-start(bf16[106496]{0:T(1024)(128)(2,1)} %constant_dynamic-update-slice_fusion.9), channel_id=1, source_target_pairs={{0,4},{4,8},{8,12},{12,0},{1,5},{5,9},{9,13},{13,1},{2,6},{6,10},{... | collective-permute-start | bytes 638984 | tf_op jit(solution)/shard_map/ppermute | solution.py:57
  8.1 2.6 %collective-permute-start.1 = (bf16[106496]{0:T(1024)(128)(2,1)}, bf16[106496]{0:T(1024)(128)(2,1)}, u32[]{:S(2)}, u32[]{:S(2)}) collective-permute-start(bf16[106496]{0:T(1024)(128)(2,1)} %constant_dynamic-update-slice_fusion.9), channel_id=1, source_target_pairs={{0,8},{4,12},{8,0},{12,4},{1,9},{5,13},{9,1},{13,5},{2,10},{6,14},... | collective-permute-start | bytes 638984 | tf_op jit(solution)/shard_map/ppermute | solution.py:57
  10.7 1.3 %collective-permute-start.2 = (bf16[106496]{0:T(1024)(128)(2,1)}, bf16[106496]{0:T(1024)(128)(2,1)}, u32[]{:S(2)}, u32[]{:S(2)}) collective-permute-start(bf16[106496]{0:T(1024)(128)(2,1)} %constant_dynamic-update-slice_fusion.9), channel_id=1, source_target_pairs={{0,12},{4,0},{8,4},{12,8},{1,13},{5,1},{9,5},{13,9},{2,14},{6,2},{... | collective-permute-start | bytes 638984 | tf_op jit(solution)/shard_map/ppermute | solution.py:57
  12.1 0.7 constant_dynamic-update-slice_fusion.8
  12.8 1.6 %constant_dynamic-update-slice_fusion.4 = bf16[2,512,256]{2,1,0:T(8,128)(2,1)} fusion(bf16[2,128,256]{2,1,0:T(8,128)(2,1)} %param.10), kind=kLoop, calls=%fused_computation.82 | loop fusion | bytes 262144
  14.4 0.9 copy.184
  15.9 3.8 %fusion.68 = (bf16[1,4096,256]{2,1,0:T(8,128)(2,1)}, bf16[1,4096,256]{2,1,0:T(8,128)(2,1)S(1)}) fusion(bf16[2,4096,256]{2,1,0:T(8,128)(2,1)} %param.11), kind=kLoop, calls=%fused_computation.111 | loop fusion | bytes 8388608 | tf_op jit(solution)/shard_map/slice | solution.py:101
  19.8 4.1 %copy.177 = bf16[1,4096,256]{1,2,0:T(8,128)(2,1)} copy(bf16[1,4096,256]{2,1,0:T(8,128)(2,1)} %get-tuple-element.8) | data formatting | bytes 4194304
  23.9 0.1 copy.176
  24.0 3.0 %copy.178 = bf16[1,4096,256]{1,2,0:T(8,128)(2,1)} copy(bf16[1,4096,256]{2,1,0:T(8,128)(2,1)S(1)} %get-tuple-element.9) | data formatting | bytes 4194304
  27.0 0.1 copy.109
  27.1 1.5 %copy.182 = bf16[32,8,16,128]{3,2,1,0:T(8,128)(2,1)S(1)} copy(bf16[32,8,16,128]{3,1,2,0:T(8,128)(2,1)} %bitcast.199) | data formatting | bytes 2097152
  28.6 3.5 %fusion.15 = (f32[256,2,8]{0,2,1:T(8,128)}, f32[2,256,256,8]{2,1,3,0:T(8,128)}) fusion(pred[256,256]{0,1:T(8,128)(4,1)S(1)} %iota_compare_fusion, bf16[256,2,128,1]{0,2,3,1:T(8,128)(2,1)S(1)} %bitcast.195, bf16[256,2,8,128]{3,2,1,0:T(8,128)(2,1)S(1)} %bitcast.181), kind=kOutput, calls=%fused_computation.20 | convolution fusion | flops 271577088 | bytes 5455872 | tf_op jit(solution)/shard_map/rkgd,skd->rkgs/dot_general | solution.py:26
  32.5 0.9 slice.228
  33.4 0.8 slice.229
  34.3 0.4 fusion.74
  34.7 8.9 %bitcast_reduce_fusion = (f32[64,2,8]{2,0,1:T(8,128)S(1)}, f32[2,64,8,4096]{3,2,1,0:T(8,128)}) fusion(pred[4096]{0:T(1024)(128)(4,1)S(1)} %iota_compare_fusion.1, bf16[4096,2,128,1]{0,2,3,1:T(8,128)(2,1)} %bitcast.183, bf16[64,2,8,128]{3,2,1,0:T(8,128)(2,1)S(1)} %bitcast.187), kind=kOutput, calls=%fused_computation.1 | convolution fusion | flops 1086323712 | bytes 19144704 | tf_op jit(solution)/shard_map/rkgd,skd->rkgs/dot_general | solution.py:26
  43.7 8.1 %fusion.1 = f32[64,2,8]{2,0,1:T(8,128)S(1)} fusion(f32[2,64,8,4096]{3,2,1,0:T(8,128)} %get-tuple-element.28, f32[64,2,8]{2,0,1:T(8,128)S(1)} %max.44, pred[4096]{0:T(1024)(128)(4,1)S(1)} %iota_compare_fusion.1), kind=kLoop, calls=%fused_computation.4 | loop fusion | flops 16776192 | bytes 16789504 | tf_op jit(solution)/shard_map/reduce_sum | solution.py:39
  51.7 0.4 fusion.31
  52.1 0.7 copy.133
  52.8 10.4 %fusion.4 = f32[2,64,8,128]{3,2,1,0:T(8,128)} fusion(bf16[4096,2,128,1]{0,2,3,1:T(8,128)(2,1)} %bitcast.190, f32[2,64,8,4096]{3,2,1,0:T(8,128)} %get-tuple-element.28, f32[64,2,8]{2,0,1:T(8,128)S(1)} %max.44, pred[4096]{0:T(1024)(128)(4,1)S(1)} %iota_compare_fusion.1), kind=kOutput, calls=%fused_computation.9 | convolution fusion | flops 1090519040 | bytes 19406848 | tf_op jit(solution)/shard_map/rkgs,skd->rkgd/dot_general | solution.py:41
  63.2 1.4 %fusion.27 = f32[64,2,8,128]{3,2,0,1:T(8,128)S(1)} fusion(f32[2,64,8,128]{3,2,1,0:T(8,128)} %fusion.4, bf16[256,2,128,1]{0,2,3,1:T(8,128)(2,1)S(1)} %bitcast.193, f32[64,2,8,256]{3,2,0,1:T(8,128)S(1)} %get-tuple-element.30, f32[64,2,8]{2,0,1:T(8,128)S(1)} %max.44), kind=kOutput, calls=%fused_computation.34 | convolution fusion | flops 67764224 | bytes 2232320 | tf_op jit(solution)/shard_map/rkgs,skd->rkgd/dot_general | solution.py:41
  64.7 0.8 slice.223
  65.4 0.7 slice.224
  66.3 0.9 slice.218
  67.3 0.9 slice.219
  68.3 0.7 constant_dynamic-update-slice_fusion.3
  68.9 0.7 constant_dynamic-update-slice_fusion.2
  69.6 0.7 constant_dynamic-update-slice_fusion.1
  70.3 1.1 %fusion.70 = (bf16[1,512,256]{2,1,0:T(8,128)(2,1)S(1)}, bf16[1,512,256]{2,1,0:T(8,128)(2,1)S(1)}) fusion(bf16[2,512,256]{2,1,0:T(8,128)(2,1)} %constant_dynamic-update-slice_fusion.1), kind=kLoop, calls=%fused_computation.113 | loop fusion | bytes 1048576 | tf_op jit(solution)/shard_map/slice | solution.py:93
  71.3 0.1 copy.102
  71.5 5.2 %bitcast_reduce_fusion.1 = (f32[256,2,8]{0,2,1:T(8,128)}, f32[2,512,256,8]{2,1,3,0:T(8,128)}) fusion(bf16[512,2,128,1]{0,2,3,1:T(8,128)(2,1)S(1)} %bitcast.197, bf16[256,2,8,128]{3,2,1,0:T(8,128)(2,1)S(1)} %bitcast.182), kind=kOutput, calls=%fused_computation.7 | convolution fusion | flops 541061120 | bytes 9715712 | tf_op jit(solution)/shard_map/rkgd,skd->rkgs/dot_general | solution.py:26
  76.7 0.3 fusion.75
  77.0 0.2 fusion.76
  77.2 0.2 fusion.51
  77.4 0.2 fusion.39
  77.7 0.7 copy.139
  78.3 0.7 copy.136
  79.0 0.2 copy.235
  79.4 0.8 fusion.69
  80.2 0.4 collective-permute-start.3
  80.7 1.7 %collective-permute-start.4 = (f32[16,2080]{1,0:T(8,128)}, f32[16,2080]{1,0:T(8,128)}, u32[]{:S(2)}, u32[]{:S(2)}) collective-permute-start(f32[16,2080]{1,0:T(8,128)} %get-tuple-element.12), channel_id=1, source_target_pairs={{0,8},{4,12},{8,0},{12,4},{1,9},{5,13},{9,1},{13,5},{2,10},{6,14},... | collective-permute-start | bytes 399368 | tf_op jit(solution)/shard_map/ppermute | solution.py:57
  82.6 0.7 copy.127
  83.3 0.2 fusion.53
  83.5 0.1 copy.101
  83.7 4.9 %fusion.7 = f32[256,2,8]{0,2,1:T(8,128)S(1)} fusion(f32[2,512,256,8]{2,1,3,0:T(8,128)} %get-tuple-element.24, f32[256,2,8]{0,2,1:T(8,128)S(1)} %max.41), kind=kLoop, calls=%fused_computation.11 | loop fusion | flops 6287360 | bytes 8421376 | tf_op jit(solution)/shard_map/reduce_sum | solution.py:39
  88.6 0.8 copy-done
  89.5 1.7 %fusion.9 = f32[2,128,256,8]{2,1,3,0:T(8,128)S(1)} fusion(bf16[512,2,128,1]{0,2,3,1:T(8,128)(2,1)S(1)} %bitcast.188, f32[2,512,256,8]{2,1,3,0:T(8,128)S(1)} %copy-done, f32[256,2,8]{0,2,1:T(8,128)S(1)} %max.41), kind=kOutput, calls=%fused_computation.13 | convolution fusion | flops 543162368 | bytes 10764288 | tf_op jit(solution)/shard_map/rkgs,skd->rkgd/dot_general | solution.py:41
  91.2 0.5 copy-done.1
  91.7 0.9 fusion.13
  92.5 2.6 %bitcast_add_fusion = f32[256,2,8,128]{0,3,2,1:T(8,128)} fusion(f32[2,128,256,8]{2,1,3,0:T(8,128)S(1)} %fusion.9, bf16[256,2,128,1]{0,2,3,1:T(8,128)(2,1)S(1)} %bitcast.194, f32[2,256,256,8]{2,1,3,0:T(8,128)S(1)} %copy-done.1, f32[256,2,8]{0,2,1:T(8,128)S(1)} %max.41, pred[256,256]{0,1:T(8,128)(4,1)S(1)} %iota_compare_fusion), kind=kOutput, calls=%fused_computation.24 | convolution fusion | flops 273154048 | bytes 8601600 | tf_op jit(solution)/shard_map/rkgs,skd->rkgd/dot_general | solution.py:41
  95.2 1.9 %copy.112 = f32[256,2048]{1,0:T(8,128)S(1)} copy(f32[256,2048]{0,1:T(8,128)} %bitcast.185) | data formatting | bytes 4194304 | tf_op jit(solution)/shard_map/reshape | solution.py:52
  97.1 0.1 copy.111
  97.2 0.6 broadcast_in_dim.71
  97.8 1.8 %fusion.18 = bf16[256,2048]{1,0:T(8,128)(2,1)} fusion(f32[256,2048]{1,0:T(8,128)S(1)} %copy.112, f32[32,8,16,128]{3,2,1,0:T(8,128)S(1)} %bitcast.184), kind=kLoop, calls=%fused_computation.23 | loop fusion | flops 1048576 | bytes 5242880 | tf_op jit(solution)/shard_map/convert_element_type | solution.py:95
  99.6 0.3 fusion.28
  100.0 0.9 fusion.60
  101.5 2.0 %fusion.46 = bf16[16,2048]{1,0:T(8,128)(2,1)} fusion(f32[2,8,16,128]{3,2,1,0:T(8,128)S(1)} %bitcast.209, f32[2,8,16,128]{3,2,1,0:T(8,128)S(1)} %bitcast.208, f32[2,8,16,128]{3,2,1,0:T(8,128)S(1)} %bitcast.207, f32[2,8,16,128]{3,2,1,0:T(8,128)S(1)} %bitcast.206, f32[2,8,16,128]{3,2,1,0:T(8,128)S(1)} %bitcast.205, f32[2,8,16,128]{3,2,1,0:T(8,128)S(1)} %bitcast.203, ...), kind=kLoop, calls=%fused_computation.59 | loop fusion | flops 360448 | bytes 1507328 | tf_op jit(solution)/shard_map/convert_element_type | solution.py:130
  (91 shorter events, 2.0 us)
Async XLA Ops:
  5.1 27.3 %collective-permute-start = (bf16[106496]{0:T(1024)(128)(2,1)}, bf16[106496]{0:T(1024)(128)(2,1)S(1)}, u32[]{:S(2)}, u32[]{:S(2)}) collective-permute-start(bf16[106496]{0:T(1024)(128)(2,1)} %constant_dynamic-update-slice_fusion.9), channel_id=1, source_target_pairs={{0,4},{4,8},{8,12},{12,0},{1,5},{5,9},{9,13},{13,1},{2,6},{6,10},{... | collective-permute-start | bytes 638984 | tf_op jit(solution)/shard_map/ppermute | solution.py:57
  8.1 24.3 %collective-permute-start.1 = (bf16[106496]{0:T(1024)(128)(2,1)}, bf16[106496]{0:T(1024)(128)(2,1)}, u32[]{:S(2)}, u32[]{:S(2)}) collective-permute-start(bf16[106496]{0:T(1024)(128)(2,1)} %constant_dynamic-update-slice_fusion.9), channel_id=1, source_target_pairs={{0,8},{4,12},{8,0},{12,4},{1,9},{5,13},{9,1},{13,5},{2,10},{6,14},... | collective-permute-start | bytes 638984 | tf_op jit(solution)/shard_map/ppermute | solution.py:57
  10.7 22.6 %collective-permute-start.2 = (bf16[106496]{0:T(1024)(128)(2,1)}, bf16[106496]{0:T(1024)(128)(2,1)}, u32[]{:S(2)}, u32[]{:S(2)}) collective-permute-start(bf16[106496]{0:T(1024)(128)(2,1)} %constant_dynamic-update-slice_fusion.9), channel_id=1, source_target_pairs={{0,12},{4,0},{8,4},{12,8},{1,13},{5,1},{9,5},{13,9},{2,14},{6,2},{... | collective-permute-start | bytes 638984 | tf_op jit(solution)/shard_map/ppermute | solution.py:57
  19.8 4.2 %copy-start.6 = (bf16[2,256,256]{2,1,0:T(8,128)(2,1)S(1)}, bf16[2,256,256]{2,1,0:T(8,128)(2,1)}, u32[]{:S(2)}) copy-start(bf16[2,256,256]{2,1,0:T(8,128)(2,1)} %param.9) | copy-start | bytes 786436
  27.0 5.1 %copy-start.15 = (s32[64]{0:T(128)S(1)}, s32[64]{0:T(128)}, u32[]{:S(2)}) copy-start(s32[64]{0:T(128)} %param.15) | copy-start | bytes 772
  27.1 7.2 %copy-start.4 = (bf16[16,2048]{1,0:T(8,128)(2,1)S(1)}, bf16[16,2048]{1,0:T(8,128)(2,1)}, u32[]{:S(2)}) copy-start(bf16[16,2048]{1,0:T(8,128)(2,1)} %param.13) | copy-start | bytes 196612
  32.4 11.2 %copy-start.7 = (bf16[106496]{0:T(1024)(128)(2,1)}, bf16[106496]{0:T(1024)(128)(2,1)S(1)}, u32[]{:S(2)}) copy-start(bf16[106496]{0:T(1024)(128)(2,1)S(1)} %collective-permute-done) | copy-start | bytes 638980
  43.6 19.6 %copy-start.3 = (f32[64,2,8]{2,0,1:T(8,128)}, f32[64,2,8]{2,0,1:T(8,128)S(1)}, u32[]{:S(2)}) copy-start(f32[64,2,8]{2,0,1:T(8,128)S(1)} %max.44) | copy-start | bytes 12292
  52.1 11.1 %copy-start.5 = (f32[64,2,8]{2,0,1:T(8,128)}, f32[64,2,8]{2,0,1:T(8,128)S(1)}, u32[]{:S(2)}) copy-start(f32[64,2,8]{2,0,1:T(8,128)S(1)} %add.103) | copy-start | bytes 12292
  52.8 11.8 %copy-start.8 = (bf16[106496]{0:T(1024)(128)(2,1)S(1)}, bf16[106496]{0:T(1024)(128)(2,1)}, u32[]{:S(2)}) copy-start(bf16[106496]{0:T(1024)(128)(2,1)} %copy-done.7) | copy-start | bytes 638980
  64.6 12.1 %copy-start.2 = (f32[64,2,8,128]{3,2,0,1:T(8,128)}, f32[64,2,8,128]{3,2,0,1:T(8,128)S(1)}, u32[]{:S(2)}) copy-start(f32[64,2,8,128]{3,2,0,1:T(8,128)S(1)} %fusion.27) | copy-start | bytes 1572868
  71.5 7.7 %copy-start.11 = (f32[64,2,8]{0,2,1:T(8,128)S(1)}, f32[64,2,8]{0,2,1:T(8,128)}, u32[]{:S(2)}) copy-start(f32[64,2,8]{0,2,1:T(8,128)} %copy.133) | copy-start | bytes 12292
  76.7 5.7 %slice-start.2 = ((f32[64,2,8]{2,0,1:T(8,128)}), f32[16,2,8]{2,0,1:T(8,128)S(1)}, s32[]{:S(2)}) async-start(f32[64,2,8]{2,0,1:T(8,128)} %copy-done.5), calls=%async_computation.2 | async-start | bytes 32768 | tf_op jit(solution)/shard_map/slice | solution.py:117
  76.7 5.9 %slice-start.1 = ((f32[64,2,8]{2,0,1:T(8,128)}), f32[16,2,8]{2,0,1:T(8,128)S(1)}, s32[]{:S(2)}) async-start(f32[64,2,8]{2,0,1:T(8,128)} %copy-done.3), calls=%async_computation.1 | async-start | bytes 32768 | tf_op jit(solution)/shard_map/slice | solution.py:116
  76.7 7.0 %copy-start.9 = (f32[256,2,8]{0,2,1:T(8,128)S(1)}, f32[256,2,8]{0,2,1:T(8,128)}, u32[]{:S(2)}) copy-start(f32[256,2,8]{0,2,1:T(8,128)} %get-tuple-element.25) | copy-start | bytes 49156
  76.7 7.0 %copy-start.10 = (f32[256,2,8]{0,2,1:T(8,128)S(1)}, f32[256,2,8]{0,2,1:T(8,128)}, u32[]{:S(2)}) copy-start(f32[256,2,8]{0,2,1:T(8,128)} %get-tuple-element.23) | copy-start | bytes 49156
  80.2 19.8 %collective-permute-start.3 = (f32[16,2080]{1,0:T(8,128)}, f32[16,2080]{1,0:T(8,128)}, u32[]{:S(2)}, u32[]{:S(2)}) collective-permute-start(f32[16,2080]{1,0:T(8,128)} %get-tuple-element.10), channel_id=1, source_target_pairs={{0,12},{4,0},{8,4},{12,8},{1,13},{5,1},{9,5},{13,9},{2,14},{6,2},{... | collective-permute-start | bytes 399368 | tf_op jit(solution)/shard_map/ppermute | solution.py:57
  80.7 19.3 %collective-permute-start.4 = (f32[16,2080]{1,0:T(8,128)}, f32[16,2080]{1,0:T(8,128)}, u32[]{:S(2)}, u32[]{:S(2)}) collective-permute-start(f32[16,2080]{1,0:T(8,128)} %get-tuple-element.12), channel_id=1, source_target_pairs={{0,8},{4,12},{8,0},{12,4},{1,9},{5,13},{9,1},{13,5},{2,10},{6,14},... | collective-permute-start | bytes 399368 | tf_op jit(solution)/shard_map/ppermute | solution.py:57
  82.4 17.6 %collective-permute-start.5 = (f32[16,2080]{1,0:T(8,128)}, f32[16,2080]{1,0:T(8,128)}, u32[]{:S(2)}, u32[]{:S(2)}) collective-permute-start(f32[16,2080]{1,0:T(8,128)} %get-tuple-element.11), channel_id=1, source_target_pairs={{0,4},{4,8},{8,12},{12,0},{1,5},{5,9},{9,13},{13,1},{2,6},{6,10},{... | collective-permute-start | bytes 399368 | tf_op jit(solution)/shard_map/ppermute | solution.py:57
  83.7 5.8 %copy-start = (f32[2,512,256,8]{2,1,3,0:T(8,128)S(1)}, f32[2,512,256,8]{2,1,3,0:T(8,128)}, u32[]{:S(2)}) copy-start(f32[2,512,256,8]{2,1,3,0:T(8,128)} %get-tuple-element.24) | copy-start | bytes 25165828
  89.5 2.2 %copy-start.1 = (f32[2,256,256,8]{2,1,3,0:T(8,128)S(1)}, f32[2,256,256,8]{2,1,3,0:T(8,128)}, u32[]{:S(2)}) copy-start(f32[2,256,256,8]{2,1,3,0:T(8,128)} %get-tuple-element.26) | copy-start | bytes 12582916
  97.2 2.8 %slice-start = ((f32[64,2,8,128]{3,2,0,1:T(8,128)}), f32[16,2,8,128]{3,2,0,1:T(8,128)S(1)}, s32[]{:S(2)}) async-start(f32[64,2,8,128]{3,2,0,1:T(8,128)} %copy-done.2), calls=%async_computation | async-start | bytes 262144 | tf_op jit(solution)/shard_map/slice | solution.py:118
  97.2 2.8 %copy-start.12 = (f32[16,16]{1,0:T(8,128)S(1)}, f32[16,16]{1,0:T(8,128)}, u32[]{:S(2)}) copy-start(f32[16,16]{1,0:T(8,128)} %copy.139) | copy-start | bytes 3076
  97.2 2.8 %copy-start.13 = (f32[16,16]{1,0:T(8,128)S(1)}, f32[16,16]{1,0:T(8,128)}, u32[]{:S(2)}) copy-start(f32[16,16]{1,0:T(8,128)} %copy.136) | copy-start | bytes 3076
  97.2 2.8 %copy-start.14 = (f32[16,16]{1,0:T(8,128)S(1)}, f32[16,16]{1,0:T(8,128)}, u32[]{:S(2)}) copy-start(f32[16,16]{1,0:T(8,128)} %copy.127) | copy-start | bytes 3076

commit v2 on v1

v2 whole, which is shorter than its diff:
```python
import functools

import jax
import jax.numpy as jnp
from jax import lax
from jax.experimental import pallas as pl
from jax.experimental.pallas import tpu as pltpu
from jax.sharding import PartitionSpec as P

HD = 128


masked_score = -1e30


def widen(per_head):
    return jnp.repeat(per_head, HD, axis=-1)


def attention_kernel(masks, normalize, group_size, *refs):
    length_ref, q_ref = refs[0], refs[1]
    part_count = len(masks)
    kv_refs = refs[2 : 2 + 2 * part_count]
    rest = refs[2 + 2 * part_count :]
    if "pos" in masks:
        key_pos_ref, own_pos_ref = rest[0], rest[1]
        rest = rest[2:]
    out_refs = rest
    rows = q_ref.shape[0]
    scale = 1.0 / jnp.sqrt(jnp.float32(HD))
    visible = []
    for index, mask in enumerate(masks):
        key_count = kv_refs[2 * index].shape[0]
        if mask is None:
            visible.append(None)
        elif mask == "cache":
            cols = lax.broadcasted_iota(jnp.int32, (rows, key_count), 1)
            visible.append(cols < length_ref[0])
        elif mask == "causal":
            cols = lax.broadcasted_iota(jnp.int32, (rows, key_count), 1)
            row_ids = lax.broadcasted_iota(jnp.int32, (rows, key_count), 0)
            visible.append(cols <= row_ids)
        else:
            visible.append(key_pos_ref[...] <= own_pos_ref[...])
    for head in range(group_size):
        columns = slice(head * HD, (head + 1) * HD)
        q_head = q_ref[:, columns]
        all_scores = []
        for index in range(part_count):
            scores = lax.dot_general(
                q_head,
                kv_refs[2 * index][...],
                (((1,), (1,)), ((), ())),
                preferred_element_type=jnp.float32,
            ) * scale
            if visible[index] is not None:
                scores = jnp.where(visible[index], scores, masked_score)
            all_scores.append(scores)
        peak = jnp.max(all_scores[0], axis=1, keepdims=True)
        for scores in all_scores[1:]:
            peak = jnp.maximum(peak, jnp.max(scores, axis=1, keepdims=True))
        total = None
        output = None
        for index, scores in enumerate(all_scores):
            weights = jnp.exp(scores - peak)
            part_total = jnp.sum(weights, axis=1, keepdims=True)
            part_output = jnp.dot(
                weights.astype(jnp.bfloat16),
                kv_refs[2 * index + 1][...],
                preferred_element_type=jnp.float32,
            )
            total = part_total if total is None else total + part_total
            output = part_output if output is None else output + part_output
        if normalize:
            out_refs[0][:, columns] = (output / total).astype(out_refs[0].dtype)
        else:
            out_refs[0][:, columns] = output
            out_refs[1][:, columns] = jnp.broadcast_to(peak, (rows, HD))
            out_refs[2][:, columns] = jnp.broadcast_to(total, (rows, HD))


def attention(queries, parts, normalize, length=None, positions=None):
    rows, query_width = queries.shape
    kv_heads = parts[0][0].shape[2] // HD
    group_size = query_width // HD // kv_heads
    group_width = group_size * HD
    if length is None:
        length = jnp.zeros((1,), jnp.int32)
    masks = tuple(mask for _, mask in parts)
    in_specs = [pl.BlockSpec((rows, group_width), lambda g, n: (0, g))]
    operands = [queries]
    for pair, _ in parts:
        key_count = pair.shape[1]
        in_specs.append(pl.BlockSpec((pl.Squeezed(), key_count, HD), lambda g, n: (0, 0, g)))
        in_specs.append(pl.BlockSpec((pl.Squeezed(), key_count, HD), lambda g, n: (1, 0, g)))
        operands += [pair, pair]
    if positions is not None:
        key_pos = positions[0].reshape(1, -1)
        own_pos = positions[1].reshape(-1, 1)
        in_specs.append(pl.BlockSpec(key_pos.shape, lambda g, n: (0, 0)))
        in_specs.append(pl.BlockSpec(own_pos.shape, lambda g, n: (0, 0)))
        operands += [key_pos, own_pos]
    out_block = pl.BlockSpec((rows, group_width), lambda g, n: (0, g))
    if normalize:
        out_shape = [jax.ShapeDtypeStruct((rows, query_width), jnp.bfloat16)]
        out_specs = [out_block]
    else:
        out_shape = [jax.ShapeDtypeStruct((rows, query_width), jnp.float32)] * 3
        out_specs = [out_block] * 3
    return pl.pallas_call(
        functools.partial(attention_kernel, masks, normalize, group_size),
        grid_spec=pltpu.PrefetchScalarGridSpec(
            num_scalar_prefetch=1,
            grid=(kv_heads,),
            in_specs=in_specs,
            out_specs=out_specs,
        ),
        out_shape=out_shape,
    )(length, *operands)


def compact(wide):
    rows, width = wide.shape
    return wide.reshape(rows, width // HD, HD)[:, :, 0]


def shifted(value, shift, count):
    return lax.ppermute(value, "ctx", [(j, (j + shift) % count) for j in range(count)])


def make_local(ctx_count):
    def local(q_block, kv_block, anchor_kv, cache_kv, cache_len, query_q, query_kv, query_pos):
        me = lax.axis_index("ctx")
        own_count = query_q.shape[0]
        anchor_rows = anchor_kv.shape[1]
        width = kv_block.shape[2]
        pieces = (anchor_kv.reshape(-1), query_q.reshape(-1), query_kv.reshape(-1))
        sizes = [piece.shape[0] for piece in pieces]
        packed = jnp.concatenate(pieces)
        slots = [packed] + [shifted(packed, k, ctx_count) for k in range(1, ctx_count)]

        def unpack(slot):
            a = slot[: sizes[0]].reshape(2, anchor_rows, width)
            q = slot[sizes[0] : sizes[0] + sizes[1]].reshape(own_count, -1)
            kv = slot[sizes[0] + sizes[1] :].reshape(2, own_count, width)
            return a, q, kv

        unpacked = [unpack(slot) for slot in slots]
        anchor = jnp.concatenate([u[0] for u in unpacked], axis=1)
        all_queries = jnp.concatenate([u[1] for u in unpacked], axis=0)
        all_query_kv = jnp.concatenate([u[2] for u in unpacked], axis=1)
        slot_pos = jnp.concatenate(
            [
                lax.dynamic_slice_in_dim(query_pos, ((me - k) % ctx_count) * own_count, own_count)
                for k in range(ctx_count)
            ]
        )
        own_pos = slot_pos[:own_count]

        (block_out,) = attention(q_block, [(anchor, None), (kv_block, "causal")], True)

        context_output, context_peak, context_totals = attention(
            all_queries, [(cache_kv, "cache"), (kv_block, None)], False, length=cache_len
        )
        local_output, local_peak, local_totals = attention(
            query_q,
            [(anchor, None), (all_query_kv, "pos")],
            False,
            positions=(slot_pos, own_pos),
        )
        context_peak = compact(context_peak)
        context_totals = compact(context_totals)
        heads = context_peak.shape[1]
        context_packed = jnp.concatenate([context_output, context_peak, context_totals], axis=1)
        remote = [context_packed[:own_count]]
        for k in range(1, ctx_count):
            section = context_packed[k * own_count : (k + 1) * own_count]
            remote.append(shifted(section, -k, ctx_count))
        peaks = [compact(local_peak)] + [r[:, -2 * heads : -heads] for r in remote]
        totals = [compact(local_totals)] + [r[:, -heads:] for r in remote]
        outputs = [local_output] + [r[:, : -2 * heads] for r in remote]
        top_score = peaks[0]
        for peak in peaks[1:]:
            top_score = jnp.maximum(top_score, peak)
        merged_totals = None
        merged_output = None
        for peak, total, output in zip(peaks, totals, outputs):
            factor = jnp.exp(peak - top_score)
            t = total * factor
            o = output * widen(factor)
            merged_totals = t if merged_totals is None else merged_totals + t
            merged_output = o if merged_output is None else merged_output + o
        query_out = (merged_output / widen(merged_totals)).astype(jnp.bfloat16)
        return (block_out, query_out)

    return local


def solution(mesh):
    in_specs = (
        P(("groups", "ctx"), "head"),
        P(None, ("groups", "ctx"), "head"),
        P(None, ("groups", "ctx"), "head"),
        P(None, ("groups", "ctx"), "head"),
        P(("groups", "ctx")),
        P(("groups", "ctx"), "head"),
        P(None, ("groups", "ctx"), "head"),
        P("groups"),
    )
    out_specs = (P(("groups", "ctx"), "head"), P(("groups", "ctx"), "head"))
    return jax.shard_map(
        make_local(mesh.shape["ctx"]),
        mesh=mesh,
        in_specs=in_specs,
        out_specs=out_specs,
        check_vma=False,
    )
```

time: 105 us -> 75.1 us (0.72)
  matrix products: 35.1 us -> 0 us
  Pallas kernels: 0 us -> 32 us
  local copies, waits for them, and re-layouts: 37.9 us -> 13.7 us
  other arithmetic: 19.5 us -> 4.69 us
  waiting for transfers between devices: 0.02 us -> 8.84 us
  starting transfers between devices: 9.11 us -> 13.8 us
    dot_general x12 -> x0, matrix products: 35.1 us -> none  [the longest x6 18.5 us: partial_attention(): jnp.einsum('rkgd,skd->rkgs', grouped, key_heads, preferred_element_type=j...]
    pallas_call x0 -> x3, Pallas kernels: none -> 32 us  [attention(): pl.pallas_call(functools.partial(attention_kernel, masks, normalize, grou...]
    reduce_sum x6 -> x0, other arithmetic: 14.6 us -> none  [partial_attention(): part_total = jnp.sum(weights, axis=-1)]
    ppermute x6, waiting for transfers between devices: 0.02 us -> 8.84 us  [shifted(): lax.ppermute(value, 'ctx', [(j, (j + shift) % count) for j in range(count)])]
    unnamed x50 -> x24, local copies, waits for them, and re-layouts: 18.6 us -> 10 us
    slice x18 -> x2, local copies, waits for them, and re-layouts: 6.22 us -> 0.02 us  [the longest x1 0.01 us: local(): totals = [compact(local_totals)] + [r[:, -heads:] for r in remote]]
    ppermute x6, starting transfers between devices: 9.11 us -> 13.8 us  [shifted(): lax.ppermute(value, 'ctx', [(j, (j + shift) % count) for j in range(count)])]
    concatenate x1 -> x2, other arithmetic: 0.08 us -> 2.21 us  [the longest x1 1.58 us: local(): all_queries = jnp.concatenate([u[1] for u in unpacked], axis=0)]
  transfers between devices with their start and end apart: 6 -> 6, of which waited for: 0 -> 2; matrix products, arithmetic and copies ran while one was open for 35% -> 9% of each run, Pallas kernels for 0% -> 20%
where the time goes in v2:
time: 75.1 us; the launch traced here: 74.6 us
  Pallas kernels  32 us (43%)
  starting transfers between devices  13.8 us (18%)
  local copies, waits for them, and re-layouts  13.7 us (18%)
  waiting for transfers between devices  8.84 us (12%)
  other arithmetic  4.69 us (6%)
  between operations  1.6 us (2%)
    pallas_call x3, Pallas kernels, attention(): pl.pallas_call(functools.partial(attention_kernel, masks, normalize, grou...  32 us
    ppermute x6, starting transfers between devices, shifted(): lax.ppermute(value, 'ctx', [(j, (j + shift) % count) for j in range(count)])  13.8 us
    unnamed x24, local copies, waits for them, and re-layouts  10 us
    ppermute x6, waiting for transfers between devices, shifted(): lax.ppermute(value, 'ctx', [(j, (j + shift) % count) for j in range(count)])  8.84 us
    convert_element_type x1, other arithmetic, local(): query_out = (merged_output / widen(merged_totals)).astype(jnp.bfloat16)  1.82 us
    concatenate x1, other arithmetic, local(): all_queries = jnp.concatenate([u[1] for u in unpacked], axis=0)  1.58 us
  transfers between devices with their start and end apart: 6, of which 2 were waited for; matrix products, arithmetic and copies ran while one was open for 9% of the time, Pallas kernels for 20%

profile of v2, /device:TPU:0, one launch (start us, length us, event | category | flops | bytes accessed | tf_op | source)
XLA Modules:
  0.0 74.6 jit_solution(17064323393912680990)
XLA Ops:
  0.6 1.0 %copy.28 = bf16[32,2,8,128]{3,1,2,0:T(2,128)(2,1)S(1)} copy(bf16[32,2,8,128]{3,2,1,0:T(8,128)(2,1)} %bitcast.102) | data formatting | bytes 262144
  1.7 0.9 %copy.29 = bf16[2,16,8,128]{3,1,2,0:T(8,128)(2,1)S(1)} copy(bf16[2,16,8,128]{3,2,1,0:T(8,128)(2,1)} %bitcast.93) | data formatting | bytes 131072
  2.5 0.7 copy.30
  3.3 3.1 %collective-permute-start = (bf16[106496]{0:T(1024)(128)(2,1)S(1)}, bf16[106496]{0:T(1024)(128)(2,1)S(1)}, u32[]{:S(2)}, u32[]{:S(2)}) collective-permute-start(bf16[106496]{0:T(1024)(128)(2,1)S(1)} %constant_dynamic-update-slice_fusion.5), channel_id=1, source_target_pairs={{0,4},{4,8},{8,12},{12,0},{1,5},{5,9},{9,13},{13,1},{2,6},{6,10},{... | collective-permute-start | bytes 638984 | tf_op jit(solution)/shard_map/ppermute | solution.py:128
  6.4 2.6 %collective-permute-start.1 = (bf16[106496]{0:T(1024)(128)(2,1)S(1)}, bf16[106496]{0:T(1024)(128)(2,1)S(1)}, u32[]{:S(2)}, u32[]{:S(2)}) collective-permute-start(bf16[106496]{0:T(1024)(128)(2,1)S(1)} %constant_dynamic-update-slice_fusion.5), channel_id=1, source_target_pairs={{0,8},{4,12},{8,0},{12,4},{1,9},{5,13},{9,1},{13,5},{2,10},{6,14},... | collective-permute-start | bytes 638984 | tf_op jit(solution)/shard_map/ppermute | solution.py:128
  8.9 1.3 %collective-permute-start.2 = (bf16[106496]{0:T(1024)(128)(2,1)S(1)}, bf16[106496]{0:T(1024)(128)(2,1)S(1)}, u32[]{:S(2)}, u32[]{:S(2)}) collective-permute-start(bf16[106496]{0:T(1024)(128)(2,1)S(1)} %constant_dynamic-update-slice_fusion.5), channel_id=1, source_target_pairs={{0,12},{4,0},{8,4},{12,8},{1,13},{5,1},{9,5},{13,9},{2,14},{6,2},{... | collective-permute-start | bytes 638984 | tf_op jit(solution)/shard_map/ppermute | solution.py:128
  10.3 0.9 %fusion.17 = (s32[16]{0:T(128)S(1)}, s32[16]{0:T(128)S(1)}, s32[16]{0:T(128)S(1)}, s32[16]{0:T(128)S(1)}) fusion(s32[64]{0:T(128)} %param.15, s32[]{:T(128)S(6)} %select_n.32, s32[]{:T(128)S(6)} %select_n.34, s32[]{:T(128)S(6)} %select_n.38, s32[]{:T(128)S(6)} %select_n.36), kind=kLoop, calls=%fused_computation.42 | loop fusion | bytes 528 | tf_op jit(solution)/shard_map/dynamic_slice | solution.py:154
  11.2 0.7 copy.15.refs_7_
  12.5 0.6 add_bitcast_fusion.refs_6_
  13.1 0.9 %constant_dynamic-update-slice_fusion.4 = bf16[2,512,256]{2,1,0:T(8,128)(2,1)S(1)} fusion(bf16[2,128,256]{2,1,0:T(8,128)(2,1)} %param.10), kind=kLoop, calls=%fused_computation.17 | loop fusion | bytes 262144
  14.0 0.6 collective-permute-done
  14.7 8.2 %collective-permute-done.1 = bf16[106496]{0:T(1024)(128)(2,1)S(1)} collective-permute-done((bf16[106496]{0:T(1024)(128)(2,1)S(1)}, bf16[106496]{0:T(1024)(128)(2,1)S(1)}, u32[]{:S(2)}, u32[]{:S(2)}) %collective-permute-start.1) | collective-permute-done | bytes 213024 | tf_op jit(solution)/shard_map/ppermute | solution.py:128
  23.0 0.0 collective-permute-done.2
  23.2 1.6 %pad_maximum_fusion.refs_1_ = bf16[64,2048]{1,0:T(8,128)(2,1)} fusion(bf16[16,2048]{1,0:T(8,128)(2,1)S(1)} %slice.174, bf16[16,2048]{1,0:T(8,128)(2,1)S(1)} %slice.172, bf16[16,2048]{1,0:T(8,128)(2,1)S(1)} %slice.170, bf16[16,2048]{1,0:T(8,128)(2,1)} %refs_1_.3), kind=kLoop, calls=%fused_computation | loop fusion | flops 1048576 | bytes 524288 | tf_op jit(solution)/shard_map/concatenate | solution.py:150
  24.8 17.0 %shard_map.97 = (f32[64,2048]{1,0:T(8,128)}, f32[64,2048]{1,0:T(8,128)}, f32[64,2048]{1,0:T(8,128)}) custom-call(s32[1]{0:T(128)S(6)} %copy.52.refs_0_, bf16[64,2048]{1,0:T(8,128)(2,1)} %pad_maximum_fusion.refs_1_, bf16[2,4096,256]{2,1,0:T(8,128)(2,1)} %refs_3_.1, bf16[2,4096,256]{2,1,0:T(8,128)(2,1)} %refs_3_.1, bf16[2,256,256]{2,1,0:T(8,128)(2,1)} %refs_5_.3, ...), custom_call_target="tpu_custom_call" | custom-call | tf_op jit(solution)/shard_map/pallas_call | solution.py:110
  41.8 0.0 copy-start.2
  41.8 1.1 %copy.32 = f32[8,8,16,128]{3,2,1,0:T(8,128)S(1)} copy(f32[8,8,16,128]{3,1,2,0:T(8,128)} %bitcast.101) | data formatting | bytes 1048576
  43.0 0.4 copy.24
  43.4 1.2 %copy.33 = f32[8,8,16,128]{3,2,1,0:T(8,128)S(1)} copy(f32[8,8,16,128]{3,1,2,0:T(8,128)} %bitcast.100) | data formatting | bytes 1048576
  44.6 0.4 copy.25
  45.0 1.1 %concatenate.23 = f32[64,2080]{1,0:T(8,128)S(1)} concatenate(f32[64,2048]{1,0:T(8,128)} %get-tuple-element.11, f32[64,16]{1,0:T(8,128)S(1)} %bitcast.107, f32[64,16]{1,0:T(8,128)S(1)} %bitcast.108), dimensions={1} | concatenate | bytes 1064960 | tf_op jit(solution)/shard_map/concatenate | solution.py:174
  46.2 6.1 %collective-permute-start.3 = (f32[16,2080]{1,0:T(8,128)S(1)}, f32[16,2080]{1,0:T(8,128)S(1)}, u32[]{:S(2)}, u32[]{:S(2)}) collective-permute-start(f32[16,2080]{1,0:T(8,128)S(1)} %get-tuple-element.20), channel_id=1, source_target_pairs={{0,12},{4,0},{8,4},{12,8},{1,13},{5,1},{9,5},{13,9},{2,14},{6,2},{... | collective-permute-start | bytes 399368 | tf_op jit(solution)/shard_map/ppermute | solution.py:128
  52.3 0.3 collective-permute-start.4
  52.6 0.3 collective-permute-start.5
  52.9 0.0 copy-done.2
  53.0 0.6 pad_maximum_fusion.1.refs_4_.refs_5_
  53.7 0.0 copy-start
  53.7 0.8 %copy-done = bf16[2,512,256]{2,1,0:T(8,128)(2,1)} copy-done((bf16[2,512,256]{2,1,0:T(8,128)(2,1)}, bf16[2,512,256]{2,1,0:T(8,128)(2,1)S(1)}, u32[]{:S(2)}) %copy-start) | copy-done | bytes 524312
  54.5 6.2 %shard_map.96 = (f32[16,2048]{1,0:T(8,128)}, f32[16,2048]{1,0:T(8,128)}, f32[16,2048]{1,0:T(8,128)}) custom-call(s32[1]{0:T(128)} %constant.35.clone.1.refs_0_, bf16[16,2048]{1,0:T(8,128)(2,1)} %refs_1_.3, bf16[2,512,256]{2,1,0:T(8,128)(2,1)} %copy-done, bf16[2,512,256]{2,1,0:T(8,128)(2,1)} %copy-done, ...), custom_call_target="tpu_custom_call" | custom-call | tf_op jit(solution)/shard_map/pallas_call | solution.py:110
  60.7 0.0 copy-start.1
  60.7 1.0 %copy.31 = f32[2,8,16,128]{3,2,1,0:T(8,128)S(1)} copy(f32[2,8,16,128]{3,1,2,0:T(8,128)} %bitcast.110) | data formatting | bytes 262144
  61.7 0.1 copy.22
  61.9 1.0 %copy.39 = f32[2,8,16,128]{3,2,1,0:T(8,128)S(1)} copy(f32[2,8,16,128]{3,1,2,0:T(8,128)} %bitcast.109) | data formatting | bytes 262144
  62.8 0.1 copy.26
  63.0 0.2 copy.23
  63.1 0.2 copy.27
  63.3 8.7 %shard_map.95 = bf16[256,2048]{1,0:T(8,128)(2,1)} custom-call(s32[1]{0:T(128)} %constant.35.clone.1.refs_0_, bf16[256,2048]{1,0:T(8,128)(2,1)} %refs_1_.2, bf16[2,512,256]{2,1,0:T(8,128)(2,1)} %copy-done, bf16[2,512,256]{2,1,0:T(8,128)(2,1)} %copy-done, bf16[2,256,256]{2,1,0:T(8,128)(2,1)} %refs_5_.3, bf16[2,256,256]{2,1,0:T(8,128)(2,1)} %refs_5_.3), custom_call_target="tpu_custom_call" | custom-call | tf_op jit(solution)/shard_map/pallas_call | solution.py:110
  72.0 0.0 collective-permute-done.3
  72.0 0.0 collective-permute-done.4
  72.0 0.0 collective-permute-done.5
  72.1 0.1 fusion.5
  72.1 0.1 broadcast_in_dim.18
  72.2 0.1 broadcast_in_dim.19
  72.3 0.1 broadcast_in_dim.20
  72.4 0.1 broadcast_in_dim.21
  72.5 0.1 broadcast_in_dim.22
  72.6 0.1 broadcast_in_dim.23
  72.7 0.0 copy-done.1
  72.7 1.8 %fusion = bf16[16,2048]{1,0:T(8,128)(2,1)} fusion(f32[2,8,16,128]{3,2,1,0:T(8,128)S(1)} %bitcast.99, f32[2,8,16,128]{3,2,1,0:T(8,128)S(1)} %bitcast.98, f32[2,8,16,128]{3,2,1,0:T(8,128)S(1)} %bitcast.97, f32[2,8,16,128]{3,2,1,0:T(8,128)S(1)} %bitcast.96, f32[2,8,16,128]{3,2,1,0:T(8,128)S(1)} %bitcast.95, f32[16,2048]{1,0:T(8,128)S(1)} %copy-done.1, ...), kind=kLoop, calls=%fused_computation.2 | loop fusion | flops 360448 | bytes 1507328 | tf_op jit(solution)/shard_map/convert_element_type | solution.py:193
  (27 shorter events, 0.4 us)
Async XLA Ops:
  3.3 11.3 %collective-permute-start = (bf16[106496]{0:T(1024)(128)(2,1)S(1)}, bf16[106496]{0:T(1024)(128)(2,1)S(1)}, u32[]{:S(2)}, u32[]{:S(2)}) collective-permute-start(bf16[106496]{0:T(1024)(128)(2,1)S(1)} %constant_dynamic-update-slice_fusion.5), channel_id=1, source_target_pairs={{0,4},{4,8},{8,12},{12,0},{1,5},{5,9},{9,13},{13,1},{2,6},{6,10},{... | collective-permute-start | bytes 638984 | tf_op jit(solution)/shard_map/ppermute | solution.py:128
  6.4 16.5 %collective-permute-start.1 = (bf16[106496]{0:T(1024)(128)(2,1)S(1)}, bf16[106496]{0:T(1024)(128)(2,1)S(1)}, u32[]{:S(2)}, u32[]{:S(2)}) collective-permute-start(bf16[106496]{0:T(1024)(128)(2,1)S(1)} %constant_dynamic-update-slice_fusion.5), channel_id=1, source_target_pairs={{0,8},{4,12},{8,0},{12,4},{1,9},{5,13},{9,1},{13,5},{2,10},{6,14},... | collective-permute-start | bytes 638984 | tf_op jit(solution)/shard_map/ppermute | solution.py:128
  8.9 14.1 %collective-permute-start.2 = (bf16[106496]{0:T(1024)(128)(2,1)S(1)}, bf16[106496]{0:T(1024)(128)(2,1)S(1)}, u32[]{:S(2)}, u32[]{:S(2)}) collective-permute-start(bf16[106496]{0:T(1024)(128)(2,1)S(1)} %constant_dynamic-update-slice_fusion.5), channel_id=1, source_target_pairs={{0,12},{4,0},{8,4},{12,8},{1,13},{5,1},{9,5},{13,9},{2,14},{6,2},{... | collective-permute-start | bytes 638984 | tf_op jit(solution)/shard_map/ppermute | solution.py:128
  41.8 11.1 %copy-start.2 = (bf16[2,16,256]{2,1,0:T(8,128)(2,1)S(1)}, bf16[2,16,256]{2,1,0:T(8,128)(2,1)}, u32[]{:S(2)}) copy-start(bf16[2,16,256]{2,1,0:T(8,128)(2,1)} %param.14) | copy-start | bytes 49156
  46.2 25.9 %collective-permute-start.3 = (f32[16,2080]{1,0:T(8,128)S(1)}, f32[16,2080]{1,0:T(8,128)S(1)}, u32[]{:S(2)}, u32[]{:S(2)}) collective-permute-start(f32[16,2080]{1,0:T(8,128)S(1)} %get-tuple-element.20), channel_id=1, source_target_pairs={{0,12},{4,0},{8,4},{12,8},{1,13},{5,1},{9,5},{13,9},{2,14},{6,2},{... | collective-permute-start | bytes 399368 | tf_op jit(solution)/shard_map/ppermute | solution.py:128
  52.3 19.8 %collective-permute-start.4 = (f32[16,2080]{1,0:T(8,128)S(1)}, f32[16,2080]{1,0:T(8,128)S(1)}, u32[]{:S(2)}, u32[]{:S(2)}) collective-permute-start(f32[16,2080]{1,0:T(8,128)S(1)} %get-tuple-element.22), channel_id=1, source_target_pairs={{0,8},{4,12},{8,0},{12,4},{1,9},{5,13},{9,1},{13,5},{2,10},{6,14},... | collective-permute-start | bytes 399368 | tf_op jit(solution)/shard_map/ppermute | solution.py:128
  52.6 19.5 %collective-permute-start.5 = (f32[16,2080]{1,0:T(8,128)S(1)}, f32[16,2080]{1,0:T(8,128)S(1)}, u32[]{:S(2)}, u32[]{:S(2)}) collective-permute-start(f32[16,2080]{1,0:T(8,128)S(1)} %get-tuple-element.21), channel_id=1, source_target_pairs={{0,4},{4,8},{8,12},{12,0},{1,5},{5,9},{9,13},{13,1},{2,6},{6,10},{... | collective-permute-start | bytes 399368 | tf_op jit(solution)/shard_map/ppermute | solution.py:128
  53.7 0.8 %copy-start = (bf16[2,512,256]{2,1,0:T(8,128)(2,1)}, bf16[2,512,256]{2,1,0:T(8,128)(2,1)S(1)}, u32[]{:S(2)}) copy-start(bf16[2,512,256]{2,1,0:T(8,128)(2,1)S(1)} %constant_dynamic-update-slice_fusion.1.refs_2_.refs_3_) | copy-start | bytes 1572868
  60.7 12.0 %copy-start.1 = (f32[16,2048]{1,0:T(8,128)S(1)}, f32[16,2048]{1,0:T(8,128)}, u32[]{:S(2)}) copy-start(f32[16,2048]{1,0:T(8,128)} %get-tuple-element.8) | copy-start | bytes 393220

commit v3 on v2

v3 whole, which is shorter than its diff:
```python
import functools

import jax
import jax.numpy as jnp
from jax import lax
from jax.experimental import pallas as pl
from jax.experimental.pallas import tpu as pltpu
from jax.sharding import PartitionSpec as P

HD = 128


masked_score = -1e30


def widen(per_head):
    return jnp.repeat(per_head, HD, axis=-1)


def chunk_size(rows, key_count):
    size = min(key_count, max(128, 32768 // rows))
    while key_count % size:
        size //= 2
    return size


def attention_kernel(masks, normalize, rows, group_size, *refs):
    length_ref, q_ref = refs[0], refs[1]
    part_count = len(masks)
    kv_refs = refs[2 : 2 + 2 * part_count]
    rest = refs[2 + 2 * part_count :]
    if "pos" in masks:
        key_pos_ref, own_pos_ref = rest[0], rest[1]
        rest = rest[2:]
    out_ref = rest[0]
    side_ref = rest[1] if len(rest) > 1 else None
    scale = 1.0 / jnp.sqrt(jnp.float32(HD))
    stack = max(1, min(group_size, 512 // rows))
    for first in range(0, group_size, stack):
        heads = list(range(first, min(group_size, first + stack)))
        lhs = jnp.concatenate([q_ref[:, h * HD : (h + 1) * HD] for h in heads], axis=0)
        m_rows = lhs.shape[0]

        def chunk_visible(index, start, size):
            mask = masks[index]
            if mask is None:
                return None
            cols = start + lax.broadcasted_iota(jnp.int32, (m_rows, size), 1)
            if mask == "cache":
                return cols < length_ref[0]
            if mask == "causal":
                tokens = lax.broadcasted_iota(jnp.int32, (m_rows, size), 0)
                if m_rows > rows:
                    tokens = lax.rem(tokens, rows)
                return cols <= tokens
            own = own_pos_ref[...]
            if m_rows > rows:
                own = jnp.concatenate([own] * (m_rows // rows), axis=0)
            return key_pos_ref[:, pl.ds(start, size)] <= own

        def raw_scores(index, start, size):
            keys = kv_refs[2 * index][pl.ds(start, size), :]
            return lax.dot_general(
                lhs, keys, (((1,), (1,)), ((), ())), preferred_element_type=jnp.float32
            )

        def over_chunks(index, body, carry):
            key_count = kv_refs[2 * index].shape[0]
            size = chunk_size(m_rows, key_count)
            count = key_count // size

            def step(c, carry):
                start = pl.multiple_of(c * size, size)
                return body(index, start, size, carry)

            if count == 1:
                return step(0, carry)
            return lax.fori_loop(0, count, step, carry)

        def max_body(index, start, size, peak):
            raw = raw_scores(index, start, size)
            visible = chunk_visible(index, start, size)
            if visible is not None:
                raw = jnp.where(visible, raw, -jnp.inf)
            return jnp.maximum(peak, jnp.max(raw, axis=1, keepdims=True))

        peak = jnp.full((m_rows, 1), -jnp.inf, jnp.float32)
        for index in range(part_count):
            peak = over_chunks(index, max_body, peak)
        peak = peak * scale

        def sum_body(index, start, size, carry):
            total, output = carry
            scores = raw_scores(index, start, size) * scale
            visible = chunk_visible(index, start, size)
            if visible is not None:
                scores = jnp.where(visible, scores, masked_score)
            weights = jnp.exp(scores - peak)
            total = total + jnp.sum(weights, axis=1, keepdims=True)
            values = kv_refs[2 * index + 1][pl.ds(start, size), :]
            output = output + jnp.dot(
                weights.astype(jnp.bfloat16), values, preferred_element_type=jnp.float32
            )
            return total, output

        carry = (jnp.zeros((m_rows, 1), jnp.float32), jnp.zeros((m_rows, HD), jnp.float32))
        for index in range(part_count):
            carry = over_chunks(index, sum_body, carry)
        total, output = carry
        for slot, h in enumerate(heads):
            rows_of = slice(slot * rows, (slot + 1) * rows)
            if normalize:
                out_ref[:, h * HD : (h + 1) * HD] = (output[rows_of] / total[rows_of]).astype(
                    out_ref.dtype
                )
            else:
                out_ref[:, h * HD : (h + 1) * HD] = output[rows_of]
                side_ref[:, h : h + 1] = peak[rows_of]
                side_ref[:, HD // 2 + h : HD // 2 + h + 1] = total[rows_of]


def attention(queries, parts, normalize, length=None, positions=None):
    rows, query_width = queries.shape
    kv_heads = parts[0][0].shape[2] // HD
    group_size = query_width // HD // kv_heads
    group_width = group_size * HD
    if length is None:
        length = jnp.zeros((1,), jnp.int32)
    masks = tuple(mask for _, mask in parts)
    in_specs = [pl.BlockSpec((rows, group_width), lambda g, n: (0, g))]
    operands = [queries]
    for pair, _ in parts:
        key_count = pair.shape[1]
        in_specs.append(pl.BlockSpec((pl.Squeezed(), key_count, HD), lambda g, n: (0, 0, g)))
        in_specs.append(pl.BlockSpec((pl.Squeezed(), key_count, HD), lambda g, n: (1, 0, g)))
        operands += [pair, pair]
    if positions is not None:
        key_pos = positions[0].reshape(1, -1)
        own_pos = positions[1].reshape(-1, 1)
        in_specs.append(pl.BlockSpec(key_pos.shape, lambda g, n: (0, 0)))
        in_specs.append(pl.BlockSpec(own_pos.shape, lambda g, n: (0, 0)))
        operands += [key_pos, own_pos]
    out_shape = [
        jax.ShapeDtypeStruct((rows, query_width), jnp.bfloat16 if normalize else jnp.float32)
    ]
    out_specs = [pl.BlockSpec((rows, group_width), lambda g, n: (0, g))]
    if not normalize:
        out_shape.append(jax.ShapeDtypeStruct((kv_heads, rows, HD), jnp.float32))
        out_specs.append(pl.BlockSpec((pl.Squeezed(), rows, HD), lambda g, n: (g, 0, 0)))
    return pl.pallas_call(
        functools.partial(attention_kernel, masks, normalize, rows, group_size),
        grid_spec=pltpu.PrefetchScalarGridSpec(
            num_scalar_prefetch=1,
            grid=(kv_heads,),
            in_specs=in_specs,
            out_specs=out_specs,
        ),
        out_shape=out_shape,
    )(length, *operands)


def shifted(value, shift, count):
    return lax.ppermute(value, "ctx", [(j, (j + shift) % count) for j in range(count)])


def make_local(ctx_count):
    def local(q_block, kv_block, anchor_kv, cache_kv, cache_len, query_q, query_kv, query_pos):
        me = lax.axis_index("ctx")
        own_count = query_q.shape[0]
        width = kv_block.shape[2]
        query_width = query_q.shape[1]
        kv_heads = width // HD
        group_size = query_width // HD // kv_heads
        packed = jnp.concatenate([query_q.reshape(-1), query_kv.reshape(-1)])
        query_slots = [packed] + [shifted(packed, k, ctx_count) for k in range(1, ctx_count)]
        anchor_slots = [anchor_kv] + [shifted(anchor_kv, k, ctx_count) for k in range(1, ctx_count)]
        split = own_count * query_width
        all_queries = jnp.concatenate(
            [slot[:split].reshape(own_count, query_width) for slot in query_slots], axis=0
        )
        all_query_kv = jnp.concatenate(
            [slot[split:].reshape(2, own_count, width) for slot in query_slots], axis=1
        )
        anchor = jnp.concatenate(anchor_slots, axis=1)
        slot_pos = jnp.concatenate(
            [
                lax.dynamic_slice_in_dim(query_pos, ((me - k) % ctx_count) * own_count, own_count)
                for k in range(ctx_count)
            ]
        )
        own_pos = slot_pos[:own_count]

        context_output, context_side = attention(
            all_queries, [(cache_kv, "cache"), (kv_block, None)], False, length=cache_len
        )
        remote = [(context_output[:own_count], context_side[:, :own_count])]
        for k in range(1, ctx_count):
            rows = slice(k * own_count, (k + 1) * own_count)
            remote.append(shifted((context_output[rows], context_side[:, rows]), -k, ctx_count))

        (block_out,) = attention(q_block, [(anchor, None), (kv_block, "causal")], True)
        local_output, local_side = attention(
            query_q,
            [(anchor, None), (all_query_kv, "pos")],
            False,
            positions=(slot_pos, own_pos),
        )

        def per_head(side, first):
            picked = side[:, :, first : first + group_size]
            return jnp.transpose(picked, (1, 0, 2)).reshape(own_count, kv_heads * group_size)

        parts = [(local_output, local_side)] + remote
        peaks = [per_head(side, 0) for _, side in parts]
        totals = [per_head(side, HD // 2) for _, side in parts]
        outputs = [output for output, _ in parts]
        top_score = peaks[0]
        for peak in peaks[1:]:
            top_score = jnp.maximum(top_score, peak)
        merged_totals = None
        merged_output = None
        for peak, total, output in zip(peaks, totals, outputs):
            factor = jnp.exp(peak - top_score)
            t = total * factor
            o = output * widen(factor)
            merged_totals = t if merged_totals is None else merged_totals + t
            merged_output = o if merged_output is None else merged_output + o
        query_out = (merged_output / widen(merged_totals)).astype(jnp.bfloat16)
        return (block_out, query_out)

    return local


def solution(mesh):
    in_specs = (
        P(("groups", "ctx"), "head"),
        P(None, ("groups", "ctx"), "head"),
        P(None, ("groups", "ctx"), "head"),
        P(None, ("groups", "ctx"), "head"),
        P(("groups", "ctx")),
        P(("groups", "ctx"), "head"),
        P(None, ("groups", "ctx"), "head"),
        P("groups"),
    )
    out_specs = (P(("groups", "ctx"), "head"), P(("groups", "ctx"), "head"))
    return jax.shard_map(
        make_local(mesh.shape["ctx"]),
        mesh=mesh,
        in_specs=in_specs,
        out_specs=out_specs,
        check_vma=False,
    )
```

time: 75.1 us -> 132 us (1.76)
  Pallas kernels: 32 us -> 88.5 us
  starting transfers between devices: 13.8 us -> 23.2 us
  waiting for transfers between devices: 8.84 us -> 2.77 us
  local copies, waits for them, and re-layouts: 13.7 us -> 10.5 us
    pallas_call x3, Pallas kernels: 32 us -> 88.5 us  [attention(): pl.pallas_call(functools.partial(attention_kernel, masks, normalize, rows...]
    ppermute x6 -> x12, starting transfers between devices: 13.8 us -> 23.2 us  [shifted(): lax.ppermute(value, 'ctx', [(j, (j + shift) % count) for j in range(count)])]
    unnamed x24 -> x12, local copies, waits for them, and re-layouts: 10 us -> 3.36 us
    ppermute x6 -> x12, waiting for transfers between devices: 8.84 us -> 2.77 us  [shifted(): lax.ppermute(value, 'ctx', [(j, (j + shift) % count) for j in range(count)])]
    transpose x0 -> x15, local copies, waits for them, and re-layouts: none -> 2.62 us  [per_head(): jnp.transpose(picked, (1, 0, 2)).reshape(own_count, kv_heads * group_size)]
    slice x18 -> x14, local copies, waits for them, and re-layouts: 0.24 us -> 1.97 us  [the longest x1 1.06 us: local(): context_output[rows]]
  transfers between devices with their start and end apart: 6 -> 12, of which waited for: 2 -> 1; matrix products, arithmetic and copies ran while one was open for 9% -> 8% of each run, Pallas kernels for 20% -> 67%
where the time goes in v3:
time: 132 us; the launch traced here: 131 us
  Pallas kernels  88.5 us (67%)
  starting transfers between devices  23.2 us (18%)
  local copies, waits for them, and re-layouts  10.5 us (8%)
  other arithmetic  4.68 us (4%)
  waiting for transfers between devices  2.77 us (2%)
  between operations  1.56 us (1%)
    pallas_call x3, Pallas kernels, attention(): pl.pallas_call(functools.partial(attention_kernel, masks, normalize, rows...  88.5 us
    ppermute x12, starting transfers between devices, shifted(): lax.ppermute(value, 'ctx', [(j, (j + shift) % count) for j in range(count)])  23.2 us
    unnamed x12, local copies, waits for them, and re-layouts  3.36 us
    ppermute x12, waiting for transfers between devices, shifted(): lax.ppermute(value, 'ctx', [(j, (j + shift) % count) for j in range(count)])  2.77 us
  transfers between devices with their start and end apart: 12, of which 1 were waited for; matrix products, arithmetic and copies ran while one was open for 8% of the time, Pallas kernels for 67%

profile of v3, /device:TPU:0, one launch (start us, length us, event | category | flops | bytes accessed | tf_op | source)
XLA Modules:
  0.0 131.2 jit_solution(9762495363252545997)
XLA Ops:
  0.6 0.9 copy.28
  1.5 0.7 copy.29
  2.2 3.1 %collective-permute-start.3 = (bf16[40960]{0:T(1024)(128)(2,1)S(1)}, bf16[40960]{0:T(1024)(128)(2,1)S(1)}, u32[]{:S(2)}, u32[]{:S(2)}) collective-permute-start(bf16[40960]{0:T(1024)(128)(2,1)S(1)} %constant_dynamic-update-slice_fusion.5), channel_id=1, source_target_pairs={{0,4},{4,8},{8,12},{12,0},{1,5},{5,9},{9,13},{13,1},{2,6},{6,10},{... | collective-permute-start | bytes 245768 | tf_op jit(solution)/shard_map/ppermute | solution.py:163
  5.3 2.6 %collective-permute-start.4 = (bf16[40960]{0:T(1024)(128)(2,1)S(1)}, bf16[40960]{0:T(1024)(128)(2,1)S(1)}, u32[]{:S(2)}, u32[]{:S(2)}) collective-permute-start(bf16[40960]{0:T(1024)(128)(2,1)S(1)} %constant_dynamic-update-slice_fusion.5), channel_id=1, source_target_pairs={{0,8},{4,12},{8,0},{12,4},{1,9},{5,13},{9,1},{13,5},{2,10},{6,14},... | collective-permute-start | bytes 245768 | tf_op jit(solution)/shard_map/ppermute | solution.py:163
  7.9 1.3 %collective-permute-start.5 = (bf16[40960]{0:T(1024)(128)(2,1)S(1)}, bf16[40960]{0:T(1024)(128)(2,1)S(1)}, u32[]{:S(2)}, u32[]{:S(2)}) collective-permute-start(bf16[40960]{0:T(1024)(128)(2,1)S(1)} %constant_dynamic-update-slice_fusion.5), channel_id=1, source_target_pairs={{0,12},{4,0},{8,4},{12,8},{1,13},{5,1},{9,5},{13,9},{2,14},{6,2},{... | collective-permute-start | bytes 245768 | tf_op jit(solution)/shard_map/ppermute | solution.py:163
  9.3 0.7 collective-permute-start
  9.9 0.3 collective-permute-start.1
  10.3 0.9 constant_dynamic-update-slice_fusion.3
  11.2 0.9 fusion.21
  12.1 0.7 copy.11.refs_7_
  13.5 0.7 add_bitcast_fusion.refs_6_
  14.1 0.0 collective-permute-done.3
  14.1 2.8 %collective-permute-start.2 = (bf16[2,128,256]{2,1,0:T(8,128)(2,1)}, bf16[2,128,256]{2,1,0:T(8,128)(2,1)S(1)}, u32[]{:S(2)}, u32[]{:S(2)}) collective-permute-start(bf16[2,128,256]{2,1,0:T(8,128)(2,1)} %param.10), channel_id=1, source_target_pairs={{0,12},{4,0},{8,4},{12,8},{1,13},{5,1},{9,5},{13,9},{2,14},{6,2},{... | collective-permute-start | bytes 393224 | tf_op jit(solution)/shard_map/ppermute | solution.py:163
  17.0 0.0 collective-permute-done.4
  17.1 0.0 collective-permute-done.5
  17.1 1.6 %pad_maximum_fusion.refs_1_ = bf16[64,2048]{1,0:T(8,128)(2,1)} fusion(bf16[16,2048]{1,0:T(8,128)(2,1)S(1)} %slice.144, bf16[16,2048]{1,0:T(8,128)(2,1)S(1)} %slice.142, bf16[16,2048]{1,0:T(8,128)(2,1)S(1)} %slice.140, bf16[16,2048]{1,0:T(8,128)(2,1)} %refs_1_.3), kind=kLoop, calls=%fused_computation | loop fusion | flops 1048576 | bytes 524288 | tf_op jit(solution)/shard_map/concatenate | solution.py:178
  18.7 48.3 %shard_map.97 = (f32[64,2048]{1,0:T(8,128)}, f32[2,64,128]{2,1,0:T(8,128)}) custom-call(s32[1]{0:T(128)S(6)} %copy.46.refs_0_, bf16[64,2048]{1,0:T(8,128)(2,1)} %pad_maximum_fusion.refs_1_, bf16[2,4096,256]{2,1,0:T(8,128)(2,1)} %refs_3_.1, bf16[2,4096,256]{2,1,0:T(8,128)(2,1)} %refs_3_.1, bf16[2,256,256]{2,1,0:T(8,128)(2,1)} %refs_5_.3, ...), custom_call_target="tpu_custom_call" | custom-call | tf_op jit(solution)/shard_map/pallas_call | solution.py:150
  67.0 0.8 fusion.20
  67.7 0.9 slice_bitcast_fusion.8
  68.7 1.4 %collective-permute-start.6 = (f32[2,16,128]{2,1,0:T(8,128)S(1)}, f32[2,16,128]{2,1,0:T(8,128)S(1)}, u32[]{:S(2)}, u32[]{:S(2)}) collective-permute-start(f32[2,16,128]{2,1,0:T(8,128)S(1)} %get-tuple-element.21), channel_id=1, source_target_pairs={{0,12},{4,0},{8,4},{12,8},{1,13},{5,1},{9,5},{13,9},{2,14},{6,2},{... | collective-permute-start | bytes 49160 | tf_op jit(solution)/shard_map/ppermute | solution.py:163
  70.1 4.3 %collective-permute-start.7 = (f32[2,16,128]{2,1,0:T(8,128)S(1)}, f32[2,16,128]{2,1,0:T(8,128)S(1)}, u32[]{:S(2)}, u32[]{:S(2)}) collective-permute-start(f32[2,16,128]{2,1,0:T(8,128)S(1)} %get-tuple-element.23), channel_id=1, source_target_pairs={{0,8},{4,12},{8,0},{12,4},{1,9},{5,13},{9,1},{13,5},{2,10},{6,14},... | collective-permute-start | bytes 49160 | tf_op jit(solution)/shard_map/ppermute | solution.py:163
  74.4 1.1 fusion.19
  75.5 0.6 pad_maximum_fusion.1.refs_4_.refs_5_
  76.1 0.1 copy.13
  76.2 0.1 copy.23
  76.3 0.0 collective-permute-done.6
  76.3 0.5 collective-permute-start.8
  76.8 0.1 slice_bitcast_fusion.5
  76.9 0.0 collective-permute-done.7
  76.9 2.2 %collective-permute-start.10 = (f32[16,2048]{1,0:T(8,128)S(1)}, f32[16,2048]{1,0:T(8,128)S(1)}, u32[]{:S(2)}, u32[]{:S(2)}) collective-permute-start(f32[16,2048]{1,0:T(8,128)S(1)} %get-tuple-element.18), channel_id=1, source_target_pairs={{0,8},{4,12},{8,0},{12,4},{1,9},{5,13},{9,1},{13,5},{2,10},{6,14},... | collective-permute-start | bytes 393224 | tf_op jit(solution)/shard_map/ppermute | solution.py:163
  79.1 0.1 slice_bitcast_fusion.4
  79.1 2.7 %collective-permute-done.8 = f32[2,16,128]{2,1,0:T(8,128)S(1)} collective-permute-done((f32[2,16,128]{2,1,0:T(8,128)S(1)}, f32[2,16,128]{2,1,0:T(8,128)S(1)}, u32[]{:S(2)}, u32[]{:S(2)}) %collective-permute-start.8) | collective-permute-done | bytes 16416 | tf_op jit(solution)/shard_map/ppermute | solution.py:163
  81.9 0.0 collective-permute-start.11
  81.9 0.1 slice_bitcast_fusion.3
  82.0 0.1 copy.14
  82.0 0.1 copy.15
  82.1 0.1 copy.16
  82.2 0.1 copy.24
  82.2 0.1 copy.25
  82.3 0.1 copy.26
  82.4 0.0 collective-permute-done
  82.4 3.8 %collective-permute-start.9 = (f32[16,2048]{1,0:T(8,128)S(1)}, f32[16,2048]{1,0:T(8,128)S(1)}, u32[]{:S(2)}, u32[]{:S(2)}) collective-permute-start(f32[16,2048]{1,0:T(8,128)S(1)} %get-tuple-element.16), channel_id=1, source_target_pairs={{0,12},{4,0},{8,4},{12,8},{1,13},{5,1},{9,5},{13,9},{2,14},{6,2},{... | collective-permute-start | bytes 393224 | tf_op jit(solution)/shard_map/ppermute | solution.py:163
  86.2 0.0 collective-permute-done.1
  86.3 0.0 collective-permute-done.2
  86.3 0.8 copy-done
  87.1 4.7 %shard_map.96 = (f32[16,2048]{1,0:T(8,128)}, f32[2,16,128]{2,1,0:T(8,128)}) custom-call(s32[1]{0:T(128)} %constant.35.clone.1.refs_0_, bf16[16,2048]{1,0:T(8,128)(2,1)} %refs_1_.3, bf16[2,512,256]{2,1,0:T(8,128)(2,1)} %copy-done, bf16[2,512,256]{2,1,0:T(8,128)(2,1)} %copy-done, bf16[2,64,256]{2,1,0:T(8,128)(2,1)} %pad_maximum_fusion.1.refs_4_.refs_5_, ...), custom_call_target="tpu_custom_call" | custom-call | tf_op jit(solution)/shard_map/pallas_call | solution.py:150
  91.8 0.9 slice_bitcast_fusion.9
  92.7 0.1 copy.12
  92.7 0.1 copy.22
  92.8 0.1 copy.17
  92.9 0.1 copy.18
  93.0 0.1 copy.19
  93.0 0.1 copy.20
  93.1 0.1 copy.21
  93.2 0.1 copy.27
  93.2 35.5 %shard_map.95 = bf16[256,2048]{1,0:T(8,128)(2,1)} custom-call(s32[1]{0:T(128)} %constant.35.clone.1.refs_0_, bf16[256,2048]{1,0:T(8,128)(2,1)} %refs_1_.2, bf16[2,512,256]{2,1,0:T(8,128)(2,1)} %copy-done, bf16[2,512,256]{2,1,0:T(8,128)(2,1)} %copy-done, bf16[2,256,256]{2,1,0:T(8,128)(2,1)} %refs_5_.3, bf16[2,256,256]{2,1,0:T(8,128)(2,1)} %refs_5_.3), custom_call_target="tpu_custom_call" | custom-call | tf_op jit(solution)/shard_map/pallas_call | solution.py:150
  128.7 0.0 collective-permute-done.9
  128.8 0.1 broadcast_in_dim.18
  128.8 0.1 broadcast_in_dim.19
  128.9 0.1 broadcast_in_dim.20
  129.0 0.1 broadcast_in_dim.21
  129.1 0.1 broadcast_in_dim.22
  129.3 0.1 broadcast_in_dim.23
  129.4 1.8 %fusion = bf16[16,2048]{1,0:T(8,128)(2,1)} fusion(f32[2,8,16,128]{3,2,1,0:T(8,128)S(1)} %bitcast.133, f32[16,2048]{1,0:T(8,128)S(1)} %collective-permute-done.11, f32[2,8,16,128]{3,2,1,0:T(8,128)S(1)} %bitcast.132, f32[16,2048]{1,0:T(8,128)S(1)} %collective-permute-done.10, f32[2,8,16,128]{3,2,1,0:T(8,128)S(1)} %bitcast.131, ...), kind=kLoop, calls=%fused_computation.2 | loop fusion | flops 360448 | bytes 1507328 | tf_op jit(solution)/shard_map/convert_element_type | solution.py:228
  (25 shorter events, 0.2 us)
Async XLA Ops:
  2.2 11.9 %collective-permute-start.3 = (bf16[40960]{0:T(1024)(128)(2,1)S(1)}, bf16[40960]{0:T(1024)(128)(2,1)S(1)}, u32[]{:S(2)}, u32[]{:S(2)}) collective-permute-start(bf16[40960]{0:T(1024)(128)(2,1)S(1)} %constant_dynamic-update-slice_fusion.5), channel_id=1, source_target_pairs={{0,4},{4,8},{8,12},{12,0},{1,5},{5,9},{9,13},{13,1},{2,6},{6,10},{... | collective-permute-start | bytes 245768 | tf_op jit(solution)/shard_map/ppermute | solution.py:163
  5.3 11.7 %collective-permute-start.4 = (bf16[40960]{0:T(1024)(128)(2,1)S(1)}, bf16[40960]{0:T(1024)(128)(2,1)S(1)}, u32[]{:S(2)}, u32[]{:S(2)}) collective-permute-start(bf16[40960]{0:T(1024)(128)(2,1)S(1)} %constant_dynamic-update-slice_fusion.5), channel_id=1, source_target_pairs={{0,8},{4,12},{8,0},{12,4},{1,9},{5,13},{9,1},{13,5},{2,10},{6,14},... | collective-permute-start | bytes 245768 | tf_op jit(solution)/shard_map/ppermute | solution.py:163
  7.9 9.2 %collective-permute-start.5 = (bf16[40960]{0:T(1024)(128)(2,1)S(1)}, bf16[40960]{0:T(1024)(128)(2,1)S(1)}, u32[]{:S(2)}, u32[]{:S(2)}) collective-permute-start(bf16[40960]{0:T(1024)(128)(2,1)S(1)} %constant_dynamic-update-slice_fusion.5), channel_id=1, source_target_pairs={{0,12},{4,0},{8,4},{12,8},{1,13},{5,1},{9,5},{13,9},{2,14},{6,2},{... | collective-permute-start | bytes 245768 | tf_op jit(solution)/shard_map/ppermute | solution.py:163
  9.3 73.1 %collective-permute-start = (bf16[2,128,256]{2,1,0:T(8,128)(2,1)}, bf16[2,128,256]{2,1,0:T(8,128)(2,1)S(1)}, u32[]{:S(2)}, u32[]{:S(2)}) collective-permute-start(bf16[2,128,256]{2,1,0:T(8,128)(2,1)} %param.10), channel_id=1, source_target_pairs={{0,4},{4,8},{8,12},{12,0},{1,5},{5,9},{9,13},{13,1},{2,6},{6,10},{... | collective-permute-start | bytes 393224 | tf_op jit(solution)/shard_map/ppermute | solution.py:163
  9.9 76.3 %collective-permute-start.1 = (bf16[2,128,256]{2,1,0:T(8,128)(2,1)}, bf16[2,128,256]{2,1,0:T(8,128)(2,1)S(1)}, u32[]{:S(2)}, u32[]{:S(2)}) collective-permute-start(bf16[2,128,256]{2,1,0:T(8,128)(2,1)} %param.10), channel_id=1, source_target_pairs={{0,8},{4,12},{8,0},{12,4},{1,9},{5,13},{9,1},{13,5},{2,10},{6,14},... | collective-permute-start | bytes 393224 | tf_op jit(solution)/shard_map/ppermute | solution.py:163
  14.1 72.1 %collective-permute-start.2 = (bf16[2,128,256]{2,1,0:T(8,128)(2,1)}, bf16[2,128,256]{2,1,0:T(8,128)(2,1)S(1)}, u32[]{:S(2)}, u32[]{:S(2)}) collective-permute-start(bf16[2,128,256]{2,1,0:T(8,128)(2,1)} %param.10), channel_id=1, source_target_pairs={{0,12},{4,0},{8,4},{12,8},{1,13},{5,1},{9,5},{13,9},{2,14},{6,2},{... | collective-permute-start | bytes 393224 | tf_op jit(solution)/shard_map/ppermute | solution.py:163
  18.7 56.8 %copy-start.2 = (bf16[2,16,256]{2,1,0:T(8,128)(2,1)S(1)}, bf16[2,16,256]{2,1,0:T(8,128)(2,1)}, u32[]{:S(2)}) copy-start(bf16[2,16,256]{2,1,0:T(8,128)(2,1)} %param.14) | copy-start | bytes 49156
  68.7 7.6 %collective-permute-start.6 = (f32[2,16,128]{2,1,0:T(8,128)S(1)}, f32[2,16,128]{2,1,0:T(8,128)S(1)}, u32[]{:S(2)}, u32[]{:S(2)}) collective-permute-start(f32[2,16,128]{2,1,0:T(8,128)S(1)} %get-tuple-element.21), channel_id=1, source_target_pairs={{0,12},{4,0},{8,4},{12,8},{1,13},{5,1},{9,5},{13,9},{2,14},{6,2},{... | collective-permute-start | bytes 49160 | tf_op jit(solution)/shard_map/ppermute | solution.py:163
  70.1 6.8 %collective-permute-start.7 = (f32[2,16,128]{2,1,0:T(8,128)S(1)}, f32[2,16,128]{2,1,0:T(8,128)S(1)}, u32[]{:S(2)}, u32[]{:S(2)}) collective-permute-start(f32[2,16,128]{2,1,0:T(8,128)S(1)} %get-tuple-element.23), channel_id=1, source_target_pairs={{0,8},{4,12},{8,0},{12,4},{1,9},{5,13},{9,1},{13,5},{2,10},{6,14},... | collective-permute-start | bytes 49160 | tf_op jit(solution)/shard_map/ppermute | solution.py:163
  76.3 5.6 %collective-permute-start.8 = (f32[2,16,128]{2,1,0:T(8,128)S(1)}, f32[2,16,128]{2,1,0:T(8,128)S(1)}, u32[]{:S(2)}, u32[]{:S(2)}) collective-permute-start(f32[2,16,128]{2,1,0:T(8,128)S(1)} %get-tuple-element.22), channel_id=1, source_target_pairs={{0,4},{4,8},{8,12},{12,0},{1,5},{5,9},{9,13},{13,1},{2,6},{6,10},{... | collective-permute-start | bytes 49160 | tf_op jit(solution)/shard_map/ppermute | solution.py:163
  76.9 51.8 %collective-permute-start.10 = (f32[16,2048]{1,0:T(8,128)S(1)}, f32[16,2048]{1,0:T(8,128)S(1)}, u32[]{:S(2)}, u32[]{:S(2)}) collective-permute-start(f32[16,2048]{1,0:T(8,128)S(1)} %get-tuple-element.18), channel_id=1, source_target_pairs={{0,8},{4,12},{8,0},{12,4},{1,9},{5,13},{9,1},{13,5},{2,10},{6,14},... | collective-permute-start | bytes 393224 | tf_op jit(solution)/shard_map/ppermute | solution.py:163
  81.9 46.8 %collective-permute-start.11 = (f32[16,2048]{1,0:T(8,128)S(1)}, f32[16,2048]{1,0:T(8,128)S(1)}, u32[]{:S(2)}, u32[]{:S(2)}) collective-permute-start(f32[16,2048]{1,0:T(8,128)S(1)} %get-tuple-element.17), channel_id=1, source_target_pairs={{0,4},{4,8},{8,12},{12,0},{1,5},{5,9},{9,13},{13,1},{2,6},{6,10},{... | collective-permute-start | bytes 393224 | tf_op jit(solution)/shard_map/ppermute | solution.py:163
  82.4 46.4 %collective-permute-start.9 = (f32[16,2048]{1,0:T(8,128)S(1)}, f32[16,2048]{1,0:T(8,128)S(1)}, u32[]{:S(2)}, u32[]{:S(2)}) collective-permute-start(f32[16,2048]{1,0:T(8,128)S(1)} %get-tuple-element.16), channel_id=1, source_target_pairs={{0,12},{4,0},{8,4},{12,8},{1,13},{5,1},{9,5},{13,9},{2,14},{6,2},{... | collective-permute-start | bytes 393224 | tf_op jit(solution)/shard_map/ppermute | solution.py:163
  86.3 0.8 copy-start
  91.8 37.6 %copy-start.1 = (f32[16,2048]{1,0:T(8,128)S(1)}, f32[16,2048]{1,0:T(8,128)}, u32[]{:S(2)}) copy-start(f32[16,2048]{1,0:T(8,128)} %get-tuple-element.6) | copy-start | bytes 393220

commit v4 on v3

--- a/solution.py
+++ b/solution.py
@@ -17,11 +17,7 @@
     return jnp.repeat(per_head, HD, axis=-1)
 
 
-def chunk_size(rows, key_count):
-    size = min(key_count, max(128, 32768 // rows))
-    while key_count % size:
-        size //= 2
-    return size
+STACK_ROWS = 512
 
 
 def attention_kernel(masks, normalize, rows, group_size, *refs):
@@ -33,80 +29,62 @@
         key_pos_ref, own_pos_ref = rest[0], rest[1]
         rest = rest[2:]
     out_ref = rest[0]
-    side_ref = rest[1] if len(rest) > 1 else None
+    side_ref = None if normalize else rest[1]
     scale = 1.0 / jnp.sqrt(jnp.float32(HD))
-    stack = max(1, min(group_size, 512 // rows))
+    stack = max(1, min(group_size, STACK_ROWS // rows))
+    visible = []
+    for index, mask in enumerate(masks):
+        key_count = kv_refs[2 * index].shape[0]
+        shape = (rows * stack, key_count)
+        if mask is None:
+            visible.append(None)
+        elif mask == "cache":
+            cols = lax.broadcasted_iota(jnp.int32, shape, 1)
+            visible.append(cols < length_ref[0])
+        elif mask == "causal":
+            cols = lax.broadcasted_iota(jnp.int32, shape, 1)
+            tokens = lax.broadcasted_iota(jnp.int32, shape, 0)
+            if stack > 1:
+                tokens = lax.rem(tokens, rows)
+            visible.append(cols <= tokens)
+        else:
+            own = own_pos_ref[...]
+            if stack > 1:
+                own = jnp.concatenate([own] * stack, axis=0)
+            visible.append(key_pos_ref[...] <= own)
     for first in range(0, group_size, stack):
         heads = list(range(first, min(group_size, first + stack)))
-        lhs = jnp.concatenate([q_ref[:, h * HD : (h + 1) * HD] for h in heads], axis=0)
+        if len(heads) == 1:
+            lhs = q_ref[:, first * HD : (first + 1) * HD]
+        else:
+            lhs = jnp.concatenate([q_ref[:, h * HD : (h + 1) * HD] for h in heads], axis=0)
         m_rows = lhs.shape[0]
-
-        def chunk_visible(index, start, size):
-            mask = masks[index]
-            if mask is None:
-                return None
-            cols = start + lax.broadcasted_iota(jnp.int32, (m_rows, size), 1)
-            if mask == "cache":
-                return cols < length_ref[0]
-            if mask == "causal":
-                tokens = lax.broadcasted_iota(jnp.int32, (m_rows, size), 0)
-                if m_rows > rows:
-                    tokens = lax.rem(tokens, rows)
-                return cols <= tokens
-            own = own_pos_ref[...]
-            if m_rows > rows:
-                own = jnp.concatenate([own] * (m_rows // rows), axis=0)
-            return key_pos_ref[:, pl.ds(start, size)] <= own
-
-        def raw_scores(index, start, size):
-            keys = kv_refs[2 * index][pl.ds(start, size), :]
-            return lax.dot_general(
-                lhs, keys, (((1,), (1,)), ((), ())), preferred_element_type=jnp.float32
+        all_scores = []
+        for index in range(part_count):
+            scores = lax.dot_general(
+                lhs,
+                kv_refs[2 * index][...],
+                (((1,), (1,)), ((), ())),
+                preferred_element_type=jnp.float32,
+            ) * scale
+            if visible[index] is not None:
+                scores = jnp.where(visible[index][:m_rows], scores, masked_score)
+            all_scores.append(scores)
+        peak = jnp.max(all_scores[0], axis=1, keepdims=True)
+        for scores in all_scores[1:]:
+            peak = jnp.maximum(peak, jnp.max(scores, axis=1, keepdims=True))
+        total = None
+        output = None
+        for index, scores in enumerate(all_scores):
+            weights = jnp.exp(scores - peak)
+            part_total = jnp.sum(weights, axis=1, keepdims=True)
+            part_output = jnp.dot(
+                weights.astype(jnp.bfloat16),
+                kv_refs[2 * index + 1][...],
+                preferred_element_type=jnp.float32,
             )
-
-        def over_chunks(index, body, carry):
-            key_count = kv_refs[2 * index].shape[0]
-            size = chunk_size(m_rows, key_count)
-            count = key_count // size
-
-            def step(c, carry):
-                start = pl.multiple_of(c * size, size)
-                return body(index, start, size, carry)
-
-            if count == 1:
-                return step(0, carry)
-            return lax.fori_loop(0, count, step, carry)
-
-        def max_body(index, start, size, peak):
-            raw = raw_scores(index, start, size)
-            visible = chunk_visible(index, start, size)
-            if visible is not None:
-                raw = jnp.where(visible, raw, -jnp.inf)
-            return jnp.maximum(peak, jnp.max(raw, axis=1, keepdims=True))
-
-        peak = jnp.full((m_rows, 1), -jnp.inf, jnp.float32)
-        for index in range(part_count):
-            peak = over_chunks(index, max_body, peak)
-        peak = peak * scale
-
-        def sum_body(index, start, size, carry):
-            total, output = carry
-            scores = raw_scores(index, start, size) * scale
-            visible = chunk_visible(index, start, size)
-            if visible is not None:
-                scores = jnp.where(visible, scores, masked_score)
-            weights = jnp.exp(scores - peak)
-            total = total + jnp.sum(weights, axis=1, keepdims=True)
-            values = kv_refs[2 * index + 1][pl.ds(start, size), :]
-            output = output + jnp.dot(
-                weights.astype(jnp.bfloat16), values, preferred_element_type=jnp.float32
-            )
-            return total, output
-
-        carry = (jnp.zeros((m_rows, 1), jnp.float32), jnp.zeros((m_rows, HD), jnp.float32))
-        for index in range(part_count):
-            carry = over_chunks(index, sum_body, carry)
-        total, output = carry
+            total = part_total if total is None else total + part_total
+            output = part_output if output is None else output + part_output
         for slot, h in enumerate(heads):
             rows_of = slice(slot * rows, (slot + 1) * rows)
             if normalize:

time: 132 us -> 69.3 us (0.53)
  Pallas kernels: 88.5 us -> 26 us
    pallas_call x3, Pallas kernels: 88.5 us -> 26 us  [attention(): pl.pallas_call(functools.partial(attention_kernel, masks, normalize, rows...]
  transfers between devices with their start and end apart: 12 -> 12, of which waited for: 1 -> 1; matrix products, arithmetic and copies ran while one was open for 8% -> 15% of each run, Pallas kernels for 67% -> 38%
where the time goes in v4:
time: 69.3 us; the launch traced here: 68.8 us
  Pallas kernels  26 us (38%)
  starting transfers between devices  23.2 us (33%)
  local copies, waits for them, and re-layouts  10.5 us (15%)
  other arithmetic  4.68 us (7%)
  waiting for transfers between devices  2.78 us (4%)
  between operations  1.56 us (2%)
    pallas_call x3, Pallas kernels, attention(): pl.pallas_call(functools.partial(attention_kernel, masks, normalize, rows...  26 us
    ppermute x12, starting transfers between devices, shifted(): lax.ppermute(value, 'ctx', [(j, (j + shift) % count) for j in range(count)])  23.2 us
    unnamed x12, local copies, waits for them, and re-layouts  3.36 us
    ppermute x12, waiting for transfers between devices, shifted(): lax.ppermute(value, 'ctx', [(j, (j + shift) % count) for j in range(count)])  2.78 us
    transpose x15, local copies, waits for them, and re-layouts, per_head(): jnp.transpose(picked, (1, 0, 2)).reshape(own_count, kv_heads * group_size)  2.62 us
    convert_element_type x1, other arithmetic, local(): query_out = (merged_output / widen(merged_totals)).astype(jnp.bfloat16)  1.81 us
    concatenate x1, other arithmetic, local(): jnp.concatenate([slot[:split].reshape(own_count, query_width) for slot in...  1.56 us
  transfers between devices with their start and end apart: 12, of which 1 were waited for; matrix products, arithmetic and copies ran while one was open for 15% of the time, Pallas kernels for 38%

profile of v4, /device:TPU:0, one launch (start us, length us, event | category | flops | bytes accessed | tf_op | source)
XLA Modules:
  0.0 68.8 jit_solution(12313267977515245311)
XLA Ops:
  0.6 0.9 %copy.28 = bf16[2,16,8,128]{3,1,2,0:T(8,128)(2,1)S(1)} copy(bf16[2,16,8,128]{3,2,1,0:T(8,128)(2,1)} %bitcast.127) | data formatting | bytes 131072
  1.5 0.7 %copy.29 = bf16[4,2,8,128]{3,1,2,0:T(2,128)(2,1)S(1)} copy(bf16[4,2,8,128]{3,2,1,0:T(8,128)(2,1)} %bitcast.136) | data formatting | bytes 32768
  2.2 3.1 %collective-permute-start.3 = (bf16[40960]{0:T(1024)(128)(2,1)S(1)}, bf16[40960]{0:T(1024)(128)(2,1)S(1)}, u32[]{:S(2)}, u32[]{:S(2)}) collective-permute-start(bf16[40960]{0:T(1024)(128)(2,1)S(1)} %constant_dynamic-update-slice_fusion.5), channel_id=1, source_target_pairs={{0,4},{4,8},{8,12},{12,0},{1,5},{5,9},{9,13},{13,1},{2,6},{6,10},{... | collective-permute-start | bytes 245768 | tf_op jit(solution)/shard_map/ppermute | solution.py:141
  5.3 2.6 %collective-permute-start.4 = (bf16[40960]{0:T(1024)(128)(2,1)S(1)}, bf16[40960]{0:T(1024)(128)(2,1)S(1)}, u32[]{:S(2)}, u32[]{:S(2)}) collective-permute-start(bf16[40960]{0:T(1024)(128)(2,1)S(1)} %constant_dynamic-update-slice_fusion.5), channel_id=1, source_target_pairs={{0,8},{4,12},{8,0},{12,4},{1,9},{5,13},{9,1},{13,5},{2,10},{6,14},... | collective-permute-start | bytes 245768 | tf_op jit(solution)/shard_map/ppermute | solution.py:141
  7.9 1.3 %collective-permute-start.5 = (bf16[40960]{0:T(1024)(128)(2,1)S(1)}, bf16[40960]{0:T(1024)(128)(2,1)S(1)}, u32[]{:S(2)}, u32[]{:S(2)}) collective-permute-start(bf16[40960]{0:T(1024)(128)(2,1)S(1)} %constant_dynamic-update-slice_fusion.5), channel_id=1, source_target_pairs={{0,12},{4,0},{8,4},{12,8},{1,13},{5,1},{9,5},{13,9},{2,14},{6,2},{... | collective-permute-start | bytes 245768 | tf_op jit(solution)/shard_map/ppermute | solution.py:141
  9.3 0.7 collective-permute-start
  9.9 0.3 collective-permute-start.1
  10.3 0.9 %constant_dynamic-update-slice_fusion.3 = bf16[2,512,256]{2,1,0:T(8,128)(2,1)S(1)} fusion(bf16[2,128,256]{2,1,0:T(8,128)(2,1)} %param.10), kind=kLoop, calls=%fused_computation.26 | loop fusion | bytes 262144
  11.2 0.9 %fusion.21 = (s32[16]{0:T(128)S(1)}, s32[16]{0:T(128)S(1)}, s32[16]{0:T(128)S(1)}, s32[16]{0:T(128)S(1)}) fusion(s32[64]{0:T(128)} %param.15, s32[]{:T(128)S(6)} %select_n.32, s32[]{:T(128)S(6)} %select_n.34, s32[]{:T(128)S(6)} %select_n.38, s32[]{:T(128)S(6)} %select_n.36), kind=kLoop, calls=%fused_computation.55 | loop fusion | bytes 528 | tf_op jit(solution)/shard_map/dynamic_slice | solution.py:165
  12.1 0.7 copy.11.refs_7_
  13.5 0.7 add_bitcast_fusion.refs_6_
  14.1 0.0 collective-permute-done.3
  14.1 2.8 %collective-permute-start.2 = (bf16[2,128,256]{2,1,0:T(8,128)(2,1)}, bf16[2,128,256]{2,1,0:T(8,128)(2,1)S(1)}, u32[]{:S(2)}, u32[]{:S(2)}) collective-permute-start(bf16[2,128,256]{2,1,0:T(8,128)(2,1)} %param.10), channel_id=1, source_target_pairs={{0,12},{4,0},{8,4},{12,8},{1,13},{5,1},{9,5},{13,9},{2,14},{6,2},{... | collective-permute-start | bytes 393224 | tf_op jit(solution)/shard_map/ppermute | solution.py:141
  17.0 0.0 collective-permute-done.4
  17.1 0.0 collective-permute-done.5
  17.1 1.6 %pad_maximum_fusion.refs_1_ = bf16[64,2048]{1,0:T(8,128)(2,1)} fusion(bf16[16,2048]{1,0:T(8,128)(2,1)S(1)} %slice.144, bf16[16,2048]{1,0:T(8,128)(2,1)S(1)} %slice.142, bf16[16,2048]{1,0:T(8,128)(2,1)S(1)} %slice.140, bf16[16,2048]{1,0:T(8,128)(2,1)} %refs_1_.3), kind=kLoop, calls=%fused_computation | loop fusion | flops 1048576 | bytes 524288 | tf_op jit(solution)/shard_map/concatenate | solution.py:156
  18.7 16.2 %shard_map.97 = (f32[64,2048]{1,0:T(8,128)}, f32[2,64,128]{2,1,0:T(8,128)}) custom-call(s32[1]{0:T(128)S(6)} %copy.46.refs_0_, bf16[64,2048]{1,0:T(8,128)(2,1)} %pad_maximum_fusion.refs_1_, bf16[2,4096,256]{2,1,0:T(8,128)(2,1)} %refs_3_.1, bf16[2,4096,256]{2,1,0:T(8,128)(2,1)} %refs_3_.1, bf16[2,256,256]{2,1,0:T(8,128)(2,1)} %refs_5_.3, ...), custom_call_target="tpu_custom_call" | custom-call | tf_op jit(solution)/shard_map/pallas_call | solution.py:128
  34.9 0.8 %fusion.20 = (f32[2,16,128]{2,1,0:T(8,128)S(1)}, f32[2,16,128]{2,1,0:T(8,128)S(1)}, f32[2,16,128]{2,1,0:T(8,128)S(1)}) fusion(f32[2,64,128]{2,1,0:T(8,128)} %get-tuple-element.8), kind=kLoop, calls=%fused_computation.54 | loop fusion | bytes 98304 | tf_op jit(solution)/shard_map/slice | solution.py:177
  35.7 0.9 %slice_bitcast_fusion.8 = (f32[16,2,8]{2,0,1:T(8,128)S(1)}, f32[16,2,8]{2,0,1:T(8,128)S(1)}) fusion(f32[2,64,128]{2,1,0:T(8,128)} %get-tuple-element.8), kind=kLoop, calls=%fused_computation.21 | loop fusion | bytes 4096 | tf_op jit(solution)/shard_map/transpose | solution.py:189
  36.6 1.4 %collective-permute-start.6 = (f32[2,16,128]{2,1,0:T(8,128)S(1)}, f32[2,16,128]{2,1,0:T(8,128)S(1)}, u32[]{:S(2)}, u32[]{:S(2)}) collective-permute-start(f32[2,16,128]{2,1,0:T(8,128)S(1)} %get-tuple-element.21), channel_id=1, source_target_pairs={{0,12},{4,0},{8,4},{12,8},{1,13},{5,1},{9,5},{13,9},{2,14},{6,2},{... | collective-permute-start | bytes 49160 | tf_op jit(solution)/shard_map/ppermute | solution.py:141
  38.0 4.3 %collective-permute-start.7 = (f32[2,16,128]{2,1,0:T(8,128)S(1)}, f32[2,16,128]{2,1,0:T(8,128)S(1)}, u32[]{:S(2)}, u32[]{:S(2)}) collective-permute-start(f32[2,16,128]{2,1,0:T(8,128)S(1)} %get-tuple-element.23), channel_id=1, source_target_pairs={{0,8},{4,12},{8,0},{12,4},{1,9},{5,13},{9,1},{13,5},{2,10},{6,14},... | collective-permute-start | bytes 49160 | tf_op jit(solution)/shard_map/ppermute | solution.py:141
  42.4 1.1 %fusion.19 = (f32[16,2048]{1,0:T(8,128)S(1)}, f32[16,2048]{1,0:T(8,128)S(1)}, f32[16,2048]{1,0:T(8,128)S(1)}) fusion(f32[64,2048]{1,0:T(8,128)} %get-tuple-element.9), kind=kLoop, calls=%fused_computation.53 | loop fusion | bytes 786432 | tf_op jit(solution)/shard_map/slice | solution.py:177
  43.4 0.6 pad_maximum_fusion.1.refs_4_.refs_5_
  44.1 0.1 copy.13
  44.1 0.1 copy.23
  44.2 0.0 collective-permute-done.6
  44.2 0.5 collective-permute-start.8
  44.8 0.1 slice_bitcast_fusion.5
  44.8 0.0 collective-permute-done.7
  44.8 2.2 %collective-permute-start.10 = (f32[16,2048]{1,0:T(8,128)S(1)}, f32[16,2048]{1,0:T(8,128)S(1)}, u32[]{:S(2)}, u32[]{:S(2)}) collective-permute-start(f32[16,2048]{1,0:T(8,128)S(1)} %get-tuple-element.18), channel_id=1, source_target_pairs={{0,8},{4,12},{8,0},{12,4},{1,9},{5,13},{9,1},{13,5},{2,10},{6,14},... | collective-permute-start | bytes 393224 | tf_op jit(solution)/shard_map/ppermute | solution.py:141
  47.0 0.1 slice_bitcast_fusion.4
  47.1 2.7 %collective-permute-done.8 = f32[2,16,128]{2,1,0:T(8,128)S(1)} collective-permute-done((f32[2,16,128]{2,1,0:T(8,128)S(1)}, f32[2,16,128]{2,1,0:T(8,128)S(1)}, u32[]{:S(2)}, u32[]{:S(2)}) %collective-permute-start.8) | collective-permute-done | bytes 16416 | tf_op jit(solution)/shard_map/ppermute | solution.py:141
  49.8 0.0 collective-permute-start.11
  49.8 0.1 slice_bitcast_fusion.3
  49.9 0.1 copy.14
  50.0 0.1 copy.15
  50.0 0.1 copy.16
  50.1 0.1 copy.24
  50.2 0.1 copy.25
  50.2 0.1 copy.26
  50.3 0.0 collective-permute-done
  50.3 3.8 %collective-permute-start.9 = (f32[16,2048]{1,0:T(8,128)S(1)}, f32[16,2048]{1,0:T(8,128)S(1)}, u32[]{:S(2)}, u32[]{:S(2)}) collective-permute-start(f32[16,2048]{1,0:T(8,128)S(1)} %get-tuple-element.16), channel_id=1, source_target_pairs={{0,12},{4,0},{8,4},{12,8},{1,13},{5,1},{9,5},{13,9},{2,14},{6,2},{... | collective-permute-start | bytes 393224 | tf_op jit(solution)/shard_map/ppermute | solution.py:141
  54.2 0.0 collective-permute-done.1
  54.2 0.8 %copy-done = bf16[2,512,256]{2,1,0:T(8,128)(2,1)} copy-done((bf16[2,512,256]{2,1,0:T(8,128)(2,1)}, bf16[2,512,256]{2,1,0:T(8,128)(2,1)S(1)}, u32[]{:S(2)}) %copy-start) | copy-done | bytes 524312
  55.0 2.6 %shard_map.96 = (f32[16,2048]{1,0:T(8,128)}, f32[2,16,128]{2,1,0:T(8,128)}) custom-call(s32[1]{0:T(128)} %constant.35.clone.1.refs_0_, bf16[16,2048]{1,0:T(8,128)(2,1)} %refs_1_.3, bf16[2,512,256]{2,1,0:T(8,128)(2,1)} %copy-done, bf16[2,512,256]{2,1,0:T(8,128)(2,1)} %copy-done, bf16[2,64,256]{2,1,0:T(8,128)(2,1)} %pad_maximum_fusion.1.refs_4_.refs_5_, ...), custom_call_target="tpu_custom_call" | custom-call | tf_op jit(solution)/shard_map/pallas_call | solution.py:128
  57.7 0.9 %slice_bitcast_fusion.9 = (f32[16,2,8]{2,0,1:T(8,128)S(1)}, f32[16,2,8]{2,0,1:T(8,128)S(1)}) fusion(f32[2,16,128]{2,1,0:T(8,128)} %get-tuple-element.7), kind=kLoop, calls=%fused_computation.22 | loop fusion | bytes 4096 | tf_op jit(solution)/shard_map/transpose | solution.py:189
  58.5 0.1 copy.12
  58.6 0.1 copy.22
  58.7 0.1 copy.17
  58.8 0.1 copy.18
  58.8 0.1 copy.19
  58.9 0.1 copy.20
  59.0 0.1 copy.21
  59.0 0.1 copy.27
  59.1 7.2 %shard_map.95 = bf16[256,2048]{1,0:T(8,128)(2,1)} custom-call(s32[1]{0:T(128)} %constant.35.clone.1.refs_0_, bf16[256,2048]{1,0:T(8,128)(2,1)} %refs_1_.2, bf16[2,512,256]{2,1,0:T(8,128)(2,1)} %copy-done, bf16[2,512,256]{2,1,0:T(8,128)(2,1)} %copy-done, bf16[2,256,256]{2,1,0:T(8,128)(2,1)} %refs_5_.3, bf16[2,256,256]{2,1,0:T(8,128)(2,1)} %refs_5_.3), custom_call_target="tpu_custom_call" | custom-call | tf_op jit(solution)/shard_map/pallas_call | solution.py:128
  66.3 0.0 collective-permute-done.10
  66.3 0.0 collective-permute-done.11
  66.3 0.1 broadcast_in_dim.18
  66.4 0.1 broadcast_in_dim.19
  66.5 0.1 broadcast_in_dim.20
  66.6 0.1 broadcast_in_dim.21
  66.7 0.1 broadcast_in_dim.22
  66.8 0.1 broadcast_in_dim.23
  66.9 1.8 %fusion = bf16[16,2048]{1,0:T(8,128)(2,1)} fusion(f32[2,8,16,128]{3,2,1,0:T(8,128)S(1)} %bitcast.133, f32[16,2048]{1,0:T(8,128)S(1)} %collective-permute-done.11, f32[2,8,16,128]{3,2,1,0:T(8,128)S(1)} %bitcast.132, f32[16,2048]{1,0:T(8,128)S(1)} %collective-permute-done.10, f32[2,8,16,128]{3,2,1,0:T(8,128)S(1)} %bitcast.131, ...), kind=kLoop, calls=%fused_computation.2 | loop fusion | flops 360448 | bytes 1507328 | tf_op jit(solution)/shard_map/convert_element_type | solution.py:206
  (25 shorter events, 0.2 us)
Async XLA Ops:
  2.2 11.9 %collective-permute-start.3 = (bf16[40960]{0:T(1024)(128)(2,1)S(1)}, bf16[40960]{0:T(1024)(128)(2,1)S(1)}, u32[]{:S(2)}, u32[]{:S(2)}) collective-permute-start(bf16[40960]{0:T(1024)(128)(2,1)S(1)} %constant_dynamic-update-slice_fusion.5), channel_id=1, source_target_pairs={{0,4},{4,8},{8,12},{12,0},{1,5},{5,9},{9,13},{13,1},{2,6},{6,10},{... | collective-permute-start | bytes 245768 | tf_op jit(solution)/shard_map/ppermute | solution.py:141
  5.3 11.7 %collective-permute-start.4 = (bf16[40960]{0:T(1024)(128)(2,1)S(1)}, bf16[40960]{0:T(1024)(128)(2,1)S(1)}, u32[]{:S(2)}, u32[]{:S(2)}) collective-permute-start(bf16[40960]{0:T(1024)(128)(2,1)S(1)} %constant_dynamic-update-slice_fusion.5), channel_id=1, source_target_pairs={{0,8},{4,12},{8,0},{12,4},{1,9},{5,13},{9,1},{13,5},{2,10},{6,14},... | collective-permute-start | bytes 245768 | tf_op jit(solution)/shard_map/ppermute | solution.py:141
  7.9 9.2 %collective-permute-start.5 = (bf16[40960]{0:T(1024)(128)(2,1)S(1)}, bf16[40960]{0:T(1024)(128)(2,1)S(1)}, u32[]{:S(2)}, u32[]{:S(2)}) collective-permute-start(bf16[40960]{0:T(1024)(128)(2,1)S(1)} %constant_dynamic-update-slice_fusion.5), channel_id=1, source_target_pairs={{0,12},{4,0},{8,4},{12,8},{1,13},{5,1},{9,5},{13,9},{2,14},{6,2},{... | collective-permute-start | bytes 245768 | tf_op jit(solution)/shard_map/ppermute | solution.py:141
  9.3 41.1 %collective-permute-start = (bf16[2,128,256]{2,1,0:T(8,128)(2,1)}, bf16[2,128,256]{2,1,0:T(8,128)(2,1)S(1)}, u32[]{:S(2)}, u32[]{:S(2)}) collective-permute-start(bf16[2,128,256]{2,1,0:T(8,128)(2,1)} %param.10), channel_id=1, source_target_pairs={{0,4},{4,8},{8,12},{12,0},{1,5},{5,9},{9,13},{13,1},{2,6},{6,10},{... | collective-permute-start | bytes 393224 | tf_op jit(solution)/shard_map/ppermute | solution.py:141
  9.9 44.2 %collective-permute-start.1 = (bf16[2,128,256]{2,1,0:T(8,128)(2,1)}, bf16[2,128,256]{2,1,0:T(8,128)(2,1)S(1)}, u32[]{:S(2)}, u32[]{:S(2)}) collective-permute-start(bf16[2,128,256]{2,1,0:T(8,128)(2,1)} %param.10), channel_id=1, source_target_pairs={{0,8},{4,12},{8,0},{12,4},{1,9},{5,13},{9,1},{13,5},{2,10},{6,14},... | collective-permute-start | bytes 393224 | tf_op jit(solution)/shard_map/ppermute | solution.py:141
  14.1 40.1 %collective-permute-start.2 = (bf16[2,128,256]{2,1,0:T(8,128)(2,1)}, bf16[2,128,256]{2,1,0:T(8,128)(2,1)S(1)}, u32[]{:S(2)}, u32[]{:S(2)}) collective-permute-start(bf16[2,128,256]{2,1,0:T(8,128)(2,1)} %param.10), channel_id=1, source_target_pairs={{0,12},{4,0},{8,4},{12,8},{1,13},{5,1},{9,5},{13,9},{2,14},{6,2},{... | collective-permute-start | bytes 393224 | tf_op jit(solution)/shard_map/ppermute | solution.py:141
  18.7 24.7 %copy-start.2 = (bf16[2,16,256]{2,1,0:T(8,128)(2,1)S(1)}, bf16[2,16,256]{2,1,0:T(8,128)(2,1)}, u32[]{:S(2)}) copy-start(bf16[2,16,256]{2,1,0:T(8,128)(2,1)} %param.14) | copy-start | bytes 49156
  36.6 7.6 %collective-permute-start.6 = (f32[2,16,128]{2,1,0:T(8,128)S(1)}, f32[2,16,128]{2,1,0:T(8,128)S(1)}, u32[]{:S(2)}, u32[]{:S(2)}) collective-permute-start(f32[2,16,128]{2,1,0:T(8,128)S(1)} %get-tuple-element.21), channel_id=1, source_target_pairs={{0,12},{4,0},{8,4},{12,8},{1,13},{5,1},{9,5},{13,9},{2,14},{6,2},{... | collective-permute-start | bytes 49160 | tf_op jit(solution)/shard_map/ppermute | solution.py:141
  38.0 6.8 %collective-permute-start.7 = (f32[2,16,128]{2,1,0:T(8,128)S(1)}, f32[2,16,128]{2,1,0:T(8,128)S(1)}, u32[]{:S(2)}, u32[]{:S(2)}) collective-permute-start(f32[2,16,128]{2,1,0:T(8,128)S(1)} %get-tuple-element.23), channel_id=1, source_target_pairs={{0,8},{4,12},{8,0},{12,4},{1,9},{5,13},{9,1},{13,5},{2,10},{6,14},... | collective-permute-start | bytes 49160 | tf_op jit(solution)/shard_map/ppermute | solution.py:141
  44.2 5.6 %collective-permute-start.8 = (f32[2,16,128]{2,1,0:T(8,128)S(1)}, f32[2,16,128]{2,1,0:T(8,128)S(1)}, u32[]{:S(2)}, u32[]{:S(2)}) collective-permute-start(f32[2,16,128]{2,1,0:T(8,128)S(1)} %get-tuple-element.22), channel_id=1, source_target_pairs={{0,4},{4,8},{8,12},{12,0},{1,5},{5,9},{9,13},{13,1},{2,6},{6,10},{... | collective-permute-start | bytes 49160 | tf_op jit(solution)/shard_map/ppermute | solution.py:141
  44.8 21.5 %collective-permute-start.10 = (f32[16,2048]{1,0:T(8,128)S(1)}, f32[16,2048]{1,0:T(8,128)S(1)}, u32[]{:S(2)}, u32[]{:S(2)}) collective-permute-start(f32[16,2048]{1,0:T(8,128)S(1)} %get-tuple-element.18), channel_id=1, source_target_pairs={{0,8},{4,12},{8,0},{12,4},{1,9},{5,13},{9,1},{13,5},{2,10},{6,14},... | collective-permute-start | bytes 393224 | tf_op jit(solution)/shard_map/ppermute | solution.py:141
  49.8 16.5 %collective-permute-start.11 = (f32[16,2048]{1,0:T(8,128)S(1)}, f32[16,2048]{1,0:T(8,128)S(1)}, u32[]{:S(2)}, u32[]{:S(2)}) collective-permute-start(f32[16,2048]{1,0:T(8,128)S(1)} %get-tuple-element.17), channel_id=1, source_target_pairs={{0,4},{4,8},{8,12},{12,0},{1,5},{5,9},{9,13},{13,1},{2,6},{6,10},{... | collective-permute-start | bytes 393224 | tf_op jit(solution)/shard_map/ppermute | solution.py:141
  50.3 16.0 %collective-permute-start.9 = (f32[16,2048]{1,0:T(8,128)S(1)}, f32[16,2048]{1,0:T(8,128)S(1)}, u32[]{:S(2)}, u32[]{:S(2)}) collective-permute-start(f32[16,2048]{1,0:T(8,128)S(1)} %get-tuple-element.16), channel_id=1, source_target_pairs={{0,12},{4,0},{8,4},{12,8},{1,13},{5,1},{9,5},{13,9},{2,14},{6,2},{... | collective-permute-start | bytes 393224 | tf_op jit(solution)/shard_map/ppermute | solution.py:141
  54.2 0.8 %copy-start = (bf16[2,512,256]{2,1,0:T(8,128)(2,1)}, bf16[2,512,256]{2,1,0:T(8,128)(2,1)S(1)}, u32[]{:S(2)}) copy-start(bf16[2,512,256]{2,1,0:T(8,128)(2,1)S(1)} %constant_dynamic-update-slice_fusion.refs_2_.refs_3_) | copy-start | bytes 1572868
  57.7 9.3 %copy-start.1 = (f32[16,2048]{1,0:T(8,128)S(1)}, f32[16,2048]{1,0:T(8,128)}, u32[]{:S(2)}) copy-start(f32[16,2048]{1,0:T(8,128)} %get-tuple-element.6) | copy-start | bytes 393220

commit v5 on v4

--- a/solution.py
+++ b/solution.py
@@ -171,10 +171,20 @@
         context_output, context_side = attention(
             all_queries, [(cache_kv, "cache"), (kv_block, None)], False, length=cache_len
         )
-        remote = [(context_output[:own_count], context_side[:, :own_count])]
+        side_width = kv_heads * HD
+        context_side = jnp.transpose(context_side, (1, 0, 2)).reshape(-1, side_width)
+        context_packed = jnp.concatenate([context_output, context_side], axis=1)
+        sections = [context_packed[:own_count]]
         for k in range(1, ctx_count):
             rows = slice(k * own_count, (k + 1) * own_count)
-            remote.append(shifted((context_output[rows], context_side[:, rows]), -k, ctx_count))
+            sections.append(shifted(context_packed[rows], -k, ctx_count))
+        remote = [
+            (
+                section[:, :query_width],
+                jnp.transpose(section[:, query_width:].reshape(own_count, kv_heads, HD), (1, 0, 2)),
+            )
+            for section in sections
+        ]
 
         (block_out,) = attention(q_block, [(anchor, None), (kv_block, "causal")], True)
         local_output, local_side = attention(

time: 69.3 us -> 61.1 us (0.88)
  starting transfers between devices: 23.2 us -> 17.9 us
  waiting for transfers between devices: 2.78 us -> 0.02 us
    ppermute x12 -> x9, starting transfers between devices: 23.2 us -> 17.9 us  [shifted(): lax.ppermute(value, 'ctx', [(j, (j + shift) % count) for j in range(count)])]
    ppermute x12 -> x9, waiting for transfers between devices: 2.78 us -> 0.02 us  [shifted(): lax.ppermute(value, 'ctx', [(j, (j + shift) % count) for j in range(count)])]
    slice x2 -> x4, local copies, waits for them, and re-layouts: 1.81 us -> 0.04 us  [the longest x1 0.03 us: local(): sections.append(shifted(context_packed[rows], -k, ctx_count))]
    transpose x15 -> x6, local copies, waits for them, and re-layouts: 2.62 us -> 1.21 us  [per_head(): jnp.transpose(picked, (1, 0, 2)).reshape(own_count, kv_heads * group_size)]
    unnamed x12 -> x13, local copies, waits for them, and re-layouts: 3.36 us -> 4.44 us
    concatenate x0 -> x1, local copies, waits for them, and re-layouts: none -> 0.85 us  [local(): context_packed = jnp.concatenate([context_output, context_side], axis=1)]
    transpose x0 -> x1, local copies, waits for them, and re-layouts: none -> 0.72 us  [local(): jnp.transpose(section[:, query_width:].reshape(own_count, kv_heads, HD),...]
  transfers between devices with their start and end apart: 12 -> 9, of which waited for: 1 -> 0; matrix products, arithmetic and copies ran while one was open for 15% -> 16% of each run, Pallas kernels for 38% -> 43%
where the time goes in v5:
time: 61.1 us; the launch traced here: 60.6 us
  Pallas kernels  26.1 us (43%)
  starting transfers between devices  17.9 us (29%)
  local copies, waits for them, and re-layouts  10.3 us (17%)
  other arithmetic  4.68 us (8%)
  between operations  1.58 us (3%)
    pallas_call x3, Pallas kernels, attention(): pl.pallas_call(functools.partial(attention_kernel, masks, normalize, rows...  26.1 us
    ppermute x9, starting transfers between devices, shifted(): lax.ppermute(value, 'ctx', [(j, (j + shift) % count) for j in range(count)])  17.9 us
    unnamed x13, local copies, waits for them, and re-layouts  4.44 us
    convert_element_type x1, other arithmetic, local(): query_out = (merged_output / widen(merged_totals)).astype(jnp.bfloat16)  1.81 us
    concatenate x1, other arithmetic, local(): jnp.concatenate([slot[:split].reshape(own_count, query_width) for slot in...  1.56 us
  transfers between devices with their start and end apart: 9, of which 0 were waited for; matrix products, arithmetic and copies ran while one was open for 16% of the time, Pallas kernels for 43%

profile of v5, /device:TPU:0, one launch (start us, length us, event | category | flops | bytes accessed | tf_op | source)
XLA Modules:
  0.0 60.6 jit_solution(15058469031225930361)
XLA Ops:
  0.6 0.9 %copy.30 = bf16[2,16,8,128]{3,1,2,0:T(8,128)(2,1)S(1)} copy(bf16[2,16,8,128]{3,2,1,0:T(8,128)(2,1)} %bitcast.153) | data formatting | bytes 131072
  1.5 0.7 %copy.31 = bf16[4,2,8,128]{3,1,2,0:T(2,128)(2,1)S(1)} copy(bf16[4,2,8,128]{3,2,1,0:T(8,128)(2,1)} %bitcast.166) | data formatting | bytes 32768
  2.2 3.1 %collective-permute-start.3 = (bf16[40960]{0:T(1024)(128)(2,1)S(1)}, bf16[40960]{0:T(1024)(128)(2,1)S(1)}, u32[]{:S(2)}, u32[]{:S(2)}) collective-permute-start(bf16[40960]{0:T(1024)(128)(2,1)S(1)} %constant_dynamic-update-slice_fusion.6), channel_id=1, source_target_pairs={{0,4},{4,8},{8,12},{12,0},{1,5},{5,9},{9,13},{13,1},{2,6},{6,10},{... | collective-permute-start | bytes 245768 | tf_op jit(solution)/shard_map/ppermute | solution.py:141
  5.3 2.6 %collective-permute-start.4 = (bf16[40960]{0:T(1024)(128)(2,1)S(1)}, bf16[40960]{0:T(1024)(128)(2,1)S(1)}, u32[]{:S(2)}, u32[]{:S(2)}) collective-permute-start(bf16[40960]{0:T(1024)(128)(2,1)S(1)} %constant_dynamic-update-slice_fusion.6), channel_id=1, source_target_pairs={{0,8},{4,12},{8,0},{12,4},{1,9},{5,13},{9,1},{13,5},{2,10},{6,14},... | collective-permute-start | bytes 245768 | tf_op jit(solution)/shard_map/ppermute | solution.py:141
  7.9 1.3 %collective-permute-start.5 = (bf16[40960]{0:T(1024)(128)(2,1)S(1)}, bf16[40960]{0:T(1024)(128)(2,1)S(1)}, u32[]{:S(2)}, u32[]{:S(2)}) collective-permute-start(bf16[40960]{0:T(1024)(128)(2,1)S(1)} %constant_dynamic-update-slice_fusion.6), channel_id=1, source_target_pairs={{0,12},{4,0},{8,4},{12,8},{1,13},{5,1},{9,5},{13,9},{2,14},{6,2},{... | collective-permute-start | bytes 245768 | tf_op jit(solution)/shard_map/ppermute | solution.py:141
  9.3 0.7 %collective-permute-start = (bf16[2,128,256]{2,1,0:T(8,128)(2,1)}, bf16[2,128,256]{2,1,0:T(8,128)(2,1)S(1)}, u32[]{:S(2)}, u32[]{:S(2)}) collective-permute-start(bf16[2,128,256]{2,1,0:T(8,128)(2,1)} %param.10), channel_id=1, source_target_pairs={{0,4},{4,8},{8,12},{12,0},{1,5},{5,9},{9,13},{13,1},{2,6},{6,10},{... | collective-permute-start | bytes 393224 | tf_op jit(solution)/shard_map/ppermute | solution.py:141
  9.9 0.3 collective-permute-start.1
  10.3 0.9 %constant_dynamic-update-slice_fusion.3 = bf16[2,512,256]{2,1,0:T(8,128)(2,1)S(1)} fusion(bf16[2,128,256]{2,1,0:T(8,128)(2,1)} %param.10), kind=kLoop, calls=%fused_computation.20 | loop fusion | bytes 262144
  11.2 0.9 %fusion.20 = (s32[16]{0:T(128)S(1)}, s32[16]{0:T(128)S(1)}, s32[16]{0:T(128)S(1)}, s32[16]{0:T(128)S(1)}) fusion(s32[64]{0:T(128)} %param.15, s32[]{:T(128)S(6)} %select_n.32, s32[]{:T(128)S(6)} %select_n.34, s32[]{:T(128)S(6)} %select_n.38, s32[]{:T(128)S(6)} %select_n.36), kind=kLoop, calls=%fused_computation.54 | loop fusion | bytes 528 | tf_op jit(solution)/shard_map/dynamic_slice | solution.py:165
  12.1 0.7 %copy.11.refs_7_ = s32[16,1]{1,0:T(8,128)} copy(s32[16,1]{0,1:T(1,128)S(1)} %bitcast.167) | data formatting | bytes 128 | tf_op jit(solution)/shard_map/reshape | solution.py:117
  13.5 0.7 %add_bitcast_fusion.refs_6_ = s32[1,64]{1,0:T(1,128)} fusion(s32[16]{0:T(128)S(1)} %get-tuple-element.25, s32[16]{0:T(128)S(1)} %get-tuple-element.26, s32[16]{0:T(128)S(1)} %get-tuple-element.24, s32[16]{0:T(128)S(1)} %get-tuple-element.23), kind=kLoop, calls=%fused_computation.52 | loop fusion | flops 192 | bytes 512 | tf_op jit(solution)/shard_map/reshape | solution.py:116
  14.1 0.0 collective-permute-done.3
  14.1 2.8 %collective-permute-start.2 = (bf16[2,128,256]{2,1,0:T(8,128)(2,1)}, bf16[2,128,256]{2,1,0:T(8,128)(2,1)S(1)}, u32[]{:S(2)}, u32[]{:S(2)}) collective-permute-start(bf16[2,128,256]{2,1,0:T(8,128)(2,1)} %param.10), channel_id=1, source_target_pairs={{0,12},{4,0},{8,4},{12,8},{1,13},{5,1},{9,5},{13,9},{2,14},{6,2},{... | collective-permute-start | bytes 393224 | tf_op jit(solution)/shard_map/ppermute | solution.py:141
  17.0 0.0 collective-permute-done.4
  17.1 0.0 collective-permute-done.5
  17.1 1.6 %pad_maximum_fusion.refs_1_ = bf16[64,2048]{1,0:T(8,128)(2,1)} fusion(bf16[16,2048]{1,0:T(8,128)(2,1)S(1)} %slice.159, bf16[16,2048]{1,0:T(8,128)(2,1)S(1)} %slice.157, bf16[16,2048]{1,0:T(8,128)(2,1)S(1)} %slice.155, bf16[16,2048]{1,0:T(8,128)(2,1)} %refs_1_.3), kind=kLoop, calls=%fused_computation | loop fusion | flops 1048576 | bytes 524288 | tf_op jit(solution)/shard_map/concatenate | solution.py:156
  18.7 0.0 copy-start.2
  18.7 16.2 %shard_map.97 = (f32[64,2048]{1,0:T(8,128)}, f32[2,64,128]{2,1,0:T(8,128)}) custom-call(s32[1]{0:T(128)S(6)} %copy.50.refs_0_, bf16[64,2048]{1,0:T(8,128)(2,1)} %pad_maximum_fusion.refs_1_, bf16[2,4096,256]{2,1,0:T(8,128)(2,1)} %refs_3_.1, bf16[2,4096,256]{2,1,0:T(8,128)(2,1)} %refs_3_.1, bf16[2,256,256]{2,1,0:T(8,128)(2,1)} %refs_5_.3, ...), custom_call_target="tpu_custom_call" | custom-call | tf_op jit(solution)/shard_map/pallas_call | solution.py:128
  34.9 1.1 %constant_dynamic-update-slice_fusion.5 = f32[64,2304]{1,0:T(8,128)S(1)} fusion(f32[64,2048]{1,0:T(8,128)} %get-tuple-element.9), kind=kLoop, calls=%fused_computation.22 | loop fusion | bytes 1048576
  36.0 0.8 %bitcast_dynamic-update-slice_fusion = f32[64,2304]{1,0:T(8,128)S(1)} fusion(f32[64,2304]{1,0:T(8,128)S(1)} %constant_dynamic-update-slice_fusion.5, f32[2,64,128]{2,1,0:T(8,128)} %get-tuple-element.8), kind=kLoop, calls=%fused_computation.12 | loop fusion | bytes 131072 | tf_op jit(solution)/shard_map/concatenate | solution.py:176
  36.9 3.2 %collective-permute-start.7 = (f32[16,2304]{1,0:T(8,128)S(1)}, f32[16,2304]{1,0:T(8,128)S(1)}, u32[]{:S(2)}, u32[]{:S(2)}) collective-permute-start(f32[16,2304]{1,0:T(8,128)S(1)} %get-tuple-element.18), channel_id=1, source_target_pairs={{0,8},{4,12},{8,0},{12,4},{1,9},{5,13},{9,1},{13,5},{2,10},{6,14},... | collective-permute-start | bytes 442376 | tf_op jit(solution)/shard_map/ppermute | solution.py:141
  40.1 1.1 %collective-permute-start.8 = (f32[16,2304]{1,0:T(8,128)S(1)}, f32[16,2304]{1,0:T(8,128)S(1)}, u32[]{:S(2)}, u32[]{:S(2)}) collective-permute-start(f32[16,2304]{1,0:T(8,128)S(1)} %get-tuple-element.17), channel_id=1, source_target_pairs={{0,4},{4,8},{8,12},{12,0},{1,5},{5,9},{9,13},{13,1},{2,6},{6,10},{... | collective-permute-start | bytes 442376 | tf_op jit(solution)/shard_map/ppermute | solution.py:141
  41.3 0.7 %slice_bitcast_fusion.2 = f32[2,16,128]{2,1,0:T(8,128)S(1)} fusion(f32[64,2,128]{2,0,1:T(8,128)} %bitcast.164), kind=kLoop, calls=%fused_computation.16 | loop fusion | bytes 32768 | tf_op jit(solution)/shard_map/transpose | solution.py:184
  42.0 0.1 slice_bitcast_fusion.1
  42.1 0.0 copy-done.2
  42.2 0.6 %pad_maximum_fusion.1.refs_4_.refs_5_ = bf16[2,64,256]{2,1,0:T(8,128)(2,1)} fusion(bf16[2,16,256]{2,1,0:T(8,128)(2,1)S(1)} %slice.152, bf16[2,16,256]{2,1,0:T(8,128)(2,1)S(1)} %slice.150, bf16[2,16,256]{2,1,0:T(8,128)(2,1)S(1)} %slice.148, bf16[2,16,256]{2,1,0:T(8,128)(2,1)S(1)} %copy-done.2), kind=kLoop, calls=%fused_computation.13 | loop fusion | flops 262144 | bytes 131072 | tf_op jit(solution)/shard_map/concatenate | solution.py:159
  42.8 0.1 copy.13
  42.9 0.1 copy.24
  42.9 0.0 collective-permute-done
  42.9 2.7 %collective-permute-start.6 = (f32[16,2304]{1,0:T(8,128)S(1)}, f32[16,2304]{1,0:T(8,128)S(1)}, u32[]{:S(2)}, u32[]{:S(2)}) collective-permute-start(f32[16,2304]{1,0:T(8,128)S(1)} %get-tuple-element.16), channel_id=1, source_target_pairs={{0,12},{4,0},{8,4},{12,8},{1,13},{5,1},{9,5},{13,9},{2,14},{6,2},{... | collective-permute-start | bytes 442376 | tf_op jit(solution)/shard_map/ppermute | solution.py:141
  45.6 0.0 collective-permute-done.1
  45.7 0.0 collective-permute-done.2
  45.7 0.0 copy-start
  45.7 0.8 %copy-done = bf16[2,512,256]{2,1,0:T(8,128)(2,1)} copy-done((bf16[2,512,256]{2,1,0:T(8,128)(2,1)}, bf16[2,512,256]{2,1,0:T(8,128)(2,1)S(1)}, u32[]{:S(2)}) %copy-start) | copy-done | bytes 524312
  46.5 2.7 %shard_map.96 = (f32[16,2048]{1,0:T(8,128)}, f32[2,16,128]{2,1,0:T(8,128)}) custom-call(s32[1]{0:T(128)} %constant.35.clone.1.refs_0_, bf16[16,2048]{1,0:T(8,128)(2,1)} %refs_1_.3, bf16[2,512,256]{2,1,0:T(8,128)(2,1)} %copy-done, bf16[2,512,256]{2,1,0:T(8,128)(2,1)} %copy-done, bf16[2,64,256]{2,1,0:T(8,128)(2,1)} %pad_maximum_fusion.1.refs_4_.refs_5_, ...), custom_call_target="tpu_custom_call" | custom-call | tf_op jit(solution)/shard_map/pallas_call | solution.py:128
  49.1 0.0 copy-start.1
  49.2 0.9 %slice_bitcast_fusion.4 = (f32[16,2,8]{2,0,1:T(8,128)S(1)}, f32[16,2,8]{2,0,1:T(8,128)S(1)}) fusion(f32[2,16,128]{2,1,0:T(8,128)} %get-tuple-element.7), kind=kLoop, calls=%fused_computation.24 | loop fusion | bytes 4096 | tf_op jit(solution)/shard_map/transpose | solution.py:199
  50.0 0.1 copy.12
  50.1 0.1 copy.23
  50.2 7.2 %shard_map.95 = bf16[256,2048]{1,0:T(8,128)(2,1)} custom-call(s32[1]{0:T(128)} %constant.35.clone.1.refs_0_, bf16[256,2048]{1,0:T(8,128)(2,1)} %refs_1_.2, bf16[2,512,256]{2,1,0:T(8,128)(2,1)} %copy-done, bf16[2,512,256]{2,1,0:T(8,128)(2,1)} %copy-done, bf16[2,256,256]{2,1,0:T(8,128)(2,1)} %refs_5_.3, bf16[2,256,256]{2,1,0:T(8,128)(2,1)} %refs_5_.3), custom_call_target="tpu_custom_call" | custom-call | tf_op jit(solution)/shard_map/pallas_call | solution.py:128
  57.4 0.0 collective-permute-done.7
  57.4 0.1 copy.27
  57.5 0.0 collective-permute-done.8
  57.5 0.1 copy.28
  57.6 0.0 collective-permute-done.6
  57.6 0.1 copy.26
  57.7 0.1 copy.18
  57.8 0.1 copy.19
  57.9 0.1 copy.20
  57.9 0.1 copy.21
  58.0 0.1 copy.22
  58.1 0.1 copy.25
  58.1 0.1 broadcast_in_dim.18
  58.2 0.1 broadcast_in_dim.19
  58.4 0.1 broadcast_in_dim.20
  58.5 0.1 broadcast_in_dim.21
  58.6 0.1 broadcast_in_dim.22
  58.7 0.1 broadcast_in_dim.23
  58.8 0.0 copy-done.1
  58.8 1.8 %fusion = bf16[16,2048]{1,0:T(8,128)(2,1)} fusion(f32[2,8,16,128]{3,2,1,0:T(8,128)S(1)} %bitcast.159, f32[2,8,16,128]{3,2,1,0:T(8,128)S(1)} %bitcast.158, f32[2,8,16,128]{3,2,1,0:T(8,128)S(1)} %bitcast.157, f32[2,8,16,128]{3,2,1,0:T(8,128)S(1)} %bitcast.156, f32[2,8,16,128]{3,2,1,0:T(8,128)S(1)} %bitcast.155, f32[16,2048]{1,0:T(8,128)S(1)} %copy-done.1, ...), kind=kLoop, calls=%fused_computation.2 | loop fusion | flops 360448 | bytes 1507328 | tf_op jit(solution)/shard_map/convert_element_type | solution.py:216
  (22 shorter events, 0.3 us)
Async XLA Ops:
  2.2 11.9 %collective-permute-start.3 = (bf16[40960]{0:T(1024)(128)(2,1)S(1)}, bf16[40960]{0:T(1024)(128)(2,1)S(1)}, u32[]{:S(2)}, u32[]{:S(2)}) collective-permute-start(bf16[40960]{0:T(1024)(128)(2,1)S(1)} %constant_dynamic-update-slice_fusion.6), channel_id=1, source_target_pairs={{0,4},{4,8},{8,12},{12,0},{1,5},{5,9},{9,13},{13,1},{2,6},{6,10},{... | collective-permute-start | bytes 245768 | tf_op jit(solution)/shard_map/ppermute | solution.py:141
  5.3 11.7 %collective-permute-start.4 = (bf16[40960]{0:T(1024)(128)(2,1)S(1)}, bf16[40960]{0:T(1024)(128)(2,1)S(1)}, u32[]{:S(2)}, u32[]{:S(2)}) collective-permute-start(bf16[40960]{0:T(1024)(128)(2,1)S(1)} %constant_dynamic-update-slice_fusion.6), channel_id=1, source_target_pairs={{0,8},{4,12},{8,0},{12,4},{1,9},{5,13},{9,1},{13,5},{2,10},{6,14},... | collective-permute-start | bytes 245768 | tf_op jit(solution)/shard_map/ppermute | solution.py:141
  7.9 9.2 %collective-permute-start.5 = (bf16[40960]{0:T(1024)(128)(2,1)S(1)}, bf16[40960]{0:T(1024)(128)(2,1)S(1)}, u32[]{:S(2)}, u32[]{:S(2)}) collective-permute-start(bf16[40960]{0:T(1024)(128)(2,1)S(1)} %constant_dynamic-update-slice_fusion.6), channel_id=1, source_target_pairs={{0,12},{4,0},{8,4},{12,8},{1,13},{5,1},{9,5},{13,9},{2,14},{6,2},{... | collective-permute-start | bytes 245768 | tf_op jit(solution)/shard_map/ppermute | solution.py:141
  9.3 33.7 %collective-permute-start = (bf16[2,128,256]{2,1,0:T(8,128)(2,1)}, bf16[2,128,256]{2,1,0:T(8,128)(2,1)S(1)}, u32[]{:S(2)}, u32[]{:S(2)}) collective-permute-start(bf16[2,128,256]{2,1,0:T(8,128)(2,1)} %param.10), channel_id=1, source_target_pairs={{0,4},{4,8},{8,12},{12,0},{1,5},{5,9},{9,13},{13,1},{2,6},{6,10},{... | collective-permute-start | bytes 393224 | tf_op jit(solution)/shard_map/ppermute | solution.py:141
  9.9 35.7 %collective-permute-start.1 = (bf16[2,128,256]{2,1,0:T(8,128)(2,1)}, bf16[2,128,256]{2,1,0:T(8,128)(2,1)S(1)}, u32[]{:S(2)}, u32[]{:S(2)}) collective-permute-start(bf16[2,128,256]{2,1,0:T(8,128)(2,1)} %param.10), channel_id=1, source_target_pairs={{0,8},{4,12},{8,0},{12,4},{1,9},{5,13},{9,1},{13,5},{2,10},{6,14},... | collective-permute-start | bytes 393224 | tf_op jit(solution)/shard_map/ppermute | solution.py:141
  14.1 31.5 %collective-permute-start.2 = (bf16[2,128,256]{2,1,0:T(8,128)(2,1)}, bf16[2,128,256]{2,1,0:T(8,128)(2,1)S(1)}, u32[]{:S(2)}, u32[]{:S(2)}) collective-permute-start(bf16[2,128,256]{2,1,0:T(8,128)(2,1)} %param.10), channel_id=1, source_target_pairs={{0,12},{4,0},{8,4},{12,8},{1,13},{5,1},{9,5},{13,9},{2,14},{6,2},{... | collective-permute-start | bytes 393224 | tf_op jit(solution)/shard_map/ppermute | solution.py:141
  18.7 23.4 %copy-start.2 = (bf16[2,16,256]{2,1,0:T(8,128)(2,1)S(1)}, bf16[2,16,256]{2,1,0:T(8,128)(2,1)}, u32[]{:S(2)}) copy-start(bf16[2,16,256]{2,1,0:T(8,128)(2,1)} %param.14) | copy-start | bytes 49156
  36.9 20.5 %collective-permute-start.7 = (f32[16,2304]{1,0:T(8,128)S(1)}, f32[16,2304]{1,0:T(8,128)S(1)}, u32[]{:S(2)}, u32[]{:S(2)}) collective-permute-start(f32[16,2304]{1,0:T(8,128)S(1)} %get-tuple-element.18), channel_id=1, source_target_pairs={{0,8},{4,12},{8,0},{12,4},{1,9},{5,13},{9,1},{13,5},{2,10},{6,14},... | collective-permute-start | bytes 442376 | tf_op jit(solution)/shard_map/ppermute | solution.py:141
  40.1 17.3 %collective-permute-start.8 = (f32[16,2304]{1,0:T(8,128)S(1)}, f32[16,2304]{1,0:T(8,128)S(1)}, u32[]{:S(2)}, u32[]{:S(2)}) collective-permute-start(f32[16,2304]{1,0:T(8,128)S(1)} %get-tuple-element.17), channel_id=1, source_target_pairs={{0,4},{4,8},{8,12},{12,0},{1,5},{5,9},{9,13},{13,1},{2,6},{6,10},{... | collective-permute-start | bytes 442376 | tf_op jit(solution)/shard_map/ppermute | solution.py:141
  42.9 14.7 %collective-permute-start.6 = (f32[16,2304]{1,0:T(8,128)S(1)}, f32[16,2304]{1,0:T(8,128)S(1)}, u32[]{:S(2)}, u32[]{:S(2)}) collective-permute-start(f32[16,2304]{1,0:T(8,128)S(1)} %get-tuple-element.16), channel_id=1, source_target_pairs={{0,12},{4,0},{8,4},{12,8},{1,13},{5,1},{9,5},{13,9},{2,14},{6,2},{... | collective-permute-start | bytes 442376 | tf_op jit(solution)/shard_map/ppermute | solution.py:141
  45.7 0.8 %copy-start = (bf16[2,512,256]{2,1,0:T(8,128)(2,1)}, bf16[2,512,256]{2,1,0:T(8,128)(2,1)S(1)}, u32[]{:S(2)}) copy-start(bf16[2,512,256]{2,1,0:T(8,128)(2,1)S(1)} %constant_dynamic-update-slice_fusion.refs_2_.refs_3_) | copy-start | bytes 1572868
  49.1 9.6 %copy-start.1 = (f32[16,2048]{1,0:T(8,128)S(1)}, f32[16,2048]{1,0:T(8,128)}, u32[]{:S(2)}) copy-start(f32[16,2048]{1,0:T(8,128)} %get-tuple-element.6) | copy-start | bytes 393220

commit v6 on v5

--- a/solution.py
+++ b/solution.py
@@ -20,7 +20,7 @@
 STACK_ROWS = 512
 
 
-def attention_kernel(masks, normalize, rows, group_size, *refs):
+def attention_kernel(masks, normalize, packed, rows, group_size, kv_heads, *refs):
     length_ref, q_ref = refs[0], refs[1]
     part_count = len(masks)
     kv_refs = refs[2 : 2 + 2 * part_count]
@@ -29,7 +29,8 @@
         key_pos_ref, own_pos_ref = rest[0], rest[1]
         rest = rest[2:]
     out_ref = rest[0]
-    side_ref = None if normalize else rest[1]
+    side_ref = None if normalize or packed else rest[1]
+    query_width = kv_heads * group_size * HD
     scale = 1.0 / jnp.sqrt(jnp.float32(HD))
     stack = max(1, min(group_size, STACK_ROWS // rows))
     visible = []
@@ -61,22 +62,23 @@
         m_rows = lhs.shape[0]
         all_scores = []
         for index in range(part_count):
-            scores = lax.dot_general(
+            raw = lax.dot_general(
                 lhs,
                 kv_refs[2 * index][...],
                 (((1,), (1,)), ((), ())),
                 preferred_element_type=jnp.float32,
-            ) * scale
+            )
             if visible[index] is not None:
-                scores = jnp.where(visible[index][:m_rows], scores, masked_score)
-            all_scores.append(scores)
+                raw = jnp.where(visible[index][:m_rows], raw, -jnp.inf)
+            all_scores.append(raw)
         peak = jnp.max(all_scores[0], axis=1, keepdims=True)
-        for scores in all_scores[1:]:
-            peak = jnp.maximum(peak, jnp.max(scores, axis=1, keepdims=True))
+        for raw in all_scores[1:]:
+            peak = jnp.maximum(peak, jnp.max(raw, axis=1, keepdims=True))
+        peak = peak * scale
         total = None
         output = None
-        for index, scores in enumerate(all_scores):
-            weights = jnp.exp(scores - peak)
+        for index, raw in enumerate(all_scores):
+            weights = jnp.exp(raw * scale - peak)
             part_total = jnp.sum(weights, axis=1, keepdims=True)
             part_output = jnp.dot(
                 weights.astype(jnp.bfloat16),
@@ -91,13 +93,25 @@
                 out_ref[:, h * HD : (h + 1) * HD] = (output[rows_of] / total[rows_of]).astype(
                     out_ref.dtype
                 )
+            elif packed:
+
+                def store(gi, h=h, rows_of=rows_of):
+                    head = gi * group_size + h
+                    out_ref[:, head * HD : (head + 1) * HD] = output[rows_of]
+                    side = query_width + gi * HD
+                    out_ref[:, side + h : side + h + 1] = peak[rows_of]
+                    side += HD // 2
+                    out_ref[:, side + h : side + h + 1] = total[rows_of]
+
+                for gi in range(kv_heads):
+                    pl.when(pl.program_id(0) == gi)(functools.partial(store, gi))
             else:
                 out_ref[:, h * HD : (h + 1) * HD] = output[rows_of]
                 side_ref[:, h : h + 1] = peak[rows_of]
                 side_ref[:, HD // 2 + h : HD // 2 + h + 1] = total[rows_of]
 
 
-def attention(queries, parts, normalize, length=None, positions=None):
+def attention(queries, parts, normalize, length=None, positions=None, packed=False):
     rows, query_width = queries.shape
     kv_heads = parts[0][0].shape[2] // HD
     group_size = query_width // HD // kv_heads
@@ -122,11 +136,15 @@
         jax.ShapeDtypeStruct((rows, query_width), jnp.bfloat16 if normalize else jnp.float32)
     ]
     out_specs = [pl.BlockSpec((rows, group_width), lambda g, n: (0, g))]
-    if not normalize:
+    if packed:
+        full = (rows, query_width + kv_heads * HD)
+        out_shape = [jax.ShapeDtypeStruct(full, jnp.float32)]
+        out_specs = [pl.BlockSpec(full, lambda g, n: (0, 0))]
+    elif not normalize:
         out_shape.append(jax.ShapeDtypeStruct((kv_heads, rows, HD), jnp.float32))
         out_specs.append(pl.BlockSpec((pl.Squeezed(), rows, HD), lambda g, n: (g, 0, 0)))
     return pl.pallas_call(
-        functools.partial(attention_kernel, masks, normalize, rows, group_size),
+        functools.partial(attention_kernel, masks, normalize, packed, rows, group_size, kv_heads),
         grid_spec=pltpu.PrefetchScalarGridSpec(
             num_scalar_prefetch=1,
             grid=(kv_heads,),
@@ -168,12 +186,13 @@
         )
         own_pos = slot_pos[:own_count]
 
-        context_output, context_side = attention(
-            all_queries, [(cache_kv, "cache"), (kv_block, None)], False, length=cache_len
-        )
-        side_width = kv_heads * HD
-        context_side = jnp.transpose(context_side, (1, 0, 2)).reshape(-1, side_width)
-        context_packed = jnp.concatenate([context_output, context_side], axis=1)
+        (context_packed,) = attention(
+            all_queries,
+            [(cache_kv, "cache"), (kv_block, None)],
+            False,
+            length=cache_len,
+            packed=True,
+        )
         sections = [context_packed[:own_count]]
         for k in range(1, ctx_count):
             rows = slice(k * own_count, (k + 1) * own_count)

time: 61.1 us -> 59.4 us (0.972)
  local copies, waits for them, and re-layouts: 10.3 us -> 9.28 us
  Pallas kernels: 26.1 us -> 25.4 us
    unnamed x13 -> x12, local copies, waits for them, and re-layouts: 4.44 us -> 3.35 us
    slice x1, local copies, waits for them, and re-layouts: 0.03 us -> 1.08 us  [local(): sections.append(shifted(context_packed[rows], -k, ctx_count))]
    concatenate x1 -> x0, local copies, waits for them, and re-layouts: 0.85 us -> none  [local(): context_packed = jnp.concatenate([context_output, context_side], axis=1)]
    transpose x1 -> x0, local copies, waits for them, and re-layouts: 0.72 us -> none  [local(): jnp.transpose(section[:, query_width:].reshape(own_count, kv_heads, HD),...]
    slice x3 -> x4, local copies, waits for them, and re-layouts: 0.01 us -> 0.73 us  [local(): section[:, query_width:].reshape(own_count, kv_heads, HD)]
    pallas_call x3, Pallas kernels: 26.1 us -> 25.4 us  [attention(): pl.pallas_call(functools.partial(attention_kernel, masks, normalize, pack...]
  transfers between devices with their start and end apart: 9 -> 9, of which waited for: 0 -> 0; matrix products, arithmetic and copies ran while one was open for 16% -> 15% of each run, Pallas kernels for 43% -> 43%
where the time goes in v6:
time: 59.4 us; the launch traced here: 58.9 us
  Pallas kernels  25.4 us (43%)
  starting transfers between devices  18 us (30%)
  local copies, waits for them, and re-layouts  9.28 us (16%)
  other arithmetic  4.62 us (8%)
  between operations  1.58 us (3%)
    pallas_call x3, Pallas kernels, attention(): pl.pallas_call(functools.partial(attention_kernel, masks, normalize, pack...  25.4 us
    ppermute x9, starting transfers between devices, shifted(): lax.ppermute(value, 'ctx', [(j, (j + shift) % count) for j in range(count)])  18 us
    unnamed x12, local copies, waits for them, and re-layouts  3.35 us
    convert_element_type x1, other arithmetic, local(): query_out = (merged_output / widen(merged_totals)).astype(jnp.bfloat16)  1.81 us
    concatenate x1, other arithmetic, local(): jnp.concatenate([slot[:split].reshape(own_count, query_width) for slot in...  1.56 us
  transfers between devices with their start and end apart: 9, of which 0 were waited for; matrix products, arithmetic and copies ran while one was open for 15% of the time, Pallas kernels for 43%

profile of v6, /device:TPU:0, one launch (start us, length us, event | category | flops | bytes accessed | tf_op | source)
XLA Modules:
  0.0 58.9 jit_solution(9182023268767386611)
XLA Ops:
  0.6 0.9 %copy.28 = bf16[2,16,8,128]{3,1,2,0:T(8,128)(2,1)S(1)} copy(bf16[2,16,8,128]{3,2,1,0:T(8,128)(2,1)} %bitcast.151) | data formatting | bytes 131072
  1.5 0.7 %copy.29 = bf16[4,2,8,128]{3,1,2,0:T(2,128)(2,1)S(1)} copy(bf16[4,2,8,128]{3,2,1,0:T(8,128)(2,1)} %bitcast.164) | data formatting | bytes 32768
  2.2 3.1 %collective-permute-start.3 = (bf16[40960]{0:T(1024)(128)(2,1)S(1)}, bf16[40960]{0:T(1024)(128)(2,1)S(1)}, u32[]{:S(2)}, u32[]{:S(2)}) collective-permute-start(bf16[40960]{0:T(1024)(128)(2,1)S(1)} %constant_dynamic-update-slice_fusion.5), channel_id=1, source_target_pairs={{0,4},{4,8},{8,12},{12,0},{1,5},{5,9},{9,13},{13,1},{2,6},{6,10},{... | collective-permute-start | bytes 245768 | tf_op jit(solution)/shard_map/ppermute | solution.py:159
  5.3 2.6 %collective-permute-start.4 = (bf16[40960]{0:T(1024)(128)(2,1)S(1)}, bf16[40960]{0:T(1024)(128)(2,1)S(1)}, u32[]{:S(2)}, u32[]{:S(2)}) collective-permute-start(bf16[40960]{0:T(1024)(128)(2,1)S(1)} %constant_dynamic-update-slice_fusion.5), channel_id=1, source_target_pairs={{0,8},{4,12},{8,0},{12,4},{1,9},{5,13},{9,1},{13,5},{2,10},{6,14},... | collective-permute-start | bytes 245768 | tf_op jit(solution)/shard_map/ppermute | solution.py:159
  7.9 1.3 %collective-permute-start.5 = (bf16[40960]{0:T(1024)(128)(2,1)S(1)}, bf16[40960]{0:T(1024)(128)(2,1)S(1)}, u32[]{:S(2)}, u32[]{:S(2)}) collective-permute-start(bf16[40960]{0:T(1024)(128)(2,1)S(1)} %constant_dynamic-update-slice_fusion.5), channel_id=1, source_target_pairs={{0,12},{4,0},{8,4},{12,8},{1,13},{5,1},{9,5},{13,9},{2,14},{6,2},{... | collective-permute-start | bytes 245768 | tf_op jit(solution)/shard_map/ppermute | solution.py:159
  9.3 0.7 %collective-permute-start = (bf16[2,128,256]{2,1,0:T(8,128)(2,1)}, bf16[2,128,256]{2,1,0:T(8,128)(2,1)S(1)}, u32[]{:S(2)}, u32[]{:S(2)}) collective-permute-start(bf16[2,128,256]{2,1,0:T(8,128)(2,1)} %param.10), channel_id=1, source_target_pairs={{0,4},{4,8},{8,12},{12,0},{1,5},{5,9},{9,13},{13,1},{2,6},{6,10},{... | collective-permute-start | bytes 393224 | tf_op jit(solution)/shard_map/ppermute | solution.py:159
  9.9 0.3 collective-permute-start.1
  10.3 0.9 %constant_dynamic-update-slice_fusion.3 = bf16[2,512,256]{2,1,0:T(8,128)(2,1)S(1)} fusion(bf16[2,128,256]{2,1,0:T(8,128)(2,1)} %param.10), kind=kLoop, calls=%fused_computation.18 | loop fusion | bytes 262144
  11.2 0.9 %fusion.19 = (s32[16]{0:T(128)S(1)}, s32[16]{0:T(128)S(1)}, s32[16]{0:T(128)S(1)}, s32[16]{0:T(128)S(1)}) fusion(s32[64]{0:T(128)} %param.15, s32[]{:T(128)S(6)} %select_n.32, s32[]{:T(128)S(6)} %select_n.34, s32[]{:T(128)S(6)} %select_n.38, s32[]{:T(128)S(6)} %select_n.36), kind=kLoop, calls=%fused_computation.50 | loop fusion | bytes 528 | tf_op jit(solution)/shard_map/dynamic_slice | solution.py:183
  12.1 0.7 %copy.11.refs_7_ = s32[16,1]{1,0:T(8,128)} copy(s32[16,1]{0,1:T(1,128)S(1)} %bitcast.165) | data formatting | bytes 128 | tf_op jit(solution)/shard_map/reshape | solution.py:131
  13.5 0.6 add_bitcast_fusion.refs_6_
  14.0 0.0 collective-permute-done.3
  14.1 2.8 %collective-permute-start.2 = (bf16[2,128,256]{2,1,0:T(8,128)(2,1)}, bf16[2,128,256]{2,1,0:T(8,128)(2,1)S(1)}, u32[]{:S(2)}, u32[]{:S(2)}) collective-permute-start(bf16[2,128,256]{2,1,0:T(8,128)(2,1)} %param.10), channel_id=1, source_target_pairs={{0,12},{4,0},{8,4},{12,8},{1,13},{5,1},{9,5},{13,9},{2,14},{6,2},{... | collective-permute-start | bytes 393224 | tf_op jit(solution)/shard_map/ppermute | solution.py:159
  16.9 0.0 collective-permute-done.4
  17.0 0.0 collective-permute-done.5
  17.1 1.6 %pad_maximum_fusion.refs_1_ = bf16[64,2048]{1,0:T(8,128)(2,1)} fusion(bf16[16,2048]{1,0:T(8,128)(2,1)S(1)} %slice.156, bf16[16,2048]{1,0:T(8,128)(2,1)S(1)} %slice.154, bf16[16,2048]{1,0:T(8,128)(2,1)S(1)} %slice.152, bf16[16,2048]{1,0:T(8,128)(2,1)} %refs_1_.3), kind=kLoop, calls=%fused_computation | loop fusion | flops 1048576 | bytes 524288 | tf_op jit(solution)/shard_map/concatenate | solution.py:174
  18.6 0.0 copy-start.2
  18.6 15.7 %shard_map.97 = f32[64,2304]{1,0:T(8,128)} custom-call(s32[1]{0:T(128)S(6)} %copy.46.refs_0_, bf16[64,2048]{1,0:T(8,128)(2,1)} %pad_maximum_fusion.refs_1_, bf16[2,4096,256]{2,1,0:T(8,128)(2,1)} %refs_3_.1, bf16[2,4096,256]{2,1,0:T(8,128)(2,1)} %refs_3_.1, bf16[2,256,256]{2,1,0:T(8,128)(2,1)} %refs_5_.3, bf16[2,256,256]{2,1,0:T(8,128)(2,1)} %refs_5_.3), custom_call_target="tpu_custom_call" | custom-call | tf_op jit(solution)/shard_map/pallas_call | solution.py:146
  34.3 1.1 %fusion.18 = (f32[16,2304]{1,0:T(8,128)S(1)}, f32[16,2304]{1,0:T(8,128)S(1)}, f32[16,2304]{1,0:T(8,128)S(1)}) fusion(f32[64,2304]{1,0:T(8,128)} %shard_map.97), kind=kLoop, calls=%fused_computation.49 | loop fusion | bytes 884736 | tf_op jit(solution)/shard_map/slice | solution.py:199
  35.5 3.3 %collective-permute-start.7 = (f32[16,2304]{1,0:T(8,128)S(1)}, f32[16,2304]{1,0:T(8,128)S(1)}, u32[]{:S(2)}, u32[]{:S(2)}) collective-permute-start(f32[16,2304]{1,0:T(8,128)S(1)} %get-tuple-element.14), channel_id=1, source_target_pairs={{0,8},{4,12},{8,0},{12,4},{1,9},{5,13},{9,1},{13,5},{2,10},{6,14},... | collective-permute-start | bytes 442376 | tf_op jit(solution)/shard_map/ppermute | solution.py:159
  38.8 1.1 %collective-permute-start.8 = (f32[16,2304]{1,0:T(8,128)S(1)}, f32[16,2304]{1,0:T(8,128)S(1)}, u32[]{:S(2)}, u32[]{:S(2)}) collective-permute-start(f32[16,2304]{1,0:T(8,128)S(1)} %get-tuple-element.13), channel_id=1, source_target_pairs={{0,4},{4,8},{8,12},{12,0},{1,5},{5,9},{9,13},{13,1},{2,6},{6,10},{... | collective-permute-start | bytes 442376 | tf_op jit(solution)/shard_map/ppermute | solution.py:159
  39.9 0.0 copy-done.2
  39.9 0.6 %pad_maximum_fusion.1.refs_4_.refs_5_ = bf16[2,64,256]{2,1,0:T(8,128)(2,1)} fusion(bf16[2,16,256]{2,1,0:T(8,128)(2,1)S(1)} %slice.149, bf16[2,16,256]{2,1,0:T(8,128)(2,1)S(1)} %slice.147, bf16[2,16,256]{2,1,0:T(8,128)(2,1)S(1)} %slice.145, bf16[2,16,256]{2,1,0:T(8,128)(2,1)S(1)} %copy-done.2), kind=kLoop, calls=%fused_computation.12 | loop fusion | flops 262144 | bytes 131072 | tf_op jit(solution)/shard_map/concatenate | solution.py:177
  40.6 0.7 %slice.183 = f32[16,256]{1,0:T(8,128)S(1)} slice(f32[64,2304]{1,0:T(8,128)} %shard_map.97), slice={[0:16], [2048:2304]} | slice | bytes 32768 | tf_op jit(solution)/shard_map/slice | solution.py:203
  41.3 0.1 copy.24
  41.4 0.0 collective-permute-done
  41.4 2.7 %collective-permute-start.6 = (f32[16,2304]{1,0:T(8,128)S(1)}, f32[16,2304]{1,0:T(8,128)S(1)}, u32[]{:S(2)}, u32[]{:S(2)}) collective-permute-start(f32[16,2304]{1,0:T(8,128)S(1)} %get-tuple-element.12), channel_id=1, source_target_pairs={{0,12},{4,0},{8,4},{12,8},{1,13},{5,1},{9,5},{13,9},{2,14},{6,2},{... | collective-permute-start | bytes 442376 | tf_op jit(solution)/shard_map/ppermute | solution.py:159
  44.1 0.0 collective-permute-done.1
  44.2 0.0 collective-permute-done.2
  44.2 0.0 copy-start
  44.2 0.8 %copy-done = bf16[2,512,256]{2,1,0:T(8,128)(2,1)} copy-done((bf16[2,512,256]{2,1,0:T(8,128)(2,1)}, bf16[2,512,256]{2,1,0:T(8,128)(2,1)S(1)}, u32[]{:S(2)}) %copy-start) | copy-done | bytes 524312
  45.0 2.7 %shard_map.96 = (f32[16,2048]{1,0:T(8,128)}, f32[2,16,128]{2,1,0:T(8,128)}) custom-call(s32[1]{0:T(128)} %constant.35.clone.1.refs_0_, bf16[16,2048]{1,0:T(8,128)(2,1)} %refs_1_.3, bf16[2,512,256]{2,1,0:T(8,128)(2,1)} %copy-done, bf16[2,512,256]{2,1,0:T(8,128)(2,1)} %copy-done, bf16[2,64,256]{2,1,0:T(8,128)(2,1)} %pad_maximum_fusion.1.refs_4_.refs_5_, ...), custom_call_target="tpu_custom_call" | custom-call | tf_op jit(solution)/shard_map/pallas_call | solution.py:146
  47.7 0.0 copy-start.1
  47.7 0.9 %slice_bitcast_fusion.1 = (f32[16,2,8]{2,0,1:T(8,128)S(1)}, f32[16,2,8]{2,0,1:T(8,128)S(1)}) fusion(f32[2,16,128]{2,1,0:T(8,128)} %get-tuple-element.5), kind=kLoop, calls=%fused_computation.14 | loop fusion | bytes 4096 | tf_op jit(solution)/shard_map/transpose | solution.py:218
  48.5 0.1 copy.12
  48.6 0.1 copy.22
  48.7 7.0 %shard_map.95 = bf16[256,2048]{1,0:T(8,128)(2,1)} custom-call(s32[1]{0:T(128)} %constant.35.clone.1.refs_0_, bf16[256,2048]{1,0:T(8,128)(2,1)} %refs_1_.2, bf16[2,512,256]{2,1,0:T(8,128)(2,1)} %copy-done, bf16[2,512,256]{2,1,0:T(8,128)(2,1)} %copy-done, bf16[2,256,256]{2,1,0:T(8,128)(2,1)} %refs_5_.3, bf16[2,256,256]{2,1,0:T(8,128)(2,1)} %refs_5_.3), custom_call_target="tpu_custom_call" | custom-call | tf_op jit(solution)/shard_map/pallas_call | solution.py:146
  55.7 0.0 collective-permute-done.7
  55.7 0.1 copy.26
  55.8 0.0 collective-permute-done.8
  55.8 0.1 copy.27
  55.9 0.0 collective-permute-done.6
  55.9 0.1 copy.25
  56.1 0.1 copy.17
  56.1 0.1 copy.18
  56.2 0.1 copy.19
  56.3 0.1 copy.20
  56.4 0.1 copy.21
  56.4 0.1 copy.23
  56.5 0.1 broadcast_in_dim.18
  56.6 0.1 broadcast_in_dim.19
  56.7 0.1 broadcast_in_dim.20
  56.8 0.1 broadcast_in_dim.21
  56.9 0.1 broadcast_in_dim.22
  57.0 0.1 broadcast_in_dim.23
  57.1 0.0 copy-done.1
  57.1 1.8 %fusion = bf16[16,2048]{1,0:T(8,128)(2,1)} fusion(f32[2,8,16,128]{3,2,1,0:T(8,128)S(1)} %bitcast.157, f32[2,8,16,128]{3,2,1,0:T(8,128)S(1)} %bitcast.156, f32[2,8,16,128]{3,2,1,0:T(8,128)S(1)} %bitcast.155, f32[2,8,16,128]{3,2,1,0:T(8,128)S(1)} %bitcast.154, f32[2,8,16,128]{3,2,1,0:T(8,128)S(1)} %bitcast.153, f32[16,2048]{1,0:T(8,128)S(1)} %copy-done.1, ...), kind=kLoop, calls=%fused_computation.2 | loop fusion | flops 360448 | bytes 1507328 | tf_op jit(solution)/shard_map/convert_element_type | solution.py:235
  (21 shorter events, 0.2 us)
Async XLA Ops:
  2.2 11.8 %collective-permute-start.3 = (bf16[40960]{0:T(1024)(128)(2,1)S(1)}, bf16[40960]{0:T(1024)(128)(2,1)S(1)}, u32[]{:S(2)}, u32[]{:S(2)}) collective-permute-start(bf16[40960]{0:T(1024)(128)(2,1)S(1)} %constant_dynamic-update-slice_fusion.5), channel_id=1, source_target_pairs={{0,4},{4,8},{8,12},{12,0},{1,5},{5,9},{9,13},{13,1},{2,6},{6,10},{... | collective-permute-start | bytes 245768 | tf_op jit(solution)/shard_map/ppermute | solution.py:159
  5.3 11.6 %collective-permute-start.4 = (bf16[40960]{0:T(1024)(128)(2,1)S(1)}, bf16[40960]{0:T(1024)(128)(2,1)S(1)}, u32[]{:S(2)}, u32[]{:S(2)}) collective-permute-start(bf16[40960]{0:T(1024)(128)(2,1)S(1)} %constant_dynamic-update-slice_fusion.5), channel_id=1, source_target_pairs={{0,8},{4,12},{8,0},{12,4},{1,9},{5,13},{9,1},{13,5},{2,10},{6,14},... | collective-permute-start | bytes 245768 | tf_op jit(solution)/shard_map/ppermute | solution.py:159
  7.9 9.1 %collective-permute-start.5 = (bf16[40960]{0:T(1024)(128)(2,1)S(1)}, bf16[40960]{0:T(1024)(128)(2,1)S(1)}, u32[]{:S(2)}, u32[]{:S(2)}) collective-permute-start(bf16[40960]{0:T(1024)(128)(2,1)S(1)} %constant_dynamic-update-slice_fusion.5), channel_id=1, source_target_pairs={{0,12},{4,0},{8,4},{12,8},{1,13},{5,1},{9,5},{13,9},{2,14},{6,2},{... | collective-permute-start | bytes 245768 | tf_op jit(solution)/shard_map/ppermute | solution.py:159
  9.3 32.1 %collective-permute-start = (bf16[2,128,256]{2,1,0:T(8,128)(2,1)}, bf16[2,128,256]{2,1,0:T(8,128)(2,1)S(1)}, u32[]{:S(2)}, u32[]{:S(2)}) collective-permute-start(bf16[2,128,256]{2,1,0:T(8,128)(2,1)} %param.10), channel_id=1, source_target_pairs={{0,4},{4,8},{8,12},{12,0},{1,5},{5,9},{9,13},{13,1},{2,6},{6,10},{... | collective-permute-start | bytes 393224 | tf_op jit(solution)/shard_map/ppermute | solution.py:159
  9.9 34.2 %collective-permute-start.1 = (bf16[2,128,256]{2,1,0:T(8,128)(2,1)}, bf16[2,128,256]{2,1,0:T(8,128)(2,1)S(1)}, u32[]{:S(2)}, u32[]{:S(2)}) collective-permute-start(bf16[2,128,256]{2,1,0:T(8,128)(2,1)} %param.10), channel_id=1, source_target_pairs={{0,8},{4,12},{8,0},{12,4},{1,9},{5,13},{9,1},{13,5},{2,10},{6,14},... | collective-permute-start | bytes 393224 | tf_op jit(solution)/shard_map/ppermute | solution.py:159
  14.1 30.1 %collective-permute-start.2 = (bf16[2,128,256]{2,1,0:T(8,128)(2,1)}, bf16[2,128,256]{2,1,0:T(8,128)(2,1)S(1)}, u32[]{:S(2)}, u32[]{:S(2)}) collective-permute-start(bf16[2,128,256]{2,1,0:T(8,128)(2,1)} %param.10), channel_id=1, source_target_pairs={{0,12},{4,0},{8,4},{12,8},{1,13},{5,1},{9,5},{13,9},{2,14},{6,2},{... | collective-permute-start | bytes 393224 | tf_op jit(solution)/shard_map/ppermute | solution.py:159
  18.6 21.3 %copy-start.2 = (bf16[2,16,256]{2,1,0:T(8,128)(2,1)S(1)}, bf16[2,16,256]{2,1,0:T(8,128)(2,1)}, u32[]{:S(2)}) copy-start(bf16[2,16,256]{2,1,0:T(8,128)(2,1)} %param.14) | copy-start | bytes 49156
  35.5 20.2 %collective-permute-start.7 = (f32[16,2304]{1,0:T(8,128)S(1)}, f32[16,2304]{1,0:T(8,128)S(1)}, u32[]{:S(2)}, u32[]{:S(2)}) collective-permute-start(f32[16,2304]{1,0:T(8,128)S(1)} %get-tuple-element.14), channel_id=1, source_target_pairs={{0,8},{4,12},{8,0},{12,4},{1,9},{5,13},{9,1},{13,5},{2,10},{6,14},... | collective-permute-start | bytes 442376 | tf_op jit(solution)/shard_map/ppermute | solution.py:159
  38.8 17.0 %collective-permute-start.8 = (f32[16,2304]{1,0:T(8,128)S(1)}, f32[16,2304]{1,0:T(8,128)S(1)}, u32[]{:S(2)}, u32[]{:S(2)}) collective-permute-start(f32[16,2304]{1,0:T(8,128)S(1)} %get-tuple-element.13), channel_id=1, source_target_pairs={{0,4},{4,8},{8,12},{12,0},{1,5},{5,9},{9,13},{13,1},{2,6},{6,10},{... | collective-permute-start | bytes 442376 | tf_op jit(solution)/shard_map/ppermute | solution.py:159
  41.4 14.5 %collective-permute-start.6 = (f32[16,2304]{1,0:T(8,128)S(1)}, f32[16,2304]{1,0:T(8,128)S(1)}, u32[]{:S(2)}, u32[]{:S(2)}) collective-permute-start(f32[16,2304]{1,0:T(8,128)S(1)} %get-tuple-element.12), channel_id=1, source_target_pairs={{0,12},{4,0},{8,4},{12,8},{1,13},{5,1},{9,5},{13,9},{2,14},{6,2},{... | collective-permute-start | bytes 442376 | tf_op jit(solution)/shard_map/ppermute | solution.py:159
  44.2 0.8 %copy-start = (bf16[2,512,256]{2,1,0:T(8,128)(2,1)}, bf16[2,512,256]{2,1,0:T(8,128)(2,1)S(1)}, u32[]{:S(2)}) copy-start(bf16[2,512,256]{2,1,0:T(8,128)(2,1)S(1)} %constant_dynamic-update-slice_fusion.refs_2_.refs_3_) | copy-start | bytes 1572868
  47.7 9.4 %copy-start.1 = (f32[16,2048]{1,0:T(8,128)S(1)}, f32[16,2048]{1,0:T(8,128)}, u32[]{:S(2)}) copy-start(f32[16,2048]{1,0:T(8,128)} %get-tuple-element.4) | copy-start | bytes 393220

commit v7 on v6

--- a/solution.py
+++ b/solution.py
@@ -8,6 +8,7 @@
 from jax.sharding import PartitionSpec as P
 
 HD = 128
+STACK_ROWS = 512
 
 
 masked_score = -1e30
@@ -17,23 +18,33 @@
     return jnp.repeat(per_head, HD, axis=-1)
 
 
-STACK_ROWS = 512
-
-
-def attention_kernel(masks, normalize, packed, rows, group_size, kv_heads, *refs):
-    length_ref, q_ref = refs[0], refs[1]
+def attention_kernel(masks, slots, normalize, packed, group_size, kv_heads, ctx_count, query_count, *refs):
+    scalar_ref = refs[0]
+    q_refs = refs[1 : 1 + query_count]
     part_count = len(masks)
-    kv_refs = refs[2 : 2 + 2 * part_count]
-    rest = refs[2 + 2 * part_count :]
+    kv_refs = refs[1 + query_count : 1 + query_count + 2 * part_count]
+    rest = refs[1 + query_count + 2 * part_count :]
     if "pos" in masks:
-        key_pos_ref, own_pos_ref = rest[0], rest[1]
-        rest = rest[2:]
+        pos_ref = rest[0]
+        rest = rest[1:]
     out_ref = rest[0]
     side_ref = None if normalize or packed else rest[1]
     query_width = kv_heads * group_size * HD
+    slot_rows = q_refs[0].shape[0]
+    rows = slot_rows * query_count
     scale = 1.0 / jnp.sqrt(jnp.float32(HD))
     stack = max(1, min(group_size, STACK_ROWS // rows))
     visible = []
+    if "pos" in masks:
+        own_row = pos_ref[pl.ds(scalar_ref[1], 1), :]
+        eye = lax.broadcasted_iota(jnp.int32, (rows, rows), 0) == lax.broadcasted_iota(
+            jnp.int32, (rows, rows), 1
+        )
+        own_col = jnp.sum(
+            jnp.where(eye, jnp.broadcast_to(own_row, (rows, rows)), 0), axis=1, keepdims=True
+        )
+        if stack > 1:
+            own_col = jnp.concatenate([own_col] * stack, axis=0)
     for index, mask in enumerate(masks):
         key_count = kv_refs[2 * index].shape[0]
         shape = (rows * stack, key_count)
@@ -41,7 +52,7 @@
             visible.append(None)
         elif mask == "cache":
             cols = lax.broadcasted_iota(jnp.int32, shape, 1)
-            visible.append(cols < length_ref[0])
+            visible.append(cols < scalar_ref[0])
         elif mask == "causal":
             cols = lax.broadcasted_iota(jnp.int32, shape, 1)
             tokens = lax.broadcasted_iota(jnp.int32, shape, 0)
@@ -49,16 +60,13 @@
                 tokens = lax.rem(tokens, rows)
             visible.append(cols <= tokens)
         else:
-            own = own_pos_ref[...]
-            if stack > 1:
-                own = jnp.concatenate([own] * stack, axis=0)
-            visible.append(key_pos_ref[...] <= own)
+            source = lax.rem(scalar_ref[1] + (ctx_count - slots[index]), ctx_count)
+            key_row = pos_ref[pl.ds(source, 1), :]
+            visible.append(key_row <= own_col)
     for first in range(0, group_size, stack):
         heads = list(range(first, min(group_size, first + stack)))
-        if len(heads) == 1:
-            lhs = q_ref[:, first * HD : (first + 1) * HD]
-        else:
-            lhs = jnp.concatenate([q_ref[:, h * HD : (h + 1) * HD] for h in heads], axis=0)
+        pieces = [q_ref[:, h * HD : (h + 1) * HD] for h in heads for q_ref in q_refs]
+        lhs = pieces[0] if len(pieces) == 1 else jnp.concatenate(pieces, axis=0)
         m_rows = lhs.shape[0]
         all_scores = []
         for index in range(part_count):
@@ -111,40 +119,62 @@
                 side_ref[:, HD // 2 + h : HD // 2 + h + 1] = total[rows_of]
 
 
-def attention(queries, parts, normalize, length=None, positions=None, packed=False):
-    rows, query_width = queries.shape
-    kv_heads = parts[0][0].shape[2] // HD
+def attention(query_slots, parts, normalize, scalars, query_width, pos=None, packed=False):
+    slot_rows = query_slots[0].shape[0]
+    rows = slot_rows * len(query_slots)
+    if parts[0][1] == "pos":
+        kv_width = (parts[0][0].shape[1] - query_width) // 2
+    else:
+        kv_width = parts[0][0].shape[-1]
+    kv_heads = kv_width // HD
     group_size = query_width // HD // kv_heads
     group_width = group_size * HD
-    if length is None:
-        length = jnp.zeros((1,), jnp.int32)
-    masks = tuple(mask for _, mask in parts)
-    in_specs = [pl.BlockSpec((rows, group_width), lambda g, n: (0, g))]
-    operands = [queries]
-    for pair, _ in parts:
-        key_count = pair.shape[1]
-        in_specs.append(pl.BlockSpec((pl.Squeezed(), key_count, HD), lambda g, n: (0, 0, g)))
-        in_specs.append(pl.BlockSpec((pl.Squeezed(), key_count, HD), lambda g, n: (1, 0, g)))
-        operands += [pair, pair]
-    if positions is not None:
-        key_pos = positions[0].reshape(1, -1)
-        own_pos = positions[1].reshape(-1, 1)
-        in_specs.append(pl.BlockSpec(key_pos.shape, lambda g, n: (0, 0)))
-        in_specs.append(pl.BlockSpec(own_pos.shape, lambda g, n: (0, 0)))
-        operands += [key_pos, own_pos]
+    masks = tuple(part[1] for part in parts)
+    slots = tuple(part[2] if len(part) > 2 else None for part in parts)
+    in_specs = [pl.BlockSpec((slot_rows, group_width), lambda g, s: (0, g)) for _ in query_slots]
+    operands = list(query_slots)
+    for part in parts:
+        array = part[0]
+        if part[1] == "pos":
+            first = query_width // HD
+            in_specs.append(pl.BlockSpec((array.shape[0], HD), lambda g, s, c=first: (0, c + g)))
+            in_specs.append(
+                pl.BlockSpec((array.shape[0], HD), lambda g, s, c=first + kv_heads: (0, c + g))
+            )
+        else:
+            key_count = array.shape[1]
+            in_specs.append(pl.BlockSpec((pl.Squeezed(), key_count, HD), lambda g, s: (0, 0, g)))
+            in_specs.append(pl.BlockSpec((pl.Squeezed(), key_count, HD), lambda g, s: (1, 0, g)))
+        operands += [array, array]
+    ctx_count = 1
+    if pos is not None:
+        ctx_count = pos.shape[0]
+        in_specs.append(pl.BlockSpec(pos.shape, lambda g, s: (0, 0)))
+        operands.append(pos)
     out_shape = [
         jax.ShapeDtypeStruct((rows, query_width), jnp.bfloat16 if normalize else jnp.float32)
     ]
-    out_specs = [pl.BlockSpec((rows, group_width), lambda g, n: (0, g))]
+    out_specs = [pl.BlockSpec((rows, group_width), lambda g, s: (0, g))]
     if packed:
         full = (rows, query_width + kv_heads * HD)
         out_shape = [jax.ShapeDtypeStruct(full, jnp.float32)]
-        out_specs = [pl.BlockSpec(full, lambda g, n: (0, 0))]
+        out_specs = [pl.BlockSpec(full, lambda g, s: (0, 0))]
     elif not normalize:
         out_shape.append(jax.ShapeDtypeStruct((kv_heads, rows, HD), jnp.float32))
-        out_specs.append(pl.BlockSpec((pl.Squeezed(), rows, HD), lambda g, n: (g, 0, 0)))
+        out_specs.append(pl.BlockSpec((pl.Squeezed(), rows, HD), lambda g, s: (g, 0, 0)))
+    kernel = functools.partial(
+        attention_kernel,
+        masks,
+        slots,
+        normalize,
+        packed,
+        group_size,
+        kv_heads,
+        ctx_count,
+        len(query_slots),
+    )
     return pl.pallas_call(
-        functools.partial(attention_kernel, masks, normalize, packed, rows, group_size, kv_heads),
+        kernel,
         grid_spec=pltpu.PrefetchScalarGridSpec(
             num_scalar_prefetch=1,
             grid=(kv_heads,),
@@ -152,7 +182,7 @@
             out_specs=out_specs,
         ),
         out_shape=out_shape,
-    )(length, *operands)
+    )(scalars, *operands)
 
 
 def shifted(value, shift, count):
@@ -167,30 +197,18 @@
         query_width = query_q.shape[1]
         kv_heads = width // HD
         group_size = query_width // HD // kv_heads
-        packed = jnp.concatenate([query_q.reshape(-1), query_kv.reshape(-1)])
+        packed = jnp.concatenate([query_q, query_kv[0], query_kv[1]], axis=1)
         query_slots = [packed] + [shifted(packed, k, ctx_count) for k in range(1, ctx_count)]
         anchor_slots = [anchor_kv] + [shifted(anchor_kv, k, ctx_count) for k in range(1, ctx_count)]
-        split = own_count * query_width
-        all_queries = jnp.concatenate(
-            [slot[:split].reshape(own_count, query_width) for slot in query_slots], axis=0
-        )
-        all_query_kv = jnp.concatenate(
-            [slot[split:].reshape(2, own_count, width) for slot in query_slots], axis=1
-        )
-        anchor = jnp.concatenate(anchor_slots, axis=1)
-        slot_pos = jnp.concatenate(
-            [
-                lax.dynamic_slice_in_dim(query_pos, ((me - k) % ctx_count) * own_count, own_count)
-                for k in range(ctx_count)
-            ]
-        )
-        own_pos = slot_pos[:own_count]
+        scalars = jnp.stack([cache_len[0], me.astype(jnp.int32)])
+        positions = query_pos.reshape(ctx_count, own_count)
 
         (context_packed,) = attention(
-            all_queries,
+            query_slots,
             [(cache_kv, "cache"), (kv_block, None)],
             False,
-            length=cache_len,
+            scalars,
+            query_width,
             packed=True,
         )
         sections = [context_packed[:own_count]]
@@ -205,12 +223,17 @@
             for section in sections
         ]
 
-        (block_out,) = attention(q_block, [(anchor, None), (kv_block, "causal")], True)
+        anchor_parts = [(slot, None) for slot in anchor_slots]
+        (block_out,) = attention(
+            [q_block], anchor_parts + [(kv_block, "causal")], True, scalars, query_width
+        )
         local_output, local_side = attention(
-            query_q,
-            [(anchor, None), (all_query_kv, "pos")],
+            [query_q],
+            anchor_parts + [(slot, "pos", k) for k, slot in enumerate(query_slots)],
             False,
-            positions=(slot_pos, own_pos),
+            scalars,
+            query_width,
+            pos=positions,
         )
 
         def per_head(side, first):

time: 59.4 us -> 64.2 us (1.081)
  Pallas kernels: 25.4 us -> 30.2 us
  starting transfers between devices: 18 us -> 19.5 us
  other arithmetic: 4.62 us -> 3.32 us
    pallas_call x3, Pallas kernels: 25.4 us -> 30.2 us  [attention(): pl.pallas_call(kernel, grid_spec=pltpu.PrefetchScalarGridSpec(num_scalar_...]
    ppermute x9, starting transfers between devices: 18 us -> 19.5 us  [shifted(): lax.ppermute(value, 'ctx', [(j, (j + shift) % count) for j in range(count)])]
    concatenate x2 -> x1, other arithmetic: 2.2 us -> 0.84 us  [local(): packed = jnp.concatenate([query_q, query_kv[0], query_kv[1]], axis=1)]
    dynamic_slice x1 -> x0, local copies, waits for them, and re-layouts: 0.89 us -> none  [local(): lax.dynamic_slice_in_dim(query_pos, (me - k) % ctx_count * own_count, own...]
    unnamed x12 -> x16, local copies, waits for them, and re-layouts: 3.35 us -> 2.54 us
    squeeze x0 -> x1, local copies, waits for them, and re-layouts: none -> 0.72 us  [local(): packed = jnp.concatenate([query_q, query_kv[0], query_kv[1]], axis=1)]
    another operation x0 -> x1, other arithmetic: none -> 0.65 us  [local(): scalars = jnp.stack([cache_len[0], me.astype(jnp.int32)])]
    reshape x1, local copies, waits for them, and re-layouts: 0.67 us -> 1.31 us  [local(): positions = query_pos.reshape(ctx_count, own_count)]
  transfers between devices with their start and end apart: 9 -> 9, of which waited for: 0 -> 1; matrix products, arithmetic and copies ran while one was open for 15% -> 8% of each run, Pallas kernels for 43% -> 47%
where the time goes in v7:
time: 64.2 us; the launch traced here: 63.7 us
  Pallas kernels  30.2 us (47%)
  starting transfers between devices  19.5 us (30%)
  local copies, waits for them, and re-layouts  8.77 us (14%)
  other arithmetic  3.32 us (5%)
  between operations  1.43 us (2%)
    pallas_call x3, Pallas kernels, attention(): pl.pallas_call(kernel, grid_spec=pltpu.PrefetchScalarGridSpec(num_scalar_...  30.2 us
    ppermute x9, starting transfers between devices, shifted(): lax.ppermute(value, 'ctx', [(j, (j + shift) % count) for j in range(count)])  19.5 us
    unnamed x16, local copies, waits for them, and re-layouts  2.54 us
    convert_element_type x1, other arithmetic, local(): query_out = (merged_output / widen(merged_totals)).astype(jnp.bfloat16)  1.81 us
    reshape x1, local copies, waits for them, and re-layouts, local(): positions = query_pos.reshape(ctx_count, own_count)  1.31 us
  transfers between devices with their start and end apart: 9, of which 1 were waited for; matrix products, arithmetic and copies ran while one was open for 8% of the time, Pallas kernels for 47%

profile of v7, /device:TPU:0, one launch (start us, length us, event | category | flops | bytes accessed | tf_op | source)
XLA Modules:
  0.0 63.7 jit_solution(9288096289161747259)
XLA Ops:
  0.6 0.7 %slice_bitcast_fusion.11 = (bf16[16,256]{1,0:T(8,128)(2,1)S(1)}, bf16[16,256]{1,0:T(8,128)(2,1)S(1)}) fusion(bf16[2,16,256]{2,1,0:T(8,128)(2,1)} %param.14), kind=kLoop, calls=%fused_computation.42 | loop fusion | bytes 32768 | tf_op jit(solution)/shard_map/squeeze | solution.py:200
  1.3 0.8 %pad_maximum_fusion.refs_10_.refs_11_.refs_1_ = bf16[16,2560]{1,0:T(8,128)(2,1)S(1)} fusion(bf16[16,256]{1,0:T(8,128)(2,1)S(1)} %get-tuple-element.18, bf16[16,256]{1,0:T(8,128)(2,1)S(1)} %get-tuple-element.17, bf16[16,2048]{1,0:T(8,128)(2,1)} %refs_1_.3), kind=kLoop, calls=%fused_computation.11 | loop fusion | flops 245760 | bytes 163840 | tf_op jit(solution)/shard_map/concatenate | solution.py:200
  2.2 0.0 copy-start.3
  2.2 5.0 %collective-permute-start.5 = (bf16[16,2560]{1,0:T(8,128)(2,1)S(1)}, bf16[16,2560]{1,0:T(8,128)(2,1)S(1)}, u32[]{:S(2)}, u32[]{:S(2)}) collective-permute-start(bf16[16,2560]{1,0:T(8,128)(2,1)S(1)} %pad_maximum_fusion.refs_10_.refs_11_.refs_1_), channel_id=1, source_target_pairs={{0,12},{4,0},{8,4},{12,8},{1,13},{5,1},{9,5},{13,9},{2,14},{6,2},{... | collective-permute-start | bytes 245768 | tf_op jit(solution)/shard_map/ppermute | solution.py:189
  7.2 0.0 collective-permute-start.4
  7.2 1.0 %collective-permute-start.3 = (bf16[16,2560]{1,0:T(8,128)(2,1)S(1)}, bf16[16,2560]{1,0:T(8,128)(2,1)S(1)}, u32[]{:S(2)}, u32[]{:S(2)}) collective-permute-start(bf16[16,2560]{1,0:T(8,128)(2,1)S(1)} %pad_maximum_fusion.refs_10_.refs_11_.refs_1_), channel_id=1, source_target_pairs={{0,4},{4,8},{8,12},{12,0},{1,5},{5,9},{9,13},{13,1},{2,6},{6,10},{... | collective-permute-start | bytes 245768 | tf_op jit(solution)/shard_map/ppermute | solution.py:189
  8.3 2.8 %collective-permute-start.2 = (bf16[2,128,256]{2,1,0:T(8,128)(2,1)}, bf16[2,128,256]{2,1,0:T(8,128)(2,1)S(1)}, u32[]{:S(2)}, u32[]{:S(2)}) collective-permute-start(bf16[2,128,256]{2,1,0:T(8,128)(2,1)} %refs_3_.3), channel_id=1, source_target_pairs={{0,12},{4,0},{8,4},{12,8},{1,13},{5,1},{9,5},{13,9},{2,14},{6,2},{... | collective-permute-start | bytes 393224 | tf_op jit(solution)/shard_map/ppermute | solution.py:189
  11.1 1.1 %collective-permute-start.1 = (bf16[2,128,256]{2,1,0:T(8,128)(2,1)}, bf16[2,128,256]{2,1,0:T(8,128)(2,1)S(1)}, u32[]{:S(2)}, u32[]{:S(2)}) collective-permute-start(bf16[2,128,256]{2,1,0:T(8,128)(2,1)} %refs_3_.3), channel_id=1, source_target_pairs={{0,8},{4,12},{8,0},{12,4},{1,9},{5,13},{9,1},{13,5},{2,10},{6,14},... | collective-permute-start | bytes 393224 | tf_op jit(solution)/shard_map/ppermute | solution.py:189
  12.8 1.3 %reshape.67.refs_18_ = s32[4,16]{1,0:T(4,128)} reshape(s32[64]{0:T(128)} %param.15) | data formatting | bytes 512 | tf_op jit(solution)/shard_map/reshape | solution.py:204
  14.2 0.6 %pad_add_fusion.refs_0_ = s32[2]{0:T(128)} fusion(s32[1]{0:T(128)} %bitcast, s32[1]{0:T(128)S(6)} %copy.38), kind=kLoop, calls=%fused_computation.43 | loop fusion | flops 2 | bytes 16 | tf_op jit(solution)/shard_map/stack | solution.py:203
  14.8 0.0 collective-permute-done.5.refs_16_.refs_17_.refs_4_
  14.8 0.0 copy-start.4
  14.8 0.0 collective-permute-start
  14.8 0.5 collective-permute-done.4.refs_14_.refs_15_.refs_3_
  15.3 0.0 copy-start.5
  15.3 0.0 collective-permute-done.3.refs_12_.refs_13_.refs_2_
  15.3 0.0 copy-done.3
  15.3 0.1 copy-done.4
  15.4 0.5 copy-done.5
  15.9 0.0 copy-start.6
  15.9 0.6 copy-done.6
  16.6 16.4 %shard_map.97 = f32[64,2304]{1,0:T(8,128)} custom-call(s32[2]{0:T(128)} %pad_add_fusion.refs_0_, bf16[16,2560]{1,0:T(8,128)(2,1)} %copy-done.3, bf16[16,2560]{1,0:T(8,128)(2,1)} %copy-done.6, bf16[16,2560]{1,0:T(8,128)(2,1)} %copy-done.5, bf16[16,2560]{1,0:T(8,128)(2,1)} %copy-done.4, bf16[2,4096,256]{2,1,0:T(8,128)(2,1)} %refs_6_.1, ...), custom_call_target="tpu_custom_call" | custom-call | tf_op jit(solution)/shard_map/pallas_call | solution.py:176
  32.9 1.1 %fusion.18 = (f32[16,2304]{1,0:T(8,128)S(1)}, f32[16,2304]{1,0:T(8,128)S(1)}, f32[16,2304]{1,0:T(8,128)S(1)}) fusion(f32[64,2304]{1,0:T(8,128)} %shard_map.97), kind=kLoop, calls=%fused_computation.44 | loop fusion | bytes 884736 | tf_op jit(solution)/shard_map/slice | solution.py:217
  34.0 0.7 %slice.95 = f32[16,256]{1,0:T(8,128)S(1)} slice(f32[64,2304]{1,0:T(8,128)} %shard_map.97), slice={[0:16], [2048:2304]} | slice | bytes 32768 | tf_op jit(solution)/shard_map/slice | solution.py:221
  34.7 0.1 copy.22
  34.8 6.2 %collective-permute-start.6 = (f32[16,2304]{1,0:T(8,128)S(1)}, f32[16,2304]{1,0:T(8,128)S(1)}, u32[]{:S(2)}, u32[]{:S(2)}) collective-permute-start(f32[16,2304]{1,0:T(8,128)S(1)} %get-tuple-element.12), channel_id=1, source_target_pairs={{0,12},{4,0},{8,4},{12,8},{1,13},{5,1},{9,5},{13,9},{2,14},{6,2},{... | collective-permute-start | bytes 442376 | tf_op jit(solution)/shard_map/ppermute | solution.py:189
  41.1 0.0 collective-permute-start.8
  41.1 0.0 collective-permute-done.2.refs_8_.refs_9_
  41.1 0.0 copy-start
  41.1 3.3 %collective-permute-start.7 = (f32[16,2304]{1,0:T(8,128)S(1)}, f32[16,2304]{1,0:T(8,128)S(1)}, u32[]{:S(2)}, u32[]{:S(2)}) collective-permute-start(f32[16,2304]{1,0:T(8,128)S(1)} %get-tuple-element.14), channel_id=1, source_target_pairs={{0,8},{4,12},{8,0},{12,4},{1,9},{5,13},{9,1},{13,5},{2,10},{6,14},... | collective-permute-start | bytes 442376 | tf_op jit(solution)/shard_map/ppermute | solution.py:189
  44.4 0.0 collective-permute-done.1.refs_6_.refs_7_
  44.4 0.0 copy-start.1
  44.4 0.0 collective-permute-done.refs_4_.refs_5_
  44.4 0.0 copy-done
  44.4 0.6 copy-done.1
  45.0 0.0 copy-start.2
  45.0 0.6 %copy-done.2 = bf16[2,128,256]{2,1,0:T(8,128)(2,1)} copy-done((bf16[2,128,256]{2,1,0:T(8,128)(2,1)}, bf16[2,128,256]{2,1,0:T(8,128)(2,1)S(1)}, u32[]{:S(2)}) %copy-start.2) | copy-done | bytes 131096
  45.7 3.6 %shard_map.96 = (f32[16,2048]{1,0:T(8,128)}, f32[2,16,128]{2,1,0:T(8,128)}) custom-call(s32[2]{0:T(128)} %pad_add_fusion.refs_0_, bf16[16,2048]{1,0:T(8,128)(2,1)} %refs_1_.3, bf16[2,128,256]{2,1,0:T(8,128)(2,1)} %refs_3_.3, bf16[2,128,256]{2,1,0:T(8,128)(2,1)} %refs_3_.3, bf16[2,128,256]{2,1,0:T(8,128)(2,1)} %copy-done.2, bf16[2,128,256]{2,1,0:T(8,128)(2,1)} %copy-done.2, ...), custom_call_target="tpu_custom_call" | custom-call | tf_op jit(solution)/shard_map/pallas_call | solution.py:176
  49.3 0.0 copy-start.7
  49.3 0.9 %slice_bitcast_fusion.1 = (f32[16,2,8]{2,0,1:T(8,128)S(1)}, f32[16,2,8]{2,0,1:T(8,128)S(1)}) fusion(f32[2,16,128]{2,1,0:T(8,128)} %get-tuple-element.5), kind=kLoop, calls=%fused_computation.13 | loop fusion | bytes 4096 | tf_op jit(solution)/shard_map/transpose | solution.py:241
  50.2 0.1 copy.10
  50.2 0.1 copy.20
  50.3 10.2 %shard_map.95 = bf16[256,2048]{1,0:T(8,128)(2,1)} custom-call(s32[2]{0:T(128)} %pad_add_fusion.refs_0_, bf16[256,2048]{1,0:T(8,128)(2,1)} %refs_1_.2, bf16[2,128,256]{2,1,0:T(8,128)(2,1)} %refs_3_.3, bf16[2,128,256]{2,1,0:T(8,128)(2,1)} %refs_3_.3, bf16[2,128,256]{2,1,0:T(8,128)(2,1)} %copy-done.2, bf16[2,128,256]{2,1,0:T(8,128)(2,1)} %copy-done.2, ...), custom_call_target="tpu_custom_call" | custom-call | tf_op jit(solution)/shard_map/pallas_call | solution.py:176
  60.5 0.0 collective-permute-done.6
  60.5 0.1 copy.23
  60.6 0.0 collective-permute-done.8
  60.6 0.1 copy.25
  60.7 0.0 collective-permute-done.7
  60.7 0.1 copy.24
  60.9 0.1 copy.21
  60.9 0.1 copy.15
  61.0 0.1 copy.16
  61.1 0.1 copy.17
  61.2 0.1 copy.18
  61.2 0.1 copy.19
  61.3 0.1 broadcast_in_dim.22
  61.4 0.1 broadcast_in_dim.21
  61.5 0.1 broadcast_in_dim.20
  61.6 0.1 broadcast_in_dim.19
  61.7 0.1 broadcast_in_dim.18
  61.8 0.1 broadcast_in_dim.23
  61.9 0.0 copy-done.7
  61.9 1.8 %fusion = bf16[16,2048]{1,0:T(8,128)(2,1)} fusion(f32[2,8,16,128]{3,2,1,0:T(8,128)S(1)} %bitcast.154, f32[2,8,16,128]{3,2,1,0:T(8,128)S(1)} %bitcast.149, f32[2,8,16,128]{3,2,1,0:T(8,128)S(1)} %bitcast.150, f32[2,8,16,128]{3,2,1,0:T(8,128)S(1)} %bitcast.151, f32[2,8,16,128]{3,2,1,0:T(8,128)S(1)} %bitcast.152, f32[16,2048]{1,0:T(8,128)S(1)} %copy-done.7, ...), kind=kLoop, calls=%fused_computation.1 | loop fusion | flops 360448 | bytes 1507328 | tf_op jit(solution)/shard_map/convert_element_type | solution.py:258
  (4 shorter events, 0.0 us)
Async XLA Ops:
  2.2 13.1 %copy-start.3 = (bf16[16,2560]{1,0:T(8,128)(2,1)}, bf16[16,2560]{1,0:T(8,128)(2,1)S(1)}, u32[]{:S(2)}) copy-start(bf16[16,2560]{1,0:T(8,128)(2,1)S(1)} %pad_maximum_fusion.refs_10_.refs_11_.refs_1_) | copy-start | bytes 245764
  2.2 12.6 %collective-permute-start.5 = (bf16[16,2560]{1,0:T(8,128)(2,1)S(1)}, bf16[16,2560]{1,0:T(8,128)(2,1)S(1)}, u32[]{:S(2)}, u32[]{:S(2)}) collective-permute-start(bf16[16,2560]{1,0:T(8,128)(2,1)S(1)} %pad_maximum_fusion.refs_10_.refs_11_.refs_1_), channel_id=1, source_target_pairs={{0,12},{4,0},{8,4},{12,8},{1,13},{5,1},{9,5},{13,9},{2,14},{6,2},{... | collective-permute-start | bytes 245768 | tf_op jit(solution)/shard_map/ppermute | solution.py:189
  7.2 8.1 %collective-permute-start.4 = (bf16[16,2560]{1,0:T(8,128)(2,1)S(1)}, bf16[16,2560]{1,0:T(8,128)(2,1)S(1)}, u32[]{:S(2)}, u32[]{:S(2)}) collective-permute-start(bf16[16,2560]{1,0:T(8,128)(2,1)S(1)} %pad_maximum_fusion.refs_10_.refs_11_.refs_1_), channel_id=1, source_target_pairs={{0,8},{4,12},{8,0},{12,4},{1,9},{5,13},{9,1},{13,5},{2,10},{6,14},... | collective-permute-start | bytes 245768 | tf_op jit(solution)/shard_map/ppermute | solution.py:189
  7.2 8.1 %collective-permute-start.3 = (bf16[16,2560]{1,0:T(8,128)(2,1)S(1)}, bf16[16,2560]{1,0:T(8,128)(2,1)S(1)}, u32[]{:S(2)}, u32[]{:S(2)}) collective-permute-start(bf16[16,2560]{1,0:T(8,128)(2,1)S(1)} %pad_maximum_fusion.refs_10_.refs_11_.refs_1_), channel_id=1, source_target_pairs={{0,4},{4,8},{8,12},{12,0},{1,5},{5,9},{9,13},{13,1},{2,6},{6,10},{... | collective-permute-start | bytes 245768 | tf_op jit(solution)/shard_map/ppermute | solution.py:189
  8.3 32.8 %collective-permute-start.2 = (bf16[2,128,256]{2,1,0:T(8,128)(2,1)}, bf16[2,128,256]{2,1,0:T(8,128)(2,1)S(1)}, u32[]{:S(2)}, u32[]{:S(2)}) collective-permute-start(bf16[2,128,256]{2,1,0:T(8,128)(2,1)} %refs_3_.3), channel_id=1, source_target_pairs={{0,12},{4,0},{8,4},{12,8},{1,13},{5,1},{9,5},{13,9},{2,14},{6,2},{... | collective-permute-start | bytes 393224 | tf_op jit(solution)/shard_map/ppermute | solution.py:189
  11.1 33.3 %collective-permute-start.1 = (bf16[2,128,256]{2,1,0:T(8,128)(2,1)}, bf16[2,128,256]{2,1,0:T(8,128)(2,1)S(1)}, u32[]{:S(2)}, u32[]{:S(2)}) collective-permute-start(bf16[2,128,256]{2,1,0:T(8,128)(2,1)} %refs_3_.3), channel_id=1, source_target_pairs={{0,8},{4,12},{8,0},{12,4},{1,9},{5,13},{9,1},{13,5},{2,10},{6,14},... | collective-permute-start | bytes 393224 | tf_op jit(solution)/shard_map/ppermute | solution.py:189
  14.8 0.6 copy-start.4
  14.8 29.5 %collective-permute-start = (bf16[2,128,256]{2,1,0:T(8,128)(2,1)}, bf16[2,128,256]{2,1,0:T(8,128)(2,1)S(1)}, u32[]{:S(2)}, u32[]{:S(2)}) collective-permute-start(bf16[2,128,256]{2,1,0:T(8,128)(2,1)} %refs_3_.3), channel_id=1, source_target_pairs={{0,4},{4,8},{8,12},{12,0},{1,5},{5,9},{9,13},{13,1},{2,6},{6,10},{... | collective-permute-start | bytes 393224 | tf_op jit(solution)/shard_map/ppermute | solution.py:189
  15.3 0.6 copy-start.5
  15.9 0.6 copy-start.6
  34.8 25.7 %collective-permute-start.6 = (f32[16,2304]{1,0:T(8,128)S(1)}, f32[16,2304]{1,0:T(8,128)S(1)}, u32[]{:S(2)}, u32[]{:S(2)}) collective-permute-start(f32[16,2304]{1,0:T(8,128)S(1)} %get-tuple-element.12), channel_id=1, source_target_pairs={{0,12},{4,0},{8,4},{12,8},{1,13},{5,1},{9,5},{13,9},{2,14},{6,2},{... | collective-permute-start | bytes 442376 | tf_op jit(solution)/shard_map/ppermute | solution.py:189
  41.1 19.5 %collective-permute-start.8 = (f32[16,2304]{1,0:T(8,128)S(1)}, f32[16,2304]{1,0:T(8,128)S(1)}, u32[]{:S(2)}, u32[]{:S(2)}) collective-permute-start(f32[16,2304]{1,0:T(8,128)S(1)} %get-tuple-element.13), channel_id=1, source_target_pairs={{0,4},{4,8},{8,12},{12,0},{1,5},{5,9},{9,13},{13,1},{2,6},{6,10},{... | collective-permute-start | bytes 442376 | tf_op jit(solution)/shard_map/ppermute | solution.py:189
  41.1 3.3 %copy-start = (bf16[2,128,256]{2,1,0:T(8,128)(2,1)}, bf16[2,128,256]{2,1,0:T(8,128)(2,1)S(1)}, u32[]{:S(2)}) copy-start(bf16[2,128,256]{2,1,0:T(8,128)(2,1)S(1)} %collective-permute-done.2.refs_8_.refs_9_) | copy-start | bytes 393220
  41.1 19.6 %collective-permute-start.7 = (f32[16,2304]{1,0:T(8,128)S(1)}, f32[16,2304]{1,0:T(8,128)S(1)}, u32[]{:S(2)}, u32[]{:S(2)}) collective-permute-start(f32[16,2304]{1,0:T(8,128)S(1)} %get-tuple-element.14), channel_id=1, source_target_pairs={{0,8},{4,12},{8,0},{12,4},{1,9},{5,13},{9,1},{13,5},{2,10},{6,14},... | collective-permute-start | bytes 442376 | tf_op jit(solution)/shard_map/ppermute | solution.py:189
  44.4 0.6 %copy-start.1 = (bf16[2,128,256]{2,1,0:T(8,128)(2,1)}, bf16[2,128,256]{2,1,0:T(8,128)(2,1)S(1)}, u32[]{:S(2)}) copy-start(bf16[2,128,256]{2,1,0:T(8,128)(2,1)S(1)} %collective-permute-done.1.refs_6_.refs_7_) | copy-start | bytes 393220
  45.0 0.7 %copy-start.2 = (bf16[2,128,256]{2,1,0:T(8,128)(2,1)}, bf16[2,128,256]{2,1,0:T(8,128)(2,1)S(1)}, u32[]{:S(2)}) copy-start(bf16[2,128,256]{2,1,0:T(8,128)(2,1)S(1)} %collective-permute-done.refs_4_.refs_5_) | copy-start | bytes 393220
  49.3 12.6 %copy-start.7 = (f32[16,2048]{1,0:T(8,128)S(1)}, f32[16,2048]{1,0:T(8,128)}, u32[]{:S(2)}) copy-start(f32[16,2048]{1,0:T(8,128)} %get-tuple-element.4) | copy-start | bytes 393220

commit v8 on v7

--- a/solution.py
+++ b/solution.py
@@ -25,8 +25,8 @@
     kv_refs = refs[1 + query_count : 1 + query_count + 2 * part_count]
     rest = refs[1 + query_count + 2 * part_count :]
     if "pos" in masks:
-        pos_ref = rest[0]
-        rest = rest[1:]
+        key_pos_ref, own_pos_ref = rest[0], rest[1]
+        rest = rest[2:]
     out_ref = rest[0]
     side_ref = None if normalize or packed else rest[1]
     query_width = kv_heads * group_size * HD
@@ -36,13 +36,7 @@
     stack = max(1, min(group_size, STACK_ROWS // rows))
     visible = []
     if "pos" in masks:
-        own_row = pos_ref[pl.ds(scalar_ref[1], 1), :]
-        eye = lax.broadcasted_iota(jnp.int32, (rows, rows), 0) == lax.broadcasted_iota(
-            jnp.int32, (rows, rows), 1
-        )
-        own_col = jnp.sum(
-            jnp.where(eye, jnp.broadcast_to(own_row, (rows, rows)), 0), axis=1, keepdims=True
-        )
+        own_col = own_pos_ref[...]
         if stack > 1:
             own_col = jnp.concatenate([own_col] * stack, axis=0)
     for index, mask in enumerate(masks):
@@ -60,9 +54,7 @@
                 tokens = lax.rem(tokens, rows)
             visible.append(cols <= tokens)
         else:
-            source = lax.rem(scalar_ref[1] + (ctx_count - slots[index]), ctx_count)
-            key_row = pos_ref[pl.ds(source, 1), :]
-            visible.append(key_row <= own_col)
+            visible.append(key_pos_ref[...] <= own_col)
     for first in range(0, group_size, stack):
         heads = list(range(first, min(group_size, first + stack)))
         pieces = [q_ref[:, h * HD : (h + 1) * HD] for h in heads for q_ref in q_refs]
@@ -122,7 +114,7 @@
 def attention(query_slots, parts, normalize, scalars, query_width, pos=None, packed=False):
     slot_rows = query_slots[0].shape[0]
     rows = slot_rows * len(query_slots)
-    if parts[0][1] == "pos":
+    if len(parts[0]) > 2:
         kv_width = (parts[0][0].shape[1] - query_width) // 2
     else:
         kv_width = parts[0][0].shape[-1]
@@ -135,7 +127,7 @@
     operands = list(query_slots)
     for part in parts:
         array = part[0]
-        if part[1] == "pos":
+        if len(part) > 2:
             first = query_width // HD
             in_specs.append(pl.BlockSpec((array.shape[0], HD), lambda g, s, c=first: (0, c + g)))
             in_specs.append(
@@ -148,9 +140,11 @@
         operands += [array, array]
     ctx_count = 1
     if pos is not None:
-        ctx_count = pos.shape[0]
-        in_specs.append(pl.BlockSpec(pos.shape, lambda g, s: (0, 0)))
-        operands.append(pos)
+        key_pos = pos[0].reshape(1, -1)
+        own_pos = pos[1].reshape(-1, 1)
+        in_specs.append(pl.BlockSpec(key_pos.shape, lambda g, s: (0, 0)))
+        in_specs.append(pl.BlockSpec(own_pos.shape, lambda g, s: (0, 0)))
+        operands += [key_pos, own_pos]
     out_shape = [
         jax.ShapeDtypeStruct((rows, query_width), jnp.bfloat16 if normalize else jnp.float32)
     ]
@@ -201,7 +195,21 @@
         query_slots = [packed] + [shifted(packed, k, ctx_count) for k in range(1, ctx_count)]
         anchor_slots = [anchor_kv] + [shifted(anchor_kv, k, ctx_count) for k in range(1, ctx_count)]
         scalars = jnp.stack([cache_len[0], me.astype(jnp.int32)])
-        positions = query_pos.reshape(ctx_count, own_count)
+        anchor = jnp.concatenate(anchor_slots, axis=1)
+        key_columns = [slot[:, query_width:] for slot in query_slots]
+        all_query_kv = jnp.stack(
+            [
+                jnp.concatenate([c[:, :width] for c in key_columns], axis=0),
+                jnp.concatenate([c[:, width:] for c in key_columns], axis=0),
+            ]
+        )
+        slot_pos = jnp.concatenate(
+            [
+                lax.dynamic_slice_in_dim(query_pos, ((me - k) % ctx_count) * own_count, own_count)
+                for k in range(ctx_count)
+            ]
+        )
+        own_pos = slot_pos[:own_count]
 
         (context_packed,) = attention(
             query_slots,
@@ -223,17 +231,16 @@
             for section in sections
         ]
 
-        anchor_parts = [(slot, None) for slot in anchor_slots]
         (block_out,) = attention(
-            [q_block], anchor_parts + [(kv_block, "causal")], True, scalars, query_width
+            [q_block], [(anchor, None), (kv_block, "causal")], True, scalars, query_width
         )
         local_output, local_side = attention(
             [query_q],
-            anchor_parts + [(slot, "pos", k) for k, slot in enumerate(query_slots)],
+            [(anchor, None), (all_query_kv, "pos")],
             False,
             scalars,
             query_width,
-            pos=positions,
+            pos=(slot_pos, own_pos),
         )
 
         def per_head(side, first):

time: 64.2 us -> 61.2 us (0.953)
  starting transfers between devices: 19.5 us -> 15.5 us
  local copies, waits for them, and re-layouts: 8.77 us -> 11.7 us
  Pallas kernels: 30.2 us -> 27.4 us
  other arithmetic: 3.32 us -> 4.57 us
    ppermute x9, starting transfers between devices: 19.5 us -> 15.5 us  [shifted(): lax.ppermute(value, 'ctx', [(j, (j + shift) % count) for j in range(count)])]
    pallas_call x3, Pallas kernels: 30.2 us -> 27.4 us  [attention(): pl.pallas_call(kernel, grid_spec=pltpu.PrefetchScalarGridSpec(num_scalar_...]
    slice x0 -> x3, local copies, waits for them, and re-layouts: none -> 2.15 us  [local(): c[:, :width]]
    dynamic_slice x0 -> x1, local copies, waits for them, and re-layouts: none -> 0.89 us  [local(): lax.dynamic_slice_in_dim(query_pos, (me - k) % ctx_count * own_count, own...]
    reshape x0 -> x1, other arithmetic: none -> 0.65 us  [attention(): key_pos = pos[0].reshape(1, -1)]
    another operation x0 -> x2, other arithmetic: none -> 0.64 us  [local(): jnp.stack([jnp.concatenate([c[:, :width] for c in key_columns], axis=0),...]
    unnamed x16 -> x15, local copies, waits for them, and re-layouts: 2.54 us -> 3.03 us
  transfers between devices with their start and end apart: 9 -> 9, of which waited for: 1 -> 0; matrix products, arithmetic and copies ran while one was open for 8% -> 16% of each run, Pallas kernels for 47% -> 45%
where the time goes in v8:
time: 61.2 us; the launch traced here: 60.7 us
  Pallas kernels  27.4 us (45%)
  starting transfers between devices  15.5 us (25%)
  local copies, waits for them, and re-layouts  11.7 us (19%)
  other arithmetic  4.57 us (7%)
  between operations  1.5 us (2%)
    pallas_call x3, Pallas kernels, attention(): pl.pallas_call(kernel, grid_spec=pltpu.PrefetchScalarGridSpec(num_scalar_...  27.4 us
    ppermute x9, starting transfers between devices, shifted(): lax.ppermute(value, 'ctx', [(j, (j + shift) % count) for j in range(count)])  15.5 us
    unnamed x15, local copies, waits for them, and re-layouts  3.03 us
    slice x3, local copies, waits for them, and re-layouts, local(): c[:, :width]  2.15 us
    convert_element_type x1, other arithmetic, local(): query_out = (merged_output / widen(merged_totals)).astype(jnp.bfloat16)  1.81 us
  transfers between devices with their start and end apart: 9, of which 0 were waited for; matrix products, arithmetic and copies ran while one was open for 16% of the time, Pallas kernels for 45%

profile of v8, /device:TPU:0, one launch (start us, length us, event | category | flops | bytes accessed | tf_op | source)
XLA Modules:
  0.0 60.7 jit_solution(14485862989755802871)
XLA Ops:
  0.6 0.7 %slice_bitcast_fusion.11 = (bf16[16,256]{1,0:T(8,128)(2,1)S(1)}, bf16[16,256]{1,0:T(8,128)(2,1)S(1)}) fusion(bf16[2,16,256]{2,1,0:T(8,128)(2,1)} %param.14), kind=kLoop, calls=%fused_computation.49 | loop fusion | bytes 32768 | tf_op jit(solution)/shard_map/squeeze | solution.py:194
  1.3 0.8 %pad_maximum_fusion.refs_1_ = bf16[16,2560]{1,0:T(8,128)(2,1)S(1)} fusion(bf16[16,256]{1,0:T(8,128)(2,1)S(1)} %get-tuple-element.24, bf16[16,256]{1,0:T(8,128)(2,1)S(1)} %get-tuple-element.23, bf16[16,2048]{1,0:T(8,128)(2,1)} %refs_1_.3), kind=kLoop, calls=%fused_computation.11 | loop fusion | flops 245760 | bytes 163840 | tf_op jit(solution)/shard_map/concatenate | solution.py:194
  2.2 0.0 copy-start.1
  2.2 3.0 %collective-permute-start.3 = (bf16[16,2560]{1,0:T(8,128)(2,1)S(1)}, bf16[16,2560]{1,0:T(8,128)(2,1)S(1)}, u32[]{:S(2)}, u32[]{:S(2)}) collective-permute-start(bf16[16,2560]{1,0:T(8,128)(2,1)S(1)} %pad_maximum_fusion.refs_1_), channel_id=1, source_target_pairs={{0,4},{4,8},{8,12},{12,0},{1,5},{5,9},{9,13},{13,1},{2,6},{6,10},{... | collective-permute-start | bytes 245768 | tf_op jit(solution)/shard_map/ppermute | solution.py:183
  5.2 2.6 %collective-permute-start.4 = (bf16[16,2560]{1,0:T(8,128)(2,1)S(1)}, bf16[16,2560]{1,0:T(8,128)(2,1)S(1)}, u32[]{:S(2)}, u32[]{:S(2)}) collective-permute-start(bf16[16,2560]{1,0:T(8,128)(2,1)S(1)} %pad_maximum_fusion.refs_1_), channel_id=1, source_target_pairs={{0,8},{4,12},{8,0},{12,4},{1,9},{5,13},{9,1},{13,5},{2,10},{6,14},... | collective-permute-start | bytes 245768 | tf_op jit(solution)/shard_map/ppermute | solution.py:183
  7.8 1.3 %collective-permute-start.5 = (bf16[16,2560]{1,0:T(8,128)(2,1)S(1)}, bf16[16,2560]{1,0:T(8,128)(2,1)S(1)}, u32[]{:S(2)}, u32[]{:S(2)}) collective-permute-start(bf16[16,2560]{1,0:T(8,128)(2,1)S(1)} %pad_maximum_fusion.refs_1_), channel_id=1, source_target_pairs={{0,12},{4,0},{8,4},{12,8},{1,13},{5,1},{9,5},{13,9},{2,14},{6,2},{... | collective-permute-start | bytes 245768 | tf_op jit(solution)/shard_map/ppermute | solution.py:183
  9.2 0.7 %collective-permute-start = (bf16[2,128,256]{2,1,0:T(8,128)(2,1)}, bf16[2,128,256]{2,1,0:T(8,128)(2,1)S(1)}, u32[]{:S(2)}, u32[]{:S(2)}) collective-permute-start(bf16[2,128,256]{2,1,0:T(8,128)(2,1)} %param.10), channel_id=1, source_target_pairs={{0,4},{4,8},{8,12},{12,0},{1,5},{5,9},{9,13},{13,1},{2,6},{6,10},{... | collective-permute-start | bytes 393224 | tf_op jit(solution)/shard_map/ppermute | solution.py:183
  9.8 0.3 collective-permute-start.1
  10.2 0.9 %constant_dynamic-update-slice_fusion.3 = bf16[2,512,256]{2,1,0:T(8,128)(2,1)S(1)} fusion(bf16[2,128,256]{2,1,0:T(8,128)(2,1)} %param.10), kind=kLoop, calls=%fused_computation.20 | loop fusion | bytes 262144
  11.1 0.9 %fusion.22 = (s32[16]{0:T(128)S(1)}, s32[16]{0:T(128)S(1)}, s32[16]{0:T(128)S(1)}, s32[16]{0:T(128)S(1)}) fusion(s32[64]{0:T(128)} %param.15, s32[]{:T(128)S(6)} %select_n.32, s32[]{:T(128)S(6)} %select_n.34, s32[]{:T(128)S(6)} %select_n.38, s32[]{:T(128)S(6)} %select_n.36), kind=kLoop, calls=%fused_computation.56 | loop fusion | bytes 528 | tf_op jit(solution)/shard_map/dynamic_slice | solution.py:208
  12.0 0.7 %copy.11.refs_7_ = s32[16,1]{1,0:T(8,128)} copy(s32[16,1]{0,1:T(1,128)S(1)} %bitcast.166) | data formatting | bytes 128 | tf_op jit(solution)/shard_map/reshape | solution.py:144
  13.4 0.6 pad_add_fusion.refs_0_
  14.0 0.7 %add_bitcast_fusion.refs_6_ = s32[1,64]{1,0:T(1,128)} fusion(s32[16]{0:T(128)S(1)} %get-tuple-element.27, s32[16]{0:T(128)S(1)} %get-tuple-element.28, s32[16]{0:T(128)S(1)} %get-tuple-element.26, s32[16]{0:T(128)S(1)} %get-tuple-element.25), kind=kLoop, calls=%fused_computation.51 | loop fusion | flops 192 | bytes 512 | tf_op jit(solution)/shard_map/reshape | solution.py:143
  14.6 0.0 collective-permute-done.3.refs_2_
  14.6 0.0 copy-start.3
  14.6 2.8 %collective-permute-start.2 = (bf16[2,128,256]{2,1,0:T(8,128)(2,1)}, bf16[2,128,256]{2,1,0:T(8,128)(2,1)S(1)}, u32[]{:S(2)}, u32[]{:S(2)}) collective-permute-start(bf16[2,128,256]{2,1,0:T(8,128)(2,1)} %param.10), channel_id=1, source_target_pairs={{0,12},{4,0},{8,4},{12,8},{1,13},{5,1},{9,5},{13,9},{2,14},{6,2},{... | collective-permute-start | bytes 393224 | tf_op jit(solution)/shard_map/ppermute | solution.py:183
  17.5 0.0 collective-permute-done.4.refs_3_
  17.5 0.0 copy-start.4
  17.5 0.0 collective-permute-done.5.refs_4_
  17.5 0.0 copy-done.1
  17.5 0.0 copy-done.3
  17.5 0.6 copy-done.4
  18.1 0.6 %copy-done.5 = bf16[16,2560]{1,0:T(8,128)(2,1)} copy-done((bf16[16,2560]{1,0:T(8,128)(2,1)}, bf16[16,2560]{1,0:T(8,128)(2,1)S(1)}, u32[]{:S(2)}) %copy-start.5) | copy-done | bytes 81944
  18.7 16.4 %shard_map.97 = f32[64,2304]{1,0:T(8,128)} custom-call(s32[2]{0:T(128)} %pad_add_fusion.refs_0_, bf16[16,2560]{1,0:T(8,128)(2,1)} %copy-done.1, bf16[16,2560]{1,0:T(8,128)(2,1)} %copy-done.3, bf16[16,2560]{1,0:T(8,128)(2,1)} %copy-done.4, bf16[16,2560]{1,0:T(8,128)(2,1)} %copy-done.5, bf16[2,4096,256]{2,1,0:T(8,128)(2,1)} %refs_6_.1, ...), custom_call_target="tpu_custom_call" | custom-call | tf_op jit(solution)/shard_map/pallas_call | solution.py:170
  35.1 1.1 %fusion.18 = (f32[16,2304]{1,0:T(8,128)S(1)}, f32[16,2304]{1,0:T(8,128)S(1)}, f32[16,2304]{1,0:T(8,128)S(1)}) fusion(f32[64,2304]{1,0:T(8,128)} %shard_map.97), kind=kLoop, calls=%fused_computation.52 | loop fusion | bytes 884736 | tf_op jit(solution)/shard_map/slice | solution.py:225
  36.2 1.3 %collective-permute-start.6 = (f32[16,2304]{1,0:T(8,128)S(1)}, f32[16,2304]{1,0:T(8,128)S(1)}, u32[]{:S(2)}, u32[]{:S(2)}) collective-permute-start(f32[16,2304]{1,0:T(8,128)S(1)} %get-tuple-element.12), channel_id=1, source_target_pairs={{0,12},{4,0},{8,4},{12,8},{1,13},{5,1},{9,5},{13,9},{2,14},{6,2},{... | collective-permute-start | bytes 442376 | tf_op jit(solution)/shard_map/ppermute | solution.py:183
  37.4 3.4 %collective-permute-start.7 = (f32[16,2304]{1,0:T(8,128)S(1)}, f32[16,2304]{1,0:T(8,128)S(1)}, u32[]{:S(2)}, u32[]{:S(2)}) collective-permute-start(f32[16,2304]{1,0:T(8,128)S(1)} %get-tuple-element.14), channel_id=1, source_target_pairs={{0,8},{4,12},{8,0},{12,4},{1,9},{5,13},{9,1},{13,5},{2,10},{6,14},... | collective-permute-start | bytes 442376 | tf_op jit(solution)/shard_map/ppermute | solution.py:183
  40.8 0.7 %fusion.19 = (bf16[16,256]{1,0:T(8,128)(2,1)S(1)}, bf16[16,256]{1,0:T(8,128)(2,1)S(1)}) fusion(bf16[16,2560]{1,0:T(8,128)(2,1)} %copy-done.3), kind=kLoop, calls=%fused_computation.53 | loop fusion | bytes 32768 | tf_op jit(solution)/shard_map/slice | solution.py:202
  41.5 0.7 %fusion.20 = (bf16[16,256]{1,0:T(8,128)(2,1)S(1)}, bf16[16,256]{1,0:T(8,128)(2,1)S(1)}) fusion(bf16[16,2560]{1,0:T(8,128)(2,1)} %copy-done.4), kind=kLoop, calls=%fused_computation.54 | loop fusion | bytes 32768 | tf_op jit(solution)/shard_map/slice | solution.py:202
  42.3 0.7 %fusion.21 = (bf16[16,256]{1,0:T(8,128)(2,1)S(1)}, bf16[16,256]{1,0:T(8,128)(2,1)S(1)}) fusion(bf16[16,2560]{1,0:T(8,128)(2,1)} %copy-done.5), kind=kLoop, calls=%fused_computation.55 | loop fusion | bytes 32768 | tf_op jit(solution)/shard_map/slice | solution.py:202
  43.0 0.6 %pad_maximum_fusion.1.refs_4_.refs_5_ = bf16[2,64,256]{2,1,0:T(8,128)(2,1)} fusion(bf16[1,64,256]{2,1,0:T(8,128)(2,1)S(1)} %get-tuple-element.30, bf16[1,64,256]{2,1,0:T(8,128)(2,1)S(1)} %get-tuple-element.29), kind=kLoop, calls=%fused_computation.12 | loop fusion | flops 32768 | bytes 131072 | tf_op jit(solution)/shard_map/stack | solution.py:200
  43.6 0.7 %slice.139 = f32[16,256]{1,0:T(8,128)S(1)} slice(f32[64,2304]{1,0:T(8,128)} %shard_map.97), slice={[0:16], [2048:2304]} | slice | bytes 32768 | tf_op jit(solution)/shard_map/slice | solution.py:229
  44.3 0.1 copy.24
  44.4 0.0 collective-permute-done
  44.5 0.1 collective-permute-start.8
  44.5 0.0 collective-permute-done.1
  44.6 0.0 collective-permute-done.2
  44.6 0.0 copy-start
  44.6 0.8 %copy-done = bf16[2,512,256]{2,1,0:T(8,128)(2,1)} copy-done((bf16[2,512,256]{2,1,0:T(8,128)(2,1)}, bf16[2,512,256]{2,1,0:T(8,128)(2,1)S(1)}, u32[]{:S(2)}) %copy-start) | copy-done | bytes 524312
  45.4 3.3 %shard_map.96 = (f32[16,2048]{1,0:T(8,128)}, f32[2,16,128]{2,1,0:T(8,128)}) custom-call(s32[2]{0:T(128)} %pad_add_fusion.refs_0_, bf16[16,2048]{1,0:T(8,128)(2,1)} %refs_1_.3, bf16[2,512,256]{2,1,0:T(8,128)(2,1)} %copy-done, bf16[2,512,256]{2,1,0:T(8,128)(2,1)} %copy-done, bf16[2,64,256]{2,1,0:T(8,128)(2,1)} %pad_maximum_fusion.1.refs_4_.refs_5_, ...), custom_call_target="tpu_custom_call" | custom-call | tf_op jit(solution)/shard_map/pallas_call | solution.py:170
  48.7 0.9 %slice_bitcast_fusion.1 = (f32[16,2,8]{2,0,1:T(8,128)S(1)}, f32[16,2,8]{2,0,1:T(8,128)S(1)}) fusion(f32[2,16,128]{2,1,0:T(8,128)} %get-tuple-element.5), kind=kLoop, calls=%fused_computation.16 | loop fusion | bytes 4096 | tf_op jit(solution)/shard_map/transpose | solution.py:248
  49.6 0.1 copy.12
  49.7 0.1 copy.22
  49.8 7.7 %shard_map.95 = bf16[256,2048]{1,0:T(8,128)(2,1)} custom-call(s32[2]{0:T(128)} %pad_add_fusion.refs_0_, bf16[256,2048]{1,0:T(8,128)(2,1)} %refs_1_.2, bf16[2,512,256]{2,1,0:T(8,128)(2,1)} %copy-done, bf16[2,512,256]{2,1,0:T(8,128)(2,1)} %copy-done, bf16[2,256,256]{2,1,0:T(8,128)(2,1)} %refs_8_.1, bf16[2,256,256]{2,1,0:T(8,128)(2,1)} %refs_8_.1), custom_call_target="tpu_custom_call" | custom-call | tf_op jit(solution)/shard_map/pallas_call | solution.py:170
  57.5 0.0 collective-permute-done.6
  57.5 0.1 copy.25
  57.6 0.0 collective-permute-done.7
  57.6 0.1 copy.26
  57.7 0.0 collective-permute-done.8
  57.7 0.1 copy.27
  57.8 0.1 copy.17
  57.9 0.1 copy.18
  58.0 0.1 copy.19
  58.0 0.1 copy.20
  58.1 0.1 copy.21
  58.2 0.1 copy.23
  58.2 0.1 broadcast_in_dim.18
  58.4 0.1 broadcast_in_dim.19
  58.5 0.1 broadcast_in_dim.20
  58.6 0.1 broadcast_in_dim.21
  58.7 0.1 broadcast_in_dim.22
  58.8 0.1 broadcast_in_dim.23
  58.9 0.0 copy-done.2
  58.9 1.8 %fusion = bf16[16,2048]{1,0:T(8,128)(2,1)} fusion(f32[2,8,16,128]{3,2,1,0:T(8,128)S(1)} %bitcast.161, f32[2,8,16,128]{3,2,1,0:T(8,128)S(1)} %bitcast.160, f32[2,8,16,128]{3,2,1,0:T(8,128)S(1)} %bitcast.159, f32[2,8,16,128]{3,2,1,0:T(8,128)S(1)} %bitcast.158, f32[2,8,16,128]{3,2,1,0:T(8,128)S(1)} %bitcast.157, f32[16,2048]{1,0:T(8,128)S(1)} %copy-done.2, ...), kind=kLoop, calls=%fused_computation.1 | loop fusion | flops 360448 | bytes 1507328 | tf_op jit(solution)/shard_map/convert_element_type | solution.py:265
  (10 shorter events, 0.1 us)
Async XLA Ops:
  2.2 15.3 %copy-start.1 = (bf16[16,2560]{1,0:T(8,128)(2,1)}, bf16[16,2560]{1,0:T(8,128)(2,1)S(1)}, u32[]{:S(2)}) copy-start(bf16[16,2560]{1,0:T(8,128)(2,1)S(1)} %pad_maximum_fusion.refs_1_) | copy-start | bytes 245764
  2.2 12.4 %collective-permute-start.3 = (bf16[16,2560]{1,0:T(8,128)(2,1)S(1)}, bf16[16,2560]{1,0:T(8,128)(2,1)S(1)}, u32[]{:S(2)}, u32[]{:S(2)}) collective-permute-start(bf16[16,2560]{1,0:T(8,128)(2,1)S(1)} %pad_maximum_fusion.refs_1_), channel_id=1, source_target_pairs={{0,4},{4,8},{8,12},{12,0},{1,5},{5,9},{9,13},{13,1},{2,6},{6,10},{... | collective-permute-start | bytes 245768 | tf_op jit(solution)/shard_map/ppermute | solution.py:183
  5.2 12.2 %collective-permute-start.4 = (bf16[16,2560]{1,0:T(8,128)(2,1)S(1)}, bf16[16,2560]{1,0:T(8,128)(2,1)S(1)}, u32[]{:S(2)}, u32[]{:S(2)}) collective-permute-start(bf16[16,2560]{1,0:T(8,128)(2,1)S(1)} %pad_maximum_fusion.refs_1_), channel_id=1, source_target_pairs={{0,8},{4,12},{8,0},{12,4},{1,9},{5,13},{9,1},{13,5},{2,10},{6,14},... | collective-permute-start | bytes 245768 | tf_op jit(solution)/shard_map/ppermute | solution.py:183
  7.8 9.7 %collective-permute-start.5 = (bf16[16,2560]{1,0:T(8,128)(2,1)S(1)}, bf16[16,2560]{1,0:T(8,128)(2,1)S(1)}, u32[]{:S(2)}, u32[]{:S(2)}) collective-permute-start(bf16[16,2560]{1,0:T(8,128)(2,1)S(1)} %pad_maximum_fusion.refs_1_), channel_id=1, source_target_pairs={{0,12},{4,0},{8,4},{12,8},{1,13},{5,1},{9,5},{13,9},{2,14},{6,2},{... | collective-permute-start | bytes 245768 | tf_op jit(solution)/shard_map/ppermute | solution.py:183
  9.2 35.3 %collective-permute-start = (bf16[2,128,256]{2,1,0:T(8,128)(2,1)}, bf16[2,128,256]{2,1,0:T(8,128)(2,1)S(1)}, u32[]{:S(2)}, u32[]{:S(2)}) collective-permute-start(bf16[2,128,256]{2,1,0:T(8,128)(2,1)} %param.10), channel_id=1, source_target_pairs={{0,4},{4,8},{8,12},{12,0},{1,5},{5,9},{9,13},{13,1},{2,6},{6,10},{... | collective-permute-start | bytes 393224 | tf_op jit(solution)/shard_map/ppermute | solution.py:183
  9.8 34.7 %collective-permute-start.1 = (bf16[2,128,256]{2,1,0:T(8,128)(2,1)}, bf16[2,128,256]{2,1,0:T(8,128)(2,1)S(1)}, u32[]{:S(2)}, u32[]{:S(2)}) collective-permute-start(bf16[2,128,256]{2,1,0:T(8,128)(2,1)} %param.10), channel_id=1, source_target_pairs={{0,8},{4,12},{8,0},{12,4},{1,9},{5,13},{9,1},{13,5},{2,10},{6,14},... | collective-permute-start | bytes 393224 | tf_op jit(solution)/shard_map/ppermute | solution.py:183
  14.6 2.9 %copy-start.3 = (bf16[16,2560]{1,0:T(8,128)(2,1)}, bf16[16,2560]{1,0:T(8,128)(2,1)S(1)}, u32[]{:S(2)}) copy-start(bf16[16,2560]{1,0:T(8,128)(2,1)S(1)} %collective-permute-done.3.refs_2_) | copy-start | bytes 245764
  14.6 30.0 %collective-permute-start.2 = (bf16[2,128,256]{2,1,0:T(8,128)(2,1)}, bf16[2,128,256]{2,1,0:T(8,128)(2,1)S(1)}, u32[]{:S(2)}, u32[]{:S(2)}) collective-permute-start(bf16[2,128,256]{2,1,0:T(8,128)(2,1)} %param.10), channel_id=1, source_target_pairs={{0,12},{4,0},{8,4},{12,8},{1,13},{5,1},{9,5},{13,9},{2,14},{6,2},{... | collective-permute-start | bytes 393224 | tf_op jit(solution)/shard_map/ppermute | solution.py:183
  17.5 0.6 %copy-start.4 = (bf16[16,2560]{1,0:T(8,128)(2,1)}, bf16[16,2560]{1,0:T(8,128)(2,1)S(1)}, u32[]{:S(2)}) copy-start(bf16[16,2560]{1,0:T(8,128)(2,1)S(1)} %collective-permute-done.4.refs_3_) | copy-start | bytes 245764
  18.1 0.6 %copy-start.5 = (bf16[16,2560]{1,0:T(8,128)(2,1)}, bf16[16,2560]{1,0:T(8,128)(2,1)S(1)}, u32[]{:S(2)}) copy-start(bf16[16,2560]{1,0:T(8,128)(2,1)S(1)} %collective-permute-done.5.refs_4_) | copy-start | bytes 245764
  36.2 21.3 %collective-permute-start.6 = (f32[16,2304]{1,0:T(8,128)S(1)}, f32[16,2304]{1,0:T(8,128)S(1)}, u32[]{:S(2)}, u32[]{:S(2)}) collective-permute-start(f32[16,2304]{1,0:T(8,128)S(1)} %get-tuple-element.12), channel_id=1, source_target_pairs={{0,12},{4,0},{8,4},{12,8},{1,13},{5,1},{9,5},{13,9},{2,14},{6,2},{... | collective-permute-start | bytes 442376 | tf_op jit(solution)/shard_map/ppermute | solution.py:183
  37.4 20.1 %collective-permute-start.7 = (f32[16,2304]{1,0:T(8,128)S(1)}, f32[16,2304]{1,0:T(8,128)S(1)}, u32[]{:S(2)}, u32[]{:S(2)}) collective-permute-start(f32[16,2304]{1,0:T(8,128)S(1)} %get-tuple-element.14), channel_id=1, source_target_pairs={{0,8},{4,12},{8,0},{12,4},{1,9},{5,13},{9,1},{13,5},{2,10},{6,14},... | collective-permute-start | bytes 442376 | tf_op jit(solution)/shard_map/ppermute | solution.py:183
  44.5 13.2 %collective-permute-start.8 = (f32[16,2304]{1,0:T(8,128)S(1)}, f32[16,2304]{1,0:T(8,128)S(1)}, u32[]{:S(2)}, u32[]{:S(2)}) collective-permute-start(f32[16,2304]{1,0:T(8,128)S(1)} %get-tuple-element.13), channel_id=1, source_target_pairs={{0,4},{4,8},{8,12},{12,0},{1,5},{5,9},{9,13},{13,1},{2,6},{6,10},{... | collective-permute-start | bytes 442376 | tf_op jit(solution)/shard_map/ppermute | solution.py:183
  44.6 0.8 %copy-start = (bf16[2,512,256]{2,1,0:T(8,128)(2,1)}, bf16[2,512,256]{2,1,0:T(8,128)(2,1)S(1)}, u32[]{:S(2)}) copy-start(bf16[2,512,256]{2,1,0:T(8,128)(2,1)S(1)} %constant_dynamic-update-slice_fusion.refs_2_.refs_3_) | copy-start | bytes 1572868
  48.7 10.1 %copy-start.2 = (f32[16,2048]{1,0:T(8,128)S(1)}, f32[16,2048]{1,0:T(8,128)}, u32[]{:S(2)}) copy-start(f32[16,2048]{1,0:T(8,128)} %get-tuple-element.4) | copy-start | bytes 393220

commit v9 on v6

--- a/solution.py
+++ b/solution.py
@@ -18,9 +18,10 @@
 
 
 STACK_ROWS = 512
-
-
-def attention_kernel(masks, normalize, packed, rows, group_size, kv_heads, *refs):
+CONTEXT_STACK_ROWS = 256
+
+
+def attention_kernel(masks, normalize, packed, rows, group_size, kv_heads, stack_rows, *refs):
     length_ref, q_ref = refs[0], refs[1]
     part_count = len(masks)
     kv_refs = refs[2 : 2 + 2 * part_count]
@@ -32,7 +33,7 @@
     side_ref = None if normalize or packed else rest[1]
     query_width = kv_heads * group_size * HD
     scale = 1.0 / jnp.sqrt(jnp.float32(HD))
-    stack = max(1, min(group_size, STACK_ROWS // rows))
+    stack = max(1, min(group_size, stack_rows // rows))
     visible = []
     for index, mask in enumerate(masks):
         key_count = kv_refs[2 * index].shape[0]
@@ -111,7 +112,9 @@
                 side_ref[:, HD // 2 + h : HD // 2 + h + 1] = total[rows_of]
 
 
-def attention(queries, parts, normalize, length=None, positions=None, packed=False):
+def attention(
+    queries, parts, normalize, length=None, positions=None, packed=False, stack_rows=STACK_ROWS
+):
     rows, query_width = queries.shape
     kv_heads = parts[0][0].shape[2] // HD
     group_size = query_width // HD // kv_heads
@@ -144,7 +147,9 @@
         out_shape.append(jax.ShapeDtypeStruct((kv_heads, rows, HD), jnp.float32))
         out_specs.append(pl.BlockSpec((pl.Squeezed(), rows, HD), lambda g, n: (g, 0, 0)))
     return pl.pallas_call(
-        functools.partial(attention_kernel, masks, normalize, packed, rows, group_size, kv_heads),
+        functools.partial(
+            attention_kernel, masks, normalize, packed, rows, group_size, kv_heads, stack_rows
+        ),
         grid_spec=pltpu.PrefetchScalarGridSpec(
             num_scalar_prefetch=1,
             grid=(kv_heads,),
@@ -192,6 +197,7 @@
             False,
             length=cache_len,
             packed=True,
+            stack_rows=CONTEXT_STACK_ROWS,
         )
         sections = [context_packed[:own_count]]
         for k in range(1, ctx_count):

time: 59.4 us -> 55.4 us (0.933)
  Pallas kernels: 25.4 us -> 21.4 us
    pallas_call x3, Pallas kernels: 25.4 us -> 21.4 us  [attention(): pl.pallas_call(functools.partial(attention_kernel, masks, normalize, pack...]
  transfers between devices with their start and end apart: 9 -> 9, of which waited for: 0 -> 0; matrix products, arithmetic and copies ran while one was open for 15% -> 16% of each run, Pallas kernels for 43% -> 39%
where the time goes in v9:
time: 55.4 us; the launch traced here: 55 us
  Pallas kernels  21.4 us (39%)
  starting transfers between devices  18 us (32%)
  local copies, waits for them, and re-layouts  9.28 us (17%)
  other arithmetic  4.62 us (8%)
  between operations  1.58 us (3%)
    pallas_call x3, Pallas kernels, attention(): pl.pallas_call(functools.partial(attention_kernel, masks, normalize, pack...  21.4 us
    ppermute x9, starting transfers between devices, shifted(): lax.ppermute(value, 'ctx', [(j, (j + shift) % count) for j in range(count)])  18 us
    unnamed x12, local copies, waits for them, and re-layouts  3.35 us
    convert_element_type x1, other arithmetic, local(): query_out = (merged_output / widen(merged_totals)).astype(jnp.bfloat16)  1.81 us
    concatenate x1, other arithmetic, local(): jnp.concatenate([slot[:split].reshape(own_count, query_width) for slot in...  1.56 us
  transfers between devices with their start and end apart: 9, of which 0 were waited for; matrix products, arithmetic and copies ran while one was open for 16% of the time, Pallas kernels for 39%

profile of v9, /device:TPU:0, one launch (start us, length us, event | category | flops | bytes accessed | tf_op | source)
XLA Modules:
  0.0 55.0 jit_solution(4671996716531414623)
XLA Ops:
  0.6 0.9 %copy.28 = bf16[2,16,8,128]{3,1,2,0:T(8,128)(2,1)S(1)} copy(bf16[2,16,8,128]{3,2,1,0:T(8,128)(2,1)} %bitcast.151) | data formatting | bytes 131072
  1.5 0.7 %copy.29 = bf16[4,2,8,128]{3,1,2,0:T(2,128)(2,1)S(1)} copy(bf16[4,2,8,128]{3,2,1,0:T(8,128)(2,1)} %bitcast.164) | data formatting | bytes 32768
  2.2 3.1 %collective-permute-start.3 = (bf16[40960]{0:T(1024)(128)(2,1)S(1)}, bf16[40960]{0:T(1024)(128)(2,1)S(1)}, u32[]{:S(2)}, u32[]{:S(2)}) collective-permute-start(bf16[40960]{0:T(1024)(128)(2,1)S(1)} %constant_dynamic-update-slice_fusion.5), channel_id=1, source_target_pairs={{0,4},{4,8},{8,12},{12,0},{1,5},{5,9},{9,13},{13,1},{2,6},{6,10},{... | collective-permute-start | bytes 245768 | tf_op jit(solution)/shard_map/ppermute | solution.py:164
  5.3 2.6 %collective-permute-start.4 = (bf16[40960]{0:T(1024)(128)(2,1)S(1)}, bf16[40960]{0:T(1024)(128)(2,1)S(1)}, u32[]{:S(2)}, u32[]{:S(2)}) collective-permute-start(bf16[40960]{0:T(1024)(128)(2,1)S(1)} %constant_dynamic-update-slice_fusion.5), channel_id=1, source_target_pairs={{0,8},{4,12},{8,0},{12,4},{1,9},{5,13},{9,1},{13,5},{2,10},{6,14},... | collective-permute-start | bytes 245768 | tf_op jit(solution)/shard_map/ppermute | solution.py:164
  7.9 1.3 %collective-permute-start.5 = (bf16[40960]{0:T(1024)(128)(2,1)S(1)}, bf16[40960]{0:T(1024)(128)(2,1)S(1)}, u32[]{:S(2)}, u32[]{:S(2)}) collective-permute-start(bf16[40960]{0:T(1024)(128)(2,1)S(1)} %constant_dynamic-update-slice_fusion.5), channel_id=1, source_target_pairs={{0,12},{4,0},{8,4},{12,8},{1,13},{5,1},{9,5},{13,9},{2,14},{6,2},{... | collective-permute-start | bytes 245768 | tf_op jit(solution)/shard_map/ppermute | solution.py:164
  9.3 0.7 %collective-permute-start = (bf16[2,128,256]{2,1,0:T(8,128)(2,1)}, bf16[2,128,256]{2,1,0:T(8,128)(2,1)S(1)}, u32[]{:S(2)}, u32[]{:S(2)}) collective-permute-start(bf16[2,128,256]{2,1,0:T(8,128)(2,1)} %param.10), channel_id=1, source_target_pairs={{0,4},{4,8},{8,12},{12,0},{1,5},{5,9},{9,13},{13,1},{2,6},{6,10},{... | collective-permute-start | bytes 393224 | tf_op jit(solution)/shard_map/ppermute | solution.py:164
  9.9 0.3 collective-permute-start.1
  10.3 0.9 %constant_dynamic-update-slice_fusion.3 = bf16[2,512,256]{2,1,0:T(8,128)(2,1)S(1)} fusion(bf16[2,128,256]{2,1,0:T(8,128)(2,1)} %param.10), kind=kLoop, calls=%fused_computation.18 | loop fusion | bytes 262144
  11.2 0.9 %fusion.19 = (s32[16]{0:T(128)S(1)}, s32[16]{0:T(128)S(1)}, s32[16]{0:T(128)S(1)}, s32[16]{0:T(128)S(1)}) fusion(s32[64]{0:T(128)} %param.15, s32[]{:T(128)S(6)} %select_n.32, s32[]{:T(128)S(6)} %select_n.34, s32[]{:T(128)S(6)} %select_n.38, s32[]{:T(128)S(6)} %select_n.36), kind=kLoop, calls=%fused_computation.50 | loop fusion | bytes 528 | tf_op jit(solution)/shard_map/dynamic_slice | solution.py:188
  12.1 0.7 %copy.11.refs_7_ = s32[16,1]{1,0:T(8,128)} copy(s32[16,1]{0,1:T(1,128)S(1)} %bitcast.165) | data formatting | bytes 128 | tf_op jit(solution)/shard_map/reshape | solution.py:134
  13.5 0.6 %add_bitcast_fusion.refs_6_ = s32[1,64]{1,0:T(1,128)} fusion(s32[16]{0:T(128)S(1)} %get-tuple-element.19, s32[16]{0:T(128)S(1)} %get-tuple-element.20, s32[16]{0:T(128)S(1)} %get-tuple-element.18, s32[16]{0:T(128)S(1)} %get-tuple-element.17), kind=kLoop, calls=%fused_computation.48 | loop fusion | flops 192 | bytes 512 | tf_op jit(solution)/shard_map/reshape | solution.py:133
  14.0 0.0 collective-permute-done.3
  14.1 2.8 %collective-permute-start.2 = (bf16[2,128,256]{2,1,0:T(8,128)(2,1)}, bf16[2,128,256]{2,1,0:T(8,128)(2,1)S(1)}, u32[]{:S(2)}, u32[]{:S(2)}) collective-permute-start(bf16[2,128,256]{2,1,0:T(8,128)(2,1)} %param.10), channel_id=1, source_target_pairs={{0,12},{4,0},{8,4},{12,8},{1,13},{5,1},{9,5},{13,9},{2,14},{6,2},{... | collective-permute-start | bytes 393224 | tf_op jit(solution)/shard_map/ppermute | solution.py:164
  16.9 0.0 collective-permute-done.4
  17.0 0.0 collective-permute-done.5
  17.1 1.6 %pad_maximum_fusion.refs_1_ = bf16[64,2048]{1,0:T(8,128)(2,1)} fusion(bf16[16,2048]{1,0:T(8,128)(2,1)S(1)} %slice.156, bf16[16,2048]{1,0:T(8,128)(2,1)S(1)} %slice.154, bf16[16,2048]{1,0:T(8,128)(2,1)S(1)} %slice.152, bf16[16,2048]{1,0:T(8,128)(2,1)} %refs_1_.3), kind=kLoop, calls=%fused_computation | loop fusion | flops 1048576 | bytes 524288 | tf_op jit(solution)/shard_map/concatenate | solution.py:179
  18.6 0.0 copy-start.2
  18.6 11.7 %shard_map.97 = f32[64,2304]{1,0:T(8,128)} custom-call(s32[1]{0:T(128)S(6)} %copy.46.refs_0_, bf16[64,2048]{1,0:T(8,128)(2,1)} %pad_maximum_fusion.refs_1_, bf16[2,4096,256]{2,1,0:T(8,128)(2,1)} %refs_3_.1, bf16[2,4096,256]{2,1,0:T(8,128)(2,1)} %refs_3_.1, bf16[2,256,256]{2,1,0:T(8,128)(2,1)} %refs_5_.3, bf16[2,256,256]{2,1,0:T(8,128)(2,1)} %refs_5_.3), custom_call_target="tpu_custom_call" | custom-call | tf_op jit(solution)/shard_map/pallas_call | solution.py:149
  30.4 1.1 %fusion.18 = (f32[16,2304]{1,0:T(8,128)S(1)}, f32[16,2304]{1,0:T(8,128)S(1)}, f32[16,2304]{1,0:T(8,128)S(1)}) fusion(f32[64,2304]{1,0:T(8,128)} %shard_map.97), kind=kLoop, calls=%fused_computation.49 | loop fusion | bytes 884736 | tf_op jit(solution)/shard_map/slice | solution.py:205
  31.5 3.3 %collective-permute-start.7 = (f32[16,2304]{1,0:T(8,128)S(1)}, f32[16,2304]{1,0:T(8,128)S(1)}, u32[]{:S(2)}, u32[]{:S(2)}) collective-permute-start(f32[16,2304]{1,0:T(8,128)S(1)} %get-tuple-element.14), channel_id=1, source_target_pairs={{0,8},{4,12},{8,0},{12,4},{1,9},{5,13},{9,1},{13,5},{2,10},{6,14},... | collective-permute-start | bytes 442376 | tf_op jit(solution)/shard_map/ppermute | solution.py:164
  34.8 1.2 %collective-permute-start.8 = (f32[16,2304]{1,0:T(8,128)S(1)}, f32[16,2304]{1,0:T(8,128)S(1)}, u32[]{:S(2)}, u32[]{:S(2)}) collective-permute-start(f32[16,2304]{1,0:T(8,128)S(1)} %get-tuple-element.13), channel_id=1, source_target_pairs={{0,4},{4,8},{8,12},{12,0},{1,5},{5,9},{9,13},{13,1},{2,6},{6,10},{... | collective-permute-start | bytes 442376 | tf_op jit(solution)/shard_map/ppermute | solution.py:164
  36.0 0.0 copy-done.2
  36.0 0.6 %pad_maximum_fusion.1.refs_4_.refs_5_ = bf16[2,64,256]{2,1,0:T(8,128)(2,1)} fusion(bf16[2,16,256]{2,1,0:T(8,128)(2,1)S(1)} %slice.149, bf16[2,16,256]{2,1,0:T(8,128)(2,1)S(1)} %slice.147, bf16[2,16,256]{2,1,0:T(8,128)(2,1)S(1)} %slice.145, bf16[2,16,256]{2,1,0:T(8,128)(2,1)S(1)} %copy-done.2), kind=kLoop, calls=%fused_computation.12 | loop fusion | flops 262144 | bytes 131072 | tf_op jit(solution)/shard_map/concatenate | solution.py:182
  36.6 0.7 %slice.183 = f32[16,256]{1,0:T(8,128)S(1)} slice(f32[64,2304]{1,0:T(8,128)} %shard_map.97), slice={[0:16], [2048:2304]} | slice | bytes 32768 | tf_op jit(solution)/shard_map/slice | solution.py:209
  37.3 0.1 copy.24
  37.4 0.0 collective-permute-done
  37.4 2.7 %collective-permute-start.6 = (f32[16,2304]{1,0:T(8,128)S(1)}, f32[16,2304]{1,0:T(8,128)S(1)}, u32[]{:S(2)}, u32[]{:S(2)}) collective-permute-start(f32[16,2304]{1,0:T(8,128)S(1)} %get-tuple-element.12), channel_id=1, source_target_pairs={{0,12},{4,0},{8,4},{12,8},{1,13},{5,1},{9,5},{13,9},{2,14},{6,2},{... | collective-permute-start | bytes 442376 | tf_op jit(solution)/shard_map/ppermute | solution.py:164
  40.2 0.0 collective-permute-done.1
  40.2 0.0 collective-permute-done.2
  40.2 0.0 copy-start
  40.3 0.8 %copy-done = bf16[2,512,256]{2,1,0:T(8,128)(2,1)} copy-done((bf16[2,512,256]{2,1,0:T(8,128)(2,1)}, bf16[2,512,256]{2,1,0:T(8,128)(2,1)S(1)}, u32[]{:S(2)}) %copy-start) | copy-done | bytes 524312
  41.0 2.7 %shard_map.96 = (f32[16,2048]{1,0:T(8,128)}, f32[2,16,128]{2,1,0:T(8,128)}) custom-call(s32[1]{0:T(128)} %constant.35.clone.1.refs_0_, bf16[16,2048]{1,0:T(8,128)(2,1)} %refs_1_.3, bf16[2,512,256]{2,1,0:T(8,128)(2,1)} %copy-done, bf16[2,512,256]{2,1,0:T(8,128)(2,1)} %copy-done, bf16[2,64,256]{2,1,0:T(8,128)(2,1)} %pad_maximum_fusion.1.refs_4_.refs_5_, ...), custom_call_target="tpu_custom_call" | custom-call | tf_op jit(solution)/shard_map/pallas_call | solution.py:149
  43.7 0.0 copy-start.1
  43.7 0.9 %slice_bitcast_fusion.1 = (f32[16,2,8]{2,0,1:T(8,128)S(1)}, f32[16,2,8]{2,0,1:T(8,128)S(1)}) fusion(f32[2,16,128]{2,1,0:T(8,128)} %get-tuple-element.5), kind=kLoop, calls=%fused_computation.14 | loop fusion | bytes 4096 | tf_op jit(solution)/shard_map/transpose | solution.py:224
  44.6 0.1 copy.12
  44.6 0.1 copy.22
  44.7 7.0 %shard_map.95 = bf16[256,2048]{1,0:T(8,128)(2,1)} custom-call(s32[1]{0:T(128)} %constant.35.clone.1.refs_0_, bf16[256,2048]{1,0:T(8,128)(2,1)} %refs_1_.2, bf16[2,512,256]{2,1,0:T(8,128)(2,1)} %copy-done, bf16[2,512,256]{2,1,0:T(8,128)(2,1)} %copy-done, bf16[2,256,256]{2,1,0:T(8,128)(2,1)} %refs_5_.3, bf16[2,256,256]{2,1,0:T(8,128)(2,1)} %refs_5_.3), custom_call_target="tpu_custom_call" | custom-call | tf_op jit(solution)/shard_map/pallas_call | solution.py:149
  51.7 0.0 collective-permute-done.7
  51.8 0.1 copy.26
  51.9 0.0 collective-permute-done.8
  51.9 0.1 copy.27
  52.0 0.0 collective-permute-done.6
  52.0 0.1 copy.25
  52.1 0.1 copy.17
  52.2 0.1 copy.18
  52.3 0.1 copy.19
  52.3 0.1 copy.20
  52.4 0.1 copy.21
  52.5 0.1 copy.23
  52.5 0.1 broadcast_in_dim.18
  52.6 0.1 broadcast_in_dim.19
  52.7 0.1 broadcast_in_dim.20
  52.8 0.1 broadcast_in_dim.21
  52.9 0.1 broadcast_in_dim.22
  53.0 0.1 broadcast_in_dim.23
  53.1 0.0 copy-done.1
  53.2 1.8 %fusion = bf16[16,2048]{1,0:T(8,128)(2,1)} fusion(f32[2,8,16,128]{3,2,1,0:T(8,128)S(1)} %bitcast.157, f32[2,8,16,128]{3,2,1,0:T(8,128)S(1)} %bitcast.156, f32[2,8,16,128]{3,2,1,0:T(8,128)S(1)} %bitcast.155, f32[2,8,16,128]{3,2,1,0:T(8,128)S(1)} %bitcast.154, f32[2,8,16,128]{3,2,1,0:T(8,128)S(1)} %bitcast.153, f32[16,2048]{1,0:T(8,128)S(1)} %copy-done.1, ...), kind=kLoop, calls=%fused_computation.2 | loop fusion | flops 360448 | bytes 1507328 | tf_op jit(solution)/shard_map/convert_element_type | solution.py:241
  (21 shorter events, 0.2 us)
Async XLA Ops:
  2.2 11.8 %collective-permute-start.3 = (bf16[40960]{0:T(1024)(128)(2,1)S(1)}, bf16[40960]{0:T(1024)(128)(2,1)S(1)}, u32[]{:S(2)}, u32[]{:S(2)}) collective-permute-start(bf16[40960]{0:T(1024)(128)(2,1)S(1)} %constant_dynamic-update-slice_fusion.5), channel_id=1, source_target_pairs={{0,4},{4,8},{8,12},{12,0},{1,5},{5,9},{9,13},{13,1},{2,6},{6,10},{... | collective-permute-start | bytes 245768 | tf_op jit(solution)/shard_map/ppermute | solution.py:164
  5.3 11.6 %collective-permute-start.4 = (bf16[40960]{0:T(1024)(128)(2,1)S(1)}, bf16[40960]{0:T(1024)(128)(2,1)S(1)}, u32[]{:S(2)}, u32[]{:S(2)}) collective-permute-start(bf16[40960]{0:T(1024)(128)(2,1)S(1)} %constant_dynamic-update-slice_fusion.5), channel_id=1, source_target_pairs={{0,8},{4,12},{8,0},{12,4},{1,9},{5,13},{9,1},{13,5},{2,10},{6,14},... | collective-permute-start | bytes 245768 | tf_op jit(solution)/shard_map/ppermute | solution.py:164
  7.9 9.1 %collective-permute-start.5 = (bf16[40960]{0:T(1024)(128)(2,1)S(1)}, bf16[40960]{0:T(1024)(128)(2,1)S(1)}, u32[]{:S(2)}, u32[]{:S(2)}) collective-permute-start(bf16[40960]{0:T(1024)(128)(2,1)S(1)} %constant_dynamic-update-slice_fusion.5), channel_id=1, source_target_pairs={{0,12},{4,0},{8,4},{12,8},{1,13},{5,1},{9,5},{13,9},{2,14},{6,2},{... | collective-permute-start | bytes 245768 | tf_op jit(solution)/shard_map/ppermute | solution.py:164
  9.3 28.2 %collective-permute-start = (bf16[2,128,256]{2,1,0:T(8,128)(2,1)}, bf16[2,128,256]{2,1,0:T(8,128)(2,1)S(1)}, u32[]{:S(2)}, u32[]{:S(2)}) collective-permute-start(bf16[2,128,256]{2,1,0:T(8,128)(2,1)} %param.10), channel_id=1, source_target_pairs={{0,4},{4,8},{8,12},{12,0},{1,5},{5,9},{9,13},{13,1},{2,6},{6,10},{... | collective-permute-start | bytes 393224 | tf_op jit(solution)/shard_map/ppermute | solution.py:164
  9.9 30.2 %collective-permute-start.1 = (bf16[2,128,256]{2,1,0:T(8,128)(2,1)}, bf16[2,128,256]{2,1,0:T(8,128)(2,1)S(1)}, u32[]{:S(2)}, u32[]{:S(2)}) collective-permute-start(bf16[2,128,256]{2,1,0:T(8,128)(2,1)} %param.10), channel_id=1, source_target_pairs={{0,8},{4,12},{8,0},{12,4},{1,9},{5,13},{9,1},{13,5},{2,10},{6,14},... | collective-permute-start | bytes 393224 | tf_op jit(solution)/shard_map/ppermute | solution.py:164
  14.1 26.2 %collective-permute-start.2 = (bf16[2,128,256]{2,1,0:T(8,128)(2,1)}, bf16[2,128,256]{2,1,0:T(8,128)(2,1)S(1)}, u32[]{:S(2)}, u32[]{:S(2)}) collective-permute-start(bf16[2,128,256]{2,1,0:T(8,128)(2,1)} %param.10), channel_id=1, source_target_pairs={{0,12},{4,0},{8,4},{12,8},{1,13},{5,1},{9,5},{13,9},{2,14},{6,2},{... | collective-permute-start | bytes 393224 | tf_op jit(solution)/shard_map/ppermute | solution.py:164
  18.6 17.4 %copy-start.2 = (bf16[2,16,256]{2,1,0:T(8,128)(2,1)S(1)}, bf16[2,16,256]{2,1,0:T(8,128)(2,1)}, u32[]{:S(2)}) copy-start(bf16[2,16,256]{2,1,0:T(8,128)(2,1)} %param.14) | copy-start | bytes 49156
  31.5 20.2 %collective-permute-start.7 = (f32[16,2304]{1,0:T(8,128)S(1)}, f32[16,2304]{1,0:T(8,128)S(1)}, u32[]{:S(2)}, u32[]{:S(2)}) collective-permute-start(f32[16,2304]{1,0:T(8,128)S(1)} %get-tuple-element.14), channel_id=1, source_target_pairs={{0,8},{4,12},{8,0},{12,4},{1,9},{5,13},{9,1},{13,5},{2,10},{6,14},... | collective-permute-start | bytes 442376 | tf_op jit(solution)/shard_map/ppermute | solution.py:164
  34.8 17.0 %collective-permute-start.8 = (f32[16,2304]{1,0:T(8,128)S(1)}, f32[16,2304]{1,0:T(8,128)S(1)}, u32[]{:S(2)}, u32[]{:S(2)}) collective-permute-start(f32[16,2304]{1,0:T(8,128)S(1)} %get-tuple-element.13), channel_id=1, source_target_pairs={{0,4},{4,8},{8,12},{12,0},{1,5},{5,9},{9,13},{13,1},{2,6},{6,10},{... | collective-permute-start | bytes 442376 | tf_op jit(solution)/shard_map/ppermute | solution.py:164
  37.4 14.5 %collective-permute-start.6 = (f32[16,2304]{1,0:T(8,128)S(1)}, f32[16,2304]{1,0:T(8,128)S(1)}, u32[]{:S(2)}, u32[]{:S(2)}) collective-permute-start(f32[16,2304]{1,0:T(8,128)S(1)} %get-tuple-element.12), channel_id=1, source_target_pairs={{0,12},{4,0},{8,4},{12,8},{1,13},{5,1},{9,5},{13,9},{2,14},{6,2},{... | collective-permute-start | bytes 442376 | tf_op jit(solution)/shard_map/ppermute | solution.py:164
  40.2 0.8 %copy-start = (bf16[2,512,256]{2,1,0:T(8,128)(2,1)}, bf16[2,512,256]{2,1,0:T(8,128)(2,1)S(1)}, u32[]{:S(2)}) copy-start(bf16[2,512,256]{2,1,0:T(8,128)(2,1)S(1)} %constant_dynamic-update-slice_fusion.refs_2_.refs_3_) | copy-start | bytes 1572868
  43.7 9.4 %copy-start.1 = (f32[16,2048]{1,0:T(8,128)S(1)}, f32[16,2048]{1,0:T(8,128)}, u32[]{:S(2)}) copy-start(f32[16,2048]{1,0:T(8,128)} %get-tuple-element.4) | copy-start | bytes 393220

commit v10 on v9

--- a/solution.py
+++ b/solution.py
@@ -21,7 +21,9 @@
 CONTEXT_STACK_ROWS = 256
 
 
-def attention_kernel(masks, normalize, packed, rows, group_size, kv_heads, stack_rows, *refs):
+def attention_kernel(
+    masks, normalize, packed, rows, group_size, kv_heads, stack_rows, merge_count, *refs
+):
     length_ref, q_ref = refs[0], refs[1]
     part_count = len(masks)
     kv_refs = refs[2 : 2 + 2 * part_count]
@@ -29,8 +31,10 @@
     if "pos" in masks:
         key_pos_ref, own_pos_ref = rest[0], rest[1]
         rest = rest[2:]
+    section_refs = rest[: 2 * merge_count]
+    rest = rest[2 * merge_count :]
     out_ref = rest[0]
-    side_ref = None if normalize or packed else rest[1]
+    side_ref = None if normalize or packed or merge_count else rest[1]
     query_width = kv_heads * group_size * HD
     scale = 1.0 / jnp.sqrt(jnp.float32(HD))
     stack = max(1, min(group_size, stack_rows // rows))
@@ -90,7 +94,30 @@
             output = part_output if output is None else output + part_output
         for slot, h in enumerate(heads):
             rows_of = slice(slot * rows, (slot + 1) * rows)
-            if normalize:
+            if merge_count:
+                peaks = [peak[rows_of]]
+                totals = [total[rows_of]]
+                outputs = [output[rows_of]]
+                for index in range(merge_count):
+                    section_o, section_side = section_refs[2 * index], section_refs[2 * index + 1]
+                    peaks.append(section_side[:, h : h + 1])
+                    totals.append(section_side[:, HD // 2 + h : HD // 2 + h + 1])
+                    outputs.append(section_o[:, h * HD : (h + 1) * HD])
+                top = peaks[0]
+                for value in peaks[1:]:
+                    top = jnp.maximum(top, value)
+                merged_total = None
+                merged_output = None
+                for value, part_total, part_output in zip(peaks, totals, outputs):
+                    factor = jnp.exp(value - top)
+                    t = part_total * factor
+                    o = part_output * factor
+                    merged_total = t if merged_total is None else merged_total + t
+                    merged_output = o if merged_output is None else merged_output + o
+                out_ref[:, h * HD : (h + 1) * HD] = (merged_output / merged_total).astype(
+                    out_ref.dtype
+                )
+            elif normalize:
                 out_ref[:, h * HD : (h + 1) * HD] = (output[rows_of] / total[rows_of]).astype(
                     out_ref.dtype
                 )
@@ -113,7 +140,14 @@
 
 
 def attention(
-    queries, parts, normalize, length=None, positions=None, packed=False, stack_rows=STACK_ROWS
+    queries,
+    parts,
+    normalize,
+    length=None,
+    positions=None,
+    packed=False,
+    stack_rows=STACK_ROWS,
+    sections=(),
 ):
     rows, query_width = queries.shape
     kv_heads = parts[0][0].shape[2] // HD
@@ -135,6 +169,13 @@
         in_specs.append(pl.BlockSpec(key_pos.shape, lambda g, n: (0, 0)))
         in_specs.append(pl.BlockSpec(own_pos.shape, lambda g, n: (0, 0)))
         operands += [key_pos, own_pos]
+    for section in sections:
+        side_block = query_width // HD
+        in_specs.append(pl.BlockSpec((rows, group_width), lambda g, n: (0, g)))
+        in_specs.append(pl.BlockSpec((rows, HD), lambda g, n, c=side_block: (0, c + g)))
+        operands += [section, section]
+    if sections:
+        normalize = True
     out_shape = [
         jax.ShapeDtypeStruct((rows, query_width), jnp.bfloat16 if normalize else jnp.float32)
     ]
@@ -148,7 +189,15 @@
         out_specs.append(pl.BlockSpec((pl.Squeezed(), rows, HD), lambda g, n: (g, 0, 0)))
     return pl.pallas_call(
         functools.partial(
-            attention_kernel, masks, normalize, packed, rows, group_size, kv_heads, stack_rows
+            attention_kernel,
+            masks,
+            normalize,
+            packed,
+            rows,
+            group_size,
+            kv_heads,
+            stack_rows,
+            len(sections),
         ),
         grid_spec=pltpu.PrefetchScalarGridSpec(
             num_scalar_prefetch=1,
@@ -203,42 +252,14 @@
         for k in range(1, ctx_count):
             rows = slice(k * own_count, (k + 1) * own_count)
             sections.append(shifted(context_packed[rows], -k, ctx_count))
-        remote = [
-            (
-                section[:, :query_width],
-                jnp.transpose(section[:, query_width:].reshape(own_count, kv_heads, HD), (1, 0, 2)),
-            )
-            for section in sections
-        ]
-
         (block_out,) = attention(q_block, [(anchor, None), (kv_block, "causal")], True)
-        local_output, local_side = attention(
+        (query_out,) = attention(
             query_q,
             [(anchor, None), (all_query_kv, "pos")],
             False,
             positions=(slot_pos, own_pos),
-        )
-
-        def per_head(side, first):
-            picked = side[:, :, first : first + group_size]
-            return jnp.transpose(picked, (1, 0, 2)).reshape(own_count, kv_heads * group_size)
-
-        parts = [(local_output, local_side)] + remote
-        peaks = [per_head(side, 0) for _, side in parts]
-        totals = [per_head(side, HD // 2) for _, side in parts]
-        outputs = [output for output, _ in parts]
-        top_score = peaks[0]
-        for peak in peaks[1:]:
-            top_score = jnp.maximum(top_score, peak)
-        merged_totals = None
-        merged_output = None
-        for peak, total, output in zip(peaks, totals, outputs):
-            factor = jnp.exp(peak - top_score)
-            t = total * factor
-            o = output * widen(factor)
-            merged_totals = t if merged_totals is None else merged_totals + t
-            merged_output = o if merged_output is None else merged_output + o
-        query_out = (merged_output / widen(merged_totals)).astype(jnp.bfloat16)
+            sections=sections,
+        )
         return (block_out, query_out)
 
     return local

time: 55.4 us -> 52.8 us (0.953)
  starting transfers between devices: 18 us -> 13.8 us
  waiting for transfers between devices: 0.02 us -> 4.09 us
  other arithmetic: 4.62 us -> 2.84 us
  local copies, waits for them, and re-layouts: 9.28 us -> 7.67 us
  Pallas kernels: 21.4 us -> 22.5 us
    ppermute x9, starting transfers between devices: 18 us -> 13.8 us  [shifted(): lax.ppermute(value, 'ctx', [(j, (j + shift) % count) for j in range(count)])]
    ppermute x9, waiting for transfers between devices: 0.02 us -> 4.09 us  [shifted(): lax.ppermute(value, 'ctx', [(j, (j + shift) % count) for j in range(count)])]
    convert_element_type x1 -> x0, other arithmetic: 1.81 us -> none  [local(): query_out = (merged_output / widen(merged_totals)).astype(jnp.bfloat16)]
    pallas_call x3, Pallas kernels: 21.4 us -> 22.5 us  [attention(): pl.pallas_call(functools.partial(attention_kernel, masks, normalize, pack...]
    transpose x3 -> x0, local copies, waits for them, and re-layouts: 1 us -> none  [per_head(): jnp.transpose(picked, (1, 0, 2)).reshape(own_count, kv_heads * group_size)]
    unnamed x12 -> x16, local copies, waits for them, and re-layouts: 3.35 us -> 4.11 us
    slice x1, local copies, waits for them, and re-layouts: 1.08 us -> 1.83 us  [local(): sections.append(shifted(context_packed[rows], -k, ctx_count))]
    slice x4 -> x0, local copies, waits for them, and re-layouts: 0.73 us -> none  [local(): section[:, query_width:].reshape(own_count, kv_heads, HD)]
  transfers between devices with their start and end apart: 9 -> 9, of which waited for: 0 -> 1; matrix products, arithmetic and copies ran while one was open for 16% -> 14% of each run, Pallas kernels for 39% -> 36%
where the time goes in v10:
time: 52.8 us; the launch traced here: 52.4 us
  Pallas kernels  22.5 us (43%)
  starting transfers between devices  13.8 us (26%)
  local copies, waits for them, and re-layouts  7.67 us (15%)
  waiting for transfers between devices  4.09 us (8%)
  other arithmetic  2.84 us (5%)
  between operations  1.5 us (3%)
    pallas_call x3, Pallas kernels, attention(): pl.pallas_call(functools.partial(attention_kernel, masks, normalize, pack...  22.5 us
    ppermute x9, starting transfers between devices, shifted(): lax.ppermute(value, 'ctx', [(j, (j + shift) % count) for j in range(count)])  13.8 us
    unnamed x16, local copies, waits for them, and re-layouts  4.11 us
    ppermute x9, waiting for transfers between devices, shifted(): lax.ppermute(value, 'ctx', [(j, (j + shift) % count) for j in range(count)])  4.09 us
    slice x1, local copies, waits for them, and re-layouts, local(): sections.append(shifted(context_packed[rows], -k, ctx_count))  1.83 us
    concatenate x1, other arithmetic, local(): jnp.concatenate([slot[:split].reshape(own_count, query_width) for slot in...  1.56 us
  transfers between devices with their start and end apart: 9, of which 1 were waited for; matrix products, arithmetic and copies ran while one was open for 14% of the time, Pallas kernels for 36%

profile of v10, /device:TPU:0, one launch (start us, length us, event | category | flops | bytes accessed | tf_op | source)
XLA Modules:
  0.0 52.4 jit_solution(15180440203984942365)
XLA Ops:
  0.6 0.9 %copy.11 = bf16[2,16,8,128]{3,1,2,0:T(8,128)(2,1)S(1)} copy(bf16[2,16,8,128]{3,2,1,0:T(8,128)(2,1)} %bitcast.7) | data formatting | bytes 131072
  1.5 0.7 %copy.12 = bf16[4,2,8,128]{3,1,2,0:T(2,128)(2,1)S(1)} copy(bf16[4,2,8,128]{3,2,1,0:T(8,128)(2,1)} %bitcast.10) | data formatting | bytes 32768
  2.2 5.1 %collective-permute-start.5 = (bf16[40960]{0:T(1024)(128)(2,1)S(1)}, bf16[40960]{0:T(1024)(128)(2,1)S(1)}, u32[]{:S(2)}, u32[]{:S(2)}) collective-permute-start(bf16[40960]{0:T(1024)(128)(2,1)S(1)} %constant_dynamic-update-slice_fusion.5), channel_id=1, source_target_pairs={{0,12},{4,0},{8,4},{12,8},{1,13},{5,1},{9,5},{13,9},{2,14},{6,2},{... | collective-permute-start | bytes 245768 | tf_op jit(solution)/shard_map/ppermute | solution.py:213
  7.3 0.0 collective-permute-start.3
  7.4 1.0 %collective-permute-start.4 = (bf16[40960]{0:T(1024)(128)(2,1)S(1)}, bf16[40960]{0:T(1024)(128)(2,1)S(1)}, u32[]{:S(2)}, u32[]{:S(2)}) collective-permute-start(bf16[40960]{0:T(1024)(128)(2,1)S(1)} %constant_dynamic-update-slice_fusion.5), channel_id=1, source_target_pairs={{0,8},{4,12},{8,0},{12,4},{1,9},{5,13},{9,1},{13,5},{2,10},{6,14},... | collective-permute-start | bytes 245768 | tf_op jit(solution)/shard_map/ppermute | solution.py:213
  8.4 3.4 %collective-permute-start = (bf16[2,128,256]{2,1,0:T(8,128)(2,1)}, bf16[2,128,256]{2,1,0:T(8,128)(2,1)S(1)}, u32[]{:S(2)}, u32[]{:S(2)}) collective-permute-start(bf16[2,128,256]{2,1,0:T(8,128)(2,1)} %param.10), channel_id=1, source_target_pairs={{0,4},{4,8},{8,12},{12,0},{1,5},{5,9},{9,13},{13,1},{2,6},{6,10},{... | collective-permute-start | bytes 393224 | tf_op jit(solution)/shard_map/ppermute | solution.py:213
  11.7 0.0 collective-permute-start.1
  11.7 1.0 %constant_dynamic-update-slice_fusion.3 = bf16[2,512,256]{2,1,0:T(8,128)(2,1)S(1)} fusion(bf16[2,128,256]{2,1,0:T(8,128)(2,1)} %param.10), kind=kLoop, calls=%fused_computation.5 | loop fusion | bytes 262144
  12.7 0.9 %fusion.1 = (s32[16]{0:T(128)S(1)}, s32[16]{0:T(128)S(1)}, s32[16]{0:T(128)S(1)}, s32[16]{0:T(128)S(1)}) fusion(s32[64]{0:T(128)} %param.15, s32[]{:T(128)S(6)} %select_n.32, s32[]{:T(128)S(6)} %select_n.34, s32[]{:T(128)S(6)} %select_n.38, s32[]{:T(128)S(6)} %select_n.36), kind=kLoop, calls=%fused_computation.10 | loop fusion | bytes 528 | tf_op jit(solution)/shard_map/dynamic_slice | solution.py:237
  13.6 0.7 %copy.10.refs_7_ = s32[16,1]{1,0:T(8,128)} copy(s32[16,1]{0,1:T(1,128)S(1)} %bitcast.11) | data formatting | bytes 128 | tf_op jit(solution)/shard_map/reshape | solution.py:168
  15.0 0.7 %add_bitcast_fusion.refs_6_ = s32[1,64]{1,0:T(1,128)} fusion(s32[16]{0:T(128)S(1)} %get-tuple-element.8, s32[16]{0:T(128)S(1)} %get-tuple-element.9, s32[16]{0:T(128)S(1)} %get-tuple-element.7, s32[16]{0:T(128)S(1)} %get-tuple-element.6), kind=kLoop, calls=%fused_computation.8 | loop fusion | flops 192 | bytes 512 | tf_op jit(solution)/shard_map/reshape | solution.py:167
  15.6 0.0 collective-permute-done.5
  15.6 2.3 %collective-permute-start.2 = (bf16[2,128,256]{2,1,0:T(8,128)(2,1)}, bf16[2,128,256]{2,1,0:T(8,128)(2,1)S(1)}, u32[]{:S(2)}, u32[]{:S(2)}) collective-permute-start(bf16[2,128,256]{2,1,0:T(8,128)(2,1)} %param.10), channel_id=1, source_target_pairs={{0,12},{4,0},{8,4},{12,8},{1,13},{5,1},{9,5},{13,9},{2,14},{6,2},{... | collective-permute-start | bytes 393224 | tf_op jit(solution)/shard_map/ppermute | solution.py:213
  18.0 0.0 collective-permute-done.3
  18.1 4.1 %collective-permute-done.4 = bf16[40960]{0:T(1024)(128)(2,1)S(1)} collective-permute-done((bf16[40960]{0:T(1024)(128)(2,1)S(1)}, bf16[40960]{0:T(1024)(128)(2,1)S(1)}, u32[]{:S(2)}, u32[]{:S(2)}) %collective-permute-start.4) | collective-permute-done | bytes 81952 | tf_op jit(solution)/shard_map/ppermute | solution.py:213
  22.2 1.6 %pad_maximum_fusion.refs_1_ = bf16[64,2048]{1,0:T(8,128)(2,1)} fusion(bf16[16,2048]{1,0:T(8,128)(2,1)S(1)} %slice.101, bf16[16,2048]{1,0:T(8,128)(2,1)S(1)} %slice.99, bf16[16,2048]{1,0:T(8,128)(2,1)S(1)} %slice.97, bf16[16,2048]{1,0:T(8,128)(2,1)} %refs_1_.3), kind=kLoop, calls=%fused_computation | loop fusion | flops 1048576 | bytes 524288 | tf_op jit(solution)/shard_map/concatenate | solution.py:228
  23.7 0.0 copy-start.4
  23.7 11.7 %shard_map.96 = f32[64,2304]{1,0:T(8,128)} custom-call(s32[1]{0:T(128)S(6)} %copy.17.refs_0_, bf16[64,2048]{1,0:T(8,128)(2,1)} %pad_maximum_fusion.refs_1_, bf16[2,4096,256]{2,1,0:T(8,128)(2,1)} %refs_3_.1, bf16[2,4096,256]{2,1,0:T(8,128)(2,1)} %refs_3_.1, bf16[2,256,256]{2,1,0:T(8,128)(2,1)} %refs_5_.3, bf16[2,256,256]{2,1,0:T(8,128)(2,1)} %refs_5_.3), custom_call_target="tpu_custom_call" | custom-call | tf_op jit(solution)/shard_map/pallas_call | solution.py:190
  35.5 1.8 %fusion = (f32[16,2304]{1,0:T(8,128)S(1)}, f32[16,2304]{1,0:T(8,128)S(1)}, f32[16,2304]{1,0:T(8,128)S(1)}, f32[16,2304]{1,0:T(8,128)}) fusion(f32[64,2304]{1,0:T(8,128)} %shard_map.96), kind=kLoop, calls=%fused_computation.9 | loop fusion | bytes 1179648 | tf_op jit(solution)/shard_map/slice | solution.py:254
  37.3 0.0 collective-permute-start.6
  37.3 0.0 collective-permute-start.7
  37.4 0.0 copy-done.4
  37.4 0.6 %pad_maximum_fusion.1.refs_4_.refs_5_ = bf16[2,64,256]{2,1,0:T(8,128)(2,1)} fusion(bf16[2,16,256]{2,1,0:T(8,128)(2,1)S(1)} %slice.95, bf16[2,16,256]{2,1,0:T(8,128)(2,1)S(1)} %slice.93, bf16[2,16,256]{2,1,0:T(8,128)(2,1)S(1)} %slice.91, bf16[2,16,256]{2,1,0:T(8,128)(2,1)S(1)} %copy-done.4), kind=kLoop, calls=%fused_computation.1 | loop fusion | flops 262144 | bytes 131072 | tf_op jit(solution)/shard_map/concatenate | solution.py:231
  38.0 0.0 collective-permute-done
  38.0 2.0 %collective-permute-start.8 = (f32[16,2304]{1,0:T(8,128)S(1)}, f32[16,2304]{1,0:T(8,128)S(1)}, u32[]{:S(2)}, u32[]{:S(2)}) collective-permute-start(f32[16,2304]{1,0:T(8,128)S(1)} %get-tuple-element.2), channel_id=1, source_target_pairs={{0,4},{4,8},{8,12},{12,0},{1,5},{5,9},{9,13},{13,1},{2,6},{6,10},{... | collective-permute-start | bytes 442376 | tf_op jit(solution)/shard_map/ppermute | solution.py:213
  40.0 0.0 collective-permute-done.1
  40.1 0.0 collective-permute-done.2
  40.1 0.0 copy-start
  40.1 0.8 %copy-done = bf16[2,512,256]{2,1,0:T(8,128)(2,1)} copy-done((bf16[2,512,256]{2,1,0:T(8,128)(2,1)}, bf16[2,512,256]{2,1,0:T(8,128)(2,1)S(1)}, u32[]{:S(2)}) %copy-start) | copy-done | bytes 524312
  40.9 7.0 %shard_map.95 = bf16[256,2048]{1,0:T(8,128)(2,1)} custom-call(s32[1]{0:T(128)} %constant.35.clone.1.refs_0_, bf16[256,2048]{1,0:T(8,128)(2,1)} %refs_1_.2, bf16[2,512,256]{2,1,0:T(8,128)(2,1)} %copy-done, bf16[2,512,256]{2,1,0:T(8,128)(2,1)} %copy-done, bf16[2,256,256]{2,1,0:T(8,128)(2,1)} %refs_5_.3, bf16[2,256,256]{2,1,0:T(8,128)(2,1)} %refs_5_.3), custom_call_target="tpu_custom_call" | custom-call | tf_op jit(solution)/shard_map/pallas_call | solution.py:190
  47.9 0.0 collective-permute-done.6.refs_10_.refs_11_
  47.9 0.0 copy-start.1
  47.9 0.0 collective-permute-done.7.refs_12_.refs_13_
  47.9 0.0 copy-start.2
  47.9 0.0 collective-permute-done.8.refs_14_.refs_15_
  48.0 0.0 copy-start.3
  48.0 0.6 %copy-done.1 = f32[16,2304]{1,0:T(8,128)} copy-done((f32[16,2304]{1,0:T(8,128)}, f32[16,2304]{1,0:T(8,128)S(1)}, u32[]{:S(2)}) %copy-start.1) | copy-done | bytes 147480
  48.6 0.0 copy-done.2
  48.6 0.1 copy-done.3
  48.7 3.7 %shard_map.97 = bf16[16,2048]{1,0:T(8,128)(2,1)} custom-call(s32[1]{0:T(128)} %constant.35.clone.1.refs_0_, bf16[16,2048]{1,0:T(8,128)(2,1)} %refs_1_.3, bf16[2,512,256]{2,1,0:T(8,128)(2,1)} %copy-done, bf16[2,512,256]{2,1,0:T(8,128)(2,1)} %copy-done, bf16[2,64,256]{2,1,0:T(8,128)(2,1)} %pad_maximum_fusion.1.refs_4_.refs_5_, ...), custom_call_target="tpu_custom_call" | custom-call | tf_op jit(solution)/shard_map/pallas_call | solution.py:190
  (17 shorter events, 0.2 us)
Async XLA Ops:
  2.2 13.4 %collective-permute-start.5 = (bf16[40960]{0:T(1024)(128)(2,1)S(1)}, bf16[40960]{0:T(1024)(128)(2,1)S(1)}, u32[]{:S(2)}, u32[]{:S(2)}) collective-permute-start(bf16[40960]{0:T(1024)(128)(2,1)S(1)} %constant_dynamic-update-slice_fusion.5), channel_id=1, source_target_pairs={{0,12},{4,0},{8,4},{12,8},{1,13},{5,1},{9,5},{13,9},{2,14},{6,2},{... | collective-permute-start | bytes 245768 | tf_op jit(solution)/shard_map/ppermute | solution.py:213
  7.3 10.6 %collective-permute-start.3 = (bf16[40960]{0:T(1024)(128)(2,1)S(1)}, bf16[40960]{0:T(1024)(128)(2,1)S(1)}, u32[]{:S(2)}, u32[]{:S(2)}) collective-permute-start(bf16[40960]{0:T(1024)(128)(2,1)S(1)} %constant_dynamic-update-slice_fusion.5), channel_id=1, source_target_pairs={{0,4},{4,8},{8,12},{12,0},{1,5},{5,9},{9,13},{13,1},{2,6},{6,10},{... | collective-permute-start | bytes 245768 | tf_op jit(solution)/shard_map/ppermute | solution.py:213
  7.4 14.8 %collective-permute-start.4 = (bf16[40960]{0:T(1024)(128)(2,1)S(1)}, bf16[40960]{0:T(1024)(128)(2,1)S(1)}, u32[]{:S(2)}, u32[]{:S(2)}) collective-permute-start(bf16[40960]{0:T(1024)(128)(2,1)S(1)} %constant_dynamic-update-slice_fusion.5), channel_id=1, source_target_pairs={{0,8},{4,12},{8,0},{12,4},{1,9},{5,13},{9,1},{13,5},{2,10},{6,14},... | collective-permute-start | bytes 245768 | tf_op jit(solution)/shard_map/ppermute | solution.py:213
  8.4 29.7 %collective-permute-start = (bf16[2,128,256]{2,1,0:T(8,128)(2,1)}, bf16[2,128,256]{2,1,0:T(8,128)(2,1)S(1)}, u32[]{:S(2)}, u32[]{:S(2)}) collective-permute-start(bf16[2,128,256]{2,1,0:T(8,128)(2,1)} %param.10), channel_id=1, source_target_pairs={{0,4},{4,8},{8,12},{12,0},{1,5},{5,9},{9,13},{13,1},{2,6},{6,10},{... | collective-permute-start | bytes 393224 | tf_op jit(solution)/shard_map/ppermute | solution.py:213
  11.7 28.3 %collective-permute-start.1 = (bf16[2,128,256]{2,1,0:T(8,128)(2,1)}, bf16[2,128,256]{2,1,0:T(8,128)(2,1)S(1)}, u32[]{:S(2)}, u32[]{:S(2)}) collective-permute-start(bf16[2,128,256]{2,1,0:T(8,128)(2,1)} %param.10), channel_id=1, source_target_pairs={{0,8},{4,12},{8,0},{12,4},{1,9},{5,13},{9,1},{13,5},{2,10},{6,14},... | collective-permute-start | bytes 393224 | tf_op jit(solution)/shard_map/ppermute | solution.py:213
  15.6 24.5 %collective-permute-start.2 = (bf16[2,128,256]{2,1,0:T(8,128)(2,1)}, bf16[2,128,256]{2,1,0:T(8,128)(2,1)S(1)}, u32[]{:S(2)}, u32[]{:S(2)}) collective-permute-start(bf16[2,128,256]{2,1,0:T(8,128)(2,1)} %param.10), channel_id=1, source_target_pairs={{0,12},{4,0},{8,4},{12,8},{1,13},{5,1},{9,5},{13,9},{2,14},{6,2},{... | collective-permute-start | bytes 393224 | tf_op jit(solution)/shard_map/ppermute | solution.py:213
  23.7 13.7 %copy-start.4 = (bf16[2,16,256]{2,1,0:T(8,128)(2,1)S(1)}, bf16[2,16,256]{2,1,0:T(8,128)(2,1)}, u32[]{:S(2)}) copy-start(bf16[2,16,256]{2,1,0:T(8,128)(2,1)} %param.14) | copy-start | bytes 49156
  37.3 10.6 %collective-permute-start.6 = (f32[16,2304]{1,0:T(8,128)S(1)}, f32[16,2304]{1,0:T(8,128)S(1)}, u32[]{:S(2)}, u32[]{:S(2)}) collective-permute-start(f32[16,2304]{1,0:T(8,128)S(1)} %get-tuple-element.4), channel_id=1, source_target_pairs={{0,12},{4,0},{8,4},{12,8},{1,13},{5,1},{9,5},{13,9},{2,14},{6,2},{... | collective-permute-start | bytes 442376 | tf_op jit(solution)/shard_map/ppermute | solution.py:213
  37.3 10.6 %collective-permute-start.7 = (f32[16,2304]{1,0:T(8,128)S(1)}, f32[16,2304]{1,0:T(8,128)S(1)}, u32[]{:S(2)}, u32[]{:S(2)}) collective-permute-start(f32[16,2304]{1,0:T(8,128)S(1)} %get-tuple-element.3), channel_id=1, source_target_pairs={{0,8},{4,12},{8,0},{12,4},{1,9},{5,13},{9,1},{13,5},{2,10},{6,14},... | collective-permute-start | bytes 442376 | tf_op jit(solution)/shard_map/ppermute | solution.py:213
  38.0 9.9 %collective-permute-start.8 = (f32[16,2304]{1,0:T(8,128)S(1)}, f32[16,2304]{1,0:T(8,128)S(1)}, u32[]{:S(2)}, u32[]{:S(2)}) collective-permute-start(f32[16,2304]{1,0:T(8,128)S(1)} %get-tuple-element.2), channel_id=1, source_target_pairs={{0,4},{4,8},{8,12},{12,0},{1,5},{5,9},{9,13},{13,1},{2,6},{6,10},{... | collective-permute-start | bytes 442376 | tf_op jit(solution)/shard_map/ppermute | solution.py:213
  40.1 0.8 %copy-start = (bf16[2,512,256]{2,1,0:T(8,128)(2,1)}, bf16[2,512,256]{2,1,0:T(8,128)(2,1)S(1)}, u32[]{:S(2)}) copy-start(bf16[2,512,256]{2,1,0:T(8,128)(2,1)S(1)} %constant_dynamic-update-slice_fusion.refs_2_.refs_3_) | copy-start | bytes 1572868
  47.9 0.7 %copy-start.1 = (f32[16,2304]{1,0:T(8,128)}, f32[16,2304]{1,0:T(8,128)S(1)}, u32[]{:S(2)}) copy-start(f32[16,2304]{1,0:T(8,128)S(1)} %collective-permute-done.6.refs_10_.refs_11_) | copy-start | bytes 442372
  47.9 0.7 %copy-start.2 = (f32[16,2304]{1,0:T(8,128)}, f32[16,2304]{1,0:T(8,128)S(1)}, u32[]{:S(2)}) copy-start(f32[16,2304]{1,0:T(8,128)S(1)} %collective-permute-done.7.refs_12_.refs_13_) | copy-start | bytes 442372
  48.0 0.7 %copy-start.3 = (f32[16,2304]{1,0:T(8,128)}, f32[16,2304]{1,0:T(8,128)S(1)}, u32[]{:S(2)}) copy-start(f32[16,2304]{1,0:T(8,128)S(1)} %collective-permute-done.8.refs_14_.refs_15_) | copy-start | bytes 442372

commit v11 on v10

--- a/solution.py
+++ b/solution.py
@@ -223,11 +223,12 @@
         group_size = query_width // HD // kv_heads
         packed = jnp.concatenate([query_q.reshape(-1), query_kv.reshape(-1)])
         query_slots = [packed] + [shifted(packed, k, ctx_count) for k in range(1, ctx_count)]
-        anchor_slots = [anchor_kv] + [shifted(anchor_kv, k, ctx_count) for k in range(1, ctx_count)]
         split = own_count * query_width
         all_queries = jnp.concatenate(
             [slot[:split].reshape(own_count, query_width) for slot in query_slots], axis=0
         )
+        anchor_kv, all_queries = lax.optimization_barrier((anchor_kv, all_queries))
+        anchor_slots = [anchor_kv] + [shifted(anchor_kv, k, ctx_count) for k in range(1, ctx_count)]
         all_query_kv = jnp.concatenate(
             [slot[split:].reshape(2, own_count, width) for slot in query_slots], axis=1
         )

time: 52.8 us -> 54.2 us (1.027)
  starting transfers between devices: 13.8 us -> 14.9 us
    ppermute x9, starting transfers between devices: 13.8 us -> 14.9 us  [shifted(): lax.ppermute(value, 'ctx', [(j, (j + shift) % count) for j in range(count)])]
  transfers between devices with their start and end apart: 9 -> 9, of which waited for: 1 -> 3; matrix products, arithmetic and copies ran while one was open for 14% -> 9% of each run, Pallas kernels for 36% -> 35%
where the time goes in v11:
time: 54.2 us; the launch traced here: 53.9 us
  Pallas kernels  22.5 us (42%)
  starting transfers between devices  14.9 us (27%)
  local copies, waits for them, and re-layouts  7.58 us (14%)
  waiting for transfers between devices  4.57 us (8%)
  other arithmetic  2.84 us (5%)
  between operations  1.44 us (3%)
    pallas_call x3, Pallas kernels, attention(): pl.pallas_call(functools.partial(attention_kernel, masks, normalize, pack...  22.5 us
    ppermute x9, starting transfers between devices, shifted(): lax.ppermute(value, 'ctx', [(j, (j + shift) % count) for j in range(count)])  14.9 us
    ppermute x9, waiting for transfers between devices, shifted(): lax.ppermute(value, 'ctx', [(j, (j + shift) % count) for j in range(count)])  4.57 us
    unnamed x16, local copies, waits for them, and re-layouts  4.03 us
    slice x1, local copies, waits for them, and re-layouts, local(): sections.append(shifted(context_packed[rows], -k, ctx_count))  1.83 us
    concatenate x1, other arithmetic, local(): jnp.concatenate([slot[:split].reshape(own_count, query_width) for slot in...  1.56 us
  transfers between devices with their start and end apart: 9, of which 3 were waited for; matrix products, arithmetic and copies ran while one was open for 9% of the time, Pallas kernels for 35%

profile of v11, /device:TPU:0, one launch (start us, length us, event | category | flops | bytes accessed | tf_op | source)
XLA Modules:
  0.0 53.9 jit_solution(6072483009489193949)
XLA Ops:
  0.6 0.9 %copy.11 = bf16[2,16,8,128]{3,1,2,0:T(8,128)(2,1)S(1)} copy(bf16[2,16,8,128]{3,2,1,0:T(8,128)(2,1)} %bitcast.7) | data formatting | bytes 131072
  1.5 0.7 %copy.12 = bf16[4,2,8,128]{3,1,2,0:T(2,128)(2,1)S(1)} copy(bf16[4,2,8,128]{3,2,1,0:T(8,128)(2,1)} %bitcast.10) | data formatting | bytes 32768
  2.2 3.1 %collective-permute-start = (bf16[40960]{0:T(1024)(128)(2,1)S(1)}, bf16[40960]{0:T(1024)(128)(2,1)S(1)}, u32[]{:S(2)}, u32[]{:S(2)}) collective-permute-start(bf16[40960]{0:T(1024)(128)(2,1)S(1)} %constant_dynamic-update-slice_fusion.5), channel_id=1, source_target_pairs={{0,4},{4,8},{8,12},{12,0},{1,5},{5,9},{9,13},{13,1},{2,6},{6,10},{... | collective-permute-start | bytes 245768 | tf_op jit(solution)/shard_map/ppermute | solution.py:213
  5.3 2.6 %collective-permute-start.1 = (bf16[40960]{0:T(1024)(128)(2,1)S(1)}, bf16[40960]{0:T(1024)(128)(2,1)S(1)}, u32[]{:S(2)}, u32[]{:S(2)}) collective-permute-start(bf16[40960]{0:T(1024)(128)(2,1)S(1)} %constant_dynamic-update-slice_fusion.5), channel_id=1, source_target_pairs={{0,8},{4,12},{8,0},{12,4},{1,9},{5,13},{9,1},{13,5},{2,10},{6,14},... | collective-permute-start | bytes 245768 | tf_op jit(solution)/shard_map/ppermute | solution.py:213
  7.9 1.3 %collective-permute-start.2 = (bf16[40960]{0:T(1024)(128)(2,1)S(1)}, bf16[40960]{0:T(1024)(128)(2,1)S(1)}, u32[]{:S(2)}, u32[]{:S(2)}) collective-permute-start(bf16[40960]{0:T(1024)(128)(2,1)S(1)} %constant_dynamic-update-slice_fusion.5), channel_id=1, source_target_pairs={{0,12},{4,0},{8,4},{12,8},{1,13},{5,1},{9,5},{13,9},{2,14},{6,2},{... | collective-permute-start | bytes 245768 | tf_op jit(solution)/shard_map/ppermute | solution.py:213
  9.3 0.9 %fusion.1 = (s32[16]{0:T(128)S(1)}, s32[16]{0:T(128)S(1)}, s32[16]{0:T(128)S(1)}, s32[16]{0:T(128)S(1)}) fusion(s32[64]{0:T(128)} %param.15, s32[]{:T(128)S(6)} %select_n.32, s32[]{:T(128)S(6)} %select_n.34, s32[]{:T(128)S(6)} %select_n.38, s32[]{:T(128)S(6)} %select_n.36), kind=kLoop, calls=%fused_computation.10 | loop fusion | bytes 528 | tf_op jit(solution)/shard_map/dynamic_slice | solution.py:238
  10.1 0.7 %copy.10.refs_7_ = s32[16,1]{1,0:T(8,128)} copy(s32[16,1]{0,1:T(1,128)S(1)} %bitcast.11) | data formatting | bytes 128 | tf_op jit(solution)/shard_map/reshape | solution.py:168
  11.5 0.7 %add_bitcast_fusion.refs_6_ = s32[1,64]{1,0:T(1,128)} fusion(s32[16]{0:T(128)S(1)} %get-tuple-element.12, s32[16]{0:T(128)S(1)} %get-tuple-element.13, s32[16]{0:T(128)S(1)} %get-tuple-element.11, s32[16]{0:T(128)S(1)} %get-tuple-element.10), kind=kLoop, calls=%fused_computation.8 | loop fusion | flops 192 | bytes 512 | tf_op jit(solution)/shard_map/reshape | solution.py:167
  12.1 0.0 collective-permute-done
  12.2 1.2 %collective-permute-done.1 = bf16[40960]{0:T(1024)(128)(2,1)S(1)} collective-permute-done((bf16[40960]{0:T(1024)(128)(2,1)S(1)}, bf16[40960]{0:T(1024)(128)(2,1)S(1)}, u32[]{:S(2)}, u32[]{:S(2)}) %collective-permute-start.1) | collective-permute-done | bytes 81952 | tf_op jit(solution)/shard_map/ppermute | solution.py:213
  13.4 0.2 collective-permute-done.2
  13.7 1.6 %pad_maximum_fusion.refs_1_ = bf16[64,2048]{1,0:T(8,128)(2,1)} fusion(bf16[16,2048]{1,0:T(8,128)(2,1)S(1)} %slice.95, bf16[16,2048]{1,0:T(8,128)(2,1)S(1)} %slice.93, bf16[16,2048]{1,0:T(8,128)(2,1)S(1)} %slice.91, bf16[16,2048]{1,0:T(8,128)(2,1)} %refs_1_.3), kind=kLoop, calls=%fused_computation | loop fusion | flops 1048576 | bytes 524288 | tf_op jit(solution)/shard_map/concatenate | solution.py:227
  15.2 0.9 %constant_dynamic-update-slice_fusion.4 = bf16[2,512,256]{2,1,0:T(8,128)(2,1)S(1)} fusion(bf16[2,128,256]{2,1,0:T(8,128)(2,1)} %param.10), kind=kLoop, calls=%fused_computation.6 | loop fusion | bytes 262144
  16.1 0.0 copy-start.4
  16.1 2.1 %collective-permute-start.3 = (bf16[2,128,256]{2,1,0:T(8,128)(2,1)}, bf16[2,128,256]{2,1,0:T(8,128)(2,1)S(1)}, u32[]{:S(2)}, u32[]{:S(2)}) collective-permute-start(bf16[2,128,256]{2,1,0:T(8,128)(2,1)} %param.10), channel_id=1, source_target_pairs={{0,4},{4,8},{8,12},{12,0},{1,5},{5,9},{9,13},{13,1},{2,6},{6,10},{... | collective-permute-start | bytes 393224 | tf_op jit(solution)/shard_map/ppermute | solution.py:213
  18.2 1.9 %collective-permute-start.4 = (bf16[2,128,256]{2,1,0:T(8,128)(2,1)}, bf16[2,128,256]{2,1,0:T(8,128)(2,1)S(1)}, u32[]{:S(2)}, u32[]{:S(2)}) collective-permute-start(bf16[2,128,256]{2,1,0:T(8,128)(2,1)} %param.10), channel_id=1, source_target_pairs={{0,8},{4,12},{8,0},{12,4},{1,9},{5,13},{9,1},{13,5},{2,10},{6,14},... | collective-permute-start | bytes 393224 | tf_op jit(solution)/shard_map/ppermute | solution.py:213
  20.1 0.6 %collective-permute-start.5 = (bf16[2,128,256]{2,1,0:T(8,128)(2,1)}, bf16[2,128,256]{2,1,0:T(8,128)(2,1)S(1)}, u32[]{:S(2)}, u32[]{:S(2)}) collective-permute-start(bf16[2,128,256]{2,1,0:T(8,128)(2,1)} %param.10), channel_id=1, source_target_pairs={{0,12},{4,0},{8,4},{12,8},{1,13},{5,1},{9,5},{13,9},{2,14},{6,2},{... | collective-permute-start | bytes 393224 | tf_op jit(solution)/shard_map/ppermute | solution.py:213
  20.8 11.7 %shard_map.96 = f32[64,2304]{1,0:T(8,128)} custom-call(s32[1]{0:T(128)S(6)} %copy.17.refs_0_, bf16[64,2048]{1,0:T(8,128)(2,1)} %pad_maximum_fusion.refs_1_, bf16[2,4096,256]{2,1,0:T(8,128)(2,1)} %refs_3_.1, bf16[2,4096,256]{2,1,0:T(8,128)(2,1)} %refs_3_.1, bf16[2,256,256]{2,1,0:T(8,128)(2,1)} %refs_5_.3, bf16[2,256,256]{2,1,0:T(8,128)(2,1)} %refs_5_.3), custom_call_target="tpu_custom_call" | custom-call | tf_op jit(solution)/shard_map/pallas_call | solution.py:190
  32.5 1.8 %fusion = (f32[16,2304]{1,0:T(8,128)S(1)}, f32[16,2304]{1,0:T(8,128)S(1)}, f32[16,2304]{1,0:T(8,128)S(1)}, f32[16,2304]{1,0:T(8,128)}) fusion(f32[64,2304]{1,0:T(8,128)} %shard_map.96), kind=kLoop, calls=%fused_computation.9 | loop fusion | bytes 1179648 | tf_op jit(solution)/shard_map/slice | solution.py:255
  34.3 1.8 %collective-permute-start.6 = (f32[16,2304]{1,0:T(8,128)S(1)}, f32[16,2304]{1,0:T(8,128)S(1)}, u32[]{:S(2)}, u32[]{:S(2)}) collective-permute-start(f32[16,2304]{1,0:T(8,128)S(1)} %get-tuple-element.8), channel_id=1, source_target_pairs={{0,12},{4,0},{8,4},{12,8},{1,13},{5,1},{9,5},{13,9},{2,14},{6,2},{... | collective-permute-start | bytes 442376 | tf_op jit(solution)/shard_map/ppermute | solution.py:213
  36.1 1.0 %collective-permute-start.7 = (f32[16,2304]{1,0:T(8,128)S(1)}, f32[16,2304]{1,0:T(8,128)S(1)}, u32[]{:S(2)}, u32[]{:S(2)}) collective-permute-start(f32[16,2304]{1,0:T(8,128)S(1)} %get-tuple-element.7), channel_id=1, source_target_pairs={{0,8},{4,12},{8,0},{12,4},{1,9},{5,13},{9,1},{13,5},{2,10},{6,14},... | collective-permute-start | bytes 442376 | tf_op jit(solution)/shard_map/ppermute | solution.py:213
  37.2 0.0 copy-done.4
  37.2 0.6 %pad_maximum_fusion.1.refs_4_.refs_5_ = bf16[2,64,256]{2,1,0:T(8,128)(2,1)} fusion(bf16[2,16,256]{2,1,0:T(8,128)(2,1)S(1)} %slice.101, bf16[2,16,256]{2,1,0:T(8,128)(2,1)S(1)} %slice.99, bf16[2,16,256]{2,1,0:T(8,128)(2,1)S(1)} %slice.97, bf16[2,16,256]{2,1,0:T(8,128)(2,1)S(1)} %copy-done.4), kind=kLoop, calls=%fused_computation.1 | loop fusion | flops 262144 | bytes 131072 | tf_op jit(solution)/shard_map/concatenate | solution.py:232
  37.9 0.0 collective-permute-done.3
  37.9 0.5 collective-permute-start.8
  38.4 0.0 collective-permute-done.4
  38.4 0.0 collective-permute-done.5
  38.4 0.0 copy-start
  38.4 0.8 %copy-done = bf16[2,512,256]{2,1,0:T(8,128)(2,1)} copy-done((bf16[2,512,256]{2,1,0:T(8,128)(2,1)}, bf16[2,512,256]{2,1,0:T(8,128)(2,1)S(1)}, u32[]{:S(2)}) %copy-start) | copy-done | bytes 524312
  39.2 7.0 %shard_map.95 = bf16[256,2048]{1,0:T(8,128)(2,1)} custom-call(s32[1]{0:T(128)} %constant.35.clone.1.refs_0_, bf16[256,2048]{1,0:T(8,128)(2,1)} %refs_1_.2, bf16[2,512,256]{2,1,0:T(8,128)(2,1)} %copy-done, bf16[2,512,256]{2,1,0:T(8,128)(2,1)} %copy-done, bf16[2,256,256]{2,1,0:T(8,128)(2,1)} %refs_5_.3, bf16[2,256,256]{2,1,0:T(8,128)(2,1)} %refs_5_.3), custom_call_target="tpu_custom_call" | custom-call | tf_op jit(solution)/shard_map/pallas_call | solution.py:190
  46.2 0.0 collective-permute-done.6.refs_10_.refs_11_
  46.2 0.0 copy-start.1
  46.2 3.2 %collective-permute-done.7.refs_12_.refs_13_ = f32[16,2304]{1,0:T(8,128)S(1)} collective-permute-done((f32[16,2304]{1,0:T(8,128)S(1)}, f32[16,2304]{1,0:T(8,128)S(1)}, u32[]{:S(2)}, u32[]{:S(2)}) %collective-permute-start.7) | collective-permute-done | bytes 147488 | tf_op jit(solution)/shard_map/ppermute | solution.py:213
  49.4 0.0 copy-start.2
  49.4 0.0 collective-permute-done.8.refs_14_.refs_15_
  49.4 0.0 copy-start.3
  49.4 0.0 copy-done.1
  49.4 0.6 %copy-done.2 = f32[16,2304]{1,0:T(8,128)} copy-done((f32[16,2304]{1,0:T(8,128)}, f32[16,2304]{1,0:T(8,128)S(1)}, u32[]{:S(2)}) %copy-start.2) | copy-done | bytes 147480
  50.0 0.1 copy-done.3
  50.1 3.7 %shard_map.97 = bf16[16,2048]{1,0:T(8,128)(2,1)} custom-call(s32[1]{0:T(128)} %constant.35.clone.1.refs_0_, bf16[16,2048]{1,0:T(8,128)(2,1)} %refs_1_.3, bf16[2,512,256]{2,1,0:T(8,128)(2,1)} %copy-done, bf16[2,512,256]{2,1,0:T(8,128)(2,1)} %copy-done, bf16[2,64,256]{2,1,0:T(8,128)(2,1)} %pad_maximum_fusion.1.refs_4_.refs_5_, ...), custom_call_target="tpu_custom_call" | custom-call | tf_op jit(solution)/shard_map/pallas_call | solution.py:190
  (17 shorter events, 0.2 us)
Async XLA Ops:
  2.2 9.9 %collective-permute-start = (bf16[40960]{0:T(1024)(128)(2,1)S(1)}, bf16[40960]{0:T(1024)(128)(2,1)S(1)}, u32[]{:S(2)}, u32[]{:S(2)}) collective-permute-start(bf16[40960]{0:T(1024)(128)(2,1)S(1)} %constant_dynamic-update-slice_fusion.5), channel_id=1, source_target_pairs={{0,4},{4,8},{8,12},{12,0},{1,5},{5,9},{9,13},{13,1},{2,6},{6,10},{... | collective-permute-start | bytes 245768 | tf_op jit(solution)/shard_map/ppermute | solution.py:213
  5.3 8.1 %collective-permute-start.1 = (bf16[40960]{0:T(1024)(128)(2,1)S(1)}, bf16[40960]{0:T(1024)(128)(2,1)S(1)}, u32[]{:S(2)}, u32[]{:S(2)}) collective-permute-start(bf16[40960]{0:T(1024)(128)(2,1)S(1)} %constant_dynamic-update-slice_fusion.5), channel_id=1, source_target_pairs={{0,8},{4,12},{8,0},{12,4},{1,9},{5,13},{9,1},{13,5},{2,10},{6,14},... | collective-permute-start | bytes 245768 | tf_op jit(solution)/shard_map/ppermute | solution.py:213
  7.9 5.7 %collective-permute-start.2 = (bf16[40960]{0:T(1024)(128)(2,1)S(1)}, bf16[40960]{0:T(1024)(128)(2,1)S(1)}, u32[]{:S(2)}, u32[]{:S(2)}) collective-permute-start(bf16[40960]{0:T(1024)(128)(2,1)S(1)} %constant_dynamic-update-slice_fusion.5), channel_id=1, source_target_pairs={{0,12},{4,0},{8,4},{12,8},{1,13},{5,1},{9,5},{13,9},{2,14},{6,2},{... | collective-permute-start | bytes 245768 | tf_op jit(solution)/shard_map/ppermute | solution.py:213
  16.1 21.1 %copy-start.4 = (bf16[2,16,256]{2,1,0:T(8,128)(2,1)S(1)}, bf16[2,16,256]{2,1,0:T(8,128)(2,1)}, u32[]{:S(2)}) copy-start(bf16[2,16,256]{2,1,0:T(8,128)(2,1)} %param.14) | copy-start | bytes 49156
  16.1 21.7 %collective-permute-start.3 = (bf16[2,128,256]{2,1,0:T(8,128)(2,1)}, bf16[2,128,256]{2,1,0:T(8,128)(2,1)S(1)}, u32[]{:S(2)}, u32[]{:S(2)}) collective-permute-start(bf16[2,128,256]{2,1,0:T(8,128)(2,1)} %param.10), channel_id=1, source_target_pairs={{0,4},{4,8},{8,12},{12,0},{1,5},{5,9},{9,13},{13,1},{2,6},{6,10},{... | collective-permute-start | bytes 393224 | tf_op jit(solution)/shard_map/ppermute | solution.py:213
  18.2 20.2 %collective-permute-start.4 = (bf16[2,128,256]{2,1,0:T(8,128)(2,1)}, bf16[2,128,256]{2,1,0:T(8,128)(2,1)S(1)}, u32[]{:S(2)}, u32[]{:S(2)}) collective-permute-start(bf16[2,128,256]{2,1,0:T(8,128)(2,1)} %param.10), channel_id=1, source_target_pairs={{0,8},{4,12},{8,0},{12,4},{1,9},{5,13},{9,1},{13,5},{2,10},{6,14},... | collective-permute-start | bytes 393224 | tf_op jit(solution)/shard_map/ppermute | solution.py:213
  20.1 18.3 %collective-permute-start.5 = (bf16[2,128,256]{2,1,0:T(8,128)(2,1)}, bf16[2,128,256]{2,1,0:T(8,128)(2,1)S(1)}, u32[]{:S(2)}, u32[]{:S(2)}) collective-permute-start(bf16[2,128,256]{2,1,0:T(8,128)(2,1)} %param.10), channel_id=1, source_target_pairs={{0,12},{4,0},{8,4},{12,8},{1,13},{5,1},{9,5},{13,9},{2,14},{6,2},{... | collective-permute-start | bytes 393224 | tf_op jit(solution)/shard_map/ppermute | solution.py:213
  34.3 11.9 %collective-permute-start.6 = (f32[16,2304]{1,0:T(8,128)S(1)}, f32[16,2304]{1,0:T(8,128)S(1)}, u32[]{:S(2)}, u32[]{:S(2)}) collective-permute-start(f32[16,2304]{1,0:T(8,128)S(1)} %get-tuple-element.8), channel_id=1, source_target_pairs={{0,12},{4,0},{8,4},{12,8},{1,13},{5,1},{9,5},{13,9},{2,14},{6,2},{... | collective-permute-start | bytes 442376 | tf_op jit(solution)/shard_map/ppermute | solution.py:213
  36.1 13.2 %collective-permute-start.7 = (f32[16,2304]{1,0:T(8,128)S(1)}, f32[16,2304]{1,0:T(8,128)S(1)}, u32[]{:S(2)}, u32[]{:S(2)}) collective-permute-start(f32[16,2304]{1,0:T(8,128)S(1)} %get-tuple-element.7), channel_id=1, source_target_pairs={{0,8},{4,12},{8,0},{12,4},{1,9},{5,13},{9,1},{13,5},{2,10},{6,14},... | collective-permute-start | bytes 442376 | tf_op jit(solution)/shard_map/ppermute | solution.py:213
  37.9 11.5 %collective-permute-start.8 = (f32[16,2304]{1,0:T(8,128)S(1)}, f32[16,2304]{1,0:T(8,128)S(1)}, u32[]{:S(2)}, u32[]{:S(2)}) collective-permute-start(f32[16,2304]{1,0:T(8,128)S(1)} %get-tuple-element.6), channel_id=1, source_target_pairs={{0,4},{4,8},{8,12},{12,0},{1,5},{5,9},{9,13},{13,1},{2,6},{6,10},{... | collective-permute-start | bytes 442376 | tf_op jit(solution)/shard_map/ppermute | solution.py:213
  38.4 0.8 %copy-start = (bf16[2,512,256]{2,1,0:T(8,128)(2,1)}, bf16[2,512,256]{2,1,0:T(8,128)(2,1)S(1)}, u32[]{:S(2)}) copy-start(bf16[2,512,256]{2,1,0:T(8,128)(2,1)S(1)} %constant_dynamic-update-slice_fusion.1.refs_2_.refs_3_) | copy-start | bytes 1572868
  46.2 3.2 %copy-start.1 = (f32[16,2304]{1,0:T(8,128)}, f32[16,2304]{1,0:T(8,128)S(1)}, u32[]{:S(2)}) copy-start(f32[16,2304]{1,0:T(8,128)S(1)} %collective-permute-done.6.refs_10_.refs_11_) | copy-start | bytes 442372
  49.4 0.7 %copy-start.2 = (f32[16,2304]{1,0:T(8,128)}, f32[16,2304]{1,0:T(8,128)S(1)}, u32[]{:S(2)}) copy-start(f32[16,2304]{1,0:T(8,128)S(1)} %collective-permute-done.7.refs_12_.refs_13_) | copy-start | bytes 442372
  49.4 0.7 %copy-start.3 = (f32[16,2304]{1,0:T(8,128)}, f32[16,2304]{1,0:T(8,128)S(1)}, u32[]{:S(2)}) copy-start(f32[16,2304]{1,0:T(8,128)S(1)} %collective-permute-done.8.refs_14_.refs_15_) | copy-start | bytes 442372

commit v12 on v10

--- a/solution.py
+++ b/solution.py
@@ -221,15 +221,16 @@
         query_width = query_q.shape[1]
         kv_heads = width // HD
         group_size = query_width // HD // kv_heads
-        packed = jnp.concatenate([query_q.reshape(-1), query_kv.reshape(-1)])
+        packed = jnp.concatenate([query_q, query_kv[0], query_kv[1]], axis=1)
         query_slots = [packed] + [shifted(packed, k, ctx_count) for k in range(1, ctx_count)]
         anchor_slots = [anchor_kv] + [shifted(anchor_kv, k, ctx_count) for k in range(1, ctx_count)]
-        split = own_count * query_width
-        all_queries = jnp.concatenate(
-            [slot[:split].reshape(own_count, query_width) for slot in query_slots], axis=0
-        )
-        all_query_kv = jnp.concatenate(
-            [slot[split:].reshape(2, own_count, width) for slot in query_slots], axis=1
+        all_rows = jnp.concatenate(query_slots, axis=0)
+        all_queries = all_rows[:, :query_width]
+        all_query_kv = jnp.stack(
+            [
+                all_rows[:, query_width : query_width + width],
+                all_rows[:, query_width + width :],
+            ]
         )
         anchor = jnp.concatenate(anchor_slots, axis=1)
         slot_pos = jnp.concatenate(

time: 52.8 us -> 55.7 us (1.055)
  starting transfers between devices: 13.8 us -> 16.6 us
  local copies, waits for them, and re-layouts: 7.67 us -> 6.55 us
  other arithmetic: 2.84 us -> 3.67 us
    ppermute x9, starting transfers between devices: 13.8 us -> 16.6 us  [shifted(): lax.ppermute(value, 'ctx', [(j, (j + shift) % count) for j in range(count)])]
    unnamed x16 -> x13, local copies, waits for them, and re-layouts: 4.11 us -> 2.45 us
    squeeze x0 -> x1, local copies, waits for them, and re-layouts: none -> 0.72 us  [local(): packed = jnp.concatenate([query_q, query_kv[0], query_kv[1]], axis=1)]
    another operation x0 -> x2, other arithmetic: none -> 0.63 us  [local(): jnp.stack([all_rows[:, query_width:query_width + width], all_rows[:, quer...]
  transfers between devices with their start and end apart: 9 -> 9, of which waited for: 1 -> 1; matrix products, arithmetic and copies ran while one was open for 14% -> 13% of each run, Pallas kernels for 36% -> 34%
where the time goes in v12:
time: 55.7 us; the launch traced here: 55.4 us
  Pallas kernels  22.5 us (40%)
  starting transfers between devices  16.6 us (30%)
  local copies, waits for them, and re-layouts  6.55 us (12%)
  waiting for transfers between devices  4.61 us (8%)
  other arithmetic  3.67 us (7%)
  between operations  1.38 us (2%)
    pallas_call x3, Pallas kernels, attention(): pl.pallas_call(functools.partial(attention_kernel, masks, normalize, pack...  22.5 us
    ppermute x9, starting transfers between devices, shifted(): lax.ppermute(value, 'ctx', [(j, (j + shift) % count) for j in range(count)])  16.6 us
    ppermute x9, waiting for transfers between devices, shifted(): lax.ppermute(value, 'ctx', [(j, (j + shift) % count) for j in range(count)])  4.61 us
    unnamed x13, local copies, waits for them, and re-layouts  2.45 us
    slice x1, local copies, waits for them, and re-layouts, local(): sections.append(shifted(context_packed[rows], -k, ctx_count))  1.81 us
    concatenate x1, other arithmetic, local(): all_rows = jnp.concatenate(query_slots, axis=0)  1.55 us
  transfers between devices with their start and end apart: 9, of which 1 were waited for; matrix products, arithmetic and copies ran while one was open for 13% of the time, Pallas kernels for 34%

profile of v12, /device:TPU:0, one launch (start us, length us, event | category | flops | bytes accessed | tf_op | source)
XLA Modules:
  0.0 55.4 jit_solution(9714284557162169462)
XLA Ops:
  0.6 0.7 %slice_bitcast_fusion.1 = (bf16[16,256]{1,0:T(8,128)(2,1)S(1)}, bf16[16,256]{1,0:T(8,128)(2,1)S(1)}) fusion(bf16[2,16,256]{2,1,0:T(8,128)(2,1)} %param.14), kind=kLoop, calls=%fused_computation.14 | loop fusion | bytes 32768 | tf_op jit(solution)/shard_map/squeeze | solution.py:224
  1.3 0.8 %pad_maximum_fusion.5 = bf16[16,2560]{1,0:T(8,128)(2,1)S(1)} fusion(bf16[16,256]{1,0:T(8,128)(2,1)S(1)} %get-tuple-element.9, bf16[16,256]{1,0:T(8,128)(2,1)S(1)} %get-tuple-element.8, bf16[16,2048]{1,0:T(8,128)(2,1)} %refs_1_.3), kind=kLoop, calls=%fused_computation.5 | loop fusion | flops 245760 | bytes 163840 | tf_op jit(solution)/shard_map/concatenate | solution.py:224
  2.2 3.0 %collective-permute-start.3 = (bf16[16,2560]{1,0:T(8,128)(2,1)S(1)}, bf16[16,2560]{1,0:T(8,128)(2,1)S(1)}, u32[]{:S(2)}, u32[]{:S(2)}) collective-permute-start(bf16[16,2560]{1,0:T(8,128)(2,1)S(1)} %pad_maximum_fusion.5), channel_id=1, source_target_pairs={{0,4},{4,8},{8,12},{12,0},{1,5},{5,9},{9,13},{13,1},{2,6},{6,10},{... | collective-permute-start | bytes 245768 | tf_op jit(solution)/shard_map/ppermute | solution.py:213
  5.2 2.6 %collective-permute-start.4 = (bf16[16,2560]{1,0:T(8,128)(2,1)S(1)}, bf16[16,2560]{1,0:T(8,128)(2,1)S(1)}, u32[]{:S(2)}, u32[]{:S(2)}) collective-permute-start(bf16[16,2560]{1,0:T(8,128)(2,1)S(1)} %pad_maximum_fusion.5), channel_id=1, source_target_pairs={{0,8},{4,12},{8,0},{12,4},{1,9},{5,13},{9,1},{13,5},{2,10},{6,14},... | collective-permute-start | bytes 245768 | tf_op jit(solution)/shard_map/ppermute | solution.py:213
  7.8 1.3 %collective-permute-start.5 = (bf16[16,2560]{1,0:T(8,128)(2,1)S(1)}, bf16[16,2560]{1,0:T(8,128)(2,1)S(1)}, u32[]{:S(2)}, u32[]{:S(2)}) collective-permute-start(bf16[16,2560]{1,0:T(8,128)(2,1)S(1)} %pad_maximum_fusion.5), channel_id=1, source_target_pairs={{0,12},{4,0},{8,4},{12,8},{1,13},{5,1},{9,5},{13,9},{2,14},{6,2},{... | collective-permute-start | bytes 245768 | tf_op jit(solution)/shard_map/ppermute | solution.py:213
  9.2 0.7 %collective-permute-start = (bf16[2,128,256]{2,1,0:T(8,128)(2,1)}, bf16[2,128,256]{2,1,0:T(8,128)(2,1)S(1)}, u32[]{:S(2)}, u32[]{:S(2)}) collective-permute-start(bf16[2,128,256]{2,1,0:T(8,128)(2,1)} %param.10), channel_id=1, source_target_pairs={{0,4},{4,8},{8,12},{12,0},{1,5},{5,9},{9,13},{13,1},{2,6},{6,10},{... | collective-permute-start | bytes 393224 | tf_op jit(solution)/shard_map/ppermute | solution.py:213
  9.8 0.3 collective-permute-start.1
  10.2 0.9 %constant_dynamic-update-slice_fusion.3 = bf16[2,512,256]{2,1,0:T(8,128)(2,1)S(1)} fusion(bf16[2,128,256]{2,1,0:T(8,128)(2,1)} %param.10), kind=kLoop, calls=%fused_computation.12 | loop fusion | bytes 262144
  11.1 0.9 %fusion.1 = (s32[16]{0:T(128)S(1)}, s32[16]{0:T(128)S(1)}, s32[16]{0:T(128)S(1)}, s32[16]{0:T(128)S(1)}) fusion(s32[64]{0:T(128)} %param.15, s32[]{:T(128)S(6)} %select_n.32, s32[]{:T(128)S(6)} %select_n.34, s32[]{:T(128)S(6)} %select_n.38, s32[]{:T(128)S(6)} %select_n.36), kind=kLoop, calls=%fused_computation.17 | loop fusion | bytes 528 | tf_op jit(solution)/shard_map/dynamic_slice | solution.py:238
  12.0 0.7 %copy.10.refs_7_ = s32[16,1]{1,0:T(8,128)} copy(s32[16,1]{0,1:T(1,128)S(1)} %bitcast.11) | data formatting | bytes 128 | tf_op jit(solution)/shard_map/reshape | solution.py:168
  13.4 0.7 %add_bitcast_fusion.refs_6_ = s32[1,64]{1,0:T(1,128)} fusion(s32[16]{0:T(128)S(1)} %get-tuple-element.12, s32[16]{0:T(128)S(1)} %get-tuple-element.13, s32[16]{0:T(128)S(1)} %get-tuple-element.11, s32[16]{0:T(128)S(1)} %get-tuple-element.10), kind=kLoop, calls=%fused_computation.15 | loop fusion | flops 192 | bytes 512 | tf_op jit(solution)/shard_map/reshape | solution.py:167
  14.0 0.0 collective-permute-done.3
  14.0 2.8 %collective-permute-start.2 = (bf16[2,128,256]{2,1,0:T(8,128)(2,1)}, bf16[2,128,256]{2,1,0:T(8,128)(2,1)S(1)}, u32[]{:S(2)}, u32[]{:S(2)}) collective-permute-start(bf16[2,128,256]{2,1,0:T(8,128)(2,1)} %param.10), channel_id=1, source_target_pairs={{0,12},{4,0},{8,4},{12,8},{1,13},{5,1},{9,5},{13,9},{2,14},{6,2},{... | collective-permute-start | bytes 393224 | tf_op jit(solution)/shard_map/ppermute | solution.py:213
  16.9 0.0 collective-permute-done.4
  16.9 0.0 collective-permute-done.5
  16.9 1.5 %pad_maximum_fusion.refs_1_ = bf16[64,2048]{1,0:T(8,128)(2,1)} fusion(bf16[16,2560]{1,0:T(8,128)(2,1)S(1)} %collective-permute-done.5, bf16[16,2560]{1,0:T(8,128)(2,1)S(1)} %collective-permute-done.4, bf16[16,2560]{1,0:T(8,128)(2,1)S(1)} %collective-permute-done.3, bf16[16,256]{1,0:T(8,128)(2,1)S(1)} %get-tuple-element.9, ...), kind=kLoop, calls=%fused_computation | loop fusion | flops 1572864 | bytes 589824 | tf_op jit(solution)/shard_map/concatenate | solution.py:227
  18.4 0.0 copy-start.1
  18.4 11.8 %shard_map.96 = f32[64,2304]{1,0:T(8,128)} custom-call(s32[1]{0:T(128)S(6)} %copy.14.refs_0_, bf16[64,2048]{1,0:T(8,128)(2,1)} %pad_maximum_fusion.refs_1_, bf16[2,4096,256]{2,1,0:T(8,128)(2,1)} %refs_3_.1, bf16[2,4096,256]{2,1,0:T(8,128)(2,1)} %refs_3_.1, bf16[2,256,256]{2,1,0:T(8,128)(2,1)} %refs_5_.3, bf16[2,256,256]{2,1,0:T(8,128)(2,1)} %refs_5_.3), custom_call_target="tpu_custom_call" | custom-call | tf_op jit(solution)/shard_map/pallas_call | solution.py:190
  30.2 1.8 %fusion = (f32[16,2304]{1,0:T(8,128)S(1)}, f32[16,2304]{1,0:T(8,128)S(1)}, f32[16,2304]{1,0:T(8,128)S(1)}, f32[16,2304]{1,0:T(8,128)}) fusion(f32[64,2304]{1,0:T(8,128)} %shard_map.96), kind=kLoop, calls=%fused_computation.16 | loop fusion | bytes 1179648 | tf_op jit(solution)/shard_map/slice | solution.py:255
  32.0 1.4 %collective-permute-start.6 = (f32[16,2304]{1,0:T(8,128)S(1)}, f32[16,2304]{1,0:T(8,128)S(1)}, u32[]{:S(2)}, u32[]{:S(2)}) collective-permute-start(f32[16,2304]{1,0:T(8,128)S(1)} %get-tuple-element.4), channel_id=1, source_target_pairs={{0,12},{4,0},{8,4},{12,8},{1,13},{5,1},{9,5},{13,9},{2,14},{6,2},{... | collective-permute-start | bytes 442376 | tf_op jit(solution)/shard_map/ppermute | solution.py:213
  33.4 4.4 %collective-permute-start.7 = (f32[16,2304]{1,0:T(8,128)S(1)}, f32[16,2304]{1,0:T(8,128)S(1)}, u32[]{:S(2)}, u32[]{:S(2)}) collective-permute-start(f32[16,2304]{1,0:T(8,128)S(1)} %get-tuple-element.3), channel_id=1, source_target_pairs={{0,8},{4,12},{8,0},{12,4},{1,9},{5,13},{9,1},{13,5},{2,10},{6,14},... | collective-permute-start | bytes 442376 | tf_op jit(solution)/shard_map/ppermute | solution.py:213
  37.8 0.0 copy-done.1
  37.8 0.6 %pad_maximum_fusion.6.refs_4_.refs_5_ = bf16[2,64,256]{2,1,0:T(8,128)(2,1)} fusion(bf16[1,64,256]{2,1,0:T(8,128)(2,1)S(1)} %get-tuple-element.7, bf16[1,64,256]{2,1,0:T(8,128)(2,1)S(1)} %get-tuple-element.6), kind=kLoop, calls=%fused_computation.6 | loop fusion | flops 32768 | bytes 131072 | tf_op jit(solution)/shard_map/stack | solution.py:229
  38.4 0.0 collective-permute-done
  38.4 0.0 collective-permute-start.8
  38.5 0.0 collective-permute-done.1
  38.5 0.0 collective-permute-done.2
  38.5 0.0 copy-start
  38.5 0.8 %copy-done = bf16[2,512,256]{2,1,0:T(8,128)(2,1)} copy-done((bf16[2,512,256]{2,1,0:T(8,128)(2,1)}, bf16[2,512,256]{2,1,0:T(8,128)(2,1)S(1)}, u32[]{:S(2)}) %copy-start) | copy-done | bytes 524312
  39.3 7.0 %shard_map.95 = bf16[256,2048]{1,0:T(8,128)(2,1)} custom-call(s32[1]{0:T(128)} %constant.35.clone.1.refs_0_, bf16[256,2048]{1,0:T(8,128)(2,1)} %refs_1_.2, bf16[2,512,256]{2,1,0:T(8,128)(2,1)} %copy-done, bf16[2,512,256]{2,1,0:T(8,128)(2,1)} %copy-done, bf16[2,256,256]{2,1,0:T(8,128)(2,1)} %refs_5_.3, bf16[2,256,256]{2,1,0:T(8,128)(2,1)} %refs_5_.3), custom_call_target="tpu_custom_call" | custom-call | tf_op jit(solution)/shard_map/pallas_call | solution.py:190
  46.3 0.0 collective-permute-done.6.refs_10_.refs_11_
  46.3 0.0 copy-start.2
  46.3 4.6 %collective-permute-done.7.refs_12_.refs_13_ = f32[16,2304]{1,0:T(8,128)S(1)} collective-permute-done((f32[16,2304]{1,0:T(8,128)S(1)}, f32[16,2304]{1,0:T(8,128)S(1)}, u32[]{:S(2)}, u32[]{:S(2)}) %collective-permute-start.7) | collective-permute-done | bytes 147488 | tf_op jit(solution)/shard_map/ppermute | solution.py:213
  50.9 0.0 copy-start.3
  50.9 0.0 collective-permute-done.8.refs_14_.refs_15_
  50.9 0.0 copy-start.4
  50.9 0.0 copy-done.2
  50.9 0.6 %copy-done.3 = f32[16,2304]{1,0:T(8,128)} copy-done((f32[16,2304]{1,0:T(8,128)}, f32[16,2304]{1,0:T(8,128)S(1)}, u32[]{:S(2)}) %copy-start.3) | copy-done | bytes 147480
  51.6 0.0 copy-done.4
  51.6 3.7 %shard_map.97 = bf16[16,2048]{1,0:T(8,128)(2,1)} custom-call(s32[1]{0:T(128)} %constant.35.clone.1.refs_0_, bf16[16,2048]{1,0:T(8,128)(2,1)} %refs_1_.3, bf16[2,512,256]{2,1,0:T(8,128)(2,1)} %copy-done, bf16[2,512,256]{2,1,0:T(8,128)(2,1)} %copy-done, bf16[2,64,256]{2,1,0:T(8,128)(2,1)} %pad_maximum_fusion.6.refs_4_.refs_5_, ...), custom_call_target="tpu_custom_call" | custom-call | tf_op jit(solution)/shard_map/pallas_call | solution.py:190
  (4 shorter events, 0.0 us)
Async XLA Ops:
  2.2 11.8 %collective-permute-start.3 = (bf16[16,2560]{1,0:T(8,128)(2,1)S(1)}, bf16[16,2560]{1,0:T(8,128)(2,1)S(1)}, u32[]{:S(2)}, u32[]{:S(2)}) collective-permute-start(bf16[16,2560]{1,0:T(8,128)(2,1)S(1)} %pad_maximum_fusion.5), channel_id=1, source_target_pairs={{0,4},{4,8},{8,12},{12,0},{1,5},{5,9},{9,13},{13,1},{2,6},{6,10},{... | collective-permute-start | bytes 245768 | tf_op jit(solution)/shard_map/ppermute | solution.py:213
  5.2 11.6 %collective-permute-start.4 = (bf16[16,2560]{1,0:T(8,128)(2,1)S(1)}, bf16[16,2560]{1,0:T(8,128)(2,1)S(1)}, u32[]{:S(2)}, u32[]{:S(2)}) collective-permute-start(bf16[16,2560]{1,0:T(8,128)(2,1)S(1)} %pad_maximum_fusion.5), channel_id=1, source_target_pairs={{0,8},{4,12},{8,0},{12,4},{1,9},{5,13},{9,1},{13,5},{2,10},{6,14},... | collective-permute-start | bytes 245768 | tf_op jit(solution)/shard_map/ppermute | solution.py:213
  7.8 9.1 %collective-permute-start.5 = (bf16[16,2560]{1,0:T(8,128)(2,1)S(1)}, bf16[16,2560]{1,0:T(8,128)(2,1)S(1)}, u32[]{:S(2)}, u32[]{:S(2)}) collective-permute-start(bf16[16,2560]{1,0:T(8,128)(2,1)S(1)} %pad_maximum_fusion.5), channel_id=1, source_target_pairs={{0,12},{4,0},{8,4},{12,8},{1,13},{5,1},{9,5},{13,9},{2,14},{6,2},{... | collective-permute-start | bytes 245768 | tf_op jit(solution)/shard_map/ppermute | solution.py:213
  9.2 29.3 %collective-permute-start = (bf16[2,128,256]{2,1,0:T(8,128)(2,1)}, bf16[2,128,256]{2,1,0:T(8,128)(2,1)S(1)}, u32[]{:S(2)}, u32[]{:S(2)}) collective-permute-start(bf16[2,128,256]{2,1,0:T(8,128)(2,1)} %param.10), channel_id=1, source_target_pairs={{0,4},{4,8},{8,12},{12,0},{1,5},{5,9},{9,13},{13,1},{2,6},{6,10},{... | collective-permute-start | bytes 393224 | tf_op jit(solution)/shard_map/ppermute | solution.py:213
  9.8 28.6 %collective-permute-start.1 = (bf16[2,128,256]{2,1,0:T(8,128)(2,1)}, bf16[2,128,256]{2,1,0:T(8,128)(2,1)S(1)}, u32[]{:S(2)}, u32[]{:S(2)}) collective-permute-start(bf16[2,128,256]{2,1,0:T(8,128)(2,1)} %param.10), channel_id=1, source_target_pairs={{0,8},{4,12},{8,0},{12,4},{1,9},{5,13},{9,1},{13,5},{2,10},{6,14},... | collective-permute-start | bytes 393224 | tf_op jit(solution)/shard_map/ppermute | solution.py:213
  14.0 24.5 %collective-permute-start.2 = (bf16[2,128,256]{2,1,0:T(8,128)(2,1)}, bf16[2,128,256]{2,1,0:T(8,128)(2,1)S(1)}, u32[]{:S(2)}, u32[]{:S(2)}) collective-permute-start(bf16[2,128,256]{2,1,0:T(8,128)(2,1)} %param.10), channel_id=1, source_target_pairs={{0,12},{4,0},{8,4},{12,8},{1,13},{5,1},{9,5},{13,9},{2,14},{6,2},{... | collective-permute-start | bytes 393224 | tf_op jit(solution)/shard_map/ppermute | solution.py:213
  18.4 19.4 %copy-start.1 = (bf16[16,2048]{1,0:T(8,128)(2,1)S(1)}, bf16[16,2048]{1,0:T(8,128)(2,1)}, u32[]{:S(2)}) copy-start(bf16[16,2048]{1,0:T(8,128)(2,1)} %refs_1_.3) | copy-start | bytes 196612
  32.0 14.4 %collective-permute-start.6 = (f32[16,2304]{1,0:T(8,128)S(1)}, f32[16,2304]{1,0:T(8,128)S(1)}, u32[]{:S(2)}, u32[]{:S(2)}) collective-permute-start(f32[16,2304]{1,0:T(8,128)S(1)} %get-tuple-element.4), channel_id=1, source_target_pairs={{0,12},{4,0},{8,4},{12,8},{1,13},{5,1},{9,5},{13,9},{2,14},{6,2},{... | collective-permute-start | bytes 442376 | tf_op jit(solution)/shard_map/ppermute | solution.py:213
  33.4 17.5 %collective-permute-start.7 = (f32[16,2304]{1,0:T(8,128)S(1)}, f32[16,2304]{1,0:T(8,128)S(1)}, u32[]{:S(2)}, u32[]{:S(2)}) collective-permute-start(f32[16,2304]{1,0:T(8,128)S(1)} %get-tuple-element.3), channel_id=1, source_target_pairs={{0,8},{4,12},{8,0},{12,4},{1,9},{5,13},{9,1},{13,5},{2,10},{6,14},... | collective-permute-start | bytes 442376 | tf_op jit(solution)/shard_map/ppermute | solution.py:213
  38.4 12.5 %collective-permute-start.8 = (f32[16,2304]{1,0:T(8,128)S(1)}, f32[16,2304]{1,0:T(8,128)S(1)}, u32[]{:S(2)}, u32[]{:S(2)}) collective-permute-start(f32[16,2304]{1,0:T(8,128)S(1)} %get-tuple-element.2), channel_id=1, source_target_pairs={{0,4},{4,8},{8,12},{12,0},{1,5},{5,9},{9,13},{13,1},{2,6},{6,10},{... | collective-permute-start | bytes 442376 | tf_op jit(solution)/shard_map/ppermute | solution.py:213
  38.5 0.8 %copy-start = (bf16[2,512,256]{2,1,0:T(8,128)(2,1)}, bf16[2,512,256]{2,1,0:T(8,128)(2,1)S(1)}, u32[]{:S(2)}) copy-start(bf16[2,512,256]{2,1,0:T(8,128)(2,1)S(1)} %constant_dynamic-update-slice_fusion.refs_2_.refs_3_) | copy-start | bytes 1572868
  46.3 4.6 %copy-start.2 = (f32[16,2304]{1,0:T(8,128)}, f32[16,2304]{1,0:T(8,128)S(1)}, u32[]{:S(2)}) copy-start(f32[16,2304]{1,0:T(8,128)S(1)} %collective-permute-done.6.refs_10_.refs_11_) | copy-start | bytes 442372
  50.9 0.7 %copy-start.3 = (f32[16,2304]{1,0:T(8,128)}, f32[16,2304]{1,0:T(8,128)S(1)}, u32[]{:S(2)}) copy-start(f32[16,2304]{1,0:T(8,128)S(1)} %collective-permute-done.7.refs_12_.refs_13_) | copy-start | bytes 442372
  50.9 0.7 %copy-start.4 = (f32[16,2304]{1,0:T(8,128)}, f32[16,2304]{1,0:T(8,128)S(1)}, u32[]{:S(2)}) copy-start(f32[16,2304]{1,0:T(8,128)S(1)} %collective-permute-done.8.refs_14_.refs_15_) | copy-start | bytes 442372

commit v13 on v10

--- a/solution.py
+++ b/solution.py
@@ -34,6 +34,7 @@
     section_refs = rest[: 2 * merge_count]
     rest = rest[2 * merge_count :]
     out_ref = rest[0]
+    out_refs = rest[: packed] if packed else None
     side_ref = None if normalize or packed or merge_count else rest[1]
     query_width = kv_heads * group_size * HD
     scale = 1.0 / jnp.sqrt(jnp.float32(HD))
@@ -125,11 +126,16 @@
 
                 def store(gi, h=h, rows_of=rows_of):
                     head = gi * group_size + h
-                    out_ref[:, head * HD : (head + 1) * HD] = output[rows_of]
                     side = query_width + gi * HD
-                    out_ref[:, side + h : side + h + 1] = peak[rows_of]
-                    side += HD // 2
-                    out_ref[:, side + h : side + h + 1] = total[rows_of]
+                    head_output = output[rows_of]
+                    head_peak = peak[rows_of]
+                    head_total = total[rows_of]
+                    own = rows // packed
+                    for k, target in enumerate(out_refs):
+                        mine = slice(k * own, (k + 1) * own)
+                        target[:, head * HD : (head + 1) * HD] = head_output[mine]
+                        target[:, side + h : side + h + 1] = head_peak[mine]
+                        target[:, side + HD // 2 + h : side + HD // 2 + h + 1] = head_total[mine]
 
                 for gi in range(kv_heads):
                     pl.when(pl.program_id(0) == gi)(functools.partial(store, gi))
@@ -181,9 +187,9 @@
     ]
     out_specs = [pl.BlockSpec((rows, group_width), lambda g, n: (0, g))]
     if packed:
-        full = (rows, query_width + kv_heads * HD)
-        out_shape = [jax.ShapeDtypeStruct(full, jnp.float32)]
-        out_specs = [pl.BlockSpec(full, lambda g, n: (0, 0))]
+        full = (rows // packed, query_width + kv_heads * HD)
+        out_shape = [jax.ShapeDtypeStruct(full, jnp.float32)] * packed
+        out_specs = [pl.BlockSpec(full, lambda g, n: (0, 0))] * packed
     elif not normalize:
         out_shape.append(jax.ShapeDtypeStruct((kv_heads, rows, HD), jnp.float32))
         out_specs.append(pl.BlockSpec((pl.Squeezed(), rows, HD), lambda g, n: (g, 0, 0)))
@@ -240,18 +246,17 @@
         )
         own_pos = slot_pos[:own_count]
 
-        (context_packed,) = attention(
+        context_slots = attention(
             all_queries,
             [(cache_kv, "cache"), (kv_block, None)],
             False,
             length=cache_len,
-            packed=True,
+            packed=ctx_count,
             stack_rows=CONTEXT_STACK_ROWS,
         )
-        sections = [context_packed[:own_count]]
-        for k in range(1, ctx_count):
-            rows = slice(k * own_count, (k + 1) * own_count)
-            sections.append(shifted(context_packed[rows], -k, ctx_count))
+        sections = [context_slots[0]] + [
+            shifted(context_slots[k], -k, ctx_count) for k in range(1, ctx_count)
+        ]
         (block_out,) = attention(q_block, [(anchor, None), (kv_block, "causal")], True)
         (query_out,) = attention(
             query_q,

time: 52.8 us -> 54.3 us (1.028)
  starting transfers between devices: 13.8 us -> 16.6 us
  local copies, waits for them, and re-layouts: 7.67 us -> 5.79 us
  waiting for transfers between devices: 4.09 us -> 4.75 us
    ppermute x9, starting transfers between devices: 13.8 us -> 16.6 us  [shifted(): lax.ppermute(value, 'ctx', [(j, (j + shift) % count) for j in range(count)])]
    slice x1 -> x0, local copies, waits for them, and re-layouts: 1.83 us -> none  [local(): sections.append(shifted(context_packed[rows], -k, ctx_count))]
    ppermute x9, waiting for transfers between devices: 4.09 us -> 4.75 us  [shifted(): lax.ppermute(value, 'ctx', [(j, (j + shift) % count) for j in range(count)])]
  transfers between devices with their start and end apart: 9 -> 9, of which waited for: 1 -> 1; matrix products, arithmetic and copies ran while one was open for 14% -> 10% of each run, Pallas kernels for 36% -> 35%
where the time goes in v13:
time: 54.3 us; the launch traced here: 54 us
  Pallas kernels  22.5 us (41%)
  starting transfers between devices  16.6 us (31%)
  local copies, waits for them, and re-layouts  5.79 us (11%)
  waiting for transfers between devices  4.75 us (9%)
  other arithmetic  2.84 us (5%)
  between operations  1.48 us (3%)
    pallas_call x3, Pallas kernels, attention(): pl.pallas_call(functools.partial(attention_kernel, masks, normalize, pack...  22.5 us
    ppermute x9, starting transfers between devices, shifted(): lax.ppermute(value, 'ctx', [(j, (j + shift) % count) for j in range(count)])  16.6 us
    ppermute x9, waiting for transfers between devices, shifted(): lax.ppermute(value, 'ctx', [(j, (j + shift) % count) for j in range(count)])  4.75 us
    unnamed x16, local copies, waits for them, and re-layouts  4.06 us
    concatenate x1, other arithmetic, local(): jnp.concatenate([slot[:split].reshape(own_count, query_width) for slot in...  1.56 us
  transfers between devices with their start and end apart: 9, of which 1 were waited for; matrix products, arithmetic and copies ran while one was open for 10% of the time, Pallas kernels for 35%

profile of v13, /device:TPU:0, one launch (start us, length us, event | category | flops | bytes accessed | tf_op | source)
XLA Modules:
  0.0 54.0 jit_solution(1142879848553574652)
XLA Ops:
  0.6 0.9 %copy.11 = bf16[2,16,8,128]{3,1,2,0:T(8,128)(2,1)S(1)} copy(bf16[2,16,8,128]{3,2,1,0:T(8,128)(2,1)} %bitcast.7) | data formatting | bytes 131072
  1.5 0.7 %copy.12 = bf16[4,2,8,128]{3,1,2,0:T(2,128)(2,1)S(1)} copy(bf16[4,2,8,128]{3,2,1,0:T(8,128)(2,1)} %bitcast.10) | data formatting | bytes 32768
  2.2 3.1 %collective-permute-start.3 = (bf16[40960]{0:T(1024)(128)(2,1)S(1)}, bf16[40960]{0:T(1024)(128)(2,1)S(1)}, u32[]{:S(2)}, u32[]{:S(2)}) collective-permute-start(bf16[40960]{0:T(1024)(128)(2,1)S(1)} %constant_dynamic-update-slice_fusion.5), channel_id=1, source_target_pairs={{0,4},{4,8},{8,12},{12,0},{1,5},{5,9},{9,13},{13,1},{2,6},{6,10},{... | collective-permute-start | bytes 245768 | tf_op jit(solution)/shard_map/ppermute | solution.py:219
  5.3 2.6 %collective-permute-start.4 = (bf16[40960]{0:T(1024)(128)(2,1)S(1)}, bf16[40960]{0:T(1024)(128)(2,1)S(1)}, u32[]{:S(2)}, u32[]{:S(2)}) collective-permute-start(bf16[40960]{0:T(1024)(128)(2,1)S(1)} %constant_dynamic-update-slice_fusion.5), channel_id=1, source_target_pairs={{0,8},{4,12},{8,0},{12,4},{1,9},{5,13},{9,1},{13,5},{2,10},{6,14},... | collective-permute-start | bytes 245768 | tf_op jit(solution)/shard_map/ppermute | solution.py:219
  7.9 1.3 %collective-permute-start.5 = (bf16[40960]{0:T(1024)(128)(2,1)S(1)}, bf16[40960]{0:T(1024)(128)(2,1)S(1)}, u32[]{:S(2)}, u32[]{:S(2)}) collective-permute-start(bf16[40960]{0:T(1024)(128)(2,1)S(1)} %constant_dynamic-update-slice_fusion.5), channel_id=1, source_target_pairs={{0,12},{4,0},{8,4},{12,8},{1,13},{5,1},{9,5},{13,9},{2,14},{6,2},{... | collective-permute-start | bytes 245768 | tf_op jit(solution)/shard_map/ppermute | solution.py:219
  9.3 0.7 %collective-permute-start = (bf16[2,128,256]{2,1,0:T(8,128)(2,1)}, bf16[2,128,256]{2,1,0:T(8,128)(2,1)S(1)}, u32[]{:S(2)}, u32[]{:S(2)}) collective-permute-start(bf16[2,128,256]{2,1,0:T(8,128)(2,1)} %param.10), channel_id=1, source_target_pairs={{0,4},{4,8},{8,12},{12,0},{1,5},{5,9},{9,13},{13,1},{2,6},{6,10},{... | collective-permute-start | bytes 393224 | tf_op jit(solution)/shard_map/ppermute | solution.py:219
  9.9 0.3 collective-permute-start.1
  10.3 0.9 %constant_dynamic-update-slice_fusion.3 = bf16[2,512,256]{2,1,0:T(8,128)(2,1)S(1)} fusion(bf16[2,128,256]{2,1,0:T(8,128)(2,1)} %param.10), kind=kLoop, calls=%fused_computation.5 | loop fusion | bytes 262144
  11.2 0.9 %fusion = (s32[16]{0:T(128)S(1)}, s32[16]{0:T(128)S(1)}, s32[16]{0:T(128)S(1)}, s32[16]{0:T(128)S(1)}) fusion(s32[64]{0:T(128)} %param.15, s32[]{:T(128)S(6)} %select_n.32, s32[]{:T(128)S(6)} %select_n.34, s32[]{:T(128)S(6)} %select_n.38, s32[]{:T(128)S(6)} %select_n.36), kind=kLoop, calls=%fused_computation.9 | loop fusion | bytes 528 | tf_op jit(solution)/shard_map/dynamic_slice | solution.py:243
  12.1 0.7 %copy.10.refs_7_ = s32[16,1]{1,0:T(8,128)} copy(s32[16,1]{0,1:T(1,128)S(1)} %bitcast.11) | data formatting | bytes 128 | tf_op jit(solution)/shard_map/reshape | solution.py:174
  13.5 0.7 %add_bitcast_fusion.refs_6_ = s32[1,64]{1,0:T(1,128)} fusion(s32[16]{0:T(128)S(1)} %get-tuple-element.12, s32[16]{0:T(128)S(1)} %get-tuple-element.13, s32[16]{0:T(128)S(1)} %get-tuple-element.11, s32[16]{0:T(128)S(1)} %get-tuple-element.10), kind=kLoop, calls=%fused_computation.8 | loop fusion | flops 192 | bytes 512 | tf_op jit(solution)/shard_map/reshape | solution.py:173
  14.1 0.0 collective-permute-done.3
  14.1 2.8 %collective-permute-start.2 = (bf16[2,128,256]{2,1,0:T(8,128)(2,1)}, bf16[2,128,256]{2,1,0:T(8,128)(2,1)S(1)}, u32[]{:S(2)}, u32[]{:S(2)}) collective-permute-start(bf16[2,128,256]{2,1,0:T(8,128)(2,1)} %param.10), channel_id=1, source_target_pairs={{0,12},{4,0},{8,4},{12,8},{1,13},{5,1},{9,5},{13,9},{2,14},{6,2},{... | collective-permute-start | bytes 393224 | tf_op jit(solution)/shard_map/ppermute | solution.py:219
  17.0 0.0 collective-permute-done.4
  17.1 0.0 collective-permute-done.5
  17.1 1.6 %pad_maximum_fusion.refs_1_ = bf16[64,2048]{1,0:T(8,128)(2,1)} fusion(bf16[16,2048]{1,0:T(8,128)(2,1)S(1)} %slice.89, bf16[16,2048]{1,0:T(8,128)(2,1)S(1)} %slice.87, bf16[16,2048]{1,0:T(8,128)(2,1)S(1)} %slice.85, bf16[16,2048]{1,0:T(8,128)(2,1)} %refs_1_.3), kind=kLoop, calls=%fused_computation | loop fusion | flops 1048576 | bytes 524288 | tf_op jit(solution)/shard_map/concatenate | solution.py:234
  18.7 0.0 copy-start.4
  18.7 11.8 %shard_map.96 = (f32[16,2304]{1,0:T(8,128)}, f32[16,2304]{1,0:T(8,128)}, f32[16,2304]{1,0:T(8,128)}, f32[16,2304]{1,0:T(8,128)}) custom-call(s32[1]{0:T(128)S(6)} %copy.17.refs_0_, bf16[64,2048]{1,0:T(8,128)(2,1)} %pad_maximum_fusion.refs_1_, bf16[2,4096,256]{2,1,0:T(8,128)(2,1)} %refs_3_.1, bf16[2,4096,256]{2,1,0:T(8,128)(2,1)} %refs_3_.1, ...), custom_call_target="tpu_custom_call" | custom-call | tf_op jit(solution)/shard_map/pallas_call | solution.py:196
  30.5 1.4 %collective-permute-start.6 = (f32[16,2304]{1,0:T(8,128)}, f32[16,2304]{1,0:T(8,128)S(1)}, u32[]{:S(2)}, u32[]{:S(2)}) collective-permute-start(f32[16,2304]{1,0:T(8,128)} %get-tuple-element.7), channel_id=1, source_target_pairs={{0,12},{4,0},{8,4},{12,8},{1,13},{5,1},{9,5},{13,9},{2,14},{6,2},{... | collective-permute-start | bytes 442376 | tf_op jit(solution)/shard_map/ppermute | solution.py:219
  31.8 4.3 %collective-permute-start.7 = (f32[16,2304]{1,0:T(8,128)}, f32[16,2304]{1,0:T(8,128)S(1)}, u32[]{:S(2)}, u32[]{:S(2)}) collective-permute-start(f32[16,2304]{1,0:T(8,128)} %get-tuple-element.8), channel_id=1, source_target_pairs={{0,8},{4,12},{8,0},{12,4},{1,9},{5,13},{9,1},{13,5},{2,10},{6,14},... | collective-permute-start | bytes 442376 | tf_op jit(solution)/shard_map/ppermute | solution.py:219
  36.2 0.0 copy-done.4
  36.2 0.6 %pad_maximum_fusion.1.refs_4_.refs_5_ = bf16[2,64,256]{2,1,0:T(8,128)(2,1)} fusion(bf16[2,16,256]{2,1,0:T(8,128)(2,1)S(1)} %slice.83, bf16[2,16,256]{2,1,0:T(8,128)(2,1)S(1)} %slice.81, bf16[2,16,256]{2,1,0:T(8,128)(2,1)S(1)} %slice.79, bf16[2,16,256]{2,1,0:T(8,128)(2,1)S(1)} %copy-done.4), kind=kLoop, calls=%fused_computation.1 | loop fusion | flops 262144 | bytes 131072 | tf_op jit(solution)/shard_map/concatenate | solution.py:237
  36.9 0.0 collective-permute-done
  36.9 0.0 collective-permute-start.8
  36.9 0.0 collective-permute-done.1
  36.9 0.0 collective-permute-done.2
  36.9 0.0 copy-start
  37.0 0.8 %copy-done = bf16[2,512,256]{2,1,0:T(8,128)(2,1)} copy-done((bf16[2,512,256]{2,1,0:T(8,128)(2,1)}, bf16[2,512,256]{2,1,0:T(8,128)(2,1)S(1)}, u32[]{:S(2)}) %copy-start) | copy-done | bytes 524312
  37.7 7.0 %shard_map.95 = bf16[256,2048]{1,0:T(8,128)(2,1)} custom-call(s32[1]{0:T(128)} %constant.35.clone.1.refs_0_, bf16[256,2048]{1,0:T(8,128)(2,1)} %refs_1_.2, bf16[2,512,256]{2,1,0:T(8,128)(2,1)} %copy-done, bf16[2,512,256]{2,1,0:T(8,128)(2,1)} %copy-done, bf16[2,256,256]{2,1,0:T(8,128)(2,1)} %refs_5_.3, bf16[2,256,256]{2,1,0:T(8,128)(2,1)} %refs_5_.3), custom_call_target="tpu_custom_call" | custom-call | tf_op jit(solution)/shard_map/pallas_call | solution.py:196
  44.8 0.0 collective-permute-done.6.refs_10_.refs_11_
  44.8 0.0 copy-start.1
  44.8 4.7 %collective-permute-done.7.refs_12_.refs_13_ = f32[16,2304]{1,0:T(8,128)S(1)} collective-permute-done((f32[16,2304]{1,0:T(8,128)}, f32[16,2304]{1,0:T(8,128)S(1)}, u32[]{:S(2)}, u32[]{:S(2)}) %collective-permute-start.7) | collective-permute-done | bytes 147488 | tf_op jit(solution)/shard_map/ppermute | solution.py:219
  49.5 0.0 copy-start.2
  49.5 0.0 collective-permute-done.8.refs_14_.refs_15_
  49.5 0.0 copy-start.3
  49.5 0.0 copy-done.1
  49.5 0.6 %copy-done.2 = f32[16,2304]{1,0:T(8,128)} copy-done((f32[16,2304]{1,0:T(8,128)}, f32[16,2304]{1,0:T(8,128)S(1)}, u32[]{:S(2)}) %copy-start.2) | copy-done | bytes 147480
  50.1 0.1 copy-done.3
  50.2 3.7 %shard_map.97 = bf16[16,2048]{1,0:T(8,128)(2,1)} custom-call(s32[1]{0:T(128)} %constant.35.clone.1.refs_0_, bf16[16,2048]{1,0:T(8,128)(2,1)} %refs_1_.3, bf16[2,512,256]{2,1,0:T(8,128)(2,1)} %copy-done, bf16[2,512,256]{2,1,0:T(8,128)(2,1)} %copy-done, bf16[2,64,256]{2,1,0:T(8,128)(2,1)} %pad_maximum_fusion.1.refs_4_.refs_5_, ...), custom_call_target="tpu_custom_call" | custom-call | tf_op jit(solution)/shard_map/pallas_call | solution.py:196
  (17 shorter events, 0.2 us)
Async XLA Ops:
  2.2 11.9 %collective-permute-start.3 = (bf16[40960]{0:T(1024)(128)(2,1)S(1)}, bf16[40960]{0:T(1024)(128)(2,1)S(1)}, u32[]{:S(2)}, u32[]{:S(2)}) collective-permute-start(bf16[40960]{0:T(1024)(128)(2,1)S(1)} %constant_dynamic-update-slice_fusion.5), channel_id=1, source_target_pairs={{0,4},{4,8},{8,12},{12,0},{1,5},{5,9},{9,13},{13,1},{2,6},{6,10},{... | collective-permute-start | bytes 245768 | tf_op jit(solution)/shard_map/ppermute | solution.py:219
  5.3 11.7 %collective-permute-start.4 = (bf16[40960]{0:T(1024)(128)(2,1)S(1)}, bf16[40960]{0:T(1024)(128)(2,1)S(1)}, u32[]{:S(2)}, u32[]{:S(2)}) collective-permute-start(bf16[40960]{0:T(1024)(128)(2,1)S(1)} %constant_dynamic-update-slice_fusion.5), channel_id=1, source_target_pairs={{0,8},{4,12},{8,0},{12,4},{1,9},{5,13},{9,1},{13,5},{2,10},{6,14},... | collective-permute-start | bytes 245768 | tf_op jit(solution)/shard_map/ppermute | solution.py:219
  7.9 9.2 %collective-permute-start.5 = (bf16[40960]{0:T(1024)(128)(2,1)S(1)}, bf16[40960]{0:T(1024)(128)(2,1)S(1)}, u32[]{:S(2)}, u32[]{:S(2)}) collective-permute-start(bf16[40960]{0:T(1024)(128)(2,1)S(1)} %constant_dynamic-update-slice_fusion.5), channel_id=1, source_target_pairs={{0,12},{4,0},{8,4},{12,8},{1,13},{5,1},{9,5},{13,9},{2,14},{6,2},{... | collective-permute-start | bytes 245768 | tf_op jit(solution)/shard_map/ppermute | solution.py:219
  9.3 27.6 %collective-permute-start = (bf16[2,128,256]{2,1,0:T(8,128)(2,1)}, bf16[2,128,256]{2,1,0:T(8,128)(2,1)S(1)}, u32[]{:S(2)}, u32[]{:S(2)}) collective-permute-start(bf16[2,128,256]{2,1,0:T(8,128)(2,1)} %param.10), channel_id=1, source_target_pairs={{0,4},{4,8},{8,12},{12,0},{1,5},{5,9},{9,13},{13,1},{2,6},{6,10},{... | collective-permute-start | bytes 393224 | tf_op jit(solution)/shard_map/ppermute | solution.py:219
  9.9 27.0 %collective-permute-start.1 = (bf16[2,128,256]{2,1,0:T(8,128)(2,1)}, bf16[2,128,256]{2,1,0:T(8,128)(2,1)S(1)}, u32[]{:S(2)}, u32[]{:S(2)}) collective-permute-start(bf16[2,128,256]{2,1,0:T(8,128)(2,1)} %param.10), channel_id=1, source_target_pairs={{0,8},{4,12},{8,0},{12,4},{1,9},{5,13},{9,1},{13,5},{2,10},{6,14},... | collective-permute-start | bytes 393224 | tf_op jit(solution)/shard_map/ppermute | solution.py:219
  14.1 22.8 %collective-permute-start.2 = (bf16[2,128,256]{2,1,0:T(8,128)(2,1)}, bf16[2,128,256]{2,1,0:T(8,128)(2,1)S(1)}, u32[]{:S(2)}, u32[]{:S(2)}) collective-permute-start(bf16[2,128,256]{2,1,0:T(8,128)(2,1)} %param.10), channel_id=1, source_target_pairs={{0,12},{4,0},{8,4},{12,8},{1,13},{5,1},{9,5},{13,9},{2,14},{6,2},{... | collective-permute-start | bytes 393224 | tf_op jit(solution)/shard_map/ppermute | solution.py:219
  18.7 17.5 %copy-start.4 = (bf16[2,16,256]{2,1,0:T(8,128)(2,1)S(1)}, bf16[2,16,256]{2,1,0:T(8,128)(2,1)}, u32[]{:S(2)}) copy-start(bf16[2,16,256]{2,1,0:T(8,128)(2,1)} %param.14) | copy-start | bytes 49156
  30.5 14.3 %collective-permute-start.6 = (f32[16,2304]{1,0:T(8,128)}, f32[16,2304]{1,0:T(8,128)S(1)}, u32[]{:S(2)}, u32[]{:S(2)}) collective-permute-start(f32[16,2304]{1,0:T(8,128)} %get-tuple-element.7), channel_id=1, source_target_pairs={{0,12},{4,0},{8,4},{12,8},{1,13},{5,1},{9,5},{13,9},{2,14},{6,2},{... | collective-permute-start | bytes 442376 | tf_op jit(solution)/shard_map/ppermute | solution.py:219
  31.8 17.7 %collective-permute-start.7 = (f32[16,2304]{1,0:T(8,128)}, f32[16,2304]{1,0:T(8,128)S(1)}, u32[]{:S(2)}, u32[]{:S(2)}) collective-permute-start(f32[16,2304]{1,0:T(8,128)} %get-tuple-element.8), channel_id=1, source_target_pairs={{0,8},{4,12},{8,0},{12,4},{1,9},{5,13},{9,1},{13,5},{2,10},{6,14},... | collective-permute-start | bytes 442376 | tf_op jit(solution)/shard_map/ppermute | solution.py:219
  36.9 12.6 %collective-permute-start.8 = (f32[16,2304]{1,0:T(8,128)}, f32[16,2304]{1,0:T(8,128)S(1)}, u32[]{:S(2)}, u32[]{:S(2)}) collective-permute-start(f32[16,2304]{1,0:T(8,128)} %get-tuple-element.9), channel_id=1, source_target_pairs={{0,4},{4,8},{8,12},{12,0},{1,5},{5,9},{9,13},{13,1},{2,6},{6,10},{... | collective-permute-start | bytes 442376 | tf_op jit(solution)/shard_map/ppermute | solution.py:219
  36.9 0.8 %copy-start = (bf16[2,512,256]{2,1,0:T(8,128)(2,1)}, bf16[2,512,256]{2,1,0:T(8,128)(2,1)S(1)}, u32[]{:S(2)}) copy-start(bf16[2,512,256]{2,1,0:T(8,128)(2,1)S(1)} %constant_dynamic-update-slice_fusion.refs_2_.refs_3_) | copy-start | bytes 1572868
  44.8 4.7 %copy-start.1 = (f32[16,2304]{1,0:T(8,128)}, f32[16,2304]{1,0:T(8,128)S(1)}, u32[]{:S(2)}) copy-start(f32[16,2304]{1,0:T(8,128)S(1)} %collective-permute-done.6.refs_10_.refs_11_) | copy-start | bytes 442372
  49.5 0.7 %copy-start.2 = (f32[16,2304]{1,0:T(8,128)}, f32[16,2304]{1,0:T(8,128)S(1)}, u32[]{:S(2)}) copy-start(f32[16,2304]{1,0:T(8,128)S(1)} %collective-permute-done.7.refs_12_.refs_13_) | copy-start | bytes 442372
  49.5 0.7 %copy-start.3 = (f32[16,2304]{1,0:T(8,128)}, f32[16,2304]{1,0:T(8,128)S(1)}, u32[]{:S(2)}) copy-start(f32[16,2304]{1,0:T(8,128)S(1)} %collective-permute-done.8.refs_14_.refs_15_) | copy-start | bytes 442372

commit v14 on v10

--- a/solution.py
+++ b/solution.py
@@ -232,12 +232,9 @@
             [slot[split:].reshape(2, own_count, width) for slot in query_slots], axis=1
         )
         anchor = jnp.concatenate(anchor_slots, axis=1)
-        slot_pos = jnp.concatenate(
-            [
-                lax.dynamic_slice_in_dim(query_pos, ((me - k) % ctx_count) * own_count, own_count)
-                for k in range(ctx_count)
-            ]
-        )
+        reversed_pos = query_pos.reshape(ctx_count, own_count)[::-1]
+        doubled = jnp.concatenate([reversed_pos, reversed_pos], axis=0)
+        slot_pos = lax.dynamic_slice_in_dim(doubled, ctx_count - 1 - me, ctx_count).reshape(-1)
         own_pos = slot_pos[:own_count]
 
         (context_packed,) = attention(

time: 52.8 us -> 55.9 us (1.059)
  starting transfers between devices: 13.8 us -> 16.8 us
  other arithmetic: 2.84 us -> 2.21 us
    ppermute x9, starting transfers between devices: 13.8 us -> 16.8 us  [shifted(): lax.ppermute(value, 'ctx', [(j, (j + shift) % count) for j in range(count)])]
    dynamic_slice x1, local copies, waits for them, and re-layouts: 0.89 us -> 0.01 us  [local(): lax.dynamic_slice_in_dim(doubled, ctx_count - 1 - me, ctx_count).reshape(-1)]
    reshape x0 -> x1, local copies, waits for them, and re-layouts: none -> 0.74 us  [local(): reversed_pos = query_pos.reshape(ctx_count, own_count)[::-1]]
    reshape x1 -> x0, other arithmetic: 0.65 us -> none  [attention(): key_pos = positions[0].reshape(1, -1)]
    another operation x0 -> x1, local copies, waits for them, and re-layouts: none -> 0.61 us  [attention(): key_pos = positions[0].reshape(1, -1)]
  transfers between devices with their start and end apart: 9 -> 9, of which waited for: 1 -> 1; matrix products, arithmetic and copies ran while one was open for 14% -> 13% of each run, Pallas kernels for 36% -> 34%
where the time goes in v14:
time: 55.9 us; the launch traced here: 55.5 us
  Pallas kernels  22.5 us (40%)
  starting transfers between devices  16.8 us (30%)
  local copies, waits for them, and re-layouts  8.08 us (14%)
  waiting for transfers between devices  4.53 us (8%)
  other arithmetic  2.21 us (4%)
  between operations  1.48 us (3%)
    pallas_call x3, Pallas kernels, attention(): pl.pallas_call(functools.partial(attention_kernel, masks, normalize, pack...  22.5 us
    ppermute x9, starting transfers between devices, shifted(): lax.ppermute(value, 'ctx', [(j, (j + shift) % count) for j in range(count)])  16.8 us
    ppermute x9, waiting for transfers between devices, shifted(): lax.ppermute(value, 'ctx', [(j, (j + shift) % count) for j in range(count)])  4.53 us
    unnamed x16, local copies, waits for them, and re-layouts  4.03 us
    slice x1, local copies, waits for them, and re-layouts, local(): sections.append(shifted(context_packed[rows], -k, ctx_count))  1.82 us
    concatenate x1, other arithmetic, local(): jnp.concatenate([slot[:split].reshape(own_count, query_width) for slot in...  1.56 us
  transfers between devices with their start and end apart: 9, of which 1 were waited for; matrix products, arithmetic and copies ran while one was open for 13% of the time, Pallas kernels for 34%

profile of v14, /device:TPU:0, one launch (start us, length us, event | category | flops | bytes accessed | tf_op | source)
XLA Modules:
  0.0 55.5 jit_solution(3517344354672665887)
XLA Ops:
  0.6 0.9 %copy.11 = bf16[2,16,8,128]{3,1,2,0:T(8,128)(2,1)S(1)} copy(bf16[2,16,8,128]{3,2,1,0:T(8,128)(2,1)} %bitcast.6) | data formatting | bytes 131072
  1.5 0.7 %copy.12 = bf16[4,2,8,128]{3,1,2,0:T(2,128)(2,1)S(1)} copy(bf16[4,2,8,128]{3,2,1,0:T(8,128)(2,1)} %bitcast.9) | data formatting | bytes 32768
  2.2 3.1 %collective-permute-start.3 = (bf16[40960]{0:T(1024)(128)(2,1)S(1)}, bf16[40960]{0:T(1024)(128)(2,1)S(1)}, u32[]{:S(2)}, u32[]{:S(2)}) collective-permute-start(bf16[40960]{0:T(1024)(128)(2,1)S(1)} %constant_dynamic-update-slice_fusion.5), channel_id=1, source_target_pairs={{0,4},{4,8},{8,12},{12,0},{1,5},{5,9},{9,13},{13,1},{2,6},{6,10},{... | collective-permute-start | bytes 245768 | tf_op jit(solution)/shard_map/ppermute | solution.py:213
  5.3 2.6 %collective-permute-start.4 = (bf16[40960]{0:T(1024)(128)(2,1)S(1)}, bf16[40960]{0:T(1024)(128)(2,1)S(1)}, u32[]{:S(2)}, u32[]{:S(2)}) collective-permute-start(bf16[40960]{0:T(1024)(128)(2,1)S(1)} %constant_dynamic-update-slice_fusion.5), channel_id=1, source_target_pairs={{0,8},{4,12},{8,0},{12,4},{1,9},{5,13},{9,1},{13,5},{2,10},{6,14},... | collective-permute-start | bytes 245768 | tf_op jit(solution)/shard_map/ppermute | solution.py:213
  7.9 1.3 %collective-permute-start.5 = (bf16[40960]{0:T(1024)(128)(2,1)S(1)}, bf16[40960]{0:T(1024)(128)(2,1)S(1)}, u32[]{:S(2)}, u32[]{:S(2)}) collective-permute-start(bf16[40960]{0:T(1024)(128)(2,1)S(1)} %constant_dynamic-update-slice_fusion.5), channel_id=1, source_target_pairs={{0,12},{4,0},{8,4},{12,8},{1,13},{5,1},{9,5},{13,9},{2,14},{6,2},{... | collective-permute-start | bytes 245768 | tf_op jit(solution)/shard_map/ppermute | solution.py:213
  9.3 0.7 %collective-permute-start = (bf16[2,128,256]{2,1,0:T(8,128)(2,1)}, bf16[2,128,256]{2,1,0:T(8,128)(2,1)S(1)}, u32[]{:S(2)}, u32[]{:S(2)}) collective-permute-start(bf16[2,128,256]{2,1,0:T(8,128)(2,1)} %param.10), channel_id=1, source_target_pairs={{0,4},{4,8},{8,12},{12,0},{1,5},{5,9},{9,13},{13,1},{2,6},{6,10},{... | collective-permute-start | bytes 393224 | tf_op jit(solution)/shard_map/ppermute | solution.py:213
  9.9 0.3 collective-permute-start.1
  10.3 0.7 %reshape.75 = s32[4,16]{1,0:T(4,128)S(1)} reshape(s32[64]{0:T(128)} %param.15) | data formatting | bytes 512 | tf_op jit(solution)/shard_map/reshape | solution.py:235
  11.1 0.6 %reshape_reshape.3.refs_6_ = s32[1,64]{1,0:T(1,128)} reshape(s32[4,16]{1,0:T(4,128)S(1)} %constant_dynamic-slice_fusion) | data formatting | bytes 512 | tf_op jit(solution)/shard_map/reshape;reshape | solution.py:167
  12.3 0.7 %copy.10.refs_7_ = s32[16,1]{1,0:T(8,128)} copy(s32[16,1]{0,1:T(1,128)S(1)} %slice_bitcast_fusion) | data formatting | bytes 128 | tf_op jit(solution)/shard_map/reshape | solution.py:168
  13.0 0.9 %constant_dynamic-update-slice_fusion.3 = bf16[2,512,256]{2,1,0:T(8,128)(2,1)S(1)} fusion(bf16[2,128,256]{2,1,0:T(8,128)(2,1)} %param.10), kind=kLoop, calls=%fused_computation.5 | loop fusion | bytes 262144
  13.9 0.0 collective-permute-done.3
  13.9 2.9 %collective-permute-start.2 = (bf16[2,128,256]{2,1,0:T(8,128)(2,1)}, bf16[2,128,256]{2,1,0:T(8,128)(2,1)S(1)}, u32[]{:S(2)}, u32[]{:S(2)}) collective-permute-start(bf16[2,128,256]{2,1,0:T(8,128)(2,1)} %param.10), channel_id=1, source_target_pairs={{0,12},{4,0},{8,4},{12,8},{1,13},{5,1},{9,5},{13,9},{2,14},{6,2},{... | collective-permute-start | bytes 393224 | tf_op jit(solution)/shard_map/ppermute | solution.py:213
  16.8 0.0 collective-permute-done.4
  16.9 0.0 collective-permute-done.5
  17.0 1.6 %pad_maximum_fusion.refs_1_ = bf16[64,2048]{1,0:T(8,128)(2,1)} fusion(bf16[16,2048]{1,0:T(8,128)(2,1)S(1)} %slice.106, bf16[16,2048]{1,0:T(8,128)(2,1)S(1)} %slice.104, bf16[16,2048]{1,0:T(8,128)(2,1)S(1)} %slice.102, bf16[16,2048]{1,0:T(8,128)(2,1)} %refs_1_.3), kind=kLoop, calls=%fused_computation | loop fusion | flops 1048576 | bytes 524288 | tf_op jit(solution)/shard_map/concatenate | solution.py:228
  18.5 0.0 copy-start.4
  18.5 11.7 %shard_map.96 = f32[64,2304]{1,0:T(8,128)} custom-call(s32[1]{0:T(128)S(6)} %copy.17.refs_0_, bf16[64,2048]{1,0:T(8,128)(2,1)} %pad_maximum_fusion.refs_1_, bf16[2,4096,256]{2,1,0:T(8,128)(2,1)} %refs_3_.1, bf16[2,4096,256]{2,1,0:T(8,128)(2,1)} %refs_3_.1, bf16[2,256,256]{2,1,0:T(8,128)(2,1)} %refs_5_.3, bf16[2,256,256]{2,1,0:T(8,128)(2,1)} %refs_5_.3), custom_call_target="tpu_custom_call" | custom-call | tf_op jit(solution)/shard_map/pallas_call | solution.py:190
  30.3 1.8 %fusion = (f32[16,2304]{1,0:T(8,128)S(1)}, f32[16,2304]{1,0:T(8,128)S(1)}, f32[16,2304]{1,0:T(8,128)S(1)}, f32[16,2304]{1,0:T(8,128)}) fusion(f32[64,2304]{1,0:T(8,128)} %shard_map.96), kind=kLoop, calls=%fused_computation.11 | loop fusion | bytes 1179648 | tf_op jit(solution)/shard_map/slice | solution.py:251
  32.1 1.5 %collective-permute-start.6 = (f32[16,2304]{1,0:T(8,128)S(1)}, f32[16,2304]{1,0:T(8,128)S(1)}, u32[]{:S(2)}, u32[]{:S(2)}) collective-permute-start(f32[16,2304]{1,0:T(8,128)S(1)} %get-tuple-element.4), channel_id=1, source_target_pairs={{0,12},{4,0},{8,4},{12,8},{1,13},{5,1},{9,5},{13,9},{2,14},{6,2},{... | collective-permute-start | bytes 442376 | tf_op jit(solution)/shard_map/ppermute | solution.py:213
  33.6 4.3 %collective-permute-start.7 = (f32[16,2304]{1,0:T(8,128)S(1)}, f32[16,2304]{1,0:T(8,128)S(1)}, u32[]{:S(2)}, u32[]{:S(2)}) collective-permute-start(f32[16,2304]{1,0:T(8,128)S(1)} %get-tuple-element.3), channel_id=1, source_target_pairs={{0,8},{4,12},{8,0},{12,4},{1,9},{5,13},{9,1},{13,5},{2,10},{6,14},... | collective-permute-start | bytes 442376 | tf_op jit(solution)/shard_map/ppermute | solution.py:213
  38.0 0.0 copy-done.4
  38.0 0.6 %pad_maximum_fusion.1.refs_4_.refs_5_ = bf16[2,64,256]{2,1,0:T(8,128)(2,1)} fusion(bf16[2,16,256]{2,1,0:T(8,128)(2,1)S(1)} %slice.99, bf16[2,16,256]{2,1,0:T(8,128)(2,1)S(1)} %slice.97, bf16[2,16,256]{2,1,0:T(8,128)(2,1)S(1)} %slice.95, bf16[2,16,256]{2,1,0:T(8,128)(2,1)S(1)} %copy-done.4), kind=kLoop, calls=%fused_computation.1 | loop fusion | flops 262144 | bytes 131072 | tf_op jit(solution)/shard_map/concatenate | solution.py:231
  38.7 0.0 collective-permute-done
  38.7 0.0 collective-permute-start.8
  38.7 0.0 collective-permute-done.1
  38.7 0.0 collective-permute-done.2
  38.8 0.0 copy-start
  38.8 0.8 %copy-done = bf16[2,512,256]{2,1,0:T(8,128)(2,1)} copy-done((bf16[2,512,256]{2,1,0:T(8,128)(2,1)}, bf16[2,512,256]{2,1,0:T(8,128)(2,1)S(1)}, u32[]{:S(2)}) %copy-start) | copy-done | bytes 524312
  39.6 7.0 %shard_map.95 = bf16[256,2048]{1,0:T(8,128)(2,1)} custom-call(s32[1]{0:T(128)} %constant.3.clone.1.refs_0_, bf16[256,2048]{1,0:T(8,128)(2,1)} %refs_1_.2, bf16[2,512,256]{2,1,0:T(8,128)(2,1)} %copy-done, bf16[2,512,256]{2,1,0:T(8,128)(2,1)} %copy-done, bf16[2,256,256]{2,1,0:T(8,128)(2,1)} %refs_5_.3, bf16[2,256,256]{2,1,0:T(8,128)(2,1)} %refs_5_.3), custom_call_target="tpu_custom_call" | custom-call | tf_op jit(solution)/shard_map/pallas_call | solution.py:190
  46.6 0.0 collective-permute-done.6.refs_10_.refs_11_
  46.6 0.0 copy-start.1
  46.6 4.5 %collective-permute-done.7.refs_12_.refs_13_ = f32[16,2304]{1,0:T(8,128)S(1)} collective-permute-done((f32[16,2304]{1,0:T(8,128)S(1)}, f32[16,2304]{1,0:T(8,128)S(1)}, u32[]{:S(2)}, u32[]{:S(2)}) %collective-permute-start.7) | collective-permute-done | bytes 147488 | tf_op jit(solution)/shard_map/ppermute | solution.py:213
  51.1 0.0 copy-start.2
  51.1 0.0 collective-permute-done.8.refs_14_.refs_15_
  51.1 0.0 copy-start.3
  51.1 0.0 copy-done.1
  51.1 0.6 %copy-done.2 = f32[16,2304]{1,0:T(8,128)} copy-done((f32[16,2304]{1,0:T(8,128)}, f32[16,2304]{1,0:T(8,128)S(1)}, u32[]{:S(2)}) %copy-start.2) | copy-done | bytes 147480
  51.7 0.1 copy-done.3
  51.8 3.7 %shard_map.97 = bf16[16,2048]{1,0:T(8,128)(2,1)} custom-call(s32[1]{0:T(128)} %constant.3.clone.1.refs_0_, bf16[16,2048]{1,0:T(8,128)(2,1)} %refs_1_.3, bf16[2,512,256]{2,1,0:T(8,128)(2,1)} %copy-done, bf16[2,512,256]{2,1,0:T(8,128)(2,1)} %copy-done, bf16[2,64,256]{2,1,0:T(8,128)(2,1)} %pad_maximum_fusion.1.refs_4_.refs_5_, ...), custom_call_target="tpu_custom_call" | custom-call | tf_op jit(solution)/shard_map/pallas_call | solution.py:190
  (21 shorter events, 0.3 us)
Async XLA Ops:
  2.2 11.7 %collective-permute-start.3 = (bf16[40960]{0:T(1024)(128)(2,1)S(1)}, bf16[40960]{0:T(1024)(128)(2,1)S(1)}, u32[]{:S(2)}, u32[]{:S(2)}) collective-permute-start(bf16[40960]{0:T(1024)(128)(2,1)S(1)} %constant_dynamic-update-slice_fusion.5), channel_id=1, source_target_pairs={{0,4},{4,8},{8,12},{12,0},{1,5},{5,9},{9,13},{13,1},{2,6},{6,10},{... | collective-permute-start | bytes 245768 | tf_op jit(solution)/shard_map/ppermute | solution.py:213
  5.3 11.5 %collective-permute-start.4 = (bf16[40960]{0:T(1024)(128)(2,1)S(1)}, bf16[40960]{0:T(1024)(128)(2,1)S(1)}, u32[]{:S(2)}, u32[]{:S(2)}) collective-permute-start(bf16[40960]{0:T(1024)(128)(2,1)S(1)} %constant_dynamic-update-slice_fusion.5), channel_id=1, source_target_pairs={{0,8},{4,12},{8,0},{12,4},{1,9},{5,13},{9,1},{13,5},{2,10},{6,14},... | collective-permute-start | bytes 245768 | tf_op jit(solution)/shard_map/ppermute | solution.py:213
  7.9 9.0 %collective-permute-start.5 = (bf16[40960]{0:T(1024)(128)(2,1)S(1)}, bf16[40960]{0:T(1024)(128)(2,1)S(1)}, u32[]{:S(2)}, u32[]{:S(2)}) collective-permute-start(bf16[40960]{0:T(1024)(128)(2,1)S(1)} %constant_dynamic-update-slice_fusion.5), channel_id=1, source_target_pairs={{0,12},{4,0},{8,4},{12,8},{1,13},{5,1},{9,5},{13,9},{2,14},{6,2},{... | collective-permute-start | bytes 245768 | tf_op jit(solution)/shard_map/ppermute | solution.py:213
  9.3 29.4 %collective-permute-start = (bf16[2,128,256]{2,1,0:T(8,128)(2,1)}, bf16[2,128,256]{2,1,0:T(8,128)(2,1)S(1)}, u32[]{:S(2)}, u32[]{:S(2)}) collective-permute-start(bf16[2,128,256]{2,1,0:T(8,128)(2,1)} %param.10), channel_id=1, source_target_pairs={{0,4},{4,8},{8,12},{12,0},{1,5},{5,9},{9,13},{13,1},{2,6},{6,10},{... | collective-permute-start | bytes 393224 | tf_op jit(solution)/shard_map/ppermute | solution.py:213
  9.9 28.8 %collective-permute-start.1 = (bf16[2,128,256]{2,1,0:T(8,128)(2,1)}, bf16[2,128,256]{2,1,0:T(8,128)(2,1)S(1)}, u32[]{:S(2)}, u32[]{:S(2)}) collective-permute-start(bf16[2,128,256]{2,1,0:T(8,128)(2,1)} %param.10), channel_id=1, source_target_pairs={{0,8},{4,12},{8,0},{12,4},{1,9},{5,13},{9,1},{13,5},{2,10},{6,14},... | collective-permute-start | bytes 393224 | tf_op jit(solution)/shard_map/ppermute | solution.py:213
  13.9 24.8 %collective-permute-start.2 = (bf16[2,128,256]{2,1,0:T(8,128)(2,1)}, bf16[2,128,256]{2,1,0:T(8,128)(2,1)S(1)}, u32[]{:S(2)}, u32[]{:S(2)}) collective-permute-start(bf16[2,128,256]{2,1,0:T(8,128)(2,1)} %param.10), channel_id=1, source_target_pairs={{0,12},{4,0},{8,4},{12,8},{1,13},{5,1},{9,5},{13,9},{2,14},{6,2},{... | collective-permute-start | bytes 393224 | tf_op jit(solution)/shard_map/ppermute | solution.py:213
  18.5 19.5 %copy-start.4 = (bf16[2,16,256]{2,1,0:T(8,128)(2,1)S(1)}, bf16[2,16,256]{2,1,0:T(8,128)(2,1)}, u32[]{:S(2)}) copy-start(bf16[2,16,256]{2,1,0:T(8,128)(2,1)} %param.14) | copy-start | bytes 49156
  32.1 14.5 %collective-permute-start.6 = (f32[16,2304]{1,0:T(8,128)S(1)}, f32[16,2304]{1,0:T(8,128)S(1)}, u32[]{:S(2)}, u32[]{:S(2)}) collective-permute-start(f32[16,2304]{1,0:T(8,128)S(1)} %get-tuple-element.4), channel_id=1, source_target_pairs={{0,12},{4,0},{8,4},{12,8},{1,13},{5,1},{9,5},{13,9},{2,14},{6,2},{... | collective-permute-start | bytes 442376 | tf_op jit(solution)/shard_map/ppermute | solution.py:213
  33.6 17.5 %collective-permute-start.7 = (f32[16,2304]{1,0:T(8,128)S(1)}, f32[16,2304]{1,0:T(8,128)S(1)}, u32[]{:S(2)}, u32[]{:S(2)}) collective-permute-start(f32[16,2304]{1,0:T(8,128)S(1)} %get-tuple-element.3), channel_id=1, source_target_pairs={{0,8},{4,12},{8,0},{12,4},{1,9},{5,13},{9,1},{13,5},{2,10},{6,14},... | collective-permute-start | bytes 442376 | tf_op jit(solution)/shard_map/ppermute | solution.py:213
  38.7 12.4 %collective-permute-start.8 = (f32[16,2304]{1,0:T(8,128)S(1)}, f32[16,2304]{1,0:T(8,128)S(1)}, u32[]{:S(2)}, u32[]{:S(2)}) collective-permute-start(f32[16,2304]{1,0:T(8,128)S(1)} %get-tuple-element.2), channel_id=1, source_target_pairs={{0,4},{4,8},{8,12},{12,0},{1,5},{5,9},{9,13},{13,1},{2,6},{6,10},{... | collective-permute-start | bytes 442376 | tf_op jit(solution)/shard_map/ppermute | solution.py:213
  38.8 0.8 %copy-start = (bf16[2,512,256]{2,1,0:T(8,128)(2,1)}, bf16[2,512,256]{2,1,0:T(8,128)(2,1)S(1)}, u32[]{:S(2)}) copy-start(bf16[2,512,256]{2,1,0:T(8,128)(2,1)S(1)} %constant_dynamic-update-slice_fusion.refs_2_.refs_3_) | copy-start | bytes 1572868
  46.6 4.5 %copy-start.1 = (f32[16,2304]{1,0:T(8,128)}, f32[16,2304]{1,0:T(8,128)S(1)}, u32[]{:S(2)}) copy-start(f32[16,2304]{1,0:T(8,128)S(1)} %collective-permute-done.6.refs_10_.refs_11_) | copy-start | bytes 442372
  51.1 0.7 %copy-start.2 = (f32[16,2304]{1,0:T(8,128)}, f32[16,2304]{1,0:T(8,128)S(1)}, u32[]{:S(2)}) copy-start(f32[16,2304]{1,0:T(8,128)S(1)} %collective-permute-done.7.refs_12_.refs_13_) | copy-start | bytes 442372
  51.1 0.7 %copy-start.3 = (f32[16,2304]{1,0:T(8,128)}, f32[16,2304]{1,0:T(8,128)S(1)}, u32[]{:S(2)}) copy-start(f32[16,2304]{1,0:T(8,128)S(1)} %collective-permute-done.8.refs_14_.refs_15_) | copy-start | bytes 442372

commit v15 on v10

--- a/solution.py
+++ b/solution.py
@@ -17,7 +17,7 @@
     return jnp.repeat(per_head, HD, axis=-1)
 
 
-STACK_ROWS = 512
+STACK_ROWS = 768
 CONTEXT_STACK_ROWS = 256
 
 

time: 52.8 us -> 52.6 us (level)
  transfers between devices with their start and end apart: 9 -> 9, of which waited for: 1 -> 1; matrix products, arithmetic and copies ran while one was open for 14% -> 14% of each run, Pallas kernels for 36% -> 35%
where the time goes in v15:
time: 52.6 us; the launch traced here: 52.2 us
  Pallas kernels  22.2 us (42%)
  starting transfers between devices  13.8 us (26%)
  local copies, waits for them, and re-layouts  7.67 us (15%)
  waiting for transfers between devices  4.09 us (8%)
  other arithmetic  2.84 us (5%)
  between operations  1.5 us (3%)
    pallas_call x3, Pallas kernels, attention(): pl.pallas_call(functools.partial(attention_kernel, masks, normalize, pack...  22.2 us
    ppermute x9, starting transfers between devices, shifted(): lax.ppermute(value, 'ctx', [(j, (j + shift) % count) for j in range(count)])  13.8 us
    unnamed x16, local copies, waits for them, and re-layouts  4.11 us
    ppermute x9, waiting for transfers between devices, shifted(): lax.ppermute(value, 'ctx', [(j, (j + shift) % count) for j in range(count)])  4.09 us
    slice x1, local copies, waits for them, and re-layouts, local(): sections.append(shifted(context_packed[rows], -k, ctx_count))  1.83 us
    concatenate x1, other arithmetic, local(): jnp.concatenate([slot[:split].reshape(own_count, query_width) for slot in...  1.56 us
  transfers between devices with their start and end apart: 9, of which 1 were waited for; matrix products, arithmetic and copies ran while one was open for 14% of the time, Pallas kernels for 35%

profile of v15, /device:TPU:0, one launch (start us, length us, event | category | flops | bytes accessed | tf_op | source)
XLA Modules:
  0.0 52.2 jit_solution(16840193412757600711)
XLA Ops:
  0.6 0.9 %copy.11 = bf16[2,16,8,128]{3,1,2,0:T(8,128)(2,1)S(1)} copy(bf16[2,16,8,128]{3,2,1,0:T(8,128)(2,1)} %bitcast.7) | data formatting | bytes 131072
  1.5 0.7 %copy.12 = bf16[4,2,8,128]{3,1,2,0:T(2,128)(2,1)S(1)} copy(bf16[4,2,8,128]{3,2,1,0:T(8,128)(2,1)} %bitcast.10) | data formatting | bytes 32768
  2.2 5.1 %collective-permute-start.5 = (bf16[40960]{0:T(1024)(128)(2,1)S(1)}, bf16[40960]{0:T(1024)(128)(2,1)S(1)}, u32[]{:S(2)}, u32[]{:S(2)}) collective-permute-start(bf16[40960]{0:T(1024)(128)(2,1)S(1)} %constant_dynamic-update-slice_fusion.5), channel_id=1, source_target_pairs={{0,12},{4,0},{8,4},{12,8},{1,13},{5,1},{9,5},{13,9},{2,14},{6,2},{... | collective-permute-start | bytes 245768 | tf_op jit(solution)/shard_map/ppermute | solution.py:213
  7.3 0.0 collective-permute-start.3
  7.4 1.0 %collective-permute-start.4 = (bf16[40960]{0:T(1024)(128)(2,1)S(1)}, bf16[40960]{0:T(1024)(128)(2,1)S(1)}, u32[]{:S(2)}, u32[]{:S(2)}) collective-permute-start(bf16[40960]{0:T(1024)(128)(2,1)S(1)} %constant_dynamic-update-slice_fusion.5), channel_id=1, source_target_pairs={{0,8},{4,12},{8,0},{12,4},{1,9},{5,13},{9,1},{13,5},{2,10},{6,14},... | collective-permute-start | bytes 245768 | tf_op jit(solution)/shard_map/ppermute | solution.py:213
  8.4 3.4 %collective-permute-start = (bf16[2,128,256]{2,1,0:T(8,128)(2,1)}, bf16[2,128,256]{2,1,0:T(8,128)(2,1)S(1)}, u32[]{:S(2)}, u32[]{:S(2)}) collective-permute-start(bf16[2,128,256]{2,1,0:T(8,128)(2,1)} %param.10), channel_id=1, source_target_pairs={{0,4},{4,8},{8,12},{12,0},{1,5},{5,9},{9,13},{13,1},{2,6},{6,10},{... | collective-permute-start | bytes 393224 | tf_op jit(solution)/shard_map/ppermute | solution.py:213
  11.7 0.0 collective-permute-start.1
  11.7 1.0 %constant_dynamic-update-slice_fusion.3 = bf16[2,512,256]{2,1,0:T(8,128)(2,1)S(1)} fusion(bf16[2,128,256]{2,1,0:T(8,128)(2,1)} %param.10), kind=kLoop, calls=%fused_computation.5 | loop fusion | bytes 262144
  12.7 0.9 %fusion.1 = (s32[16]{0:T(128)S(1)}, s32[16]{0:T(128)S(1)}, s32[16]{0:T(128)S(1)}, s32[16]{0:T(128)S(1)}) fusion(s32[64]{0:T(128)} %param.15, s32[]{:T(128)S(6)} %select_n.32, s32[]{:T(128)S(6)} %select_n.34, s32[]{:T(128)S(6)} %select_n.38, s32[]{:T(128)S(6)} %select_n.36), kind=kLoop, calls=%fused_computation.10 | loop fusion | bytes 528 | tf_op jit(solution)/shard_map/dynamic_slice | solution.py:237
  13.6 0.7 %copy.10.refs_7_ = s32[16,1]{1,0:T(8,128)} copy(s32[16,1]{0,1:T(1,128)S(1)} %bitcast.11) | data formatting | bytes 128 | tf_op jit(solution)/shard_map/reshape | solution.py:168
  15.0 0.7 %add_bitcast_fusion.refs_6_ = s32[1,64]{1,0:T(1,128)} fusion(s32[16]{0:T(128)S(1)} %get-tuple-element.8, s32[16]{0:T(128)S(1)} %get-tuple-element.9, s32[16]{0:T(128)S(1)} %get-tuple-element.7, s32[16]{0:T(128)S(1)} %get-tuple-element.6), kind=kLoop, calls=%fused_computation.8 | loop fusion | flops 192 | bytes 512 | tf_op jit(solution)/shard_map/reshape | solution.py:167
  15.6 0.0 collective-permute-done.5
  15.6 2.3 %collective-permute-start.2 = (bf16[2,128,256]{2,1,0:T(8,128)(2,1)}, bf16[2,128,256]{2,1,0:T(8,128)(2,1)S(1)}, u32[]{:S(2)}, u32[]{:S(2)}) collective-permute-start(bf16[2,128,256]{2,1,0:T(8,128)(2,1)} %param.10), channel_id=1, source_target_pairs={{0,12},{4,0},{8,4},{12,8},{1,13},{5,1},{9,5},{13,9},{2,14},{6,2},{... | collective-permute-start | bytes 393224 | tf_op jit(solution)/shard_map/ppermute | solution.py:213
  18.0 0.0 collective-permute-done.3
  18.1 4.1 %collective-permute-done.4 = bf16[40960]{0:T(1024)(128)(2,1)S(1)} collective-permute-done((bf16[40960]{0:T(1024)(128)(2,1)S(1)}, bf16[40960]{0:T(1024)(128)(2,1)S(1)}, u32[]{:S(2)}, u32[]{:S(2)}) %collective-permute-start.4) | collective-permute-done | bytes 81952 | tf_op jit(solution)/shard_map/ppermute | solution.py:213
  22.2 1.6 %pad_maximum_fusion.refs_1_ = bf16[64,2048]{1,0:T(8,128)(2,1)} fusion(bf16[16,2048]{1,0:T(8,128)(2,1)S(1)} %slice.101, bf16[16,2048]{1,0:T(8,128)(2,1)S(1)} %slice.99, bf16[16,2048]{1,0:T(8,128)(2,1)S(1)} %slice.97, bf16[16,2048]{1,0:T(8,128)(2,1)} %refs_1_.3), kind=kLoop, calls=%fused_computation | loop fusion | flops 1048576 | bytes 524288 | tf_op jit(solution)/shard_map/concatenate | solution.py:228
  23.7 0.0 copy-start.4
  23.7 11.7 %shard_map.96 = f32[64,2304]{1,0:T(8,128)} custom-call(s32[1]{0:T(128)S(6)} %copy.17.refs_0_, bf16[64,2048]{1,0:T(8,128)(2,1)} %pad_maximum_fusion.refs_1_, bf16[2,4096,256]{2,1,0:T(8,128)(2,1)} %refs_3_.1, bf16[2,4096,256]{2,1,0:T(8,128)(2,1)} %refs_3_.1, bf16[2,256,256]{2,1,0:T(8,128)(2,1)} %refs_5_.3, bf16[2,256,256]{2,1,0:T(8,128)(2,1)} %refs_5_.3), custom_call_target="tpu_custom_call" | custom-call | tf_op jit(solution)/shard_map/pallas_call | solution.py:190
  35.5 1.8 %fusion = (f32[16,2304]{1,0:T(8,128)S(1)}, f32[16,2304]{1,0:T(8,128)S(1)}, f32[16,2304]{1,0:T(8,128)S(1)}, f32[16,2304]{1,0:T(8,128)}) fusion(f32[64,2304]{1,0:T(8,128)} %shard_map.96), kind=kLoop, calls=%fused_computation.9 | loop fusion | bytes 1179648 | tf_op jit(solution)/shard_map/slice | solution.py:254
  37.3 0.0 collective-permute-start.6
  37.3 0.0 collective-permute-start.7
  37.4 0.0 copy-done.4
  37.4 0.6 %pad_maximum_fusion.1.refs_4_.refs_5_ = bf16[2,64,256]{2,1,0:T(8,128)(2,1)} fusion(bf16[2,16,256]{2,1,0:T(8,128)(2,1)S(1)} %slice.95, bf16[2,16,256]{2,1,0:T(8,128)(2,1)S(1)} %slice.93, bf16[2,16,256]{2,1,0:T(8,128)(2,1)S(1)} %slice.91, bf16[2,16,256]{2,1,0:T(8,128)(2,1)S(1)} %copy-done.4), kind=kLoop, calls=%fused_computation.1 | loop fusion | flops 262144 | bytes 131072 | tf_op jit(solution)/shard_map/concatenate | solution.py:231
  38.0 0.0 collective-permute-done
  38.0 2.0 %collective-permute-start.8 = (f32[16,2304]{1,0:T(8,128)S(1)}, f32[16,2304]{1,0:T(8,128)S(1)}, u32[]{:S(2)}, u32[]{:S(2)}) collective-permute-start(f32[16,2304]{1,0:T(8,128)S(1)} %get-tuple-element.2), channel_id=1, source_target_pairs={{0,4},{4,8},{8,12},{12,0},{1,5},{5,9},{9,13},{13,1},{2,6},{6,10},{... | collective-permute-start | bytes 442376 | tf_op jit(solution)/shard_map/ppermute | solution.py:213
  40.0 0.0 collective-permute-done.1
  40.1 0.0 collective-permute-done.2
  40.1 0.0 copy-start
  40.1 0.8 %copy-done = bf16[2,512,256]{2,1,0:T(8,128)(2,1)} copy-done((bf16[2,512,256]{2,1,0:T(8,128)(2,1)}, bf16[2,512,256]{2,1,0:T(8,128)(2,1)S(1)}, u32[]{:S(2)}) %copy-start) | copy-done | bytes 524312
  40.9 6.8 %shard_map.95 = bf16[256,2048]{1,0:T(8,128)(2,1)} custom-call(s32[1]{0:T(128)} %constant.35.clone.1.refs_0_, bf16[256,2048]{1,0:T(8,128)(2,1)} %refs_1_.2, bf16[2,512,256]{2,1,0:T(8,128)(2,1)} %copy-done, bf16[2,512,256]{2,1,0:T(8,128)(2,1)} %copy-done, bf16[2,256,256]{2,1,0:T(8,128)(2,1)} %refs_5_.3, bf16[2,256,256]{2,1,0:T(8,128)(2,1)} %refs_5_.3), custom_call_target="tpu_custom_call" | custom-call | tf_op jit(solution)/shard_map/pallas_call | solution.py:190
  47.7 0.0 collective-permute-done.6.refs_10_.refs_11_
  47.7 0.0 copy-start.1
  47.7 0.0 collective-permute-done.7.refs_12_.refs_13_
  47.7 0.0 copy-start.2
  47.7 0.0 collective-permute-done.8.refs_14_.refs_15_
  47.7 0.0 copy-start.3
  47.7 0.6 %copy-done.1 = f32[16,2304]{1,0:T(8,128)} copy-done((f32[16,2304]{1,0:T(8,128)}, f32[16,2304]{1,0:T(8,128)S(1)}, u32[]{:S(2)}) %copy-start.1) | copy-done | bytes 147480
  48.3 0.0 copy-done.2
  48.4 0.1 copy-done.3
  48.4 3.7 %shard_map.97 = bf16[16,2048]{1,0:T(8,128)(2,1)} custom-call(s32[1]{0:T(128)} %constant.35.clone.1.refs_0_, bf16[16,2048]{1,0:T(8,128)(2,1)} %refs_1_.3, bf16[2,512,256]{2,1,0:T(8,128)(2,1)} %copy-done, bf16[2,512,256]{2,1,0:T(8,128)(2,1)} %copy-done, bf16[2,64,256]{2,1,0:T(8,128)(2,1)} %pad_maximum_fusion.1.refs_4_.refs_5_, ...), custom_call_target="tpu_custom_call" | custom-call | tf_op jit(solution)/shard_map/pallas_call | solution.py:190
  (17 shorter events, 0.2 us)
Async XLA Ops:
  2.2 13.4 %collective-permute-start.5 = (bf16[40960]{0:T(1024)(128)(2,1)S(1)}, bf16[40960]{0:T(1024)(128)(2,1)S(1)}, u32[]{:S(2)}, u32[]{:S(2)}) collective-permute-start(bf16[40960]{0:T(1024)(128)(2,1)S(1)} %constant_dynamic-update-slice_fusion.5), channel_id=1, source_target_pairs={{0,12},{4,0},{8,4},{12,8},{1,13},{5,1},{9,5},{13,9},{2,14},{6,2},{... | collective-permute-start | bytes 245768 | tf_op jit(solution)/shard_map/ppermute | solution.py:213
  7.3 10.6 %collective-permute-start.3 = (bf16[40960]{0:T(1024)(128)(2,1)S(1)}, bf16[40960]{0:T(1024)(128)(2,1)S(1)}, u32[]{:S(2)}, u32[]{:S(2)}) collective-permute-start(bf16[40960]{0:T(1024)(128)(2,1)S(1)} %constant_dynamic-update-slice_fusion.5), channel_id=1, source_target_pairs={{0,4},{4,8},{8,12},{12,0},{1,5},{5,9},{9,13},{13,1},{2,6},{6,10},{... | collective-permute-start | bytes 245768 | tf_op jit(solution)/shard_map/ppermute | solution.py:213
  7.4 14.8 %collective-permute-start.4 = (bf16[40960]{0:T(1024)(128)(2,1)S(1)}, bf16[40960]{0:T(1024)(128)(2,1)S(1)}, u32[]{:S(2)}, u32[]{:S(2)}) collective-permute-start(bf16[40960]{0:T(1024)(128)(2,1)S(1)} %constant_dynamic-update-slice_fusion.5), channel_id=1, source_target_pairs={{0,8},{4,12},{8,0},{12,4},{1,9},{5,13},{9,1},{13,5},{2,10},{6,14},... | collective-permute-start | bytes 245768 | tf_op jit(solution)/shard_map/ppermute | solution.py:213
  8.4 29.7 %collective-permute-start = (bf16[2,128,256]{2,1,0:T(8,128)(2,1)}, bf16[2,128,256]{2,1,0:T(8,128)(2,1)S(1)}, u32[]{:S(2)}, u32[]{:S(2)}) collective-permute-start(bf16[2,128,256]{2,1,0:T(8,128)(2,1)} %param.10), channel_id=1, source_target_pairs={{0,4},{4,8},{8,12},{12,0},{1,5},{5,9},{9,13},{13,1},{2,6},{6,10},{... | collective-permute-start | bytes 393224 | tf_op jit(solution)/shard_map/ppermute | solution.py:213
  11.7 28.3 %collective-permute-start.1 = (bf16[2,128,256]{2,1,0:T(8,128)(2,1)}, bf16[2,128,256]{2,1,0:T(8,128)(2,1)S(1)}, u32[]{:S(2)}, u32[]{:S(2)}) collective-permute-start(bf16[2,128,256]{2,1,0:T(8,128)(2,1)} %param.10), channel_id=1, source_target_pairs={{0,8},{4,12},{8,0},{12,4},{1,9},{5,13},{9,1},{13,5},{2,10},{6,14},... | collective-permute-start | bytes 393224 | tf_op jit(solution)/shard_map/ppermute | solution.py:213
  15.6 24.5 %collective-permute-start.2 = (bf16[2,128,256]{2,1,0:T(8,128)(2,1)}, bf16[2,128,256]{2,1,0:T(8,128)(2,1)S(1)}, u32[]{:S(2)}, u32[]{:S(2)}) collective-permute-start(bf16[2,128,256]{2,1,0:T(8,128)(2,1)} %param.10), channel_id=1, source_target_pairs={{0,12},{4,0},{8,4},{12,8},{1,13},{5,1},{9,5},{13,9},{2,14},{6,2},{... | collective-permute-start | bytes 393224 | tf_op jit(solution)/shard_map/ppermute | solution.py:213
  23.7 13.7 %copy-start.4 = (bf16[2,16,256]{2,1,0:T(8,128)(2,1)S(1)}, bf16[2,16,256]{2,1,0:T(8,128)(2,1)}, u32[]{:S(2)}) copy-start(bf16[2,16,256]{2,1,0:T(8,128)(2,1)} %param.14) | copy-start | bytes 49156
  37.3 10.4 %collective-permute-start.6 = (f32[16,2304]{1,0:T(8,128)S(1)}, f32[16,2304]{1,0:T(8,128)S(1)}, u32[]{:S(2)}, u32[]{:S(2)}) collective-permute-start(f32[16,2304]{1,0:T(8,128)S(1)} %get-tuple-element.4), channel_id=1, source_target_pairs={{0,12},{4,0},{8,4},{12,8},{1,13},{5,1},{9,5},{13,9},{2,14},{6,2},{... | collective-permute-start | bytes 442376 | tf_op jit(solution)/shard_map/ppermute | solution.py:213
  37.3 10.4 %collective-permute-start.7 = (f32[16,2304]{1,0:T(8,128)S(1)}, f32[16,2304]{1,0:T(8,128)S(1)}, u32[]{:S(2)}, u32[]{:S(2)}) collective-permute-start(f32[16,2304]{1,0:T(8,128)S(1)} %get-tuple-element.3), channel_id=1, source_target_pairs={{0,8},{4,12},{8,0},{12,4},{1,9},{5,13},{9,1},{13,5},{2,10},{6,14},... | collective-permute-start | bytes 442376 | tf_op jit(solution)/shard_map/ppermute | solution.py:213
  38.0 9.7 %collective-permute-start.8 = (f32[16,2304]{1,0:T(8,128)S(1)}, f32[16,2304]{1,0:T(8,128)S(1)}, u32[]{:S(2)}, u32[]{:S(2)}) collective-permute-start(f32[16,2304]{1,0:T(8,128)S(1)} %get-tuple-element.2), channel_id=1, source_target_pairs={{0,4},{4,8},{8,12},{12,0},{1,5},{5,9},{9,13},{13,1},{2,6},{6,10},{... | collective-permute-start | bytes 442376 | tf_op jit(solution)/shard_map/ppermute | solution.py:213
  40.1 0.8 %copy-start = (bf16[2,512,256]{2,1,0:T(8,128)(2,1)}, bf16[2,512,256]{2,1,0:T(8,128)(2,1)S(1)}, u32[]{:S(2)}) copy-start(bf16[2,512,256]{2,1,0:T(8,128)(2,1)S(1)} %constant_dynamic-update-slice_fusion.refs_2_.refs_3_) | copy-start | bytes 1572868
  47.7 0.7 %copy-start.1 = (f32[16,2304]{1,0:T(8,128)}, f32[16,2304]{1,0:T(8,128)S(1)}, u32[]{:S(2)}) copy-start(f32[16,2304]{1,0:T(8,128)S(1)} %collective-permute-done.6.refs_10_.refs_11_) | copy-start | bytes 442372
  47.7 0.7 %copy-start.2 = (f32[16,2304]{1,0:T(8,128)}, f32[16,2304]{1,0:T(8,128)S(1)}, u32[]{:S(2)}) copy-start(f32[16,2304]{1,0:T(8,128)S(1)} %collective-permute-done.7.refs_12_.refs_13_) | copy-start | bytes 442372
  47.7 0.7 %copy-start.3 = (f32[16,2304]{1,0:T(8,128)}, f32[16,2304]{1,0:T(8,128)S(1)}, u32[]{:S(2)}) copy-start(f32[16,2304]{1,0:T(8,128)S(1)} %collective-permute-done.8.refs_14_.refs_15_) | copy-start | bytes 442372

commit v16 on v15

--- a/solution.py
+++ b/solution.py
@@ -48,11 +48,12 @@
             cols = lax.broadcasted_iota(jnp.int32, shape, 1)
             visible.append(cols < length_ref[0])
         elif mask == "causal":
-            cols = lax.broadcasted_iota(jnp.int32, shape, 1)
-            tokens = lax.broadcasted_iota(jnp.int32, shape, 0)
+            cols = lax.broadcasted_iota(jnp.int32, (rows, key_count), 1)
+            tokens = lax.broadcasted_iota(jnp.int32, (rows, key_count), 0)
+            causal = cols <= tokens
             if stack > 1:
-                tokens = lax.rem(tokens, rows)
-            visible.append(cols <= tokens)
+                causal = jnp.concatenate([causal] * stack, axis=0)
+            visible.append(causal)
         else:
             own = own_pos_ref[...]
             if stack > 1:

time: 52.6 us -> 52.5 us (level)
  no operation moved by 1% of the time
where the time goes in v16:
time: 52.5 us; the launch traced here: 52.2 us
  Pallas kernels  22.2 us (42%)
  starting transfers between devices  13.8 us (26%)
  local copies, waits for them, and re-layouts  7.67 us (15%)
  waiting for transfers between devices  4.09 us (8%)
  other arithmetic  2.84 us (5%)
  between operations  1.5 us (3%)
    pallas_call x3, Pallas kernels, attention(): pl.pallas_call(functools.partial(attention_kernel, masks, normalize, pack...  22.2 us
    ppermute x9, starting transfers between devices, shifted(): lax.ppermute(value, 'ctx', [(j, (j + shift) % count) for j in range(count)])  13.8 us
    unnamed x16, local copies, waits for them, and re-layouts  4.11 us
    ppermute x9, waiting for transfers between devices, shifted(): lax.ppermute(value, 'ctx', [(j, (j + shift) % count) for j in range(count)])  4.09 us
    slice x1, local copies, waits for them, and re-layouts, local(): sections.append(shifted(context_packed[rows], -k, ctx_count))  1.83 us
    concatenate x1, other arithmetic, local(): jnp.concatenate([slot[:split].reshape(own_count, query_width) for slot in...  1.56 us
  transfers between devices with their start and end apart: 9, of which 1 were waited for; matrix products, arithmetic and copies ran while one was open for 14% of the time, Pallas kernels for 35%

profile of v16, /device:TPU:0, one launch (start us, length us, event | category | flops | bytes accessed | tf_op | source)
XLA Modules:
  0.0 52.2 jit_solution(3289060855739058924)
XLA Ops:
  0.6 0.9 %copy.11 = bf16[2,16,8,128]{3,1,2,0:T(8,128)(2,1)S(1)} copy(bf16[2,16,8,128]{3,2,1,0:T(8,128)(2,1)} %bitcast.7) | data formatting | bytes 131072
  1.5 0.7 %copy.12 = bf16[4,2,8,128]{3,1,2,0:T(2,128)(2,1)S(1)} copy(bf16[4,2,8,128]{3,2,1,0:T(8,128)(2,1)} %bitcast.10) | data formatting | bytes 32768
  2.2 5.1 %collective-permute-start.5 = (bf16[40960]{0:T(1024)(128)(2,1)S(1)}, bf16[40960]{0:T(1024)(128)(2,1)S(1)}, u32[]{:S(2)}, u32[]{:S(2)}) collective-permute-start(bf16[40960]{0:T(1024)(128)(2,1)S(1)} %constant_dynamic-update-slice_fusion.5), channel_id=1, source_target_pairs={{0,12},{4,0},{8,4},{12,8},{1,13},{5,1},{9,5},{13,9},{2,14},{6,2},{... | collective-permute-start | bytes 245768 | tf_op jit(solution)/shard_map/ppermute | solution.py:214
  7.3 0.0 collective-permute-start.3
  7.4 1.0 %collective-permute-start.4 = (bf16[40960]{0:T(1024)(128)(2,1)S(1)}, bf16[40960]{0:T(1024)(128)(2,1)S(1)}, u32[]{:S(2)}, u32[]{:S(2)}) collective-permute-start(bf16[40960]{0:T(1024)(128)(2,1)S(1)} %constant_dynamic-update-slice_fusion.5), channel_id=1, source_target_pairs={{0,8},{4,12},{8,0},{12,4},{1,9},{5,13},{9,1},{13,5},{2,10},{6,14},... | collective-permute-start | bytes 245768 | tf_op jit(solution)/shard_map/ppermute | solution.py:214
  8.4 3.4 %collective-permute-start = (bf16[2,128,256]{2,1,0:T(8,128)(2,1)}, bf16[2,128,256]{2,1,0:T(8,128)(2,1)S(1)}, u32[]{:S(2)}, u32[]{:S(2)}) collective-permute-start(bf16[2,128,256]{2,1,0:T(8,128)(2,1)} %param.10), channel_id=1, source_target_pairs={{0,4},{4,8},{8,12},{12,0},{1,5},{5,9},{9,13},{13,1},{2,6},{6,10},{... | collective-permute-start | bytes 393224 | tf_op jit(solution)/shard_map/ppermute | solution.py:214
  11.7 0.0 collective-permute-start.1
  11.7 1.0 %constant_dynamic-update-slice_fusion.3 = bf16[2,512,256]{2,1,0:T(8,128)(2,1)S(1)} fusion(bf16[2,128,256]{2,1,0:T(8,128)(2,1)} %param.10), kind=kLoop, calls=%fused_computation.5 | loop fusion | bytes 262144
  12.7 0.9 %fusion.1 = (s32[16]{0:T(128)S(1)}, s32[16]{0:T(128)S(1)}, s32[16]{0:T(128)S(1)}, s32[16]{0:T(128)S(1)}) fusion(s32[64]{0:T(128)} %param.15, s32[]{:T(128)S(6)} %select_n.32, s32[]{:T(128)S(6)} %select_n.34, s32[]{:T(128)S(6)} %select_n.38, s32[]{:T(128)S(6)} %select_n.36), kind=kLoop, calls=%fused_computation.10 | loop fusion | bytes 528 | tf_op jit(solution)/shard_map/dynamic_slice | solution.py:238
  13.6 0.7 %copy.10.refs_7_ = s32[16,1]{1,0:T(8,128)} copy(s32[16,1]{0,1:T(1,128)S(1)} %bitcast.11) | data formatting | bytes 128 | tf_op jit(solution)/shard_map/reshape | solution.py:169
  15.0 0.7 %add_bitcast_fusion.refs_6_ = s32[1,64]{1,0:T(1,128)} fusion(s32[16]{0:T(128)S(1)} %get-tuple-element.8, s32[16]{0:T(128)S(1)} %get-tuple-element.9, s32[16]{0:T(128)S(1)} %get-tuple-element.7, s32[16]{0:T(128)S(1)} %get-tuple-element.6), kind=kLoop, calls=%fused_computation.8 | loop fusion | flops 192 | bytes 512 | tf_op jit(solution)/shard_map/reshape | solution.py:168
  15.6 0.0 collective-permute-done.5
  15.6 2.3 %collective-permute-start.2 = (bf16[2,128,256]{2,1,0:T(8,128)(2,1)}, bf16[2,128,256]{2,1,0:T(8,128)(2,1)S(1)}, u32[]{:S(2)}, u32[]{:S(2)}) collective-permute-start(bf16[2,128,256]{2,1,0:T(8,128)(2,1)} %param.10), channel_id=1, source_target_pairs={{0,12},{4,0},{8,4},{12,8},{1,13},{5,1},{9,5},{13,9},{2,14},{6,2},{... | collective-permute-start | bytes 393224 | tf_op jit(solution)/shard_map/ppermute | solution.py:214
  18.0 0.0 collective-permute-done.3
  18.1 4.1 %collective-permute-done.4 = bf16[40960]{0:T(1024)(128)(2,1)S(1)} collective-permute-done((bf16[40960]{0:T(1024)(128)(2,1)S(1)}, bf16[40960]{0:T(1024)(128)(2,1)S(1)}, u32[]{:S(2)}, u32[]{:S(2)}) %collective-permute-start.4) | collective-permute-done | bytes 81952 | tf_op jit(solution)/shard_map/ppermute | solution.py:214
  22.2 1.6 %pad_maximum_fusion.refs_1_ = bf16[64,2048]{1,0:T(8,128)(2,1)} fusion(bf16[16,2048]{1,0:T(8,128)(2,1)S(1)} %slice.101, bf16[16,2048]{1,0:T(8,128)(2,1)S(1)} %slice.99, bf16[16,2048]{1,0:T(8,128)(2,1)S(1)} %slice.97, bf16[16,2048]{1,0:T(8,128)(2,1)} %refs_1_.3), kind=kLoop, calls=%fused_computation | loop fusion | flops 1048576 | bytes 524288 | tf_op jit(solution)/shard_map/concatenate | solution.py:229
  23.7 0.0 copy-start.4
  23.7 11.7 %shard_map.96 = f32[64,2304]{1,0:T(8,128)} custom-call(s32[1]{0:T(128)S(6)} %copy.17.refs_0_, bf16[64,2048]{1,0:T(8,128)(2,1)} %pad_maximum_fusion.refs_1_, bf16[2,4096,256]{2,1,0:T(8,128)(2,1)} %refs_3_.1, bf16[2,4096,256]{2,1,0:T(8,128)(2,1)} %refs_3_.1, bf16[2,256,256]{2,1,0:T(8,128)(2,1)} %refs_5_.3, bf16[2,256,256]{2,1,0:T(8,128)(2,1)} %refs_5_.3), custom_call_target="tpu_custom_call" | custom-call | tf_op jit(solution)/shard_map/pallas_call | solution.py:191
  35.5 1.8 %fusion = (f32[16,2304]{1,0:T(8,128)S(1)}, f32[16,2304]{1,0:T(8,128)S(1)}, f32[16,2304]{1,0:T(8,128)S(1)}, f32[16,2304]{1,0:T(8,128)}) fusion(f32[64,2304]{1,0:T(8,128)} %shard_map.96), kind=kLoop, calls=%fused_computation.9 | loop fusion | bytes 1179648 | tf_op jit(solution)/shard_map/slice | solution.py:255
  37.3 0.0 collective-permute-start.6
  37.3 0.0 collective-permute-start.7
  37.4 0.0 copy-done.4
  37.4 0.6 %pad_maximum_fusion.1.refs_4_.refs_5_ = bf16[2,64,256]{2,1,0:T(8,128)(2,1)} fusion(bf16[2,16,256]{2,1,0:T(8,128)(2,1)S(1)} %slice.95, bf16[2,16,256]{2,1,0:T(8,128)(2,1)S(1)} %slice.93, bf16[2,16,256]{2,1,0:T(8,128)(2,1)S(1)} %slice.91, bf16[2,16,256]{2,1,0:T(8,128)(2,1)S(1)} %copy-done.4), kind=kLoop, calls=%fused_computation.1 | loop fusion | flops 262144 | bytes 131072 | tf_op jit(solution)/shard_map/concatenate | solution.py:232
  38.0 0.0 collective-permute-done
  38.0 2.0 %collective-permute-start.8 = (f32[16,2304]{1,0:T(8,128)S(1)}, f32[16,2304]{1,0:T(8,128)S(1)}, u32[]{:S(2)}, u32[]{:S(2)}) collective-permute-start(f32[16,2304]{1,0:T(8,128)S(1)} %get-tuple-element.2), channel_id=1, source_target_pairs={{0,4},{4,8},{8,12},{12,0},{1,5},{5,9},{9,13},{13,1},{2,6},{6,10},{... | collective-permute-start | bytes 442376 | tf_op jit(solution)/shard_map/ppermute | solution.py:214
  40.0 0.0 collective-permute-done.1
  40.1 0.0 collective-permute-done.2
  40.1 0.0 copy-start
  40.1 0.8 %copy-done = bf16[2,512,256]{2,1,0:T(8,128)(2,1)} copy-done((bf16[2,512,256]{2,1,0:T(8,128)(2,1)}, bf16[2,512,256]{2,1,0:T(8,128)(2,1)S(1)}, u32[]{:S(2)}) %copy-start) | copy-done | bytes 524312
  40.9 6.8 %shard_map.95 = bf16[256,2048]{1,0:T(8,128)(2,1)} custom-call(s32[1]{0:T(128)} %constant.35.clone.1.refs_0_, bf16[256,2048]{1,0:T(8,128)(2,1)} %refs_1_.2, bf16[2,512,256]{2,1,0:T(8,128)(2,1)} %copy-done, bf16[2,512,256]{2,1,0:T(8,128)(2,1)} %copy-done, bf16[2,256,256]{2,1,0:T(8,128)(2,1)} %refs_5_.3, bf16[2,256,256]{2,1,0:T(8,128)(2,1)} %refs_5_.3), custom_call_target="tpu_custom_call" | custom-call | tf_op jit(solution)/shard_map/pallas_call | solution.py:191
  47.7 0.0 collective-permute-done.6.refs_10_.refs_11_
  47.7 0.0 copy-start.1
  47.7 0.0 collective-permute-done.7.refs_12_.refs_13_
  47.7 0.0 copy-start.2
  47.7 0.0 collective-permute-done.8.refs_14_.refs_15_
  47.7 0.0 copy-start.3
  47.7 0.6 %copy-done.1 = f32[16,2304]{1,0:T(8,128)} copy-done((f32[16,2304]{1,0:T(8,128)}, f32[16,2304]{1,0:T(8,128)S(1)}, u32[]{:S(2)}) %copy-start.1) | copy-done | bytes 147480
  48.3 0.0 copy-done.2
  48.4 0.1 copy-done.3
  48.4 3.7 %shard_map.97 = bf16[16,2048]{1,0:T(8,128)(2,1)} custom-call(s32[1]{0:T(128)} %constant.35.clone.1.refs_0_, bf16[16,2048]{1,0:T(8,128)(2,1)} %refs_1_.3, bf16[2,512,256]{2,1,0:T(8,128)(2,1)} %copy-done, bf16[2,512,256]{2,1,0:T(8,128)(2,1)} %copy-done, bf16[2,64,256]{2,1,0:T(8,128)(2,1)} %pad_maximum_fusion.1.refs_4_.refs_5_, ...), custom_call_target="tpu_custom_call" | custom-call | tf_op jit(solution)/shard_map/pallas_call | solution.py:191
  (17 shorter events, 0.2 us)
Async XLA Ops:
  2.2 13.4 %collective-permute-start.5 = (bf16[40960]{0:T(1024)(128)(2,1)S(1)}, bf16[40960]{0:T(1024)(128)(2,1)S(1)}, u32[]{:S(2)}, u32[]{:S(2)}) collective-permute-start(bf16[40960]{0:T(1024)(128)(2,1)S(1)} %constant_dynamic-update-slice_fusion.5), channel_id=1, source_target_pairs={{0,12},{4,0},{8,4},{12,8},{1,13},{5,1},{9,5},{13,9},{2,14},{6,2},{... | collective-permute-start | bytes 245768 | tf_op jit(solution)/shard_map/ppermute | solution.py:214
  7.3 10.6 %collective-permute-start.3 = (bf16[40960]{0:T(1024)(128)(2,1)S(1)}, bf16[40960]{0:T(1024)(128)(2,1)S(1)}, u32[]{:S(2)}, u32[]{:S(2)}) collective-permute-start(bf16[40960]{0:T(1024)(128)(2,1)S(1)} %constant_dynamic-update-slice_fusion.5), channel_id=1, source_target_pairs={{0,4},{4,8},{8,12},{12,0},{1,5},{5,9},{9,13},{13,1},{2,6},{6,10},{... | collective-permute-start | bytes 245768 | tf_op jit(solution)/shard_map/ppermute | solution.py:214
  7.4 14.8 %collective-permute-start.4 = (bf16[40960]{0:T(1024)(128)(2,1)S(1)}, bf16[40960]{0:T(1024)(128)(2,1)S(1)}, u32[]{:S(2)}, u32[]{:S(2)}) collective-permute-start(bf16[40960]{0:T(1024)(128)(2,1)S(1)} %constant_dynamic-update-slice_fusion.5), channel_id=1, source_target_pairs={{0,8},{4,12},{8,0},{12,4},{1,9},{5,13},{9,1},{13,5},{2,10},{6,14},... | collective-permute-start | bytes 245768 | tf_op jit(solution)/shard_map/ppermute | solution.py:214
  8.4 29.7 %collective-permute-start = (bf16[2,128,256]{2,1,0:T(8,128)(2,1)}, bf16[2,128,256]{2,1,0:T(8,128)(2,1)S(1)}, u32[]{:S(2)}, u32[]{:S(2)}) collective-permute-start(bf16[2,128,256]{2,1,0:T(8,128)(2,1)} %param.10), channel_id=1, source_target_pairs={{0,4},{4,8},{8,12},{12,0},{1,5},{5,9},{9,13},{13,1},{2,6},{6,10},{... | collective-permute-start | bytes 393224 | tf_op jit(solution)/shard_map/ppermute | solution.py:214
  11.7 28.3 %collective-permute-start.1 = (bf16[2,128,256]{2,1,0:T(8,128)(2,1)}, bf16[2,128,256]{2,1,0:T(8,128)(2,1)S(1)}, u32[]{:S(2)}, u32[]{:S(2)}) collective-permute-start(bf16[2,128,256]{2,1,0:T(8,128)(2,1)} %param.10), channel_id=1, source_target_pairs={{0,8},{4,12},{8,0},{12,4},{1,9},{5,13},{9,1},{13,5},{2,10},{6,14},... | collective-permute-start | bytes 393224 | tf_op jit(solution)/shard_map/ppermute | solution.py:214
  15.6 24.5 %collective-permute-start.2 = (bf16[2,128,256]{2,1,0:T(8,128)(2,1)}, bf16[2,128,256]{2,1,0:T(8,128)(2,1)S(1)}, u32[]{:S(2)}, u32[]{:S(2)}) collective-permute-start(bf16[2,128,256]{2,1,0:T(8,128)(2,1)} %param.10), channel_id=1, source_target_pairs={{0,12},{4,0},{8,4},{12,8},{1,13},{5,1},{9,5},{13,9},{2,14},{6,2},{... | collective-permute-start | bytes 393224 | tf_op jit(solution)/shard_map/ppermute | solution.py:214
  23.7 13.7 %copy-start.4 = (bf16[2,16,256]{2,1,0:T(8,128)(2,1)S(1)}, bf16[2,16,256]{2,1,0:T(8,128)(2,1)}, u32[]{:S(2)}) copy-start(bf16[2,16,256]{2,1,0:T(8,128)(2,1)} %param.14) | copy-start | bytes 49156
  37.3 10.4 %collective-permute-start.6 = (f32[16,2304]{1,0:T(8,128)S(1)}, f32[16,2304]{1,0:T(8,128)S(1)}, u32[]{:S(2)}, u32[]{:S(2)}) collective-permute-start(f32[16,2304]{1,0:T(8,128)S(1)} %get-tuple-element.4), channel_id=1, source_target_pairs={{0,12},{4,0},{8,4},{12,8},{1,13},{5,1},{9,5},{13,9},{2,14},{6,2},{... | collective-permute-start | bytes 442376 | tf_op jit(solution)/shard_map/ppermute | solution.py:214
  37.3 10.4 %collective-permute-start.7 = (f32[16,2304]{1,0:T(8,128)S(1)}, f32[16,2304]{1,0:T(8,128)S(1)}, u32[]{:S(2)}, u32[]{:S(2)}) collective-permute-start(f32[16,2304]{1,0:T(8,128)S(1)} %get-tuple-element.3), channel_id=1, source_target_pairs={{0,8},{4,12},{8,0},{12,4},{1,9},{5,13},{9,1},{13,5},{2,10},{6,14},... | collective-permute-start | bytes 442376 | tf_op jit(solution)/shard_map/ppermute | solution.py:214
  38.0 9.7 %collective-permute-start.8 = (f32[16,2304]{1,0:T(8,128)S(1)}, f32[16,2304]{1,0:T(8,128)S(1)}, u32[]{:S(2)}, u32[]{:S(2)}) collective-permute-start(f32[16,2304]{1,0:T(8,128)S(1)} %get-tuple-element.2), channel_id=1, source_target_pairs={{0,4},{4,8},{8,12},{12,0},{1,5},{5,9},{9,13},{13,1},{2,6},{6,10},{... | collective-permute-start | bytes 442376 | tf_op jit(solution)/shard_map/ppermute | solution.py:214
  40.1 0.8 %copy-start = (bf16[2,512,256]{2,1,0:T(8,128)(2,1)}, bf16[2,512,256]{2,1,0:T(8,128)(2,1)S(1)}, u32[]{:S(2)}) copy-start(bf16[2,512,256]{2,1,0:T(8,128)(2,1)S(1)} %constant_dynamic-update-slice_fusion.refs_2_.refs_3_) | copy-start | bytes 1572868
  47.7 0.7 %copy-start.1 = (f32[16,2304]{1,0:T(8,128)}, f32[16,2304]{1,0:T(8,128)S(1)}, u32[]{:S(2)}) copy-start(f32[16,2304]{1,0:T(8,128)S(1)} %collective-permute-done.6.refs_10_.refs_11_) | copy-start | bytes 442372
  47.7 0.7 %copy-start.2 = (f32[16,2304]{1,0:T(8,128)}, f32[16,2304]{1,0:T(8,128)S(1)}, u32[]{:S(2)}) copy-start(f32[16,2304]{1,0:T(8,128)S(1)} %collective-permute-done.7.refs_12_.refs_13_) | copy-start | bytes 442372
  47.7 0.7 %copy-start.3 = (f32[16,2304]{1,0:T(8,128)}, f32[16,2304]{1,0:T(8,128)S(1)}, u32[]{:S(2)}) copy-start(f32[16,2304]{1,0:T(8,128)S(1)} %collective-permute-done.8.refs_14_.refs_15_) | copy-start | bytes 442372
